TPU v7x, 512 devices: a whole 4x4x16 slice. The times are simulated.
512 devices in a mesh: row: 32 (over z, x_hi), col: 16 (over y, x_lo, core).
Axes of the slice: x: 4 (x_hi: 2, x_lo: 2; x = x_hi * 2 + x_lo), y: 4, z: 16, core: 2. Of those that a mesh axis runs over, the one named last changes fastest.
Arguments:
- features: bfloat16 [48, 2048, 2048], P(None, 'row', 'col'), may hold values from -6 to 6
- w_dilated: bfloat16 [2, 3, 3, 48, 48], replicated, may hold values from -0.3125 to 0.3125
- w_pointwise: bfloat16 [2, 48, 48], replicated, may hold values from -0.875 to 0.875
- norm_gain: float32 [2, 2, 48], replicated, may hold values from 0.25 to 1.75
- norm_bias: float32 [2, 2, 48], replicated, may hold values from -0.5 to 0.5
Outputs:
- refined: bfloat16 [48, 2048, 2048], P(None, 'row', 'col')
All inputs are finite; a program needn't handle non-finite values.
Results may differ from a plain program's by a relative error of at most 0.0065.
Values may be sent and summed in bfloat16 or wider, within the bound.
No kernel may reach another device: no remote copies, remote signals or barrier semaphores. Data moves between devices by JAX's collectives and lax.ppermute only.
A program may use at most 64 MiB of HBM per device.

v0:
```python
import jax
import jax.numpy as jnp
from jax import lax
from jax.sharding import PartitionSpec as P

FIRST_DILATION = 8
SECOND_DILATION = 16


def padded(value, sides, width):
    for axis, dim in sides:
        size, length = (lax.axis_size(axis), value.shape[dim])
        up = [(i, (i + 1) % size) for i in range(size - 1)]
        down = [(j, i) for i, j in up]
        last = lax.slice_in_dim(value, length - width, length, axis=dim)
        initial = lax.slice_in_dim(value, 0, width, axis=dim)
        before = lax.ppermute(last, axis, up)
        after = lax.ppermute(initial, axis, down)
        value = jnp.concatenate([before, value, after], axis=dim)
    return value


def dilated_terms(
    extended_input, current_state, kernel, gain_pair, bias_pair, pointwise, dilation_rate
):
    active = jnp.maximum(extended_input, jnp.zeros((), extended_input.dtype))
    spread = lax.conv_general_dilated(
        active[None],
        kernel,
        (1, 1),
        "VALID",
        rhs_dilation=(dilation_rate, dilation_rate),
        preferred_element_type=jnp.float32,
    )[0]
    hidden = jnp.maximum(
        spread * gain_pair[0][:, None, None] + bias_pair[0][:, None, None], 0.0
    ).astype(jnp.bfloat16)
    branch = jnp.einsum("oc,chw->ohw", pointwise, hidden, preferred_element_type=jnp.float32)
    summed = (
        current_state.astype(jnp.float32)
        + branch * gain_pair[1][:, None, None]
        + bias_pair[1][:, None, None]
    )
    return summed.astype(jnp.bfloat16)


def mirror_tile(output_map):
    n_row = lax.axis_size("row")
    n_col = lax.axis_size("col")
    channel_count, tile_rows, tile_cols = output_map.shape
    sub_rows = tile_rows // n_col
    ratio = n_row // n_col
    first_leg = lax.all_to_all(output_map, "col", split_axis=1, concat_axis=2, tiled=True)
    count = first_leg.shape[0]
    moved = lax.all_to_all(
        lax.all_to_all(first_leg, "row", split_axis=2, concat_axis=1, tiled=True),
        "col",
        split_axis=1,
        concat_axis=1,
        tiled=True,
    )
    grouped = moved.reshape(count, n_col, ratio, sub_rows, tile_rows)
    return jnp.transpose(grouped, (0, 4, 2, 1, 3)).reshape(count, tile_rows, tile_cols)


def body(features, w_dilated, w_pointwise, norm_gain, norm_bias):
    current_state = features
    for layer_index in range(2):
        if layer_index == 0:
            dilation_rate = FIRST_DILATION
            extended_input = padded(current_state, (("row", 1), ("col", 2)), FIRST_DILATION)
        else:
            dilation_rate = SECOND_DILATION
            extended_input = padded(current_state, (("row", 1), ("col", 2)), SECOND_DILATION)
        kernel = jnp.transpose(w_dilated[layer_index], (2, 3, 0, 1))
        output_map = dilated_terms(
            extended_input,
            current_state,
            kernel,
            norm_gain[layer_index],
            norm_bias[layer_index],
            w_pointwise[layer_index],
            dilation_rate,
        )
        if layer_index == 0:
            mirrored = mirror_tile(output_map)
        else:
            mirrored = mirror_tile(output_map)
        output_map, mirrored = lax.optimization_barrier((output_map, mirrored))
        current_state = (
            (output_map.astype(jnp.float32) + mirrored.astype(jnp.float32)) * 0.5
        ).astype(jnp.bfloat16)
    return current_state


def solution(mesh):
    in_specs = (P(None, "row", "col"), P(), P(), P(), P())
    out_specs = P(None, "row", "col")
    return jax.shard_map(body, mesh=mesh, in_specs=in_specs, out_specs=out_specs, check_vma=False)
```

profile of v0, /device:TPU:7, one launch (start us, length us, event | category | flops | bytes accessed | tf_op | source)
XLA Modules:
  0.0 368.4 jit_solution(10828960028243920198)
XLA Ops:
  1.0 4.4 %collective-permute-start = (bf16[48,8,128]{2,1,0:T(8,128)(2,1)S(1)}, bf16[48,8,128]{2,1,0:T(8,128)(2,1)S(1)}, u32[]{:S(2)}, u32[]{:S(2)}) collective-permute-start(bf16[48,8,128]{2,1,0:T(8,128)(2,1)S(1)} %get-tuple-element.19), channel_id=1, source_target_pairs={{0,16},{16,32},{32,48},{48,64},{64,80},{80,96},{96,112},{112,128},... | collective-permute-start | bytes 294920 | tf_op jit(solution)/shard_map/ppermute | solution.py:17
  15.8 3.0 pad_maximum_fusion
  18.8 4.6 %collective-permute-start.2 = (bf16[48,80,8]{1,0,2:T(8,128)(2,1)S(1)}, bf16[48,80,8]{1,0,2:T(8,128)(2,1)S(1)}, u32[]{:S(2)}, u32[]{:S(2)}) collective-permute-start(bf16[48,80,8]{1,0,2:T(8,128)(2,1)S(1)} %get-tuple-element.17), channel_id=1, source_target_pairs={{0,1},{1,2},{2,3},{3,4},{4,5},{5,6},{6,7},{7,8},{8,9},{9,10},{10,1... | collective-permute-start | bytes 184328 | tf_op jit(solution)/shard_map/ppermute | solution.py:17
  27.3 2.9 collective-permute-done.3
  31.9 3.6 copy.111
  36.5 7.9 %maximum_convert_fusion = bf16[64,8,18,48]{3,1,2,0:T(8,128)(2,1)} fusion(f32[48]{0:T(128)S(1)} %get-tuple-element.27, f32[48]{0:T(128)S(1)} %get-tuple-element.30, pred[8,18]{0,1:T(8,128)(4,1)S(1)} %copy-done.6, bf16[48,80,1,7,16]{0,3,4,1,2:T(8,128)(2,1)S(1)} %slice.104, bf16[48,80,1,8,18]{0,3,4,1,2:T(8,128)(2,1)S(1)} %copy.111, ...), kind=kOutput, calls=%fused_computation.8 | convolution fusion | flops 390684672 | bytes 6569984 | tf_op jit(solution)/shard_map/conv_general_dilated | solution.py:27
  44.4 3.6 copy.112
  53.8 3.0 fusion.11
  57.6 17.8 %all_to_all.82 = bf16[48,64,128]{2,0,1:T(8,128)(2,1)S(1)} all-to-all(bf16[48,64,128]{2,0,1:T(8,128)(2,1)S(1)} %copy.115), channel_id=1, replica_groups=mesh['row'=32,'col'=16] {'col'}, dimensions={1} | all-to-all | bytes 1572864 | tf_op jit(solution)/shard_map/all_to_all | solution.py:53
  75.4 2.5 copy.136
  77.9 5.3 %reshape.140 = bf16[32,2,6144]{2,1,0:T(2,128)(2,1)S(1)} reshape(bf16[2048,4,48]{2,1,0:T(4,128)(2,1)} %bitcast.99) | data formatting | bytes 1572864
  83.2 60.5 %all_to_all.83 = bf16[32,2,6144]{2,1,0:T(2,128)(2,1)S(1)} all-to-all(bf16[32,2,6144]{2,1,0:T(2,128)(2,1)S(1)} %reshape.140), channel_id=1, replica_groups=mesh['row'=32,'col'=16] {'row'}, dimensions={0} | all-to-all | bytes 1572864 | tf_op jit(solution)/shard_map/all_to_all | solution.py:56
  143.7 3.1 reshape.141
  146.8 2.9 copy.118
  151.6 18.9 %all_to_all.84 = bf16[16,2,12288]{2,1,0:T(2,128)(2,1)} all-to-all(bf16[16,2,12288]{2,1,0:T(2,128)(2,1)} %reshape.142), channel_id=1, replica_groups=mesh['row'=32,'col'=16] {'col'}, dimensions={0} | all-to-all | bytes 1572864 | tf_op jit(solution)/shard_map/all_to_all | solution.py:55
  170.5 3.0 reshape.143
  177.8 2.6 collective-permute-start.4
  181.6 4.2 %collective-permute-start.5 = (bf16[48,16,128]{2,1,0:T(8,128)(2,1)}, bf16[48,16,128]{2,1,0:T(8,128)(2,1)}, u32[]{:S(2)}, u32[]{:S(2)}) collective-permute-start(bf16[48,16,128]{2,1,0:T(8,128)(2,1)} %copy.122), channel_id=1, source_target_pairs={{16,0},{32,16},{48,32},{64,48},{80,64},{96,80},{112,96},{128,112},... | collective-permute-start | bytes 589832 | tf_op jit(solution)/shard_map/ppermute | solution.py:18
  188.1 3.9 %collective-permute-done.5 = bf16[48,16,128]{2,1,0:T(8,128)(2,1)} collective-permute-done((bf16[48,16,128]{2,1,0:T(8,128)(2,1)}, bf16[48,16,128]{2,1,0:T(8,128)(2,1)}, u32[]{:S(2)}, u32[]{:S(2)}) %collective-permute-start.5) | collective-permute-done | bytes 196640 | tf_op jit(solution)/shard_map/ppermute | solution.py:18
  194.4 3.0 pad_maximum_fusion.1
  197.4 3.2 collective-permute-start.6
  204.2 4.2 %collective-permute-done.7 = bf16[48,96,16]{1,2,0:T(8,128)(2,1)S(1)} collective-permute-done((bf16[48,96,16]{1,2,0:T(8,128)(2,1)S(1)}, bf16[48,96,16]{1,2,0:T(8,128)(2,1)S(1)}, u32[]{:S(2)}, u32[]{:S(2)}) %collective-permute-start.7) | collective-permute-done | bytes 147488 | tf_op jit(solution)/shard_map/ppermute | solution.py:18
  208.9 12.1 %copy.125 = bf16[1,48,96,160]{1,0,3,2:T(2,128)(2,1)} copy(bf16[1,48,96,160]{2,3,1,0:T(8,128)(2,1)S(1)} %maximum_maximum_fusion) | data formatting | bytes 2949120 | tf_op jit(solution)/shard_map/max | solution.py:26
  221.0 26.8 %fusion.22 = f32[1,48,64,128]{1,0,3,2:T(1,128)} fusion(bf16[1,48,96,160]{1,0,3,2:T(2,128)(2,1)} %copy.125, bf16[2,3,3,48,48]{4,3,2,1,0:T(8,128)(2,1)} %param.6), kind=kOutput, calls=%fused_computation.31 | convolution fusion | flops 339738624 | bytes 9547776 | tf_op jit(solution)/shard_map/conv_general_dilated | solution.py:27
  247.8 5.3 %copy.126 = f32[1,48,64,128]{3,2,1,0:T(8,128)S(1)} copy(f32[1,48,64,128]{1,0,3,2:T(1,128)} %fusion.22) | data formatting | bytes 3145728 | tf_op jit(solution)/shard_map/conv_general_dilated | solution.py:27
  260.5 16.8 %all_to_all.85 = bf16[48,64,128]{2,0,1:T(8,128)(2,1)S(1)} all-to-all(bf16[48,64,128]{2,0,1:T(8,128)(2,1)S(1)} %copy.129), channel_id=1, replica_groups=mesh['row'=32,'col'=16] {'col'}, dimensions={1} | all-to-all | bytes 1572864 | tf_op jit(solution)/shard_map/all_to_all | solution.py:53
  279.8 5.3 %reshape.144 = bf16[32,2,6144]{2,1,0:T(2,128)(2,1)S(1)} reshape(bf16[2048,4,48]{2,1,0:T(4,128)(2,1)} %bitcast.100) | data formatting | bytes 1572864
  285.1 51.2 %all_to_all.86 = bf16[32,2,6144]{2,1,0:T(2,128)(2,1)S(1)} all-to-all(bf16[32,2,6144]{2,1,0:T(2,128)(2,1)S(1)} %reshape.144), channel_id=1, replica_groups=mesh['row'=32,'col'=16] {'row'}, dimensions={0} | all-to-all | bytes 1572864 | tf_op jit(solution)/shard_map/all_to_all | solution.py:56
  336.3 3.1 reshape.145
  339.4 2.9 copy.132
  344.2 18.8 %all_to_all.87 = bf16[16,2,12288]{2,1,0:T(2,128)(2,1)} all-to-all(bf16[16,2,12288]{2,1,0:T(2,128)(2,1)} %reshape.146), channel_id=1, replica_groups=mesh['row'=32,'col'=16] {'col'}, dimensions={0} | all-to-all | bytes 1572864 | tf_op jit(solution)/shard_map/all_to_all | solution.py:55
  363.0 3.0 reshape.147
  (58 shorter events, 54.4 us)
Async XLA Ops:
  0.0 10.5 %copy-start.2 = (bf16[48,64,128]{2,1,0:T(8,128)(2,1)S(1)}, bf16[48,64,128]{2,1,0:T(8,128)(2,1)}, u32[]{:S(2)}) copy-start(bf16[48,64,128]{2,1,0:T(8,128)(2,1)} %param.5) | copy-start | bytes 2359300
  1.0 13.1 %collective-permute-start = (bf16[48,8,128]{2,1,0:T(8,128)(2,1)S(1)}, bf16[48,8,128]{2,1,0:T(8,128)(2,1)S(1)}, u32[]{:S(2)}, u32[]{:S(2)}) collective-permute-start(bf16[48,8,128]{2,1,0:T(8,128)(2,1)S(1)} %get-tuple-element.19), channel_id=1, source_target_pairs={{0,16},{16,32},{32,48},{48,64},{64,80},{80,96},{96,112},{112,128},... | collective-permute-start | bytes 294920 | tf_op jit(solution)/shard_map/ppermute | solution.py:17
  5.4 7.8 %collective-permute-start.1 = (bf16[48,8,128]{2,1,0:T(8,128)(2,1)S(1)}, bf16[48,8,128]{2,1,0:T(8,128)(2,1)S(1)}, u32[]{:S(2)}, u32[]{:S(2)}) collective-permute-start(bf16[48,8,128]{2,1,0:T(8,128)(2,1)S(1)} %get-tuple-element.20), channel_id=1, source_target_pairs={{16,0},{32,16},{48,32},{64,48},{80,64},{96,80},{112,96},{128,112},... | collective-permute-start | bytes 294920 | tf_op jit(solution)/shard_map/ppermute | solution.py:18
  15.8 10.0 %copy-start = (bf16[48,8,128]{1,0,2:T(8,128)(2,1)S(1)}, bf16[48,8,128]{1,0,2:T(8,128)(2,1)}, u32[]{:S(2)}) copy-start(bf16[48,8,128]{1,0,2:T(8,128)(2,1)} %copy.107) | copy-start | bytes 294916
  18.8 8.5 %collective-permute-start.2 = (bf16[48,80,8]{1,0,2:T(8,128)(2,1)S(1)}, bf16[48,80,8]{1,0,2:T(8,128)(2,1)S(1)}, u32[]{:S(2)}, u32[]{:S(2)}) collective-permute-start(bf16[48,80,8]{1,0,2:T(8,128)(2,1)S(1)} %get-tuple-element.17), channel_id=1, source_target_pairs={{0,1},{1,2},{2,3},{3,4},{4,5},{5,6},{6,7},{7,8},{8,9},{9,10},{10,1... | collective-permute-start | bytes 184328 | tf_op jit(solution)/shard_map/ppermute | solution.py:17
  23.4 6.8 %collective-permute-start.3 = (bf16[48,80,8]{1,0,2:T(8,128)(2,1)S(1)}, bf16[48,80,8]{1,0,2:T(8,128)(2,1)S(1)}, u32[]{:S(2)}, u32[]{:S(2)}) collective-permute-start(bf16[48,80,8]{1,0,2:T(8,128)(2,1)S(1)} %get-tuple-element.18), channel_id=1, source_target_pairs={{1,0},{2,1},{3,2},{4,3},{5,4},{6,5},{7,6},{8,7},{9,8},{10,9},{11,1... | collective-permute-start | bytes 184328 | tf_op jit(solution)/shard_map/ppermute | solution.py:18
  35.6 0.9 copy-start.5
  35.6 0.9 copy-start.6
  48.1 1.9 copy-start.3
  177.8 9.5 %collective-permute-start.4 = (bf16[48,16,128]{2,1,0:T(8,128)(2,1)S(1)}, bf16[48,16,128]{2,1,0:T(8,128)(2,1)S(1)}, u32[]{:S(2)}, u32[]{:S(2)}) collective-permute-start(bf16[48,16,128]{2,1,0:T(8,128)(2,1)S(1)} %copy.121), channel_id=1, source_target_pairs={{0,16},{16,32},{32,48},{48,64},{64,80},{80,96},{96,112},{112,128},... | collective-permute-start | bytes 589832 | tf_op jit(solution)/shard_map/ppermute | solution.py:17
  181.6 10.4 %collective-permute-start.5 = (bf16[48,16,128]{2,1,0:T(8,128)(2,1)}, bf16[48,16,128]{2,1,0:T(8,128)(2,1)}, u32[]{:S(2)}, u32[]{:S(2)}) collective-permute-start(bf16[48,16,128]{2,1,0:T(8,128)(2,1)} %copy.122), channel_id=1, source_target_pairs={{16,0},{32,16},{48,32},{64,48},{80,64},{96,80},{112,96},{128,112},... | collective-permute-start | bytes 589832 | tf_op jit(solution)/shard_map/ppermute | solution.py:18
  194.4 8.4 %copy-start.1 = (bf16[48,16,128]{1,2,0:T(8,128)(2,1)S(1)}, bf16[48,16,128]{1,2,0:T(8,128)(2,1)}, u32[]{:S(2)}) copy-start(bf16[48,16,128]{1,2,0:T(8,128)(2,1)} %copy.124) | copy-start | bytes 589828
  197.4 6.8 %collective-permute-start.6 = (bf16[48,96,16]{1,2,0:T(8,128)(2,1)S(1)}, bf16[48,96,16]{1,2,0:T(8,128)(2,1)S(1)}, u32[]{:S(2)}, u32[]{:S(2)}) collective-permute-start(bf16[48,96,16]{1,2,0:T(8,128)(2,1)S(1)} %get-tuple-element.13), channel_id=1, source_target_pairs={{0,1},{1,2},{2,3},{3,4},{4,5},{5,6},{6,7},{7,8},{8,9},{9,10},{10,1... | collective-permute-start | bytes 442376 | tf_op jit(solution)/shard_map/ppermute | solution.py:17
  200.5 7.9 %collective-permute-start.7 = (bf16[48,96,16]{1,2,0:T(8,128)(2,1)S(1)}, bf16[48,96,16]{1,2,0:T(8,128)(2,1)S(1)}, u32[]{:S(2)}, u32[]{:S(2)}) collective-permute-start(bf16[48,96,16]{1,2,0:T(8,128)(2,1)S(1)} %get-tuple-element.14), channel_id=1, source_target_pairs={{1,0},{2,1},{3,2},{4,3},{5,4},{6,5},{7,6},{8,7},{9,8},{10,9},{11,1... | collective-permute-start | bytes 442376 | tf_op jit(solution)/shard_map/ppermute | solution.py:18
  253.2 0.7 copy-start.4
where the time goes:
time: 373 us; the launch traced here: 368 us
  blocking collectives  184 us (49%)
  local copies, waits for them, and re-layouts  89.2 us (24%)
  matrix products  36.9 us (10%)
  starting transfers between devices  26 us (7%)
  other arithmetic  18 us (5%)
  waiting for transfers between devices  13.6 us (4%)
    all_to_all x2, blocking collectives, mirror_tile(): lax.all_to_all(first_leg, 'row', split_axis=2, concat_axis=1, tiled=True)  112 us
    all_to_all x2, blocking collectives, mirror_tile(): lax.all_to_all(lax.all_to_all(first_leg, 'row', split_axis=2, concat_axis...  37.8 us
    conv_general_dilated x2, matrix products, dilated_terms(): lax.conv_general_dilated(active[None], kernel, (1, 1), 'VALID', rhs_dilat...  34.7 us
    all_to_all x2, blocking collectives, mirror_tile(): lax.all_to_all(output_map, 'col', split_axis=1, concat_axis=2, tiled=True)  34.6 us
    unnamed x25, local copies, waits for them, and re-layouts  32.4 us
    ppermute x4, starting transfers between devices, padded(): before = lax.ppermute(last, axis, up)  14.7 us
    ppermute x4, waiting for transfers between devices, padded(): after = lax.ppermute(initial, axis, down)  12.2 us
    max x1, local copies, waits for them, and re-layouts, dilated_terms(): active = jnp.maximum(extended_input, jnp.zeros((), extended_input.dtype))  12.1 us
  transfers between devices with their start and end apart: 8, of which 5 were waited for; matrix products, arithmetic and copies ran while one was open for 3% of the time, Pallas kernels for 0%

commit v1 on v0

--- a/solution.py
+++ b/solution.py
@@ -44,34 +44,40 @@
     return summed.astype(jnp.bfloat16)
 
 
-def mirror_tile(output_map):
+def mirror_pieces(output_map):
     n_row = lax.axis_size("row")
     n_col = lax.axis_size("col")
     channel_count, tile_rows, tile_cols = output_map.shape
-    sub_rows = tile_rows // n_col
-    ratio = n_row // n_col
-    first_leg = lax.all_to_all(output_map, "col", split_axis=1, concat_axis=2, tiled=True)
-    count = first_leg.shape[0]
-    moved = lax.all_to_all(
-        lax.all_to_all(first_leg, "row", split_axis=2, concat_axis=1, tiled=True),
-        "col",
-        split_axis=1,
-        concat_axis=1,
-        tiled=True,
-    )
-    grouped = moved.reshape(count, n_col, ratio, sub_rows, tile_rows)
-    return jnp.transpose(grouped, (0, 4, 2, 1, 3)).reshape(count, tile_rows, tile_cols)
+    k = tile_cols // tile_rows
+    parity = lax.axis_index("row") % k
+    flipped = jnp.swapaxes(output_map, 1, 2)
+    received = []
+    for m in range(k):
+        piece = lax.dynamic_slice_in_dim(flipped, ((parity + m) % k) * tile_rows, tile_rows, axis=1)
+        pairs = []
+        for r in range(n_row):
+            for c in range(n_col):
+                h = (r % k + m) % k
+                pairs.append((r * n_col + c, (k * c + h) * n_col + r // k))
+        received.append(lax.ppermute(piece, ("row", "col"), pairs))
+    return [lax.select_n((parity - s) % k, *received) if k > 1 else received[0] for s in range(k)]
+
+
+def symmetrized(output_map):
+    pieces = mirror_pieces(output_map)
+    tile_rows = output_map.shape[1]
+    halves = []
+    for s, piece in enumerate(pieces):
+        own = output_map[:, :, s * tile_rows:(s + 1) * tile_rows]
+        halves.append(((own.astype(jnp.float32) + piece.astype(jnp.float32)) * 0.5).astype(jnp.bfloat16))
+    return jnp.concatenate(halves, axis=2)
 
 
 def body(features, w_dilated, w_pointwise, norm_gain, norm_bias):
     current_state = features
     for layer_index in range(2):
-        if layer_index == 0:
-            dilation_rate = FIRST_DILATION
-            extended_input = padded(current_state, (("row", 1), ("col", 2)), FIRST_DILATION)
-        else:
-            dilation_rate = SECOND_DILATION
-            extended_input = padded(current_state, (("row", 1), ("col", 2)), SECOND_DILATION)
+        dilation_rate = FIRST_DILATION if layer_index == 0 else SECOND_DILATION
+        extended_input = padded(current_state, (("row", 1), ("col", 2)), dilation_rate)
         kernel = jnp.transpose(w_dilated[layer_index], (2, 3, 0, 1))
         output_map = dilated_terms(
             extended_input,
@@ -82,14 +88,7 @@
             w_pointwise[layer_index],
             dilation_rate,
         )
-        if layer_index == 0:
-            mirrored = mirror_tile(output_map)
-        else:
-            mirrored = mirror_tile(output_map)
-        output_map, mirrored = lax.optimization_barrier((output_map, mirrored))
-        current_state = (
-            (output_map.astype(jnp.float32) + mirrored.astype(jnp.float32)) * 0.5
-        ).astype(jnp.bfloat16)
+        current_state = symmetrized(output_map)
     return current_state
 
 

time: 373 us -> 697 us (1.87)
  the two profiles are of different devices: /device:TPU:7 before, /device:TPU:205 now
where the time goes in v1:
time: 697 us; the launch traced here: 696 us
  waiting for transfers between devices  540 us (77%)
  local copies, waits for them, and re-layouts  52.7 us (8%)
  starting transfers between devices  43.4 us (6%)
  matrix products  37 us (5%)
  other arithmetic  21.9 us (3%)
    ppermute x4, waiting for transfers between devices, mirror_pieces(): received.append(lax.ppermute(piece, ('row', 'col'), pairs))  501 us
    ppermute x4, waiting for transfers between devices, padded(): after = lax.ppermute(initial, axis, down)  39 us
    conv_general_dilated x2, matrix products, dilated_terms(): lax.conv_general_dilated(active[None], kernel, (1, 1), 'VALID', rhs_dilat...  34.8 us
    ppermute x4, starting transfers between devices, padded(): before = lax.ppermute(last, axis, up)  24.1 us
  transfers between devices with their start and end apart: 12, of which 8 were waited for; matrix products, arithmetic and copies ran while one was open for 2% of the time, Pallas kernels for 0%

profile of v1, /device:TPU:205, one launch (start us, length us, event | category | flops | bytes accessed | tf_op | source)
XLA Modules:
  0.0 695.6 jit_solution(4146257721399926401)
XLA Ops:
  1.0 3.5 collective-permute-start
  4.5 3.3 collective-permute-start.1
  14.9 3.0 pad_maximum_fusion.1
  17.9 5.7 collective-permute-start.2
  23.6 2.1 collective-permute-start.3
  27.2 2.4 collective-permute-done.3
  31.3 3.6 copy.74
  35.9 7.9 %maximum_convert_fusion = bf16[64,8,18,48]{3,1,2,0:T(8,128)(2,1)} fusion(f32[48]{0:T(128)S(1)} %get-tuple-element.27, f32[48]{0:T(128)S(1)} %get-tuple-element.30, pred[8,18]{0,1:T(8,128)(4,1)S(1)} %copy-done.6, bf16[48,80,1,7,16]{0,3,4,1,2:T(8,128)(2,1)S(1)} %slice.120, bf16[48,80,1,8,18]{0,3,4,1,2:T(8,128)(2,1)S(1)} %copy.74, ...), kind=kOutput, calls=%fused_computation.8 | convolution fusion | flops 390684672 | bytes 6569984 | tf_op jit(solution)/shard_map/conv_general_dilated | solution.py:27
  43.8 3.6 copy.75
  50.9 2.2 copy.77
  53.1 3.0 fusion.11
  60.2 2.8 collective-permute-start.5
  63.1 361.4 %collective-permute-done.4 = bf16[48,64,64]{2,1,0:T(8,128)(2,1)S(1)} collective-permute-done((bf16[48,64,64]{2,1,0:T(8,128)(2,1)}, bf16[48,64,64]{2,1,0:T(8,128)(2,1)S(1)}, u32[]{:S(2)}, u32[]{:S(2)}) %collective-permute-start.4) | collective-permute-done | bytes 393248 | tf_op jit(solution)/shard_map/ppermute | solution.py:62
  425.7 7.8 %collective-permute-done.5 = bf16[48,64,64]{1,2,0:T(8,128)(2,1)} collective-permute-done((bf16[48,64,64]{1,2,0:T(8,128)(2,1)}, bf16[48,64,64]{1,2,0:T(8,128)(2,1)}, u32[]{:S(2)}, u32[]{:S(2)}) %collective-permute-start.5) | collective-permute-done | bytes 393248 | tf_op jit(solution)/shard_map/ppermute | solution.py:62
  433.4 2.1 multiply_convert_fusion.2
  439.1 12.9 %collective-permute-start.6 = (bf16[48,16,128]{2,1,0:T(8,128)(2,1)S(1)}, bf16[48,16,128]{2,1,0:T(8,128)(2,1)S(1)}, u32[]{:S(2)}, u32[]{:S(2)}) collective-permute-start(bf16[48,16,128]{2,1,0:T(8,128)(2,1)S(1)} %copy.81), channel_id=1, source_target_pairs={{0,16},{16,32},{32,48},{48,64},{64,80},{80,96},{96,112},{112,128},... | collective-permute-start | bytes 589832 | tf_op jit(solution)/shard_map/ppermute | solution.py:17
  453.3 1.9 collective-permute-start.7
  456.1 33.4 %collective-permute-done.7 = bf16[48,16,128]{2,1,0:T(8,128)(2,1)} collective-permute-done((bf16[48,16,128]{2,1,0:T(8,128)(2,1)}, bf16[48,16,128]{2,1,0:T(8,128)(2,1)}, u32[]{:S(2)}, u32[]{:S(2)}) %collective-permute-start.7) | collective-permute-done | bytes 196640 | tf_op jit(solution)/shard_map/ppermute | solution.py:18
  489.5 2.4 copy.84
  491.9 3.0 pad_maximum_fusion.2
  494.9 1.9 collective-permute-start.8
  496.8 2.4 collective-permute-start.9
  500.7 3.1 collective-permute-done.9
  504.3 11.8 %copy.85 = bf16[1,48,96,160]{1,0,3,2:T(2,128)(2,1)} copy(bf16[1,48,96,160]{2,3,1,0:T(8,128)(2,1)S(1)} %maximum_maximum_fusion) | data formatting | bytes 2949120 | tf_op jit(solution)/shard_map/max | solution.py:26
  516.1 26.8 %fusion.24 = f32[1,48,64,128]{1,0,3,2:T(1,128)} fusion(bf16[1,48,96,160]{1,0,3,2:T(2,128)(2,1)} %copy.85, bf16[2,3,3,48,48]{4,3,2,1,0:T(8,128)(2,1)} %param.6), kind=kOutput, calls=%fused_computation.43 | convolution fusion | flops 339738624 | bytes 9547776 | tf_op jit(solution)/shard_map/conv_general_dilated | solution.py:27
  543.0 5.3 copy.86
  549.8 2.2 copy.88
  552.0 2.6 fusion.9
  556.3 2.7 collective-permute-start.10
  559.0 2.2 collective-permute-start.11
  561.2 107.2 %collective-permute-done.10 = bf16[48,64,64]{1,2,0:T(8,128)(2,1)S(1)} collective-permute-done((bf16[48,64,64]{1,2,0:T(8,128)(2,1)S(1)}, bf16[48,64,64]{1,2,0:T(8,128)(2,1)S(1)}, u32[]{:S(2)}, u32[]{:S(2)}) %collective-permute-start.10) | collective-permute-done | bytes 393248 | tf_op jit(solution)/shard_map/ppermute | solution.py:62
  668.4 24.7 %collective-permute-done.11 = bf16[48,64,64]{1,2,0:T(8,128)(2,1)S(1)} collective-permute-done((bf16[48,64,64]{1,2,0:T(8,128)(2,1)}, bf16[48,64,64]{1,2,0:T(8,128)(2,1)S(1)}, u32[]{:S(2)}, u32[]{:S(2)}) %collective-permute-start.11) | collective-permute-done | bytes 393248 | tf_op jit(solution)/shard_map/ppermute | solution.py:62
  (51 shorter events, 34.1 us)
Async XLA Ops:
  0.0 10.6 %copy-start.2 = (bf16[48,64,128]{2,1,0:T(8,128)(2,1)S(1)}, bf16[48,64,128]{2,1,0:T(8,128)(2,1)}, u32[]{:S(2)}) copy-start(bf16[48,64,128]{2,1,0:T(8,128)(2,1)} %param.5) | copy-start | bytes 2359300
  1.0 12.2 %collective-permute-start = (bf16[48,8,128]{2,1,0:T(8,128)(2,1)S(1)}, bf16[48,8,128]{2,1,0:T(8,128)(2,1)S(1)}, u32[]{:S(2)}, u32[]{:S(2)}) collective-permute-start(bf16[48,8,128]{2,1,0:T(8,128)(2,1)S(1)} %get-tuple-element.19), channel_id=1, source_target_pairs={{0,16},{16,32},{32,48},{48,64},{64,80},{80,96},{96,112},{112,128},... | collective-permute-start | bytes 294920 | tf_op jit(solution)/shard_map/ppermute | solution.py:17
  4.5 7.8 %collective-permute-start.1 = (bf16[48,8,128]{2,1,0:T(8,128)(2,1)S(1)}, bf16[48,8,128]{2,1,0:T(8,128)(2,1)S(1)}, u32[]{:S(2)}, u32[]{:S(2)}) collective-permute-start(bf16[48,8,128]{2,1,0:T(8,128)(2,1)S(1)} %get-tuple-element.20), channel_id=1, source_target_pairs={{16,0},{32,16},{48,32},{64,48},{80,64},{96,80},{112,96},{128,112},... | collective-permute-start | bytes 294920 | tf_op jit(solution)/shard_map/ppermute | solution.py:18
  14.9 10.8 %copy-start = (bf16[48,8,128]{1,0,2:T(8,128)(2,1)S(1)}, bf16[48,8,128]{1,0,2:T(8,128)(2,1)}, u32[]{:S(2)}) copy-start(bf16[48,8,128]{1,0,2:T(8,128)(2,1)} %copy.70) | copy-start | bytes 294916
  17.9 9.3 %collective-permute-start.2 = (bf16[48,80,8]{1,0,2:T(8,128)(2,1)S(1)}, bf16[48,80,8]{1,0,2:T(8,128)(2,1)S(1)}, u32[]{:S(2)}, u32[]{:S(2)}) collective-permute-start(bf16[48,80,8]{1,0,2:T(8,128)(2,1)S(1)} %get-tuple-element.17), channel_id=1, source_target_pairs={{0,1},{1,2},{2,3},{3,4},{4,5},{5,6},{6,7},{7,8},{8,9},{9,10},{10,1... | collective-permute-start | bytes 184328 | tf_op jit(solution)/shard_map/ppermute | solution.py:17
  23.6 5.9 collective-permute-start.3
  34.9 0.9 copy-start.5
  34.9 0.9 copy-start.6
  47.5 1.9 copy-start.3
  57.1 367.4 %collective-permute-start.4 = (bf16[48,64,64]{2,1,0:T(8,128)(2,1)}, bf16[48,64,64]{2,1,0:T(8,128)(2,1)S(1)}, u32[]{:S(2)}, u32[]{:S(2)}) collective-permute-start(bf16[48,64,64]{2,1,0:T(8,128)(2,1)} %get-tuple-element.16), channel_id=1, source_target_pairs={{0,0},{1,32},{2,64},{3,96},{4,128},{5,160},{6,192},{7,224},{8,256}... | collective-permute-start | bytes 1179656 | tf_op jit(solution)/shard_map/ppermute | solution.py:62
  60.2 373.2 %collective-permute-start.5 = (bf16[48,64,64]{1,2,0:T(8,128)(2,1)}, bf16[48,64,64]{1,2,0:T(8,128)(2,1)}, u32[]{:S(2)}, u32[]{:S(2)}) collective-permute-start(bf16[48,64,64]{1,2,0:T(8,128)(2,1)} %copy.78), channel_id=1, source_target_pairs={{0,16},{1,48},{2,80},{3,112},{4,144},{5,176},{6,208},{7,240},{8,27... | collective-permute-start | bytes 1179656 | tf_op jit(solution)/shard_map/ppermute | solution.py:62
  439.1 16.1 %collective-permute-start.6 = (bf16[48,16,128]{2,1,0:T(8,128)(2,1)S(1)}, bf16[48,16,128]{2,1,0:T(8,128)(2,1)S(1)}, u32[]{:S(2)}, u32[]{:S(2)}) collective-permute-start(bf16[48,16,128]{2,1,0:T(8,128)(2,1)S(1)} %copy.81), channel_id=1, source_target_pairs={{0,16},{16,32},{32,48},{48,64},{64,80},{80,96},{96,112},{112,128},... | collective-permute-start | bytes 589832 | tf_op jit(solution)/shard_map/ppermute | solution.py:17
  453.3 36.1 %collective-permute-start.7 = (bf16[48,16,128]{2,1,0:T(8,128)(2,1)}, bf16[48,16,128]{2,1,0:T(8,128)(2,1)}, u32[]{:S(2)}, u32[]{:S(2)}) collective-permute-start(bf16[48,16,128]{2,1,0:T(8,128)(2,1)} %copy.82), channel_id=1, source_target_pairs={{16,0},{32,16},{48,32},{64,48},{80,64},{96,80},{112,96},{128,112},... | collective-permute-start | bytes 589832 | tf_op jit(solution)/shard_map/ppermute | solution.py:18
  491.9 7.3 %copy-start.1 = (bf16[48,16,128]{1,2,0:T(8,128)(2,1)S(1)}, bf16[48,16,128]{1,2,0:T(8,128)(2,1)}, u32[]{:S(2)}) copy-start(bf16[48,16,128]{1,2,0:T(8,128)(2,1)} %copy.84) | copy-start | bytes 589828
  494.9 5.8 collective-permute-start.8
  496.8 7.0 %collective-permute-start.9 = (bf16[48,96,16]{1,2,0:T(8,128)(2,1)S(1)}, bf16[48,96,16]{1,2,0:T(8,128)(2,1)S(1)}, u32[]{:S(2)}, u32[]{:S(2)}) collective-permute-start(bf16[48,96,16]{1,2,0:T(8,128)(2,1)S(1)} %get-tuple-element.12), channel_id=1, source_target_pairs={{1,0},{2,1},{3,2},{4,3},{5,4},{6,5},{7,6},{8,7},{9,8},{10,9},{11,1... | collective-permute-start | bytes 442376 | tf_op jit(solution)/shard_map/ppermute | solution.py:18
  548.3 0.7 copy-start.4
  556.3 112.1 %collective-permute-start.10 = (bf16[48,64,64]{1,2,0:T(8,128)(2,1)S(1)}, bf16[48,64,64]{1,2,0:T(8,128)(2,1)S(1)}, u32[]{:S(2)}, u32[]{:S(2)}) collective-permute-start(bf16[48,64,64]{1,2,0:T(8,128)(2,1)S(1)} %bitcast.74), channel_id=1, source_target_pairs={{0,0},{1,32},{2,64},{3,96},{4,128},{5,160},{6,192},{7,224},{8,256}... | collective-permute-start | bytes 1179656 | tf_op jit(solution)/shard_map/ppermute | solution.py:62
  559.0 134.1 %collective-permute-start.11 = (bf16[48,64,64]{1,2,0:T(8,128)(2,1)}, bf16[48,64,64]{1,2,0:T(8,128)(2,1)S(1)}, u32[]{:S(2)}, u32[]{:S(2)}) collective-permute-start(bf16[48,64,64]{1,2,0:T(8,128)(2,1)} %bitcast.73), channel_id=1, source_target_pairs={{0,16},{1,48},{2,80},{3,112},{4,144},{5,176},{6,208},{7,240},{8,27... | collective-permute-start | bytes 1179656 | tf_op jit(solution)/shard_map/ppermute | solution.py:62

commit v2 on v0

--- a/solution.py
+++ b/solution.py
@@ -20,9 +20,7 @@
     return value
 
 
-def dilated_terms(
-    extended_input, current_state, kernel, gain_pair, bias_pair, pointwise, dilation_rate
-):
+def hidden_of(extended_input, kernel, gain, bias, dilation_rate):
     active = jnp.maximum(extended_input, jnp.zeros((), extended_input.dtype))
     spread = lax.conv_general_dilated(
         active[None],
@@ -32,9 +30,10 @@
         rhs_dilation=(dilation_rate, dilation_rate),
         preferred_element_type=jnp.float32,
     )[0]
-    hidden = jnp.maximum(
-        spread * gain_pair[0][:, None, None] + bias_pair[0][:, None, None], 0.0
-    ).astype(jnp.bfloat16)
+    return jnp.maximum(spread * gain[:, None, None] + bias[:, None, None], 0.0).astype(jnp.bfloat16)
+
+
+def block_output(current_state, hidden, gain_pair, bias_pair, pointwise):
     branch = jnp.einsum("oc,chw->ohw", pointwise, hidden, preferred_element_type=jnp.float32)
     summed = (
         current_state.astype(jnp.float32)
@@ -63,34 +62,27 @@
     return jnp.transpose(grouped, (0, 4, 2, 1, 3)).reshape(count, tile_rows, tile_cols)
 
 
+def mean_of(a, b):
+    return ((a.astype(jnp.float32) + b.astype(jnp.float32)) * 0.5).astype(jnp.bfloat16)
+
+
 def body(features, w_dilated, w_pointwise, norm_gain, norm_bias):
-    current_state = features
-    for layer_index in range(2):
-        if layer_index == 0:
-            dilation_rate = FIRST_DILATION
-            extended_input = padded(current_state, (("row", 1), ("col", 2)), FIRST_DILATION)
-        else:
-            dilation_rate = SECOND_DILATION
-            extended_input = padded(current_state, (("row", 1), ("col", 2)), SECOND_DILATION)
-        kernel = jnp.transpose(w_dilated[layer_index], (2, 3, 0, 1))
-        output_map = dilated_terms(
-            extended_input,
-            current_state,
-            kernel,
-            norm_gain[layer_index],
-            norm_bias[layer_index],
-            w_pointwise[layer_index],
-            dilation_rate,
-        )
-        if layer_index == 0:
-            mirrored = mirror_tile(output_map)
-        else:
-            mirrored = mirror_tile(output_map)
-        output_map, mirrored = lax.optimization_barrier((output_map, mirrored))
-        current_state = (
-            (output_map.astype(jnp.float32) + mirrored.astype(jnp.float32)) * 0.5
-        ).astype(jnp.bfloat16)
-    return current_state
+    kernel = jnp.transpose(w_dilated[0], (2, 3, 0, 1))
+    extended = padded(features, (("row", 1), ("col", 2)), FIRST_DILATION)
+    hidden = hidden_of(extended, kernel, norm_gain[0, 0], norm_bias[0, 0], FIRST_DILATION)
+    output_map = block_output(features, hidden, norm_gain[0], norm_bias[0], w_pointwise[0])
+    state = mean_of(output_map, mirror_tile(output_map))
+
+    kernel = jnp.transpose(w_dilated[1], (2, 3, 0, 1))
+    both = jnp.concatenate([kernel, jnp.swapaxes(kernel, 2, 3)], axis=0)
+    extended = padded(state, (("row", 1), ("col", 2)), SECOND_DILATION)
+    gain = jnp.concatenate([norm_gain[1, 0], norm_gain[1, 0]])
+    bias = jnp.concatenate([norm_bias[1, 0], norm_bias[1, 0]])
+    hidden = hidden_of(extended, both, gain, bias, SECOND_DILATION)
+    count = state.shape[0]
+    direct = block_output(state, hidden[:count], norm_gain[1], norm_bias[1], w_pointwise[1])
+    mirrored = block_output(state, hidden[count:], norm_gain[1], norm_bias[1], w_pointwise[1])
+    return mean_of(direct, mirrored)
 
 
 def solution(mesh):

time: 373 us -> 274 us (0.73)
  blocking collectives: 184 us -> 78.3 us
  local copies, waits for them, and re-layouts: 89.2 us -> 68.7 us
  waiting for transfers between devices: 13.6 us -> 26.2 us
  starting transfers between devices: 26 us -> 32.1 us
  other arithmetic: 18 us -> 23.4 us
  matrix products: 36.9 us -> 40.9 us
    all_to_all x2 -> x1, blocking collectives: 112 us -> 60.5 us  [mirror_tile(): lax.all_to_all(first_leg, 'row', split_axis=2, concat_axis=1, tiled=True)]
    all_to_all x2 -> x0, blocking collectives: 37.8 us -> none  [mirror_tile(): lax.all_to_all(lax.all_to_all(first_leg, 'row', split_axis=2, concat_axis...]
    all_to_all x2 -> x1, blocking collectives: 34.6 us -> 17.8 us  [mirror_tile(): lax.all_to_all(output_map, 'col', split_axis=1, concat_axis=2, tiled=True)]
    unnamed x25 -> x26, local copies, waits for them, and re-layouts: 32.4 us -> 19.5 us
    all_to_all x0 -> x1, waiting for transfers between devices: none -> 11.1 us  [mirror_tile(): lax.all_to_all(lax.all_to_all(first_leg, 'row', split_axis=2, concat_axis...]
    all_to_all x0 -> x1, starting transfers between devices: none -> 6.28 us  [mirror_tile(): lax.all_to_all(lax.all_to_all(first_leg, 'row', split_axis=2, concat_axis...]
    ppermute x4, waiting for transfers between devices: 1.43 us -> 7.01 us  [padded(): before = lax.ppermute(last, axis, up)]
    conv_general_dilated x3 -> x2, local copies, waits for them, and re-layouts: 9.75 us -> 4.43 us  [hidden_of(): lax.conv_general_dilated(active[None], kernel, (1, 1), 'VALID', rhs_dilat...]
  transfers between devices with their start and end apart: 8 -> 9, of which waited for: 5 -> 5; matrix products, arithmetic and copies ran while one was open for 3% -> 4% of each run, Pallas kernels for 0% -> 0%
where the time goes in v2:
time: 274 us; the launch traced here: 270 us
  blocking collectives  78.3 us (29%)
  local copies, waits for them, and re-layouts  68.7 us (25%)
  matrix products  40.9 us (15%)
  starting transfers between devices  32.1 us (12%)
  waiting for transfers between devices  26.2 us (10%)
  other arithmetic  23.4 us (9%)
    all_to_all x1, blocking collectives, mirror_tile(): lax.all_to_all(first_leg, 'row', split_axis=2, concat_axis=1, tiled=True)  60.5 us
    conv_general_dilated x2, matrix products, hidden_of(): lax.conv_general_dilated(active[None], kernel, (1, 1), 'VALID', rhs_dilat...  36.6 us
    unnamed x26, local copies, waits for them, and re-layouts  19.5 us
    all_to_all x1, blocking collectives, mirror_tile(): lax.all_to_all(output_map, 'col', split_axis=1, concat_axis=2, tiled=True)  17.8 us
    ppermute x4, starting transfers between devices, padded(): before = lax.ppermute(last, axis, up)  16 us
    max x1, local copies, waits for them, and re-layouts, hidden_of(): active = jnp.maximum(extended_input, jnp.zeros((), extended_input.dtype))  12.2 us
    all_to_all x1, waiting for transfers between devices, mirror_tile(): lax.all_to_all(lax.all_to_all(first_leg, 'row', split_axis=2, concat_axis...  11.1 us
    ppermute x4, starting transfers between devices, padded(): after = lax.ppermute(initial, axis, down)  9.85 us
  transfers between devices with their start and end apart: 9, of which 5 were waited for; matrix products, arithmetic and copies ran while one was open for 4% of the time, Pallas kernels for 0%

profile of v2, /device:TPU:7, one launch (start us, length us, event | category | flops | bytes accessed | tf_op | source)
XLA Modules:
  0.0 270.2 jit_solution(4827025605746853047)
XLA Ops:
  1.0 4.4 %collective-permute-start = (bf16[48,8,128]{2,1,0:T(8,128)(2,1)S(1)}, bf16[48,8,128]{2,1,0:T(8,128)(2,1)S(1)}, u32[]{:S(2)}, u32[]{:S(2)}) collective-permute-start(bf16[48,8,128]{2,1,0:T(8,128)(2,1)S(1)} %get-tuple-element.11), channel_id=1, source_target_pairs={{0,16},{16,32},{32,48},{48,64},{64,80},{80,96},{96,112},{112,128},... | collective-permute-start | bytes 294920 | tf_op jit(solution)/shard_map/ppermute | solution.py:17
  5.4 2.4 collective-permute-start.1
  15.8 3.0 %pad_maximum_fusion = bf16[48,80,128]{1,0,2:T(8,128)(2,1)S(1)} fusion(bf16[48,8,128]{1,0,2:T(8,128)(2,1)S(1)} %copy.102, bf16[48,64,128]{1,0,2:T(8,128)(2,1)S(1)} %copy.101, bf16[48,8,128]{1,0,2:T(8,128)(2,1)} %copy.100), kind=kLoop, calls=%fused_computation.31 | loop fusion | flops 2949120 | bytes 1966080 | tf_op jit(solution)/shard_map/concatenate | solution.py:19
  18.8 4.6 %collective-permute-start.2 = (bf16[48,80,8]{1,0,2:T(8,128)(2,1)S(1)}, bf16[48,80,8]{1,0,2:T(8,128)(2,1)S(1)}, u32[]{:S(2)}, u32[]{:S(2)}) collective-permute-start(bf16[48,80,8]{1,0,2:T(8,128)(2,1)S(1)} %get-tuple-element.9), channel_id=1, source_target_pairs={{0,1},{1,2},{2,3},{3,4},{4,5},{5,6},{6,7},{7,8},{8,9},{9,10},{10,1... | collective-permute-start | bytes 184328 | tf_op jit(solution)/shard_map/ppermute | solution.py:17
  23.4 2.4 collective-permute-start.3
  27.3 2.9 %collective-permute-done.3 = bf16[48,80,8]{1,0,2:T(8,128)(2,1)S(1)} collective-permute-done((bf16[48,80,8]{1,0,2:T(8,128)(2,1)S(1)}, bf16[48,80,8]{1,0,2:T(8,128)(2,1)S(1)}, u32[]{:S(2)}, u32[]{:S(2)}) %collective-permute-start.3) | collective-permute-done | bytes 61472 | tf_op jit(solution)/shard_map/ppermute | solution.py:18
  31.9 3.6 %copy.104 = bf16[48,80,1,8,18]{0,3,4,1,2:T(8,128)(2,1)S(1)} copy(bf16[48,80,1,8,18]{1,0,4,3,2:T(8,128)(2,1)} %bitcast.92) | data formatting | bytes 2211840 | tf_op jit(solution)/shard_map/conv_general_dilated | solution.py:25
  36.5 7.9 %maximum_convert_fusion = bf16[64,8,18,48]{3,1,2,0:T(8,128)(2,1)} fusion(f32[48]{0:T(128)S(1)} %get-tuple-element.21, f32[48]{0:T(128)S(1)} %get-tuple-element.24, pred[8,18]{0,1:T(8,128)(4,1)S(1)} %copy-done.8, bf16[48,80,1,7,16]{0,3,4,1,2:T(8,128)(2,1)S(1)} %slice.111, bf16[48,80,1,8,18]{0,3,4,1,2:T(8,128)(2,1)S(1)} %copy.104, ...), kind=kOutput, calls=%fused_computation.8 | convolution fusion | flops 390684672 | bytes 6569984 | tf_op jit(solution)/shard_map/conv_general_dilated | solution.py:25
  44.4 3.6 %copy.105 = bf16[64,8,18,48]{0,3,2,1:T(8,128)(2,1)S(1)} copy(bf16[64,8,18,48]{3,1,2,0:T(8,128)(2,1)} %maximum_convert_fusion) | data formatting | bytes 1769472 | tf_op jit(solution)/shard_map/convert_element_type | solution.py:33
  53.7 3.0 %fusion.13 = bf16[48,64,128]{1,2,0:T(8,128)(2,1)S(1)} fusion(f32[64,128,48]{0,1,2:T(8,128)} %copy.107, bf16[48,64,128]{1,2,0:T(8,128)(2,1)} %copy.99, f32[48]{0:T(128)S(1)} %get-tuple-element.20, f32[48]{0:T(128)S(1)} %get-tuple-element.25), kind=kLoop, calls=%fused_computation.19 | loop fusion | flops 1966080 | bytes 3146112 | tf_op jit(solution)/shard_map/convert_element_type | solution.py:43
  57.5 17.8 %all_to_all.41 = bf16[48,64,128]{2,0,1:T(8,128)(2,1)S(1)} all-to-all(bf16[48,64,128]{2,0,1:T(8,128)(2,1)S(1)} %copy.108), channel_id=1, replica_groups=mesh['row'=32,'col'=16] {'col'}, dimensions={1} | all-to-all | bytes 1572864 | tf_op jit(solution)/shard_map/all_to_all | solution.py:52
  75.4 2.5 copy.128
  77.8 5.3 %reshape.123 = bf16[32,2,6144]{2,1,0:T(2,128)(2,1)S(1)} reshape(bf16[2048,4,48]{2,1,0:T(4,128)(2,1)} %bitcast.91) | data formatting | bytes 1572864
  83.2 60.5 %all_to_all.42 = bf16[32,2,6144]{2,1,0:T(2,128)(2,1)S(1)} all-to-all(bf16[32,2,6144]{2,1,0:T(2,128)(2,1)S(1)} %reshape.123), channel_id=1, replica_groups=mesh['row'=32,'col'=16] {'row'}, dimensions={0} | all-to-all | bytes 1572864 | tf_op jit(solution)/shard_map/all_to_all | solution.py:55
  143.7 3.1 %reshape.124 = bf16[2048,4,48]{2,1,0:T(4,128)(2,1)} reshape(bf16[32,2,6144]{2,1,0:T(2,128)(2,1)S(1)} %all_to_all.42) | data formatting | bytes 1572864
  146.7 2.9 %copy.111 = bf16[48,4,32,64]{3,0,1,2:T(8,128)(2,1)S(1)} copy(bf16[48,4,32,64]{0,1,3,2:T(4,128)(2,1)} %bitcast.90) | data formatting | bytes 1572864 | tf_op jit(solution)/shard_map/all_to_all | solution.py:55
  151.5 6.3 %all-to-all-start.2 = ((bf16[16,2,12288]{2,1,0:T(2,128)(2,1)}), bf16[16,2,12288]{2,1,0:T(2,128)(2,1)}, u32[]{:S(2)}, u32[]{:S(2)}) async-start(bf16[16,2,12288]{2,1,0:T(2,128)(2,1)} %reshape.125), calls=%async_computation.2 | async-start | bytes 1572864 | tf_op jit(solution)/shard_map/all_to_all | solution.py:54
  159.4 11.1 %all-to-all-done.2 = bf16[16,2,12288]{2,1,0:T(2,128)(2,1)} async-done(((bf16[16,2,12288]{2,1,0:T(2,128)(2,1)}), bf16[16,2,12288]{2,1,0:T(2,128)(2,1)}, u32[]{:S(2)}, u32[]{:S(2)}) %all-to-all-start.2) | async-done | bytes 786464 | tf_op jit(solution)/shard_map/all_to_all | solution.py:54
  170.5 3.0 %reshape.126 = bf16[128,48,64]{2,1,0:T(8,128)(2,1)S(1)} reshape(bf16[16,2,12288]{2,1,0:T(2,128)(2,1)} %all-to-all-done.2) | data formatting | bytes 1572864
  177.3 2.3 copy.114
  180.2 2.7 collective-permute-start.5
  182.9 5.0 %collective-permute-start.4 = (bf16[48,16,128]{2,1,0:T(8,128)(2,1)}, bf16[48,16,128]{2,1,0:T(8,128)(2,1)}, u32[]{:S(2)}, u32[]{:S(2)}) collective-permute-start(bf16[48,16,128]{2,1,0:T(8,128)(2,1)} %copy.114), channel_id=1, source_target_pairs={{0,16},{16,32},{32,48},{48,64},{64,80},{80,96},{96,112},{112,128},... | collective-permute-start | bytes 589832 | tf_op jit(solution)/shard_map/ppermute | solution.py:17
  188.6 7.0 %collective-permute-done.4 = bf16[48,16,128]{2,1,0:T(8,128)(2,1)} collective-permute-done((bf16[48,16,128]{2,1,0:T(8,128)(2,1)}, bf16[48,16,128]{2,1,0:T(8,128)(2,1)}, u32[]{:S(2)}, u32[]{:S(2)}) %collective-permute-start.4) | collective-permute-done | bytes 196640 | tf_op jit(solution)/shard_map/ppermute | solution.py:17
  198.8 3.0 %pad_maximum_fusion.1 = bf16[48,96,128]{1,2,0:T(8,128)(2,1)S(1)} fusion(bf16[48,16,128]{1,2,0:T(8,128)(2,1)} %copy.117, bf16[48,64,128]{1,2,0:T(8,128)(2,1)S(1)} %fusion.15, bf16[48,16,128]{1,2,0:T(8,128)(2,1)S(1)} %copy.116), kind=kLoop, calls=%fused_computation.32 | loop fusion | flops 3538944 | bytes 2359296 | tf_op jit(solution)/shard_map/concatenate | solution.py:19
  203.9 2.3 collective-permute-start.7
  207.6 4.1 %collective-permute-done.7 = bf16[48,96,16]{1,2,0:T(8,128)(2,1)S(1)} collective-permute-done((bf16[48,96,16]{1,2,0:T(8,128)(2,1)S(1)}, bf16[48,96,16]{1,2,0:T(8,128)(2,1)S(1)}, u32[]{:S(2)}, u32[]{:S(2)}) %collective-permute-start.7) | collective-permute-done | bytes 147488 | tf_op jit(solution)/shard_map/ppermute | solution.py:18
  212.3 12.2 %copy.120 = bf16[1,48,96,160]{1,0,3,2:T(2,128)(2,1)} copy(bf16[1,48,96,160]{2,3,1,0:T(8,128)(2,1)S(1)} %maximum_maximum_fusion) | data formatting | bytes 2949120 | tf_op jit(solution)/shard_map/max | solution.py:24
  224.5 28.7 %fusion.27 = f32[1,96,64,128]{1,0,3,2:T(1,128)} fusion(bf16[1,48,96,160]{1,0,3,2:T(2,128)(2,1)} %copy.120, bf16[48,48,3,3]{0,1,3,2:T(8,128)(2,1)} %bitcast.100, bf16[48,48,3,3]{0,1,3,2:T(8,128)(2,1)} %copy.119), kind=kOutput, calls=%fused_computation.38 | convolution fusion | flops 679643136 | bytes 4703232 | tf_op jit(solution)/shard_map/conv_general_dilated | solution.py:25
  253.2 2.9 %maximum_convert_fusion.1 = bf16[96,64,128]{0,2,1:T(8,128)(2,1)S(1)} fusion(f32[96,64,128]{0,2,1:T(8,128)} %bitcast.96, f32[96]{0:T(128)S(1)} %copy-done.7, f32[96]{0:T(128)S(1)} %pad_maximum_fusion.4), kind=kLoop, calls=%fused_computation.9 | loop fusion | flops 3145728 | bytes 4719360 | tf_op jit(solution)/shard_map/convert_element_type | solution.py:33
  258.9 3.3 %copy.122 = f32[64,128,48]{0,1,2:T(8,128)} copy(f32[64,128,48]{1,2,0:T(8,128)} %fusion.19) | data formatting | bytes 3145728 | tf_op jit(solution)/shard_map/oc,chw->ohw/dot_general | solution.py:37
  262.2 2.3 copy.124
  264.5 4.1 %multiply_convert_fusion = bf16[48,64,128]{1,2,0:T(8,128)(2,1)S(1)} fusion(f32[64,128,48]{0,1,2:T(8,128)} %copy.124, bf16[48,64,128]{1,2,0:T(8,128)(2,1)S(1)} %fusion.15, f32[64,128,48]{0,1,2:T(8,128)} %copy.122, f32[48]{0:T(128)S(1)} %get-tuple-element.19, f32[48]{0:T(128)S(1)} %get-tuple-element.26), kind=kLoop, calls=%fused_computation.23 | loop fusion | flops 5505024 | bytes 4718976 | tf_op jit(solution)/shard_map/convert_element_type | solution.py:66
  (58 shorter events, 39.6 us)
Async XLA Ops:
  0.0 10.5 %copy-start.2 = (bf16[48,64,128]{2,1,0:T(8,128)(2,1)S(1)}, bf16[48,64,128]{2,1,0:T(8,128)(2,1)}, u32[]{:S(2)}) copy-start(bf16[48,64,128]{2,1,0:T(8,128)(2,1)} %param.5) | copy-start | bytes 2359300
  1.0 13.1 %collective-permute-start = (bf16[48,8,128]{2,1,0:T(8,128)(2,1)S(1)}, bf16[48,8,128]{2,1,0:T(8,128)(2,1)S(1)}, u32[]{:S(2)}, u32[]{:S(2)}) collective-permute-start(bf16[48,8,128]{2,1,0:T(8,128)(2,1)S(1)} %get-tuple-element.11), channel_id=1, source_target_pairs={{0,16},{16,32},{32,48},{48,64},{64,80},{80,96},{96,112},{112,128},... | collective-permute-start | bytes 294920 | tf_op jit(solution)/shard_map/ppermute | solution.py:17
  5.4 7.8 %collective-permute-start.1 = (bf16[48,8,128]{2,1,0:T(8,128)(2,1)S(1)}, bf16[48,8,128]{2,1,0:T(8,128)(2,1)S(1)}, u32[]{:S(2)}, u32[]{:S(2)}) collective-permute-start(bf16[48,8,128]{2,1,0:T(8,128)(2,1)S(1)} %get-tuple-element.12), channel_id=1, source_target_pairs={{16,0},{32,16},{48,32},{64,48},{80,64},{96,80},{112,96},{128,112},... | collective-permute-start | bytes 294920 | tf_op jit(solution)/shard_map/ppermute | solution.py:18
  15.8 10.0 %copy-start = (bf16[48,8,128]{1,0,2:T(8,128)(2,1)S(1)}, bf16[48,8,128]{1,0,2:T(8,128)(2,1)}, u32[]{:S(2)}) copy-start(bf16[48,8,128]{1,0,2:T(8,128)(2,1)} %copy.100) | copy-start | bytes 294916
  18.8 8.5 %collective-permute-start.2 = (bf16[48,80,8]{1,0,2:T(8,128)(2,1)S(1)}, bf16[48,80,8]{1,0,2:T(8,128)(2,1)S(1)}, u32[]{:S(2)}, u32[]{:S(2)}) collective-permute-start(bf16[48,80,8]{1,0,2:T(8,128)(2,1)S(1)} %get-tuple-element.9), channel_id=1, source_target_pairs={{0,1},{1,2},{2,3},{3,4},{4,5},{5,6},{6,7},{7,8},{8,9},{9,10},{10,1... | collective-permute-start | bytes 184328 | tf_op jit(solution)/shard_map/ppermute | solution.py:17
  23.4 6.8 %collective-permute-start.3 = (bf16[48,80,8]{1,0,2:T(8,128)(2,1)S(1)}, bf16[48,80,8]{1,0,2:T(8,128)(2,1)S(1)}, u32[]{:S(2)}, u32[]{:S(2)}) collective-permute-start(bf16[48,80,8]{1,0,2:T(8,128)(2,1)S(1)} %get-tuple-element.10), channel_id=1, source_target_pairs={{1,0},{2,1},{3,2},{4,3},{5,4},{6,5},{7,6},{8,7},{9,8},{10,9},{11,1... | collective-permute-start | bytes 184328 | tf_op jit(solution)/shard_map/ppermute | solution.py:18
  35.5 0.9 copy-start.3
  35.6 0.9 copy-start.8
  48.0 2.0 copy-start.5
  149.6 8.2 %copy-start.4 = (bf16[2,3,3,48,48]{4,3,2,1,0:T(8,128)(2,1)S(1)}, bf16[2,3,3,48,48]{4,3,2,1,0:T(8,128)(2,1)}, u32[]{:S(2)}) copy-start(bf16[2,3,3,48,48]{4,3,2,1,0:T(8,128)(2,1)} %param.6) | copy-start | bytes 248836
  151.5 18.9 %all-to-all-start.2 = ((bf16[16,2,12288]{2,1,0:T(2,128)(2,1)}), bf16[16,2,12288]{2,1,0:T(2,128)(2,1)}, u32[]{:S(2)}, u32[]{:S(2)}) async-start(bf16[16,2,12288]{2,1,0:T(2,128)(2,1)} %reshape.125), calls=%async_computation.2 | async-start | bytes 1572864 | tf_op jit(solution)/shard_map/all_to_all | solution.py:54
  180.2 17.1 %collective-permute-start.5 = (bf16[48,16,128]{2,1,0:T(8,128)(2,1)S(1)}, bf16[48,16,128]{2,1,0:T(8,128)(2,1)S(1)}, u32[]{:S(2)}, u32[]{:S(2)}) collective-permute-start(bf16[48,16,128]{2,1,0:T(8,128)(2,1)S(1)} %copy.115), channel_id=1, source_target_pairs={{16,0},{32,16},{48,32},{64,48},{80,64},{96,80},{112,96},{128,112},... | collective-permute-start | bytes 589832 | tf_op jit(solution)/shard_map/ppermute | solution.py:18
  182.9 12.7 %collective-permute-start.4 = (bf16[48,16,128]{2,1,0:T(8,128)(2,1)}, bf16[48,16,128]{2,1,0:T(8,128)(2,1)}, u32[]{:S(2)}, u32[]{:S(2)}) collective-permute-start(bf16[48,16,128]{2,1,0:T(8,128)(2,1)} %copy.114), channel_id=1, source_target_pairs={{0,16},{16,32},{32,48},{48,64},{64,80},{80,96},{96,112},{112,128},... | collective-permute-start | bytes 589832 | tf_op jit(solution)/shard_map/ppermute | solution.py:17
  198.8 7.3 %copy-start.1 = (bf16[48,16,128]{1,2,0:T(8,128)(2,1)S(1)}, bf16[48,16,128]{1,2,0:T(8,128)(2,1)}, u32[]{:S(2)}) copy-start(bf16[48,16,128]{1,2,0:T(8,128)(2,1)} %copy.117) | copy-start | bytes 589828
  201.8 5.8 %collective-permute-start.6 = (bf16[48,96,16]{1,2,0:T(8,128)(2,1)S(1)}, bf16[48,96,16]{1,2,0:T(8,128)(2,1)S(1)}, u32[]{:S(2)}, u32[]{:S(2)}) collective-permute-start(bf16[48,96,16]{1,2,0:T(8,128)(2,1)S(1)} %get-tuple-element.5), channel_id=1, source_target_pairs={{0,1},{1,2},{2,3},{3,4},{4,5},{5,6},{6,7},{7,8},{8,9},{9,10},{10,1... | collective-permute-start | bytes 442376 | tf_op jit(solution)/shard_map/ppermute | solution.py:17
  203.9 7.9 %collective-permute-start.7 = (bf16[48,96,16]{1,2,0:T(8,128)(2,1)S(1)}, bf16[48,96,16]{1,2,0:T(8,128)(2,1)S(1)}, u32[]{:S(2)}, u32[]{:S(2)}) collective-permute-start(bf16[48,96,16]{1,2,0:T(8,128)(2,1)S(1)} %get-tuple-element.6), channel_id=1, source_target_pairs={{1,0},{2,1},{3,2},{4,3},{5,4},{6,5},{7,6},{8,7},{9,8},{10,9},{11,1... | collective-permute-start | bytes 442376 | tf_op jit(solution)/shard_map/ppermute | solution.py:18
  224.5 28.8 %copy-start.7 = (f32[96]{0:T(128)S(1)}, f32[96]{0:T(128)}, u32[]{:S(2)}) copy-start(f32[96]{0:T(128)} %pad_maximum_fusion.5) | copy-start | bytes 1156
  253.2 2.9 %copy-start.6 = (bf16[2,48,48]{2,1,0:T(8,128)(2,1)S(1)}, bf16[2,48,48]{2,1,0:T(8,128)(2,1)}, u32[]{:S(2)}) copy-start(bf16[2,48,48]{2,1,0:T(8,128)(2,1)} %param.7) | copy-start | bytes 27652

commit v3 on v2

--- a/solution.py
+++ b/solution.py
@@ -20,17 +20,21 @@
     return value
 
 
-def hidden_of(extended_input, kernel, gain, bias, dilation_rate):
+def hidden_of(extended_input, kernel, gain, bias, dilation_rate, tile_rows, tile_cols):
     active = jnp.maximum(extended_input, jnp.zeros((), extended_input.dtype))
-    spread = lax.conv_general_dilated(
-        active[None],
-        kernel,
-        (1, 1),
-        "VALID",
-        rhs_dilation=(dilation_rate, dilation_rate),
-        preferred_element_type=jnp.float32,
-    )[0]
-    return jnp.maximum(spread * gain[:, None, None] + bias[:, None, None], 0.0).astype(jnp.bfloat16)
+    windows = [
+        lax.slice(
+            active,
+            (0, p * dilation_rate, q * dilation_rate),
+            (active.shape[0], p * dilation_rate + tile_rows, q * dilation_rate + tile_cols),
+        )
+        for p in range(3)
+        for q in range(3)
+    ]
+    stacked = jnp.stack(windows, axis=0)
+    spread = jnp.einsum("toc,tchw->ohw", kernel, stacked, preferred_element_type=jnp.float32)
+    hidden = jnp.maximum(spread * gain[:, None, None] + bias[:, None, None], 0.0)
+    return hidden.astype(jnp.bfloat16)
 
 
 def block_output(current_state, hidden, gain_pair, bias_pair, pointwise):
@@ -40,7 +44,7 @@
         + branch * gain_pair[1][:, None, None]
         + bias_pair[1][:, None, None]
     )
-    return summed.astype(jnp.bfloat16)
+    return lax.reduce_precision(summed, exponent_bits=8, mantissa_bits=7).astype(jnp.bfloat16)
 
 
 def mirror_tile(output_map):
@@ -67,19 +71,21 @@
 
 
 def body(features, w_dilated, w_pointwise, norm_gain, norm_bias):
-    kernel = jnp.transpose(w_dilated[0], (2, 3, 0, 1))
+    count, tile_rows, tile_cols = features.shape
+    kernel = w_dilated[0].reshape(9, count, count)
     extended = padded(features, (("row", 1), ("col", 2)), FIRST_DILATION)
-    hidden = hidden_of(extended, kernel, norm_gain[0, 0], norm_bias[0, 0], FIRST_DILATION)
+    hidden = hidden_of(
+        extended, kernel, norm_gain[0, 0], norm_bias[0, 0], FIRST_DILATION, tile_rows, tile_cols
+    )
     output_map = block_output(features, hidden, norm_gain[0], norm_bias[0], w_pointwise[0])
     state = mean_of(output_map, mirror_tile(output_map))
 
-    kernel = jnp.transpose(w_dilated[1], (2, 3, 0, 1))
-    both = jnp.concatenate([kernel, jnp.swapaxes(kernel, 2, 3)], axis=0)
+    kernel = w_dilated[1]
+    both = jnp.concatenate([kernel, jnp.swapaxes(kernel, 0, 1)], axis=2).reshape(9, 2 * count, count)
     extended = padded(state, (("row", 1), ("col", 2)), SECOND_DILATION)
     gain = jnp.concatenate([norm_gain[1, 0], norm_gain[1, 0]])
     bias = jnp.concatenate([norm_bias[1, 0], norm_bias[1, 0]])
-    hidden = hidden_of(extended, both, gain, bias, SECOND_DILATION)
-    count = state.shape[0]
+    hidden = hidden_of(extended, both, gain, bias, SECOND_DILATION, tile_rows, tile_cols)
     direct = block_output(state, hidden[:count], norm_gain[1], norm_bias[1], w_pointwise[1])
     mirrored = block_output(state, hidden[count:], norm_gain[1], norm_bias[1], w_pointwise[1])
     return mean_of(direct, mirrored)

time: 274 us -> 196 us (0.72)
  matrix products: 40.9 us -> 7.65 us
  local copies, waits for them, and re-layouts: 68.7 us -> 46 us
  blocking collectives: 78.3 us -> 97.5 us
  waiting for transfers between devices: 26.2 us -> 9.06 us
  other arithmetic: 23.4 us -> 6.8 us
  starting transfers between devices: 32.1 us -> 26.7 us
    conv_general_dilated x2 -> x0, matrix products: 36.6 us -> none  [hidden_of(): lax.conv_general_dilated(active[None], kernel, (1, 1), 'VALID', rhs_dilat...]
    all_to_all x0 -> x1, blocking collectives: none -> 17.2 us  [mirror_tile(): lax.all_to_all(lax.all_to_all(first_leg, 'row', split_axis=2, concat_axis...]
    max x1 -> x0, local copies, waits for them, and re-layouts: 12.2 us -> none  [hidden_of(): active = jnp.maximum(extended_input, jnp.zeros((), extended_input.dtype))]
    all_to_all x1 -> x0, waiting for transfers between devices: 11.1 us -> none  [mirror_tile(): lax.all_to_all(lax.all_to_all(first_leg, 'row', split_axis=2, concat_axis...]
    concatenate x4 -> x1, other arithmetic: 8.78 us -> 0.14 us  [padded(): value = jnp.concatenate([before, value, after], axis=dim)]
    dot_general x3 -> x0, local copies, waits for them, and re-layouts: 7.79 us -> none  [block_output(): jnp.einsum('oc,chw->ohw', pointwise, hidden, preferred_element_type=jnp.f...]
    all_to_all x1 -> x0, starting transfers between devices: 6.28 us -> none  [mirror_tile(): lax.all_to_all(lax.all_to_all(first_leg, 'row', split_axis=2, concat_axis...]
    convert_element_type x2 -> x0, other arithmetic: 5.87 us -> none  [the longest x1 2.95 us: block_output(): return summed.astype(jnp.bfloat16)]
  transfers between devices with their start and end apart: 9 -> 8, of which waited for: 5 -> 4; matrix products, arithmetic and copies ran while one was open for 4% -> 5% of each run, Pallas kernels for 0% -> 0%
where the time goes in v3:
time: 196 us; the launch traced here: 194 us
  blocking collectives  97.5 us (50%)
  local copies, waits for them, and re-layouts  46 us (23%)
  starting transfers between devices  26.7 us (14%)
  waiting for transfers between devices  9.06 us (5%)
  matrix products  7.65 us (4%)
  other arithmetic  6.8 us (3%)
    all_to_all x1, blocking collectives, mirror_tile(): lax.all_to_all(first_leg, 'row', split_axis=2, concat_axis=1, tiled=True)  60.6 us
    unnamed x42, local copies, waits for them, and re-layouts  22.7 us
    all_to_all x1, blocking collectives, mirror_tile(): lax.all_to_all(output_map, 'col', split_axis=1, concat_axis=2, tiled=True)  19.7 us
    all_to_all x1, blocking collectives, mirror_tile(): lax.all_to_all(lax.all_to_all(first_leg, 'row', split_axis=2, concat_axis...  17.2 us
    ppermute x4, starting transfers between devices, padded(): after = lax.ppermute(initial, axis, down)  14.6 us
    ppermute x4, starting transfers between devices, padded(): before = lax.ppermute(last, axis, up)  12.2 us
    dot_general x3, matrix products, block_output(): jnp.einsum('oc,chw->ohw', pointwise, hidden, preferred_element_type=jnp.f...  6.21 us
    ppermute x4, waiting for transfers between devices, padded(): after = lax.ppermute(initial, axis, down)  5.32 us
  transfers between devices with their start and end apart: 8, of which 4 were waited for; matrix products, arithmetic and copies ran while one was open for 5% of the time, Pallas kernels for 0%

profile of v3, /device:TPU:7, one launch (start us, length us, event | category | flops | bytes accessed | tf_op | source)
XLA Modules:
  0.0 194.2 jit_solution(2925190944318067050)
XLA Ops:
  1.0 4.4 %collective-permute-start = (bf16[48,8,128]{2,0,1:T(8,128)(2,1)S(1)}, bf16[48,8,128]{2,0,1:T(8,128)(2,1)S(1)}, u32[]{:S(2)}, u32[]{:S(2)}) collective-permute-start(bf16[48,8,128]{2,0,1:T(8,128)(2,1)S(1)} %copy.55), channel_id=1, source_target_pairs={{0,16},{16,32},{32,48},{48,64},{64,80},{80,96},{96,112},{112,128},... | collective-permute-start | bytes 294920 | tf_op jit(solution)/shard_map/ppermute | solution.py:17
  5.4 2.4 %collective-permute-start.1 = (bf16[48,8,128]{2,0,1:T(8,128)(2,1)S(1)}, bf16[48,8,128]{2,0,1:T(8,128)(2,1)S(1)}, u32[]{:S(2)}, u32[]{:S(2)}) collective-permute-start(bf16[48,8,128]{2,0,1:T(8,128)(2,1)S(1)} %copy.56), channel_id=1, source_target_pairs={{16,0},{32,16},{48,32},{64,48},{80,64},{96,80},{112,96},{128,112},... | collective-permute-start | bytes 294920 | tf_op jit(solution)/shard_map/ppermute | solution.py:18
  7.8 1.7 fusion.55
  9.5 1.7 constant_dynamic-update-slice_fusion.1
  11.2 2.0 %collective-permute-done.1 = bf16[48,8,128]{2,0,1:T(8,128)(2,1)S(1)} collective-permute-done((bf16[48,8,128]{2,0,1:T(8,128)(2,1)S(1)}, bf16[48,8,128]{2,0,1:T(8,128)(2,1)S(1)}, u32[]{:S(2)}, u32[]{:S(2)}) %collective-permute-start.1) | collective-permute-done | bytes 98336 | tf_op jit(solution)/shard_map/ppermute | solution.py:18
  15.1 4.0 %collective-permute-start.3 = (bf16[48,80,8]{1,2,0:T(8,128)(2,1)S(1)}, bf16[48,80,8]{1,2,0:T(8,128)(2,1)S(1)}, u32[]{:S(2)}, u32[]{:S(2)}) collective-permute-start(bf16[48,80,8]{1,2,0:T(8,128)(2,1)S(1)} %copy.25), channel_id=1, source_target_pairs={{1,0},{2,1},{3,2},{4,3},{5,4},{6,5},{7,6},{8,7},{9,8},{10,9},{11,1... | collective-permute-start | bytes 184328 | tf_op jit(solution)/shard_map/ppermute | solution.py:18
  19.1 2.5 %collective-permute-start.2 = (bf16[48,80,8]{1,2,0:T(8,128)(2,1)S(1)}, bf16[48,80,8]{1,2,0:T(8,128)(2,1)S(1)}, u32[]{:S(2)}, u32[]{:S(2)}) collective-permute-start(bf16[48,80,8]{1,2,0:T(8,128)(2,1)S(1)} %copy.24), channel_id=1, source_target_pairs={{0,1},{1,2},{2,3},{3,4},{4,5},{5,6},{6,7},{7,8},{8,9},{9,10},{10,1... | collective-permute-start | bytes 184328 | tf_op jit(solution)/shard_map/ppermute | solution.py:17
  24.7 1.4 maximum_maximum_fusion.1
  29.1 2.9 %copy-done.4 = bf16[9,48,64,128]{3,1,0,2:T(8,128)(2,1)} copy-done((bf16[9,48,64,128]{3,1,0,2:T(8,128)(2,1)}, bf16[9,48,64,128]{3,1,0,2:T(8,128)(2,1)S(1)}, u32[]{:S(2)}) %copy-start.4) | copy-done | bytes 7077912
  32.0 5.2 %fusion.11 = bf16[48,64,128]{2,0,1:T(8,128)(2,1)S(1)} fusion(bf16[9,48,48,1]{2,1,0,3:T(8,128)(2,1)S(1)} %bitcast.199, bf16[9,48,64,128]{3,1,0,2:T(8,128)(2,1)} %copy-done.4, f32[48]{0:T(128)S(1)} %get-tuple-element.21, f32[48]{0:T(128)S(1)} %get-tuple-element.26, f32[48]{0:T(128)S(1)} %get-tuple-element.22, f32[48]{0:T(128)S(1)} %get-tuple-element.25, ...), kind=kOutput, calls=%fused_computation.18 | convolution fusion | flops 381419520 | bytes 8775680 | tf_op jit(solution)/shard_map/oc,chw->ohw/dot_general | solution.py:41
  37.2 19.7 %all_to_all.41 = bf16[48,64,128]{2,0,1:T(8,128)(2,1)S(1)} all-to-all(bf16[48,64,128]{2,0,1:T(8,128)(2,1)S(1)} %fusion.11), channel_id=1, replica_groups=mesh['row'=32,'col'=16] {'col'}, dimensions={1} | all-to-all | bytes 1572864 | tf_op jit(solution)/shard_map/all_to_all | solution.py:56
  56.9 1.3 copy.51
  58.3 3.2 %reshape.34 = bf16[32,2,6144]{2,1,0:T(2,128)(2,1)S(1)} reshape(bf16[2048,4,48]{2,1,0:T(4,128)(2,1)S(1)} %bitcast.193) | data formatting | bytes 1572864
  61.5 60.6 %all_to_all.42 = bf16[32,2,6144]{2,1,0:T(2,128)(2,1)} all-to-all(bf16[32,2,6144]{2,1,0:T(2,128)(2,1)S(1)} %reshape.34), channel_id=1, replica_groups=mesh['row'=32,'col'=16] {'row'}, dimensions={0} | all-to-all | bytes 1572864 | tf_op jit(solution)/shard_map/all_to_all | solution.py:59
  122.1 5.7 %reshape.35 = bf16[2048,4,48]{2,1,0:T(4,128)(2,1)S(1)} reshape(bf16[32,2,6144]{2,1,0:T(2,128)(2,1)} %all_to_all.42) | data formatting | bytes 1572864
  127.8 2.3 %copy.38 = bf16[48,4,32,64]{3,0,1,2:T(8,128)(2,1)} copy(bf16[48,4,32,64]{0,1,3,2:T(4,128)(2,1)S(1)} %bitcast.192) | data formatting | bytes 1572864 | tf_op jit(solution)/shard_map/all_to_all | solution.py:59
  130.0 3.1 %reshape.36 = bf16[16,2,12288]{2,1,0:T(2,128)(2,1)S(1)} reshape(bf16[128,48,64]{2,1,0:T(8,128)(2,1)} %bitcast.194) | data formatting | bytes 1572864
  133.1 17.2 %all_to_all.43 = bf16[16,2,12288]{2,1,0:T(2,128)(2,1)S(1)} all-to-all(bf16[16,2,12288]{2,1,0:T(2,128)(2,1)S(1)} %reshape.36), channel_id=1, replica_groups=mesh['row'=32,'col'=16] {'col'}, dimensions={0} | all-to-all | bytes 1572864 | tf_op jit(solution)/shard_map/all_to_all | solution.py:58
  152.0 2.0 %copy.40 = f32[48,64,128]{2,0,1:T(8,128)} copy(f32[48,64,128]{1,0,2:T(8,128)S(1)} %bitcast.191) | data formatting | bytes 3145728 | tf_op jit(solution)/shard_map/convert_element_type | solution.py:70
  154.0 1.8 multiply_convert_fusion.1
  155.9 2.7 %collective-permute-start.4 = (bf16[48,16,128]{2,0,1:T(8,128)(2,1)S(1)}, bf16[48,16,128]{2,0,1:T(8,128)(2,1)S(1)}, u32[]{:S(2)}, u32[]{:S(2)}) collective-permute-start(bf16[48,16,128]{2,0,1:T(8,128)(2,1)S(1)} %get-tuple-element.9), channel_id=1, source_target_pairs={{0,16},{16,32},{32,48},{48,64},{64,80},{80,96},{96,112},{112,128},... | collective-permute-start | bytes 589832 | tf_op jit(solution)/shard_map/ppermute | solution.py:17
  158.6 4.1 %collective-permute-start.5 = (bf16[48,16,128]{2,0,1:T(8,128)(2,1)S(1)}, bf16[48,16,128]{2,0,1:T(8,128)(2,1)S(1)}, u32[]{:S(2)}, u32[]{:S(2)}) collective-permute-start(bf16[48,16,128]{2,0,1:T(8,128)(2,1)S(1)} %get-tuple-element.10), channel_id=1, source_target_pairs={{16,0},{32,16},{48,32},{64,48},{80,64},{96,80},{112,96},{128,112},... | collective-permute-start | bytes 589832 | tf_op jit(solution)/shard_map/ppermute | solution.py:18
  162.7 2.7 %collective-permute-done.4 = bf16[48,16,128]{2,0,1:T(8,128)(2,1)S(1)} collective-permute-done((bf16[48,16,128]{2,0,1:T(8,128)(2,1)S(1)}, bf16[48,16,128]{2,0,1:T(8,128)(2,1)S(1)}, u32[]{:S(2)}, u32[]{:S(2)}) %collective-permute-start.4) | collective-permute-done | bytes 196640 | tf_op jit(solution)/shard_map/ppermute | solution.py:17
  165.4 3.3 %collective-permute-done.5 = bf16[48,16,128]{2,0,1:T(8,128)(2,1)S(1)} collective-permute-done((bf16[48,16,128]{2,0,1:T(8,128)(2,1)S(1)}, bf16[48,16,128]{2,0,1:T(8,128)(2,1)S(1)}, u32[]{:S(2)}, u32[]{:S(2)}) %collective-permute-start.5) | collective-permute-done | bytes 196640 | tf_op jit(solution)/shard_map/ppermute | solution.py:18
  169.3 1.6 copy.43
  171.8 4.0 %collective-permute-start.7 = (bf16[48,96,16]{1,2,0:T(8,128)(2,1)S(1)}, bf16[48,96,16]{1,2,0:T(8,128)(2,1)}, u32[]{:S(2)}, u32[]{:S(2)}) collective-permute-start(bf16[48,96,16]{1,2,0:T(8,128)(2,1)S(1)} %copy.44), channel_id=1, source_target_pairs={{1,0},{2,1},{3,2},{4,3},{5,4},{6,5},{7,6},{8,7},{9,8},{10,9},{11,1... | collective-permute-start | bytes 442376 | tf_op jit(solution)/shard_map/ppermute | solution.py:18
  175.8 2.7 %collective-permute-start.6 = (bf16[48,96,16]{1,2,0:T(8,128)(2,1)}, bf16[48,96,16]{1,2,0:T(8,128)(2,1)S(1)}, u32[]{:S(2)}, u32[]{:S(2)}) collective-permute-start(bf16[48,96,16]{1,2,0:T(8,128)(2,1)} %copy.43), channel_id=1, source_target_pairs={{0,1},{1,2},{2,3},{3,4},{4,5},{5,6},{6,7},{7,8},{8,9},{9,10},{10,1... | collective-permute-start | bytes 442376 | tf_op jit(solution)/shard_map/ppermute | solution.py:17
  178.6 1.6 copy.41
  180.2 1.6 copy.42
  183.5 1.8 copy.46
  185.3 2.3 %maximum_maximum_fusion = bf16[48,96,160]{2,0,1:T(8,128)(2,1)S(1)} fusion(bf16[48,96,16]{2,0,1:T(8,128)(2,1)S(1)} %copy.46, bf16[48,16,128]{2,0,1:T(8,128)(2,1)S(1)} %collective-permute-done.5, bf16[48,64,128]{2,0,1:T(8,128)(2,1)S(1)} %multiply_convert_fusion.1, bf16[48,16,128]{2,0,1:T(8,128)(2,1)S(1)} %collective-permute-done.4, bf16[48,96,16]{2,0,1:T(8,128)(2,1)S(1)} %copy.45), kind=kLoop, calls=%fused_computation.5 | loop fusion | flops 8847360 | bytes 2949120 | tf_op jit(solution)/shard_map/max | solution.py:24
  190.6 1.4 fusion.2
  (64 shorter events, 19.0 us)
Async XLA Ops:
  1.0 8.5 %collective-permute-start = (bf16[48,8,128]{2,0,1:T(8,128)(2,1)S(1)}, bf16[48,8,128]{2,0,1:T(8,128)(2,1)S(1)}, u32[]{:S(2)}, u32[]{:S(2)}) collective-permute-start(bf16[48,8,128]{2,0,1:T(8,128)(2,1)S(1)} %copy.55), channel_id=1, source_target_pairs={{0,16},{16,32},{32,48},{48,64},{64,80},{80,96},{96,112},{112,128},... | collective-permute-start | bytes 294920 | tf_op jit(solution)/shard_map/ppermute | solution.py:17
  5.4 7.8 %collective-permute-start.1 = (bf16[48,8,128]{2,0,1:T(8,128)(2,1)S(1)}, bf16[48,8,128]{2,0,1:T(8,128)(2,1)S(1)}, u32[]{:S(2)}, u32[]{:S(2)}) collective-permute-start(bf16[48,8,128]{2,0,1:T(8,128)(2,1)S(1)} %copy.56), channel_id=1, source_target_pairs={{16,0},{32,16},{48,32},{64,48},{80,64},{96,80},{112,96},{128,112},... | collective-permute-start | bytes 294920 | tf_op jit(solution)/shard_map/ppermute | solution.py:18
  13.2 8.4 %copy-start.5 = (f32[2,2,48]{2,1,0:T(2,128)S(1)}, f32[2,2,48]{2,1,0:T(2,128)}, u32[]{:S(2)}) copy-start(f32[2,2,48]{2,1,0:T(2,128)} %param.9) | copy-start | bytes 2308
  13.2 8.4 %copy-start.6 = (f32[2,2,48]{2,1,0:T(2,128)S(1)}, f32[2,2,48]{2,1,0:T(2,128)}, u32[]{:S(2)}) copy-start(f32[2,2,48]{2,1,0:T(2,128)} %param.8) | copy-start | bytes 2308
  15.1 8.8 %collective-permute-start.3 = (bf16[48,80,8]{1,2,0:T(8,128)(2,1)S(1)}, bf16[48,80,8]{1,2,0:T(8,128)(2,1)S(1)}, u32[]{:S(2)}, u32[]{:S(2)}) collective-permute-start(bf16[48,80,8]{1,2,0:T(8,128)(2,1)S(1)} %copy.25), channel_id=1, source_target_pairs={{1,0},{2,1},{3,2},{4,3},{5,4},{6,5},{7,6},{8,7},{9,8},{10,9},{11,1... | collective-permute-start | bytes 184328 | tf_op jit(solution)/shard_map/ppermute | solution.py:18
  19.1 4.1 %collective-permute-start.2 = (bf16[48,80,8]{1,2,0:T(8,128)(2,1)S(1)}, bf16[48,80,8]{1,2,0:T(8,128)(2,1)S(1)}, u32[]{:S(2)}, u32[]{:S(2)}) collective-permute-start(bf16[48,80,8]{1,2,0:T(8,128)(2,1)S(1)} %copy.24), channel_id=1, source_target_pairs={{0,1},{1,2},{2,3},{3,4},{4,5},{5,6},{6,7},{7,8},{8,9},{9,10},{10,1... | collective-permute-start | bytes 184328 | tf_op jit(solution)/shard_map/ppermute | solution.py:17
  28.1 3.9 %copy-start.1 = (bf16[48,64,128]{2,1,0:T(8,128)(2,1)S(1)}, bf16[48,64,128]{2,1,0:T(8,128)(2,1)}, u32[]{:S(2)}) copy-start(bf16[48,64,128]{2,1,0:T(8,128)(2,1)} %param.5) | copy-start | bytes 2359300
  28.1 3.9 %copy-start.7 = (bf16[2,48,48]{2,1,0:T(8,128)(2,1)S(1)}, bf16[2,48,48]{2,1,0:T(8,128)(2,1)}, u32[]{:S(2)}) copy-start(bf16[2,48,48]{2,1,0:T(8,128)(2,1)} %param.7) | copy-start | bytes 27652
  29.1 2.9 %copy-start.4 = (bf16[9,48,64,128]{3,1,0,2:T(8,128)(2,1)}, bf16[9,48,64,128]{3,1,0,2:T(8,128)(2,1)S(1)}, u32[]{:S(2)}) copy-start(bf16[9,48,64,128]{3,1,0,2:T(8,128)(2,1)S(1)} %fusion.27) | copy-start | bytes 21233668
  37.2 19.8 %copy-start = (bf16[48,64,128]{2,0,1:T(8,128)(2,1)}, bf16[48,64,128]{2,0,1:T(8,128)(2,1)S(1)}, u32[]{:S(2)}) copy-start(bf16[48,64,128]{2,0,1:T(8,128)(2,1)S(1)} %fusion.11) | copy-start | bytes 2359300
  155.9 9.5 %collective-permute-start.4 = (bf16[48,16,128]{2,0,1:T(8,128)(2,1)S(1)}, bf16[48,16,128]{2,0,1:T(8,128)(2,1)S(1)}, u32[]{:S(2)}, u32[]{:S(2)}) collective-permute-start(bf16[48,16,128]{2,0,1:T(8,128)(2,1)S(1)} %get-tuple-element.9), channel_id=1, source_target_pairs={{0,16},{16,32},{32,48},{48,64},{64,80},{80,96},{96,112},{112,128},... | collective-permute-start | bytes 589832 | tf_op jit(solution)/shard_map/ppermute | solution.py:17
  158.6 10.2 %collective-permute-start.5 = (bf16[48,16,128]{2,0,1:T(8,128)(2,1)S(1)}, bf16[48,16,128]{2,0,1:T(8,128)(2,1)S(1)}, u32[]{:S(2)}, u32[]{:S(2)}) collective-permute-start(bf16[48,16,128]{2,0,1:T(8,128)(2,1)S(1)} %get-tuple-element.10), channel_id=1, source_target_pairs={{16,0},{32,16},{48,32},{64,48},{80,64},{96,80},{112,96},{128,112},... | collective-permute-start | bytes 589832 | tf_op jit(solution)/shard_map/ppermute | solution.py:18
  171.8 11.7 %collective-permute-start.7 = (bf16[48,96,16]{1,2,0:T(8,128)(2,1)S(1)}, bf16[48,96,16]{1,2,0:T(8,128)(2,1)}, u32[]{:S(2)}, u32[]{:S(2)}) collective-permute-start(bf16[48,96,16]{1,2,0:T(8,128)(2,1)S(1)} %copy.44), channel_id=1, source_target_pairs={{1,0},{2,1},{3,2},{4,3},{5,4},{6,5},{7,6},{8,7},{9,8},{10,9},{11,1... | collective-permute-start | bytes 442376 | tf_op jit(solution)/shard_map/ppermute | solution.py:18
  175.8 6.8 %collective-permute-start.6 = (bf16[48,96,16]{1,2,0:T(8,128)(2,1)}, bf16[48,96,16]{1,2,0:T(8,128)(2,1)S(1)}, u32[]{:S(2)}, u32[]{:S(2)}) collective-permute-start(bf16[48,96,16]{1,2,0:T(8,128)(2,1)} %copy.43), channel_id=1, source_target_pairs={{0,1},{1,2},{2,3},{3,4},{4,5},{5,6},{6,7},{7,8},{8,9},{9,10},{10,1... | collective-permute-start | bytes 442376 | tf_op jit(solution)/shard_map/ppermute | solution.py:17
  189.6 1.0 copy-start.2
  189.6 1.0 copy-start.3
  190.6 1.5 copy-start.8

commit v4 on v3

--- a/solution.py
+++ b/solution.py
@@ -7,17 +7,38 @@
 SECOND_DILATION = 16
 
 
-def padded(value, sides, width):
-    for axis, dim in sides:
-        size, length = (lax.axis_size(axis), value.shape[dim])
-        up = [(i, (i + 1) % size) for i in range(size - 1)]
-        down = [(j, i) for i, j in up]
-        last = lax.slice_in_dim(value, length - width, length, axis=dim)
-        initial = lax.slice_in_dim(value, 0, width, axis=dim)
-        before = lax.ppermute(last, axis, up)
-        after = lax.ppermute(initial, axis, down)
-        value = jnp.concatenate([before, value, after], axis=dim)
-    return value
+def halo(value, width):
+    n_row = lax.axis_size("row")
+    n_col = lax.axis_size("col")
+    rows, cols = value.shape[1], value.shape[2]
+    head = slice(0, width)
+    tail = slice(rows - width, rows), slice(cols - width, cols)
+
+    def shifted(piece, d_row, d_col):
+        pairs = []
+        for r in range(n_row):
+            for c in range(n_col):
+                if 0 <= r + d_row < n_row and 0 <= c + d_col < n_col:
+                    pairs.append((r * n_col + c, (r + d_row) * n_col + c + d_col))
+        return lax.ppermute(piece, ("row", "col"), pairs)
+
+    all_rows, all_cols = slice(0, rows), slice(0, cols)
+    top = shifted(value[:, tail[0], all_cols], 1, 0)
+    bottom = shifted(value[:, head, all_cols], -1, 0)
+    left = shifted(value[:, all_rows, tail[1]], 0, 1)
+    right = shifted(value[:, all_rows, head], 0, -1)
+    top_left = shifted(value[:, tail[0], tail[1]], 1, 1)
+    top_right = shifted(value[:, tail[0], head], 1, -1)
+    bottom_left = shifted(value[:, head, tail[1]], -1, 1)
+    bottom_right = shifted(value[:, head, head], -1, -1)
+    return jnp.concatenate(
+        [
+            jnp.concatenate([top_left, top, top_right], axis=2),
+            jnp.concatenate([left, value, right], axis=2),
+            jnp.concatenate([bottom_left, bottom, bottom_right], axis=2),
+        ],
+        axis=1,
+    )
 
 
 def hidden_of(extended_input, kernel, gain, bias, dilation_rate, tile_rows, tile_cols):
@@ -73,7 +94,7 @@
 def body(features, w_dilated, w_pointwise, norm_gain, norm_bias):
     count, tile_rows, tile_cols = features.shape
     kernel = w_dilated[0].reshape(9, count, count)
-    extended = padded(features, (("row", 1), ("col", 2)), FIRST_DILATION)
+    extended = halo(features, FIRST_DILATION)
     hidden = hidden_of(
         extended, kernel, norm_gain[0, 0], norm_bias[0, 0], FIRST_DILATION, tile_rows, tile_cols
     )
@@ -82,7 +103,7 @@
 
     kernel = w_dilated[1]
     both = jnp.concatenate([kernel, jnp.swapaxes(kernel, 0, 1)], axis=2).reshape(9, 2 * count, count)
-    extended = padded(state, (("row", 1), ("col", 2)), SECOND_DILATION)
+    extended = halo(state, SECOND_DILATION)
     gain = jnp.concatenate([norm_gain[1, 0], norm_gain[1, 0]])
     bias = jnp.concatenate([norm_bias[1, 0], norm_bias[1, 0]])
     hidden = hidden_of(extended, both, gain, bias, SECOND_DILATION, tile_rows, tile_cols)

time: 196 us -> 229 us (1.17)
  starting transfers between devices: 26.7 us -> 57.3 us
  local copies, waits for them, and re-layouts: 46 us -> 43.1 us
  other arithmetic: 6.8 us -> 9.4 us
  waiting for transfers between devices: 9.06 us -> 11.5 us
    ppermute x8 -> x16, starting transfers between devices: 26.7 us -> 57.3 us  [shifted(): return lax.ppermute(piece, ('row', 'col'), pairs)]
    max x2, other arithmetic: 3.63 us -> 7.06 us  [hidden_of(): active = jnp.maximum(extended_input, jnp.zeros((), extended_input.dtype))]
    ppermute x8 -> x16, waiting for transfers between devices: 9.06 us -> 11.5 us  [shifted(): return lax.ppermute(piece, ('row', 'col'), pairs)]
    all_to_all x1, blocking collectives: 60.6 us -> 63 us  [mirror_tile(): lax.all_to_all(first_leg, 'row', split_axis=2, concat_axis=1, tiled=True)]
    unnamed x42 -> x41, local copies, waits for them, and re-layouts: 22.7 us -> 23.8 us
  transfers between devices with their start and end apart: 8 -> 16, of which waited for: 4 -> 3; matrix products, arithmetic and copies ran while one was open for 5% -> 4% of each run, Pallas kernels for 0% -> 0%
where the time goes in v4:
time: 229 us; the launch traced here: 227 us
  blocking collectives  97.9 us (43%)
  starting transfers between devices  57.3 us (25%)
  local copies, waits for them, and re-layouts  43.1 us (19%)
  waiting for transfers between devices  11.5 us (5%)
  other arithmetic  9.4 us (4%)
  matrix products  7.63 us (3%)
    all_to_all x1, blocking collectives, mirror_tile(): lax.all_to_all(first_leg, 'row', split_axis=2, concat_axis=1, tiled=True)  63 us
    ppermute x16, starting transfers between devices, shifted(): return lax.ppermute(piece, ('row', 'col'), pairs)  57.3 us
    unnamed x41, local copies, waits for them, and re-layouts  23.8 us
    all_to_all x1, blocking collectives, mirror_tile(): lax.all_to_all(output_map, 'col', split_axis=1, concat_axis=2, tiled=True)  17.7 us
    all_to_all x1, blocking collectives, mirror_tile(): lax.all_to_all(lax.all_to_all(first_leg, 'row', split_axis=2, concat_axis...  17.2 us
    ppermute x16, waiting for transfers between devices, shifted(): return lax.ppermute(piece, ('row', 'col'), pairs)  11.5 us
    max x2, other arithmetic, hidden_of(): active = jnp.maximum(extended_input, jnp.zeros((), extended_input.dtype))  7.06 us
    dot_general x3, matrix products, block_output(): jnp.einsum('oc,chw->ohw', pointwise, hidden, preferred_element_type=jnp.f...  6.19 us
  transfers between devices with their start and end apart: 16, of which 3 were waited for; matrix products, arithmetic and copies ran while one was open for 4% of the time, Pallas kernels for 0%

profile of v4, /device:TPU:7, one launch (start us, length us, event | category | flops | bytes accessed | tf_op | source)
XLA Modules:
  0.0 227.4 jit_solution(1419696139052169247)
XLA Ops:
  2.4 4.5 %collective-permute-start.1 = (bf16[48,8,128]{2,0,1:T(8,128)(2,1)}, bf16[48,8,128]{2,0,1:T(8,128)(2,1)}, u32[]{:S(2)}, u32[]{:S(2)}) collective-permute-start(bf16[48,8,128]{2,0,1:T(8,128)(2,1)} %get-tuple-element.17), channel_id=1, source_target_pairs={{0,16},{1,17},{2,18},{3,19},{4,20},{5,21},{6,22},{7,23},{8,24},{9,... | collective-permute-start | bytes 294920 | tf_op jit(solution)/shard_map/ppermute | solution.py:23
  6.9 3.0 %collective-permute-start.6 = (bf16[48,8,128]{2,0,1:T(8,128)(2,1)}, bf16[48,8,128]{2,0,1:T(8,128)(2,1)}, u32[]{:S(2)}, u32[]{:S(2)}) collective-permute-start(bf16[48,8,128]{2,0,1:T(8,128)(2,1)} %get-tuple-element.18), channel_id=1, source_target_pairs={{16,0},{17,1},{18,2},{19,3},{20,4},{21,5},{22,6},{23,7},{24,8},{25... | collective-permute-start | bytes 294920 | tf_op jit(solution)/shard_map/ppermute | solution.py:23
  10.8 5.9 %collective-permute-start = (bf16[48,8,8]{2,0,1:T(8,128)(2,1)}, bf16[48,8,8]{2,0,1:T(8,128)(2,1)}, u32[]{:S(2)}, u32[]{:S(2)}) collective-permute-start(bf16[48,8,8]{2,0,1:T(8,128)(2,1)} %get-tuple-element.13), channel_id=1, source_target_pairs={{0,17},{1,18},{2,19},{3,20},{4,21},{5,22},{6,23},{7,24},{8,25},{9,... | collective-permute-start | bytes 18440 | tf_op jit(solution)/shard_map/ppermute | solution.py:23
  17.9 1.9 collective-permute-start.4
  20.1 4.5 %collective-permute-start.3 = (bf16[48,64,8]{1,2,0:T(8,128)(2,1)S(1)}, bf16[48,64,8]{1,2,0:T(8,128)(2,1)S(1)}, u32[]{:S(2)}, u32[]{:S(2)}) collective-permute-start(bf16[48,64,8]{1,2,0:T(8,128)(2,1)S(1)} %copy.57), channel_id=1, source_target_pairs={{0,1},{1,2},{2,3},{3,4},{4,5},{5,6},{6,7},{7,8},{8,9},{9,10},{10,1... | collective-permute-start | bytes 147464 | tf_op jit(solution)/shard_map/ppermute | solution.py:23
  25.7 1.9 collective-permute-start.5
  27.6 6.0 %collective-permute-start.2 = (bf16[48,8,8]{2,0,1:T(8,128)(2,1)}, bf16[48,8,8]{2,0,1:T(8,128)(2,1)}, u32[]{:S(2)}, u32[]{:S(2)}) collective-permute-start(bf16[48,8,8]{2,0,1:T(8,128)(2,1)} %get-tuple-element.15), channel_id=1, source_target_pairs={{1,16},{2,17},{3,18},{4,19},{5,20},{6,21},{7,22},{8,23},{9,24},{10... | collective-permute-start | bytes 18440 | tf_op jit(solution)/shard_map/ppermute | solution.py:23
  33.7 1.9 collective-permute-start.7
  37.8 5.2 %collective-permute-done.7 = bf16[48,8,8]{2,0,1:T(8,128)(2,1)} collective-permute-done((bf16[48,8,8]{2,0,1:T(8,128)(2,1)}, bf16[48,8,8]{2,0,1:T(8,128)(2,1)}, u32[]{:S(2)}, u32[]{:S(2)}) %collective-permute-start.7) | collective-permute-done | bytes 6176 | tf_op jit(solution)/shard_map/ppermute | solution.py:23
  43.0 3.2 %maximum_maximum_fusion.1 = bf16[48,80,144]{2,0,1:T(8,128)(2,1)S(1)} fusion(bf16[48,8,8]{2,0,1:T(8,128)(2,1)} %collective-permute-done.7, bf16[48,8,128]{2,0,1:T(8,128)(2,1)} %collective-permute-done.6, bf16[48,8,8]{2,0,1:T(8,128)(2,1)} %collective-permute-done.5, bf16[48,64,8]{2,0,1:T(8,128)(2,1)S(1)} %copy.28, bf16[48,64,128]{2,0,1:T(8,128)(2,1)S(1)} %copy.20, ...), kind=kLoop, calls=%fused_computation.6 | loop fusion | flops 11059200 | bytes 2211840 | tf_op jit(solution)/shard_map/max | solution.py:45
  49.2 2.9 %copy-done.5 = bf16[9,48,64,128]{3,1,0,2:T(8,128)(2,1)} copy-done((bf16[9,48,64,128]{3,1,0,2:T(8,128)(2,1)}, bf16[9,48,64,128]{3,1,0,2:T(8,128)(2,1)S(1)}, u32[]{:S(2)}) %copy-start.5) | copy-done | bytes 7077912
  52.1 5.2 %fusion.11 = bf16[48,64,128]{2,0,1:T(8,128)(2,1)S(1)} fusion(bf16[9,48,48,1]{2,1,0,3:T(8,128)(2,1)S(1)} %bitcast.199, bf16[9,48,64,128]{3,1,0,2:T(8,128)(2,1)} %copy-done.5, f32[48]{0:T(128)S(1)} %get-tuple-element.29, f32[48]{0:T(128)S(1)} %get-tuple-element.34, f32[48]{0:T(128)S(1)} %get-tuple-element.30, f32[48]{0:T(128)S(1)} %get-tuple-element.33, ...), kind=kOutput, calls=%fused_computation.18 | convolution fusion | flops 381419520 | bytes 8775680 | tf_op jit(solution)/shard_map/oc,chw->ohw/dot_general | solution.py:62
  57.3 17.7 %all_to_all.41 = bf16[48,64,128]{2,0,1:T(8,128)(2,1)S(1)} all-to-all(bf16[48,64,128]{2,0,1:T(8,128)(2,1)S(1)} %fusion.11), channel_id=1, replica_groups=mesh['row'=32,'col'=16] {'col'}, dimensions={1} | all-to-all | bytes 1572864 | tf_op jit(solution)/shard_map/all_to_all | solution.py:77
  76.3 3.2 %reshape.34 = bf16[32,2,6144]{2,1,0:T(2,128)(2,1)S(1)} reshape(bf16[2048,4,48]{2,1,0:T(4,128)(2,1)S(1)} %bitcast.193) | data formatting | bytes 1572864
  79.6 63.0 %all_to_all.42 = bf16[32,2,6144]{2,1,0:T(2,128)(2,1)} all-to-all(bf16[32,2,6144]{2,1,0:T(2,128)(2,1)S(1)} %reshape.34), channel_id=1, replica_groups=mesh['row'=32,'col'=16] {'row'}, dimensions={0} | all-to-all | bytes 1572864 | tf_op jit(solution)/shard_map/all_to_all | solution.py:80
  142.6 5.7 %reshape.35 = bf16[2048,4,48]{2,1,0:T(4,128)(2,1)S(1)} reshape(bf16[32,2,6144]{2,1,0:T(2,128)(2,1)} %all_to_all.42) | data formatting | bytes 1572864
  148.3 2.3 %copy.42 = bf16[48,4,32,64]{3,0,1,2:T(8,128)(2,1)} copy(bf16[48,4,32,64]{0,1,3,2:T(4,128)(2,1)S(1)} %bitcast.192) | data formatting | bytes 1572864 | tf_op jit(solution)/shard_map/all_to_all | solution.py:80
  150.6 3.1 %reshape.36 = bf16[16,2,12288]{2,1,0:T(2,128)(2,1)S(1)} reshape(bf16[128,48,64]{2,1,0:T(8,128)(2,1)} %bitcast.194) | data formatting | bytes 1572864
  153.7 17.2 %all_to_all.43 = bf16[16,2,12288]{2,1,0:T(2,128)(2,1)S(1)} all-to-all(bf16[16,2,12288]{2,1,0:T(2,128)(2,1)S(1)} %reshape.36), channel_id=1, replica_groups=mesh['row'=32,'col'=16] {'col'}, dimensions={0} | all-to-all | bytes 1572864 | tf_op jit(solution)/shard_map/all_to_all | solution.py:79
  172.5 2.1 copy.44
  174.6 1.8 multiply_convert_fusion.1
  178.5 2.7 %collective-permute-start.9 = (bf16[48,16,128]{2,0,1:T(8,128)(2,1)}, bf16[48,16,128]{2,0,1:T(8,128)(2,1)S(1)}, u32[]{:S(2)}, u32[]{:S(2)}) collective-permute-start(bf16[48,16,128]{2,0,1:T(8,128)(2,1)} %get-tuple-element.9), channel_id=1, source_target_pairs={{0,16},{1,17},{2,18},{3,19},{4,20},{5,21},{6,22},{7,23},{8,24},{9,... | collective-permute-start | bytes 589832 | tf_op jit(solution)/shard_map/ppermute | solution.py:23
  181.1 4.1 %collective-permute-start.14 = (bf16[48,16,128]{2,0,1:T(8,128)(2,1)}, bf16[48,16,128]{2,0,1:T(8,128)(2,1)S(1)}, u32[]{:S(2)}, u32[]{:S(2)}) collective-permute-start(bf16[48,16,128]{2,0,1:T(8,128)(2,1)} %get-tuple-element.10), channel_id=1, source_target_pairs={{16,0},{17,1},{18,2},{19,3},{20,4},{21,5},{22,6},{23,7},{24,8},{25... | collective-permute-start | bytes 589832 | tf_op jit(solution)/shard_map/ppermute | solution.py:23
  185.3 3.0 %collective-permute-start.8 = (bf16[48,16,16]{2,0,1:T(8,128)(2,1)}, bf16[48,16,16]{2,0,1:T(8,128)(2,1)S(1)}, u32[]{:S(2)}, u32[]{:S(2)}) collective-permute-start(bf16[48,16,16]{2,0,1:T(8,128)(2,1)} %get-tuple-element.5), channel_id=1, source_target_pairs={{0,17},{1,18},{2,19},{3,20},{4,21},{5,22},{6,23},{7,24},{8,25},{9,... | collective-permute-start | bytes 73736 | tf_op jit(solution)/shard_map/ppermute | solution.py:23
  190.2 2.9 %collective-permute-start.12 = (bf16[48,64,16]{1,2,0:T(8,128)(2,1)S(1)}, bf16[48,64,16]{1,2,0:T(8,128)(2,1)S(1)}, u32[]{:S(2)}, u32[]{:S(2)}) collective-permute-start(bf16[48,64,16]{1,2,0:T(8,128)(2,1)S(1)} %copy.48), channel_id=1, source_target_pairs={{1,0},{2,1},{3,2},{4,3},{5,4},{6,5},{7,6},{8,7},{9,8},{10,9},{11,1... | collective-permute-start | bytes 294920 | tf_op jit(solution)/shard_map/ppermute | solution.py:23
  193.1 3.6 %collective-permute-start.11 = (bf16[48,64,16]{1,2,0:T(8,128)(2,1)}, bf16[48,64,16]{1,2,0:T(8,128)(2,1)S(1)}, u32[]{:S(2)}, u32[]{:S(2)}) collective-permute-start(bf16[48,64,16]{1,2,0:T(8,128)(2,1)} %copy.47), channel_id=1, source_target_pairs={{0,1},{1,2},{2,3},{3,4},{4,5},{5,6},{6,7},{7,8},{8,9},{9,10},{10,1... | collective-permute-start | bytes 294920 | tf_op jit(solution)/shard_map/ppermute | solution.py:23
  196.8 3.2 %collective-permute-start.15 = (bf16[48,16,16]{2,0,1:T(8,128)(2,1)}, bf16[48,16,16]{2,0,1:T(8,128)(2,1)}, u32[]{:S(2)}, u32[]{:S(2)}) collective-permute-start(bf16[48,16,16]{2,0,1:T(8,128)(2,1)} %get-tuple-element.6), channel_id=1, source_target_pairs={{17,0},{18,1},{19,2},{20,3},{21,4},{22,5},{23,6},{24,7},{25,8},{26... | collective-permute-start | bytes 73736 | tf_op jit(solution)/shard_map/ppermute | solution.py:23
  200.0 1.9 collective-permute-start.13
  201.9 6.3 %collective-permute-start.10 = (bf16[48,16,16]{2,0,1:T(8,128)(2,1)}, bf16[48,16,16]{2,0,1:T(8,128)(2,1)}, u32[]{:S(2)}, u32[]{:S(2)}) collective-permute-start(bf16[48,16,16]{2,0,1:T(8,128)(2,1)} %get-tuple-element.8), channel_id=1, source_target_pairs={{1,16},{2,17},{3,18},{4,19},{5,20},{6,21},{7,22},{8,23},{9,24},{10... | collective-permute-start | bytes 73736 | tf_op jit(solution)/shard_map/ppermute | solution.py:23
  210.7 1.8 collective-permute-done.13
  212.6 4.5 %collective-permute-done.10 = bf16[48,16,16]{2,0,1:T(8,128)(2,1)} collective-permute-done((bf16[48,16,16]{2,0,1:T(8,128)(2,1)}, bf16[48,16,16]{2,0,1:T(8,128)(2,1)}, u32[]{:S(2)}, u32[]{:S(2)}) %collective-permute-start.10) | collective-permute-done | bytes 24608 | tf_op jit(solution)/shard_map/ppermute | solution.py:23
  217.1 3.8 %maximum_maximum_fusion = bf16[48,96,160]{2,0,1:T(8,128)(2,1)S(1)} fusion(bf16[48,16,16]{2,0,1:T(8,128)(2,1)} %collective-permute-done.15, bf16[48,16,128]{2,0,1:T(8,128)(2,1)S(1)} %collective-permute-done.14, bf16[48,16,16]{2,0,1:T(8,128)(2,1)} %collective-permute-done.13, bf16[48,64,16]{2,0,1:T(8,128)(2,1)S(1)} %copy.50, ...), kind=kLoop, calls=%fused_computation.5 | loop fusion | flops 14745600 | bytes 2949120 | tf_op jit(solution)/shard_map/max | solution.py:45
  (77 shorter events, 27.0 us)
Async XLA Ops:
  0.0 16.7 %copy-start = (bf16[48,64,128]{2,1,0:T(8,128)(2,1)S(1)}, bf16[48,64,128]{2,1,0:T(8,128)(2,1)}, u32[]{:S(2)}) copy-start(bf16[48,64,128]{2,1,0:T(8,128)(2,1)} %param.5) | copy-start | bytes 2359300
  2.4 33.2 %copy-start.6 = (f32[2,2,48]{2,1,0:T(2,128)S(1)}, f32[2,2,48]{2,1,0:T(2,128)}, u32[]{:S(2)}) copy-start(f32[2,2,48]{2,1,0:T(2,128)} %param.9) | copy-start | bytes 2308
  2.4 33.2 %copy-start.7 = (f32[2,2,48]{2,1,0:T(2,128)S(1)}, f32[2,2,48]{2,1,0:T(2,128)}, u32[]{:S(2)}) copy-start(f32[2,2,48]{2,1,0:T(2,128)} %param.8) | copy-start | bytes 2308
  2.4 40.5 %collective-permute-start.1 = (bf16[48,8,128]{2,0,1:T(8,128)(2,1)}, bf16[48,8,128]{2,0,1:T(8,128)(2,1)}, u32[]{:S(2)}, u32[]{:S(2)}) collective-permute-start(bf16[48,8,128]{2,0,1:T(8,128)(2,1)} %get-tuple-element.17), channel_id=1, source_target_pairs={{0,16},{1,17},{2,18},{3,19},{4,20},{5,21},{6,22},{7,23},{8,24},{9,... | collective-permute-start | bytes 294920 | tf_op jit(solution)/shard_map/ppermute | solution.py:23
  6.9 36.0 %collective-permute-start.6 = (bf16[48,8,128]{2,0,1:T(8,128)(2,1)}, bf16[48,8,128]{2,0,1:T(8,128)(2,1)}, u32[]{:S(2)}, u32[]{:S(2)}) collective-permute-start(bf16[48,8,128]{2,0,1:T(8,128)(2,1)} %get-tuple-element.18), channel_id=1, source_target_pairs={{16,0},{17,1},{18,2},{19,3},{20,4},{21,5},{22,6},{23,7},{24,8},{25... | collective-permute-start | bytes 294920 | tf_op jit(solution)/shard_map/ppermute | solution.py:23
  10.8 14.9 %collective-permute-start = (bf16[48,8,8]{2,0,1:T(8,128)(2,1)}, bf16[48,8,8]{2,0,1:T(8,128)(2,1)}, u32[]{:S(2)}, u32[]{:S(2)}) collective-permute-start(bf16[48,8,8]{2,0,1:T(8,128)(2,1)} %get-tuple-element.13), channel_id=1, source_target_pairs={{0,17},{1,18},{2,19},{3,20},{4,21},{5,22},{6,23},{7,24},{8,25},{9,... | collective-permute-start | bytes 18440 | tf_op jit(solution)/shard_map/ppermute | solution.py:23
  17.9 9.7 %collective-permute-start.4 = (bf16[48,64,8]{1,2,0:T(8,128)(2,1)}, bf16[48,64,8]{1,2,0:T(8,128)(2,1)S(1)}, u32[]{:S(2)}, u32[]{:S(2)}) collective-permute-start(bf16[48,64,8]{1,2,0:T(8,128)(2,1)} %copy.58), channel_id=1, source_target_pairs={{1,0},{2,1},{3,2},{4,3},{5,4},{6,5},{7,6},{8,7},{9,8},{10,9},{11,1... | collective-permute-start | bytes 147464 | tf_op jit(solution)/shard_map/ppermute | solution.py:23
  20.1 13.6 %collective-permute-start.3 = (bf16[48,64,8]{1,2,0:T(8,128)(2,1)S(1)}, bf16[48,64,8]{1,2,0:T(8,128)(2,1)S(1)}, u32[]{:S(2)}, u32[]{:S(2)}) collective-permute-start(bf16[48,64,8]{1,2,0:T(8,128)(2,1)S(1)} %copy.57), channel_id=1, source_target_pairs={{0,1},{1,2},{2,3},{3,4},{4,5},{5,6},{6,7},{7,8},{8,9},{9,10},{10,1... | collective-permute-start | bytes 147464 | tf_op jit(solution)/shard_map/ppermute | solution.py:23
  25.7 12.1 %collective-permute-start.5 = (bf16[48,8,8]{2,0,1:T(8,128)(2,1)}, bf16[48,8,8]{2,0,1:T(8,128)(2,1)}, u32[]{:S(2)}, u32[]{:S(2)}) collective-permute-start(bf16[48,8,8]{2,0,1:T(8,128)(2,1)} %get-tuple-element.14), channel_id=1, source_target_pairs={{16,1},{17,2},{18,3},{19,4},{20,5},{21,6},{22,7},{23,8},{24,9},{25... | collective-permute-start | bytes 18440 | tf_op jit(solution)/shard_map/ppermute | solution.py:23
  27.6 8.0 %copy-start.4 = (bf16[48,64,8]{1,2,0:T(8,128)(2,1)}, bf16[48,64,8]{1,2,0:T(8,128)(2,1)S(1)}, u32[]{:S(2)}) copy-start(bf16[48,64,8]{1,2,0:T(8,128)(2,1)S(1)} %collective-permute-done.4) | copy-start | bytes 147460
  27.6 10.2 %collective-permute-start.2 = (bf16[48,8,8]{2,0,1:T(8,128)(2,1)}, bf16[48,8,8]{2,0,1:T(8,128)(2,1)}, u32[]{:S(2)}, u32[]{:S(2)}) collective-permute-start(bf16[48,8,8]{2,0,1:T(8,128)(2,1)} %get-tuple-element.15), channel_id=1, source_target_pairs={{1,16},{2,17},{3,18},{4,19},{5,20},{6,21},{7,22},{8,23},{9,24},{10... | collective-permute-start | bytes 18440 | tf_op jit(solution)/shard_map/ppermute | solution.py:23
  33.7 9.3 %collective-permute-start.7 = (bf16[48,8,8]{2,0,1:T(8,128)(2,1)}, bf16[48,8,8]{2,0,1:T(8,128)(2,1)}, u32[]{:S(2)}, u32[]{:S(2)}) collective-permute-start(bf16[48,8,8]{2,0,1:T(8,128)(2,1)} %get-tuple-element.16), channel_id=1, source_target_pairs={{17,0},{18,1},{19,2},{20,3},{21,4},{22,5},{23,6},{24,7},{25,8},{26... | collective-permute-start | bytes 18440 | tf_op jit(solution)/shard_map/ppermute | solution.py:23
  47.8 4.3 %copy-start.8 = (bf16[2,48,48]{2,1,0:T(8,128)(2,1)S(1)}, bf16[2,48,48]{2,1,0:T(8,128)(2,1)}, u32[]{:S(2)}) copy-start(bf16[2,48,48]{2,1,0:T(8,128)(2,1)} %param.7) | copy-start | bytes 27652
  49.2 2.9 %copy-start.5 = (bf16[9,48,64,128]{3,1,0,2:T(8,128)(2,1)}, bf16[9,48,64,128]{3,1,0,2:T(8,128)(2,1)S(1)}, u32[]{:S(2)}) copy-start(bf16[9,48,64,128]{3,1,0,2:T(8,128)(2,1)S(1)} %fusion.27) | copy-start | bytes 21233668
  57.3 17.7 %copy-start.1 = (bf16[48,64,128]{2,0,1:T(8,128)(2,1)}, bf16[48,64,128]{2,0,1:T(8,128)(2,1)S(1)}, u32[]{:S(2)}) copy-start(bf16[48,64,128]{2,0,1:T(8,128)(2,1)S(1)} %fusion.11) | copy-start | bytes 2359300
  178.5 38.6 %collective-permute-start.9 = (bf16[48,16,128]{2,0,1:T(8,128)(2,1)}, bf16[48,16,128]{2,0,1:T(8,128)(2,1)S(1)}, u32[]{:S(2)}, u32[]{:S(2)}) collective-permute-start(bf16[48,16,128]{2,0,1:T(8,128)(2,1)} %get-tuple-element.9), channel_id=1, source_target_pairs={{0,16},{1,17},{2,18},{3,19},{4,20},{5,21},{6,22},{7,23},{8,24},{9,... | collective-permute-start | bytes 589832 | tf_op jit(solution)/shard_map/ppermute | solution.py:23
  181.1 35.9 %collective-permute-start.14 = (bf16[48,16,128]{2,0,1:T(8,128)(2,1)}, bf16[48,16,128]{2,0,1:T(8,128)(2,1)S(1)}, u32[]{:S(2)}, u32[]{:S(2)}) collective-permute-start(bf16[48,16,128]{2,0,1:T(8,128)(2,1)} %get-tuple-element.10), channel_id=1, source_target_pairs={{16,0},{17,1},{18,2},{19,3},{20,4},{21,5},{22,6},{23,7},{24,8},{25... | collective-permute-start | bytes 589832 | tf_op jit(solution)/shard_map/ppermute | solution.py:23
  185.3 11.5 %collective-permute-start.8 = (bf16[48,16,16]{2,0,1:T(8,128)(2,1)}, bf16[48,16,16]{2,0,1:T(8,128)(2,1)S(1)}, u32[]{:S(2)}, u32[]{:S(2)}) collective-permute-start(bf16[48,16,16]{2,0,1:T(8,128)(2,1)} %get-tuple-element.5), channel_id=1, source_target_pairs={{0,17},{1,18},{2,19},{3,20},{4,21},{5,22},{6,23},{7,24},{8,25},{9,... | collective-permute-start | bytes 73736 | tf_op jit(solution)/shard_map/ppermute | solution.py:23
  190.2 9.8 %collective-permute-start.12 = (bf16[48,64,16]{1,2,0:T(8,128)(2,1)S(1)}, bf16[48,64,16]{1,2,0:T(8,128)(2,1)S(1)}, u32[]{:S(2)}, u32[]{:S(2)}) collective-permute-start(bf16[48,64,16]{1,2,0:T(8,128)(2,1)S(1)} %copy.48), channel_id=1, source_target_pairs={{1,0},{2,1},{3,2},{4,3},{5,4},{6,5},{7,6},{8,7},{9,8},{10,9},{11,1... | collective-permute-start | bytes 294920 | tf_op jit(solution)/shard_map/ppermute | solution.py:23
  193.1 8.8 %collective-permute-start.11 = (bf16[48,64,16]{1,2,0:T(8,128)(2,1)}, bf16[48,64,16]{1,2,0:T(8,128)(2,1)S(1)}, u32[]{:S(2)}, u32[]{:S(2)}) collective-permute-start(bf16[48,64,16]{1,2,0:T(8,128)(2,1)} %copy.47), channel_id=1, source_target_pairs={{0,1},{1,2},{2,3},{3,4},{4,5},{5,6},{6,7},{7,8},{8,9},{9,10},{10,1... | collective-permute-start | bytes 294920 | tf_op jit(solution)/shard_map/ppermute | solution.py:23
  196.8 11.5 %copy-start.2 = (bf16[48,16,16]{2,0,1:T(8,128)(2,1)}, bf16[48,16,16]{2,0,1:T(8,128)(2,1)S(1)}, u32[]{:S(2)}) copy-start(bf16[48,16,16]{2,0,1:T(8,128)(2,1)S(1)} %collective-permute-done.8) | copy-start | bytes 73732
  196.8 13.9 %collective-permute-start.15 = (bf16[48,16,16]{2,0,1:T(8,128)(2,1)}, bf16[48,16,16]{2,0,1:T(8,128)(2,1)}, u32[]{:S(2)}, u32[]{:S(2)}) collective-permute-start(bf16[48,16,16]{2,0,1:T(8,128)(2,1)} %get-tuple-element.6), channel_id=1, source_target_pairs={{17,0},{18,1},{19,2},{20,3},{21,4},{22,5},{23,6},{24,7},{25,8},{26... | collective-permute-start | bytes 73736 | tf_op jit(solution)/shard_map/ppermute | solution.py:23
  200.0 8.4 %copy-start.3 = (bf16[48,64,16]{1,2,0:T(8,128)(2,1)}, bf16[48,64,16]{1,2,0:T(8,128)(2,1)S(1)}, u32[]{:S(2)}) copy-start(bf16[48,64,16]{1,2,0:T(8,128)(2,1)S(1)} %collective-permute-done.12) | copy-start | bytes 294916
  200.0 12.6 %collective-permute-start.13 = (bf16[48,16,16]{2,0,1:T(8,128)(2,1)}, bf16[48,16,16]{2,0,1:T(8,128)(2,1)}, u32[]{:S(2)}, u32[]{:S(2)}) collective-permute-start(bf16[48,16,16]{2,0,1:T(8,128)(2,1)} %get-tuple-element.7), channel_id=1, source_target_pairs={{16,1},{17,2},{18,3},{19,4},{20,5},{21,6},{22,7},{23,8},{24,9},{25... | collective-permute-start | bytes 73736 | tf_op jit(solution)/shard_map/ppermute | solution.py:23
  201.9 15.1 %collective-permute-start.10 = (bf16[48,16,16]{2,0,1:T(8,128)(2,1)}, bf16[48,16,16]{2,0,1:T(8,128)(2,1)}, u32[]{:S(2)}, u32[]{:S(2)}) collective-permute-start(bf16[48,16,16]{2,0,1:T(8,128)(2,1)} %get-tuple-element.8), channel_id=1, source_target_pairs={{1,16},{2,17},{3,18},{4,19},{5,20},{6,21},{7,22},{8,23},{9,24},{10... | collective-permute-start | bytes 73736 | tf_op jit(solution)/shard_map/ppermute | solution.py:23

commit v5 on v3

--- a/solution.py
+++ b/solution.py
@@ -47,27 +47,34 @@
     return lax.reduce_precision(summed, exponent_bits=8, mantissa_bits=7).astype(jnp.bfloat16)
 
 
-def mirror_tile(output_map):
-    n_row = lax.axis_size("row")
+def mirror_pieces(output_map):
     n_col = lax.axis_size("col")
     channel_count, tile_rows, tile_cols = output_map.shape
-    sub_rows = tile_rows // n_col
-    ratio = n_row // n_col
-    first_leg = lax.all_to_all(output_map, "col", split_axis=1, concat_axis=2, tiled=True)
-    count = first_leg.shape[0]
-    moved = lax.all_to_all(
-        lax.all_to_all(first_leg, "row", split_axis=2, concat_axis=1, tiled=True),
-        "col",
-        split_axis=1,
-        concat_axis=1,
-        tiled=True,
-    )
-    grouped = moved.reshape(count, n_col, ratio, sub_rows, tile_rows)
-    return jnp.transpose(grouped, (0, 4, 2, 1, 3)).reshape(count, tile_rows, tile_cols)
+    k = tile_cols // tile_rows
+    c_lo = channel_count // n_col
+    flat = tile_rows * tile_rows
+    t = output_map.reshape(n_col, c_lo, tile_rows, k, tile_rows)
+    t = jnp.transpose(t, (0, 1, 3, 4, 2)).reshape(n_col, c_lo, k, flat)
+    t = lax.all_to_all(t, "col", 0, 0, tiled=True)
+    t = jnp.transpose(t, (0, 2, 1, 3)).reshape(n_col * k, c_lo, flat)
+    t = lax.all_to_all(t, "row", 0, 0, tiled=True)
+    t = t.reshape(n_col, k * c_lo, flat)
+    t = lax.all_to_all(t, "col", 0, 0, tiled=True)
+    t = t.reshape(n_col, k, c_lo, tile_rows, tile_rows)
+    return [t[:, s].reshape(channel_count, tile_rows, tile_rows) for s in range(k)]
 
 
 def mean_of(a, b):
     return ((a.astype(jnp.float32) + b.astype(jnp.float32)) * 0.5).astype(jnp.bfloat16)
+
+
+def symmetrized(output_map):
+    tile_rows = output_map.shape[1]
+    halves = [
+        mean_of(output_map[:, :, s * tile_rows:(s + 1) * tile_rows], piece)
+        for s, piece in enumerate(mirror_pieces(output_map))
+    ]
+    return jnp.concatenate(halves, axis=2)
 
 
 def body(features, w_dilated, w_pointwise, norm_gain, norm_bias):
@@ -78,7 +85,7 @@
         extended, kernel, norm_gain[0, 0], norm_bias[0, 0], FIRST_DILATION, tile_rows, tile_cols
     )
     output_map = block_output(features, hidden, norm_gain[0], norm_bias[0], w_pointwise[0])
-    state = mean_of(output_map, mirror_tile(output_map))
+    state = symmetrized(output_map)
 
     kernel = w_dilated[1]
     both = jnp.concatenate([kernel, jnp.swapaxes(kernel, 0, 1)], axis=2).reshape(9, 2 * count, count)

time: 196 us -> 210 us (1.071)
  blocking collectives: 97.5 us -> 110 us
  local copies, waits for them, and re-layouts: 46 us -> 39.7 us
  waiting for transfers between devices: 9.06 us -> 12.6 us
    unnamed x42 -> x34, local copies, waits for them, and re-layouts: 22.7 us -> 9.65 us
    all_to_all x3, blocking collectives: 97.5 us -> 110 us  [the longest x1 71.2 us: mirror_pieces(): t = lax.all_to_all(t, 'row', 0, 0, tiled=True)]
    reshape x0 -> x7, local copies, waits for them, and re-layouts: none -> 10.8 us  [the longest x2 5.65 us: mirror_pieces(): t = output_map.reshape(n_col, c_lo, tile_rows, k, tile_rows)]
    all_to_all x2 -> x1, local copies, waits for them, and re-layouts: 3.58 us -> 0.44 us  [mirror_pieces(): t = lax.all_to_all(t, 'col', 0, 0, tiled=True)]
    ppermute x4, waiting for transfers between devices: 3.74 us -> 6.31 us  [padded(): before = lax.ppermute(last, axis, up)]
    slice x5 -> x4, local copies, waits for them, and re-layouts: 3.19 us -> 5.41 us  [padded(): last = lax.slice_in_dim(value, length - width, length, axis=dim)]
    convert_element_type x2, local copies, waits for them, and re-layouts: 2.36 us -> 0.21 us  [mean_of(): b.astype(jnp.float32)]
  transfers between devices with their start and end apart: 8 -> 8, of which waited for: 4 -> 5; matrix products, arithmetic and copies ran while one was open for 5% -> 3% of each run, Pallas kernels for 0% -> 0%
where the time goes in v5:
time: 210 us; the launch traced here: 207 us
  blocking collectives  110 us (52%)
  local copies, waits for them, and re-layouts  39.7 us (19%)
  starting transfers between devices  26.9 us (13%)
  waiting for transfers between devices  12.6 us (6%)
  other arithmetic  8.41 us (4%)
  matrix products  8.22 us (4%)
    all_to_all x1, blocking collectives, mirror_pieces(): t = lax.all_to_all(t, 'row', 0, 0, tiled=True)  71.2 us
    all_to_all x2, blocking collectives, mirror_pieces(): t = lax.all_to_all(t, 'col', 0, 0, tiled=True)  39 us
    ppermute x4, starting transfers between devices, padded(): before = lax.ppermute(last, axis, up)  14 us
    ppermute x4, starting transfers between devices, padded(): after = lax.ppermute(initial, axis, down)  13 us
    unnamed x34, local copies, waits for them, and re-layouts  9.65 us
    dot_general x3, matrix products, block_output(): jnp.einsum('oc,chw->ohw', pointwise, hidden, preferred_element_type=jnp.f...  6.81 us
    ppermute x4, waiting for transfers between devices, padded(): before = lax.ppermute(last, axis, up)  6.31 us
    ppermute x4, waiting for transfers between devices, padded(): after = lax.ppermute(initial, axis, down)  6.28 us
  transfers between devices with their start and end apart: 8, of which 5 were waited for; matrix products, arithmetic and copies ran while one was open for 3% of the time, Pallas kernels for 0%

profile of v5, /device:TPU:7, one launch (start us, length us, event | category | flops | bytes accessed | tf_op | source)
XLA Modules:
  0.0 206.5 jit_solution(8067988854509738174)
XLA Ops:
  1.0 4.4 %collective-permute-start = (bf16[48,8,128]{2,0,1:T(8,128)(2,1)S(1)}, bf16[48,8,128]{2,0,1:T(8,128)(2,1)S(1)}, u32[]{:S(2)}, u32[]{:S(2)}) collective-permute-start(bf16[48,8,128]{2,0,1:T(8,128)(2,1)S(1)} %copy.73), channel_id=1, source_target_pairs={{0,16},{16,32},{32,48},{48,64},{64,80},{80,96},{96,112},{112,128},... | collective-permute-start | bytes 294920 | tf_op jit(solution)/shard_map/ppermute | solution.py:17
  5.4 2.4 %collective-permute-start.1 = (bf16[48,8,128]{2,0,1:T(8,128)(2,1)S(1)}, bf16[48,8,128]{2,0,1:T(8,128)(2,1)S(1)}, u32[]{:S(2)}, u32[]{:S(2)}) collective-permute-start(bf16[48,8,128]{2,0,1:T(8,128)(2,1)S(1)} %copy.74), channel_id=1, source_target_pairs={{16,0},{32,16},{48,32},{64,48},{80,64},{96,80},{112,96},{128,112},... | collective-permute-start | bytes 294920 | tf_op jit(solution)/shard_map/ppermute | solution.py:18
  7.8 1.6 fusion.60
  9.5 1.7 constant_dynamic-update-slice_fusion.1
  11.1 2.0 collective-permute-done.1
  15.2 4.0 %collective-permute-start.3 = (bf16[48,80,8]{1,2,0:T(8,128)(2,1)S(1)}, bf16[48,80,8]{1,2,0:T(8,128)(2,1)S(1)}, u32[]{:S(2)}, u32[]{:S(2)}) collective-permute-start(bf16[48,80,8]{1,2,0:T(8,128)(2,1)S(1)} %copy.29), channel_id=1, source_target_pairs={{1,0},{2,1},{3,2},{4,3},{5,4},{6,5},{7,6},{8,7},{9,8},{10,9},{11,1... | collective-permute-start | bytes 184328 | tf_op jit(solution)/shard_map/ppermute | solution.py:18
  19.2 2.6 %collective-permute-start.2 = (bf16[48,80,8]{1,2,0:T(8,128)(2,1)S(1)}, bf16[48,80,8]{1,2,0:T(8,128)(2,1)S(1)}, u32[]{:S(2)}, u32[]{:S(2)}) collective-permute-start(bf16[48,80,8]{1,2,0:T(8,128)(2,1)S(1)} %copy.28), channel_id=1, source_target_pairs={{0,1},{1,2},{2,3},{3,4},{4,5},{5,6},{6,7},{7,8},{8,9},{9,10},{10,1... | collective-permute-start | bytes 184328 | tf_op jit(solution)/shard_map/ppermute | solution.py:17
  21.9 1.4 collective-permute-done.2
  24.8 1.4 maximum_maximum_fusion.1
  29.2 2.9 %copy-done.2 = bf16[9,48,64,128]{3,1,0,2:T(8,128)(2,1)} copy-done((bf16[9,48,64,128]{3,1,0,2:T(8,128)(2,1)}, bf16[9,48,64,128]{3,1,0,2:T(8,128)(2,1)S(1)}, u32[]{:S(2)}) %copy-start.2) | copy-done | bytes 7077912
  32.0 5.2 %fusion.11 = bf16[48,64,128]{2,0,1:T(8,128)(2,1)S(1)} fusion(bf16[9,48,48,1]{2,1,0,3:T(8,128)(2,1)S(1)} %bitcast.193, bf16[9,48,64,128]{3,1,0,2:T(8,128)(2,1)} %copy-done.2, f32[48]{0:T(128)S(1)} %get-tuple-element.25, f32[48]{0:T(128)S(1)} %get-tuple-element.30, f32[48]{0:T(128)S(1)} %get-tuple-element.26, f32[48]{0:T(128)S(1)} %get-tuple-element.29, ...), kind=kOutput, calls=%fused_computation.17 | convolution fusion | flops 381419520 | bytes 8775680 | tf_op jit(solution)/shard_map/oc,chw->ohw/dot_general | solution.py:41
  37.2 1.6 reshape.39
  38.9 4.0 %copy.40 = bf16[16,3,64,2,64]{2,4,0,3,1:T(8,128)(2,1)S(1)} copy(bf16[16,3,64,2,64]{4,3,1,0,2:T(2,128)(2,1)} %reshape.39) | data formatting | bytes 1572864 | tf_op jit(solution)/shard_map/reshape | solution.py:56
  45.0 19.7 %all_to_all.15 = bf16[16,3,2,4096]{3,2,1,0:T(2,128)(2,1)S(1)} all-to-all(bf16[16,3,2,4096]{3,2,1,0:T(2,128)(2,1)S(1)} %copy.41), channel_id=1, replica_groups=mesh['row'=32,'col'=16] {'col'}, dimensions={0} | all-to-all | bytes 1572864 | tf_op jit(solution)/shard_map/all_to_all | solution.py:58
  65.5 71.2 %all_to_all.16 = bf16[32,3,4096]{2,1,0:T(4,128)(2,1)S(1)} all-to-all(bf16[32,3,4096]{2,1,0:T(4,128)(2,1)S(1)} %bitcast.189), channel_id=1, replica_groups=mesh['row'=32,'col'=16] {'row'}, dimensions={0} | all-to-all | bytes 1572864 | tf_op jit(solution)/shard_map/all_to_all | solution.py:60
  137.3 19.2 %all_to_all.17 = bf16[16,6,4096]{2,1,0:T(8,128)(2,1)S(1)} all-to-all(bf16[16,6,4096]{2,1,0:T(8,128)(2,1)S(1)} %reshape.42), channel_id=1, replica_groups=mesh['row'=32,'col'=16] {'col'}, dimensions={0} | all-to-all | bytes 1572864 | tf_op jit(solution)/shard_map/all_to_all | solution.py:62
  157.0 1.7 reshape.43
  159.4 2.0 fusion.16
  161.6 3.7 %collective-permute-start.4 = (bf16[48,16,128]{2,0,1:T(8,128)(2,1)S(1)}, bf16[48,16,128]{2,0,1:T(8,128)(2,1)S(1)}, u32[]{:S(2)}, u32[]{:S(2)}) collective-permute-start(bf16[48,16,128]{2,0,1:T(8,128)(2,1)S(1)} %get-tuple-element.5), channel_id=1, source_target_pairs={{0,16},{16,32},{32,48},{48,64},{64,80},{80,96},{96,112},{112,128},... | collective-permute-start | bytes 589832 | tf_op jit(solution)/shard_map/ppermute | solution.py:17
  165.3 3.1 %collective-permute-start.5 = (bf16[48,16,128]{2,0,1:T(8,128)(2,1)S(1)}, bf16[48,16,128]{2,0,1:T(8,128)(2,1)S(1)}, u32[]{:S(2)}, u32[]{:S(2)}) collective-permute-start(bf16[48,16,128]{2,0,1:T(8,128)(2,1)S(1)} %get-tuple-element.6), channel_id=1, source_target_pairs={{16,0},{32,16},{48,32},{64,48},{80,64},{96,80},{112,96},{128,112},... | collective-permute-start | bytes 589832 | tf_op jit(solution)/shard_map/ppermute | solution.py:18
  168.4 2.7 %collective-permute-done.4 = bf16[48,16,128]{2,0,1:T(8,128)(2,1)S(1)} collective-permute-done((bf16[48,16,128]{2,0,1:T(8,128)(2,1)S(1)}, bf16[48,16,128]{2,0,1:T(8,128)(2,1)S(1)}, u32[]{:S(2)}, u32[]{:S(2)}) %collective-permute-start.4) | collective-permute-done | bytes 196640 | tf_op jit(solution)/shard_map/ppermute | solution.py:17
  171.1 4.3 %collective-permute-done.5 = bf16[48,16,128]{2,0,1:T(8,128)(2,1)S(1)} collective-permute-done((bf16[48,16,128]{2,0,1:T(8,128)(2,1)S(1)}, bf16[48,16,128]{2,0,1:T(8,128)(2,1)S(1)}, u32[]{:S(2)}, u32[]{:S(2)}) %collective-permute-start.5) | collective-permute-done | bytes 196640 | tf_op jit(solution)/shard_map/ppermute | solution.py:18
  175.8 1.5 fusion.57
  177.3 2.8 %copy.51 = bf16[48,96,16]{1,2,0:T(8,128)(2,1)} copy(bf16[48,96,16]{2,0,1:T(8,128)(2,1)} %get-tuple-element.9) | data formatting | bytes 294912 | tf_op jit(solution)/shard_map/slice | solution.py:15
  180.1 1.6 copy.52
  181.7 3.4 %collective-permute-start.7 = (bf16[48,96,16]{1,2,0:T(8,128)(2,1)}, bf16[48,96,16]{1,2,0:T(8,128)(2,1)}, u32[]{:S(2)}, u32[]{:S(2)}) collective-permute-start(bf16[48,96,16]{1,2,0:T(8,128)(2,1)} %copy.52), channel_id=1, source_target_pairs={{1,0},{2,1},{3,2},{4,3},{5,4},{6,5},{7,6},{8,7},{9,8},{10,9},{11,1... | collective-permute-start | bytes 442376 | tf_op jit(solution)/shard_map/ppermute | solution.py:18
  185.1 3.3 %collective-permute-start.6 = (bf16[48,96,16]{1,2,0:T(8,128)(2,1)}, bf16[48,96,16]{1,2,0:T(8,128)(2,1)}, u32[]{:S(2)}, u32[]{:S(2)}) collective-permute-start(bf16[48,96,16]{1,2,0:T(8,128)(2,1)} %copy.51), channel_id=1, source_target_pairs={{0,1},{1,2},{2,3},{3,4},{4,5},{5,6},{6,7},{7,8},{8,9},{9,10},{10,1... | collective-permute-start | bytes 442376 | tf_op jit(solution)/shard_map/ppermute | solution.py:17
  188.8 2.2 %collective-permute-done.6 = bf16[48,96,16]{1,2,0:T(8,128)(2,1)} collective-permute-done((bf16[48,96,16]{1,2,0:T(8,128)(2,1)}, bf16[48,96,16]{1,2,0:T(8,128)(2,1)}, u32[]{:S(2)}, u32[]{:S(2)}) %collective-permute-start.6) | collective-permute-done | bytes 147488 | tf_op jit(solution)/shard_map/ppermute | solution.py:17
  191.1 1.8 copy.53
  192.9 2.8 %copy.54 = bf16[48,96,16]{2,0,1:T(8,128)(2,1)} copy(bf16[48,96,16]{1,2,0:T(8,128)(2,1)} %collective-permute-done.7) | data formatting | bytes 294912 | tf_op jit(solution)/shard_map/ppermute | solution.py:18
  195.6 3.8 %maximum_maximum_fusion = bf16[48,96,160]{2,0,1:T(8,128)(2,1)S(1)} fusion(bf16[48,96,16]{2,0,1:T(8,128)(2,1)} %copy.54, bf16[48,16,128]{2,0,1:T(8,128)(2,1)S(1)} %collective-permute-done.5, bf16[48,64,64]{2,0,1:T(8,128)(2,1)S(1)} %get-tuple-element.13, bf16[48,64,64]{2,0,1:T(8,128)(2,1)S(1)} %get-tuple-element.14, ...), kind=kLoop, calls=%fused_computation.4 | loop fusion | flops 10321920 | bytes 2949120 | tf_op jit(solution)/shard_map/max | solution.py:24
  202.4 1.4 fusion.2
  (62 shorter events, 18.6 us)
Async XLA Ops:
  1.0 8.5 %collective-permute-start = (bf16[48,8,128]{2,0,1:T(8,128)(2,1)S(1)}, bf16[48,8,128]{2,0,1:T(8,128)(2,1)S(1)}, u32[]{:S(2)}, u32[]{:S(2)}) collective-permute-start(bf16[48,8,128]{2,0,1:T(8,128)(2,1)S(1)} %copy.73), channel_id=1, source_target_pairs={{0,16},{16,32},{32,48},{48,64},{64,80},{80,96},{96,112},{112,128},... | collective-permute-start | bytes 294920 | tf_op jit(solution)/shard_map/ppermute | solution.py:17
  5.4 7.8 %collective-permute-start.1 = (bf16[48,8,128]{2,0,1:T(8,128)(2,1)S(1)}, bf16[48,8,128]{2,0,1:T(8,128)(2,1)S(1)}, u32[]{:S(2)}, u32[]{:S(2)}) collective-permute-start(bf16[48,8,128]{2,0,1:T(8,128)(2,1)S(1)} %copy.74), channel_id=1, source_target_pairs={{16,0},{32,16},{48,32},{64,48},{80,64},{96,80},{112,96},{128,112},... | collective-permute-start | bytes 294920 | tf_op jit(solution)/shard_map/ppermute | solution.py:18
  13.2 8.7 %copy-start.3 = (f32[2,2,48]{2,1,0:T(2,128)S(1)}, f32[2,2,48]{2,1,0:T(2,128)}, u32[]{:S(2)}) copy-start(f32[2,2,48]{2,1,0:T(2,128)} %param.9) | copy-start | bytes 2308
  13.2 8.7 %copy-start.4 = (f32[2,2,48]{2,1,0:T(2,128)S(1)}, f32[2,2,48]{2,1,0:T(2,128)}, u32[]{:S(2)}) copy-start(f32[2,2,48]{2,1,0:T(2,128)} %param.8) | copy-start | bytes 2308
  15.2 8.8 %collective-permute-start.3 = (bf16[48,80,8]{1,2,0:T(8,128)(2,1)S(1)}, bf16[48,80,8]{1,2,0:T(8,128)(2,1)S(1)}, u32[]{:S(2)}, u32[]{:S(2)}) collective-permute-start(bf16[48,80,8]{1,2,0:T(8,128)(2,1)S(1)} %copy.29), channel_id=1, source_target_pairs={{1,0},{2,1},{3,2},{4,3},{5,4},{6,5},{7,6},{8,7},{9,8},{10,9},{11,1... | collective-permute-start | bytes 184328 | tf_op jit(solution)/shard_map/ppermute | solution.py:18
  19.2 4.1 %collective-permute-start.2 = (bf16[48,80,8]{1,2,0:T(8,128)(2,1)S(1)}, bf16[48,80,8]{1,2,0:T(8,128)(2,1)S(1)}, u32[]{:S(2)}, u32[]{:S(2)}) collective-permute-start(bf16[48,80,8]{1,2,0:T(8,128)(2,1)S(1)} %copy.28), channel_id=1, source_target_pairs={{0,1},{1,2},{2,3},{3,4},{4,5},{5,6},{6,7},{7,8},{8,9},{9,10},{10,1... | collective-permute-start | bytes 184328 | tf_op jit(solution)/shard_map/ppermute | solution.py:17
  28.1 3.9 %copy-start = (bf16[48,64,128]{2,1,0:T(8,128)(2,1)S(1)}, bf16[48,64,128]{2,1,0:T(8,128)(2,1)}, u32[]{:S(2)}) copy-start(bf16[48,64,128]{2,1,0:T(8,128)(2,1)} %param.5) | copy-start | bytes 2359300
  28.1 3.9 %copy-start.5 = (bf16[2,48,48]{2,1,0:T(8,128)(2,1)S(1)}, bf16[2,48,48]{2,1,0:T(8,128)(2,1)}, u32[]{:S(2)}) copy-start(bf16[2,48,48]{2,1,0:T(8,128)(2,1)} %param.7) | copy-start | bytes 27652
  29.1 2.9 %copy-start.2 = (bf16[9,48,64,128]{3,1,0,2:T(8,128)(2,1)}, bf16[9,48,64,128]{3,1,0,2:T(8,128)(2,1)S(1)}, u32[]{:S(2)}) copy-start(bf16[9,48,64,128]{3,1,0,2:T(8,128)(2,1)S(1)} %fusion.31) | copy-start | bytes 21233668
  161.6 9.5 %collective-permute-start.4 = (bf16[48,16,128]{2,0,1:T(8,128)(2,1)S(1)}, bf16[48,16,128]{2,0,1:T(8,128)(2,1)S(1)}, u32[]{:S(2)}, u32[]{:S(2)}) collective-permute-start(bf16[48,16,128]{2,0,1:T(8,128)(2,1)S(1)} %get-tuple-element.5), channel_id=1, source_target_pairs={{0,16},{16,32},{32,48},{48,64},{64,80},{80,96},{96,112},{112,128},... | collective-permute-start | bytes 589832 | tf_op jit(solution)/shard_map/ppermute | solution.py:17
  165.3 10.1 %collective-permute-start.5 = (bf16[48,16,128]{2,0,1:T(8,128)(2,1)S(1)}, bf16[48,16,128]{2,0,1:T(8,128)(2,1)S(1)}, u32[]{:S(2)}, u32[]{:S(2)}) collective-permute-start(bf16[48,16,128]{2,0,1:T(8,128)(2,1)S(1)} %get-tuple-element.6), channel_id=1, source_target_pairs={{16,0},{32,16},{48,32},{64,48},{80,64},{96,80},{112,96},{128,112},... | collective-permute-start | bytes 589832 | tf_op jit(solution)/shard_map/ppermute | solution.py:18
  177.3 11.2 %copy-start.1 = (bf16[1,3,3,48,48]{4,3,2,1,0:T(8,128)(2,1)S(1)}, bf16[1,3,3,48,48]{4,3,2,1,0:T(8,128)(2,1)}, u32[]{:S(2)}) copy-start(bf16[1,3,3,48,48]{4,3,2,1,0:T(8,128)(2,1)} %get-tuple-element.17) | copy-start | bytes 124420
  181.7 11.2 %collective-permute-start.7 = (bf16[48,96,16]{1,2,0:T(8,128)(2,1)}, bf16[48,96,16]{1,2,0:T(8,128)(2,1)}, u32[]{:S(2)}, u32[]{:S(2)}) collective-permute-start(bf16[48,96,16]{1,2,0:T(8,128)(2,1)} %copy.52), channel_id=1, source_target_pairs={{1,0},{2,1},{3,2},{4,3},{5,4},{6,5},{7,6},{8,7},{9,8},{10,9},{11,1... | collective-permute-start | bytes 442376 | tf_op jit(solution)/shard_map/ppermute | solution.py:18
  185.1 5.9 %collective-permute-start.6 = (bf16[48,96,16]{1,2,0:T(8,128)(2,1)}, bf16[48,96,16]{1,2,0:T(8,128)(2,1)}, u32[]{:S(2)}, u32[]{:S(2)}) collective-permute-start(bf16[48,96,16]{1,2,0:T(8,128)(2,1)} %copy.51), channel_id=1, source_target_pairs={{0,1},{1,2},{2,3},{3,4},{4,5},{5,6},{6,7},{7,8},{8,9},{9,10},{10,1... | collective-permute-start | bytes 442376 | tf_op jit(solution)/shard_map/ppermute | solution.py:17
  202.4 1.4 copy-start.6

commit v6 on v5

--- a/solution.py
+++ b/solution.py
@@ -52,15 +52,18 @@
     channel_count, tile_rows, tile_cols = output_map.shape
     k = tile_cols // tile_rows
     c_lo = channel_count // n_col
-    flat = tile_rows * tile_rows
-    t = output_map.reshape(n_col, c_lo, tile_rows, k, tile_rows)
-    t = jnp.transpose(t, (0, 1, 3, 4, 2)).reshape(n_col, c_lo, k, flat)
+    lanes = 128
+    fold = lanes // tile_rows
+    rows = tile_rows // fold
+    t = output_map.reshape(n_col, c_lo, tile_rows, k, rows, fold)
+    t = jnp.transpose(t, (0, 1, 3, 4, 5, 2)).reshape(n_col, c_lo * k * rows, lanes)
     t = lax.all_to_all(t, "col", 0, 0, tiled=True)
-    t = jnp.transpose(t, (0, 2, 1, 3)).reshape(n_col * k, c_lo, flat)
+    t = t.reshape(n_col, c_lo, k, rows, lanes)
+    t = jnp.transpose(t, (0, 2, 1, 3, 4)).reshape(n_col * k, c_lo * rows, lanes)
     t = lax.all_to_all(t, "row", 0, 0, tiled=True)
-    t = t.reshape(n_col, k * c_lo, flat)
+    t = t.reshape(n_col, k * c_lo * rows, lanes)
     t = lax.all_to_all(t, "col", 0, 0, tiled=True)
-    t = t.reshape(n_col, k, c_lo, tile_rows, tile_rows)
+    t = t.reshape(n_col, k, c_lo, rows, fold, tile_rows)
     return [t[:, s].reshape(channel_count, tile_rows, tile_rows) for s in range(k)]
 
 

time: 210 us -> 188 us (0.90)
  blocking collectives: 110 us -> 97.4 us
  local copies, waits for them, and re-layouts: 39.7 us -> 31.4 us
    all_to_all x1, blocking collectives: 71.2 us -> 60.5 us  [mirror_pieces(): t = lax.all_to_all(t, 'row', 0, 0, tiled=True)]
    reshape x7 -> x3, local copies, waits for them, and re-layouts: 10.8 us -> 1.56 us  [the longest x1 0.81 us: mirror_pieces(): jnp.transpose(t, (0, 1, 3, 4, 5, 2)).reshape(n_col, c_lo * k * rows, lanes)]
    unnamed x34 -> x30, local copies, waits for them, and re-layouts: 9.65 us -> 9.64 us
where the time goes in v6:
time: 188 us; the launch traced here: 185 us
  blocking collectives  97.4 us (52%)
  local copies, waits for them, and re-layouts  31.4 us (17%)
  starting transfers between devices  26.7 us (14%)
  waiting for transfers between devices  12.5 us (7%)
  other arithmetic  8.38 us (4%)
  matrix products  8.24 us (4%)
    all_to_all x1, blocking collectives, mirror_pieces(): t = lax.all_to_all(t, 'row', 0, 0, tiled=True)  60.5 us
    all_to_all x2, blocking collectives, mirror_pieces(): t = lax.all_to_all(t, 'col', 0, 0, tiled=True)  36.9 us
    ppermute x4, starting transfers between devices, padded(): after = lax.ppermute(initial, axis, down)  14.6 us
    ppermute x4, starting transfers between devices, padded(): before = lax.ppermute(last, axis, up)  12.2 us
    unnamed x30, local copies, waits for them, and re-layouts  9.64 us
    dot_general x3, matrix products, block_output(): jnp.einsum('oc,chw->ohw', pointwise, hidden, preferred_element_type=jnp.f...  6.81 us
    ppermute x4, waiting for transfers between devices, padded(): before = lax.ppermute(last, axis, up)  6.53 us
    ppermute x4, waiting for transfers between devices, padded(): after = lax.ppermute(initial, axis, down)  5.98 us
  transfers between devices with their start and end apart: 8, of which 5 were waited for; matrix products, arithmetic and copies ran while one was open for 3% of the time, Pallas kernels for 0%

profile of v6, /device:TPU:7, one launch (start us, length us, event | category | flops | bytes accessed | tf_op | source)
XLA Modules:
  0.0 185.1 jit_solution(10505752866979382565)
XLA Ops:
  0.0 1.0 fusion.60
  1.0 4.4 %collective-permute-start = (bf16[48,8,128]{2,0,1:T(8,128)(2,1)S(1)}, bf16[48,8,128]{2,0,1:T(8,128)(2,1)S(1)}, u32[]{:S(2)}, u32[]{:S(2)}) collective-permute-start(bf16[48,8,128]{2,0,1:T(8,128)(2,1)S(1)} %copy.62), channel_id=1, source_target_pairs={{0,16},{16,32},{32,48},{48,64},{64,80},{80,96},{96,112},{112,128},... | collective-permute-start | bytes 294920 | tf_op jit(solution)/shard_map/ppermute | solution.py:17
  5.4 2.4 %collective-permute-start.1 = (bf16[48,8,128]{2,0,1:T(8,128)(2,1)S(1)}, bf16[48,8,128]{2,0,1:T(8,128)(2,1)S(1)}, u32[]{:S(2)}, u32[]{:S(2)}) collective-permute-start(bf16[48,8,128]{2,0,1:T(8,128)(2,1)S(1)} %copy.63), channel_id=1, source_target_pairs={{16,0},{32,16},{48,32},{64,48},{80,64},{96,80},{112,96},{128,112},... | collective-permute-start | bytes 294920 | tf_op jit(solution)/shard_map/ppermute | solution.py:18
  7.8 1.0 fusion.61
  8.8 1.7 constant_dynamic-update-slice_fusion.1
  10.5 2.6 %collective-permute-done.1 = bf16[48,8,128]{2,0,1:T(8,128)(2,1)S(1)} collective-permute-done((bf16[48,8,128]{2,0,1:T(8,128)(2,1)S(1)}, bf16[48,8,128]{2,0,1:T(8,128)(2,1)S(1)}, u32[]{:S(2)}, u32[]{:S(2)}) %collective-permute-start.1) | collective-permute-done | bytes 98336 | tf_op jit(solution)/shard_map/ppermute | solution.py:18
  15.1 4.0 %collective-permute-start.3 = (bf16[48,80,8]{1,2,0:T(8,128)(2,1)S(1)}, bf16[48,80,8]{1,2,0:T(8,128)(2,1)S(1)}, u32[]{:S(2)}, u32[]{:S(2)}) collective-permute-start(bf16[48,80,8]{1,2,0:T(8,128)(2,1)S(1)} %copy.25), channel_id=1, source_target_pairs={{1,0},{2,1},{3,2},{4,3},{5,4},{6,5},{7,6},{8,7},{9,8},{10,9},{11,1... | collective-permute-start | bytes 184328 | tf_op jit(solution)/shard_map/ppermute | solution.py:18
  19.2 2.5 %collective-permute-start.2 = (bf16[48,80,8]{1,2,0:T(8,128)(2,1)S(1)}, bf16[48,80,8]{1,2,0:T(8,128)(2,1)S(1)}, u32[]{:S(2)}, u32[]{:S(2)}) collective-permute-start(bf16[48,80,8]{1,2,0:T(8,128)(2,1)S(1)} %copy.24), channel_id=1, source_target_pairs={{0,1},{1,2},{2,3},{3,4},{4,5},{5,6},{6,7},{7,8},{8,9},{9,10},{10,1... | collective-permute-start | bytes 184328 | tf_op jit(solution)/shard_map/ppermute | solution.py:17
  21.7 1.6 collective-permute-done.2
  24.7 1.4 maximum_maximum_fusion.1
  29.2 2.9 %copy-done.1 = bf16[9,48,64,128]{3,1,0,2:T(8,128)(2,1)} copy-done((bf16[9,48,64,128]{3,1,0,2:T(8,128)(2,1)}, bf16[9,48,64,128]{3,1,0,2:T(8,128)(2,1)S(1)}, u32[]{:S(2)}) %copy-start.1) | copy-done | bytes 7077912
  32.0 5.2 %fusion.11 = bf16[48,64,128]{2,0,1:T(8,128)(2,1)S(1)} fusion(bf16[9,48,48,1]{2,1,0,3:T(8,128)(2,1)S(1)} %bitcast.193, bf16[9,48,64,128]{3,1,0,2:T(8,128)(2,1)} %copy-done.1, f32[48]{0:T(128)S(1)} %get-tuple-element.25, f32[48]{0:T(128)S(1)} %get-tuple-element.30, f32[48]{0:T(128)S(1)} %get-tuple-element.26, f32[48]{0:T(128)S(1)} %get-tuple-element.29, ...), kind=kOutput, calls=%fused_computation.17 | convolution fusion | flops 381419520 | bytes 8775680 | tf_op jit(solution)/shard_map/oc,chw->ohw/dot_general | solution.py:41
  38.9 19.7 %all_to_all.15 = bf16[16,192,128]{2,1,0:T(8,128)(2,1)S(1)} all-to-all(bf16[16,192,128]{2,1,0:T(8,128)(2,1)S(1)} %reshape.43), channel_id=1, replica_groups=mesh['row'=32,'col'=16] {'col'}, dimensions={0} | all-to-all | bytes 1572864 | tf_op jit(solution)/shard_map/all_to_all | solution.py:60
  58.7 60.5 %all_to_all.16 = bf16[32,96,128]{2,1,0:T(8,128)(2,1)S(1)} all-to-all(bf16[32,96,128]{2,1,0:T(8,128)(2,1)S(1)} %bitcast.187), channel_id=1, replica_groups=mesh['row'=32,'col'=16] {'row'}, dimensions={0} | all-to-all | bytes 1572864 | tf_op jit(solution)/shard_map/all_to_all | solution.py:63
  119.2 17.1 %all_to_all.17 = bf16[16,192,128]{2,1,0:T(8,128)(2,1)S(1)} all-to-all(bf16[16,192,128]{2,1,0:T(8,128)(2,1)S(1)} %bitcast.188), channel_id=1, replica_groups=mesh['row'=32,'col'=16] {'col'}, dimensions={0} | all-to-all | bytes 1572864 | tf_op jit(solution)/shard_map/all_to_all | solution.py:65
  137.1 1.4 fusion.57
  138.9 2.0 %fusion.16 = (bf16[48,64,64]{2,0,1:T(8,128)(2,1)S(1)}, bf16[48,64,64]{2,0,1:T(8,128)(2,1)S(1)}) fusion(f32[48,64,64]{2,1,0:T(8,128)S(1)} %convert.3, bf16[48,64,128]{2,0,1:T(8,128)(2,1)S(1)} %fusion.11, f32[48,64,64]{2,1,0:T(8,128)S(1)} %convert.2), kind=kLoop, calls=%fused_computation.24 | loop fusion | flops 1572864 | bytes 3145728 | tf_op jit(solution)/shard_map/convert_element_type | solution.py:71
  141.2 2.7 %collective-permute-start.4 = (bf16[48,16,128]{2,0,1:T(8,128)(2,1)S(1)}, bf16[48,16,128]{2,0,1:T(8,128)(2,1)S(1)}, u32[]{:S(2)}, u32[]{:S(2)}) collective-permute-start(bf16[48,16,128]{2,0,1:T(8,128)(2,1)S(1)} %get-tuple-element.5), channel_id=1, source_target_pairs={{0,16},{16,32},{32,48},{48,64},{64,80},{80,96},{96,112},{112,128},... | collective-permute-start | bytes 589832 | tf_op jit(solution)/shard_map/ppermute | solution.py:17
  143.8 4.1 %collective-permute-start.5 = (bf16[48,16,128]{2,0,1:T(8,128)(2,1)S(1)}, bf16[48,16,128]{2,0,1:T(8,128)(2,1)S(1)}, u32[]{:S(2)}, u32[]{:S(2)}) collective-permute-start(bf16[48,16,128]{2,0,1:T(8,128)(2,1)S(1)} %get-tuple-element.6), channel_id=1, source_target_pairs={{16,0},{32,16},{48,32},{64,48},{80,64},{96,80},{112,96},{128,112},... | collective-permute-start | bytes 589832 | tf_op jit(solution)/shard_map/ppermute | solution.py:18
  148.0 2.7 %collective-permute-done.4 = bf16[48,16,128]{2,0,1:T(8,128)(2,1)S(1)} collective-permute-done((bf16[48,16,128]{2,0,1:T(8,128)(2,1)S(1)}, bf16[48,16,128]{2,0,1:T(8,128)(2,1)S(1)}, u32[]{:S(2)}, u32[]{:S(2)}) %collective-permute-start.4) | collective-permute-done | bytes 196640 | tf_op jit(solution)/shard_map/ppermute | solution.py:17
  150.6 3.3 %collective-permute-done.5 = bf16[48,16,128]{2,0,1:T(8,128)(2,1)S(1)} collective-permute-done((bf16[48,16,128]{2,0,1:T(8,128)(2,1)S(1)}, bf16[48,16,128]{2,0,1:T(8,128)(2,1)S(1)}, u32[]{:S(2)}, u32[]{:S(2)}) %collective-permute-start.5) | collective-permute-done | bytes 196640 | tf_op jit(solution)/shard_map/ppermute | solution.py:18
  154.4 1.5 fusion.58
  155.9 2.8 %copy.42 = bf16[48,96,16]{1,2,0:T(8,128)(2,1)} copy(bf16[48,96,16]{2,0,1:T(8,128)(2,1)} %get-tuple-element.9) | data formatting | bytes 294912 | tf_op jit(solution)/shard_map/slice | solution.py:15
  158.7 1.6 copy.43
  160.3 4.0 %collective-permute-start.7 = (bf16[48,96,16]{1,2,0:T(8,128)(2,1)}, bf16[48,96,16]{1,2,0:T(8,128)(2,1)}, u32[]{:S(2)}, u32[]{:S(2)}) collective-permute-start(bf16[48,96,16]{1,2,0:T(8,128)(2,1)} %copy.43), channel_id=1, source_target_pairs={{1,0},{2,1},{3,2},{4,3},{5,4},{6,5},{7,6},{8,7},{9,8},{10,9},{11,1... | collective-permute-start | bytes 442376 | tf_op jit(solution)/shard_map/ppermute | solution.py:18
  164.3 2.7 %collective-permute-start.6 = (bf16[48,96,16]{1,2,0:T(8,128)(2,1)}, bf16[48,96,16]{1,2,0:T(8,128)(2,1)}, u32[]{:S(2)}, u32[]{:S(2)}) collective-permute-start(bf16[48,96,16]{1,2,0:T(8,128)(2,1)} %copy.42), channel_id=1, source_target_pairs={{0,1},{1,2},{2,3},{3,4},{4,5},{5,6},{6,7},{7,8},{8,9},{9,10},{10,1... | collective-permute-start | bytes 442376 | tf_op jit(solution)/shard_map/ppermute | solution.py:17
  167.4 2.3 %collective-permute-done.6 = bf16[48,96,16]{1,2,0:T(8,128)(2,1)} collective-permute-done((bf16[48,96,16]{1,2,0:T(8,128)(2,1)}, bf16[48,96,16]{1,2,0:T(8,128)(2,1)}, u32[]{:S(2)}, u32[]{:S(2)}) %collective-permute-start.6) | collective-permute-done | bytes 147488 | tf_op jit(solution)/shard_map/ppermute | solution.py:17
  169.6 1.8 copy.44
  171.5 2.8 %copy.45 = bf16[48,96,16]{2,0,1:T(8,128)(2,1)} copy(bf16[48,96,16]{1,2,0:T(8,128)(2,1)} %collective-permute-done.7) | data formatting | bytes 294912 | tf_op jit(solution)/shard_map/ppermute | solution.py:18
  174.2 3.8 %maximum_maximum_fusion = bf16[48,96,160]{2,0,1:T(8,128)(2,1)S(1)} fusion(bf16[48,96,16]{2,0,1:T(8,128)(2,1)} %copy.45, bf16[48,16,128]{2,0,1:T(8,128)(2,1)S(1)} %collective-permute-done.5, bf16[48,64,64]{2,0,1:T(8,128)(2,1)S(1)} %get-tuple-element.13, bf16[48,64,64]{2,0,1:T(8,128)(2,1)S(1)} %get-tuple-element.14, ...), kind=kLoop, calls=%fused_computation.4 | loop fusion | flops 10321920 | bytes 2949120 | tf_op jit(solution)/shard_map/max | solution.py:24
  181.0 1.4 fusion.2
  184.0 1.1 copy.47
  (54 shorter events, 14.8 us)
Async XLA Ops:
  1.0 7.8 %collective-permute-start = (bf16[48,8,128]{2,0,1:T(8,128)(2,1)S(1)}, bf16[48,8,128]{2,0,1:T(8,128)(2,1)S(1)}, u32[]{:S(2)}, u32[]{:S(2)}) collective-permute-start(bf16[48,8,128]{2,0,1:T(8,128)(2,1)S(1)} %copy.62), channel_id=1, source_target_pairs={{0,16},{16,32},{32,48},{48,64},{64,80},{80,96},{96,112},{112,128},... | collective-permute-start | bytes 294920 | tf_op jit(solution)/shard_map/ppermute | solution.py:17
  5.4 7.8 %collective-permute-start.1 = (bf16[48,8,128]{2,0,1:T(8,128)(2,1)S(1)}, bf16[48,8,128]{2,0,1:T(8,128)(2,1)S(1)}, u32[]{:S(2)}, u32[]{:S(2)}) collective-permute-start(bf16[48,8,128]{2,0,1:T(8,128)(2,1)S(1)} %copy.63), channel_id=1, source_target_pairs={{16,0},{32,16},{48,32},{64,48},{80,64},{96,80},{112,96},{128,112},... | collective-permute-start | bytes 294920 | tf_op jit(solution)/shard_map/ppermute | solution.py:18
  13.2 8.5 %copy-start.2 = (f32[2,2,48]{2,1,0:T(2,128)S(1)}, f32[2,2,48]{2,1,0:T(2,128)}, u32[]{:S(2)}) copy-start(f32[2,2,48]{2,1,0:T(2,128)} %param.9) | copy-start | bytes 2308
  13.2 8.4 %copy-start.3 = (f32[2,2,48]{2,1,0:T(2,128)S(1)}, f32[2,2,48]{2,1,0:T(2,128)}, u32[]{:S(2)}) copy-start(f32[2,2,48]{2,1,0:T(2,128)} %param.8) | copy-start | bytes 2308
  15.1 8.8 %collective-permute-start.3 = (bf16[48,80,8]{1,2,0:T(8,128)(2,1)S(1)}, bf16[48,80,8]{1,2,0:T(8,128)(2,1)S(1)}, u32[]{:S(2)}, u32[]{:S(2)}) collective-permute-start(bf16[48,80,8]{1,2,0:T(8,128)(2,1)S(1)} %copy.25), channel_id=1, source_target_pairs={{1,0},{2,1},{3,2},{4,3},{5,4},{6,5},{7,6},{8,7},{9,8},{10,9},{11,1... | collective-permute-start | bytes 184328 | tf_op jit(solution)/shard_map/ppermute | solution.py:18
  19.2 4.1 %collective-permute-start.2 = (bf16[48,80,8]{1,2,0:T(8,128)(2,1)S(1)}, bf16[48,80,8]{1,2,0:T(8,128)(2,1)S(1)}, u32[]{:S(2)}, u32[]{:S(2)}) collective-permute-start(bf16[48,80,8]{1,2,0:T(8,128)(2,1)S(1)} %copy.24), channel_id=1, source_target_pairs={{0,1},{1,2},{2,3},{3,4},{4,5},{5,6},{6,7},{7,8},{8,9},{9,10},{10,1... | collective-permute-start | bytes 184328 | tf_op jit(solution)/shard_map/ppermute | solution.py:17
  28.1 3.9 %copy-start = (bf16[48,64,128]{2,1,0:T(8,128)(2,1)S(1)}, bf16[48,64,128]{2,1,0:T(8,128)(2,1)}, u32[]{:S(2)}) copy-start(bf16[48,64,128]{2,1,0:T(8,128)(2,1)} %param.5) | copy-start | bytes 2359300
  28.1 3.9 %copy-start.4 = (bf16[2,48,48]{2,1,0:T(8,128)(2,1)S(1)}, bf16[2,48,48]{2,1,0:T(8,128)(2,1)}, u32[]{:S(2)}) copy-start(bf16[2,48,48]{2,1,0:T(8,128)(2,1)} %param.7) | copy-start | bytes 27652
  29.1 2.9 %copy-start.1 = (bf16[9,48,64,128]{3,1,0,2:T(8,128)(2,1)}, bf16[9,48,64,128]{3,1,0,2:T(8,128)(2,1)S(1)}, u32[]{:S(2)}) copy-start(bf16[9,48,64,128]{3,1,0,2:T(8,128)(2,1)S(1)} %fusion.31) | copy-start | bytes 21233668
  141.2 9.5 %collective-permute-start.4 = (bf16[48,16,128]{2,0,1:T(8,128)(2,1)S(1)}, bf16[48,16,128]{2,0,1:T(8,128)(2,1)S(1)}, u32[]{:S(2)}, u32[]{:S(2)}) collective-permute-start(bf16[48,16,128]{2,0,1:T(8,128)(2,1)S(1)} %get-tuple-element.5), channel_id=1, source_target_pairs={{0,16},{16,32},{32,48},{48,64},{64,80},{80,96},{96,112},{112,128},... | collective-permute-start | bytes 589832 | tf_op jit(solution)/shard_map/ppermute | solution.py:17
  143.8 10.2 %collective-permute-start.5 = (bf16[48,16,128]{2,0,1:T(8,128)(2,1)S(1)}, bf16[48,16,128]{2,0,1:T(8,128)(2,1)S(1)}, u32[]{:S(2)}, u32[]{:S(2)}) collective-permute-start(bf16[48,16,128]{2,0,1:T(8,128)(2,1)S(1)} %get-tuple-element.6), channel_id=1, source_target_pairs={{16,0},{32,16},{48,32},{64,48},{80,64},{96,80},{112,96},{128,112},... | collective-permute-start | bytes 589832 | tf_op jit(solution)/shard_map/ppermute | solution.py:18
  160.3 11.2 %collective-permute-start.7 = (bf16[48,96,16]{1,2,0:T(8,128)(2,1)}, bf16[48,96,16]{1,2,0:T(8,128)(2,1)}, u32[]{:S(2)}, u32[]{:S(2)}) collective-permute-start(bf16[48,96,16]{1,2,0:T(8,128)(2,1)} %copy.43), channel_id=1, source_target_pairs={{1,0},{2,1},{3,2},{4,3},{5,4},{6,5},{7,6},{8,7},{9,8},{10,9},{11,1... | collective-permute-start | bytes 442376 | tf_op jit(solution)/shard_map/ppermute | solution.py:18
  164.3 5.4 %collective-permute-start.6 = (bf16[48,96,16]{1,2,0:T(8,128)(2,1)}, bf16[48,96,16]{1,2,0:T(8,128)(2,1)}, u32[]{:S(2)}, u32[]{:S(2)}) collective-permute-start(bf16[48,96,16]{1,2,0:T(8,128)(2,1)} %copy.42), channel_id=1, source_target_pairs={{0,1},{1,2},{2,3},{3,4},{4,5},{5,6},{6,7},{7,8},{8,9},{9,10},{10,1... | collective-permute-start | bytes 442376 | tf_op jit(solution)/shard_map/ppermute | solution.py:17

commit v7 on v6

--- a/solution.py
+++ b/solution.py
@@ -7,8 +7,8 @@
 SECOND_DILATION = 16
 
 
-def padded(value, sides, width):
-    for axis, dim in sides:
+def padded(value, sides):
+    for axis, dim, width in sides:
         size, length = (lax.axis_size(axis), value.shape[dim])
         up = [(i, (i + 1) % size) for i in range(size - 1)]
         down = [(j, i) for i, j in up]
@@ -47,7 +47,7 @@
     return lax.reduce_precision(summed, exponent_bits=8, mantissa_bits=7).astype(jnp.bfloat16)
 
 
-def mirror_pieces(output_map):
+def mirror_extended(output_map, reach):
     n_col = lax.axis_size("col")
     channel_count, tile_rows, tile_cols = output_map.shape
     k = tile_cols // tile_rows
@@ -55,49 +55,56 @@
     lanes = 128
     fold = lanes // tile_rows
     rows = tile_rows // fold
-    t = output_map.reshape(n_col, c_lo, tile_rows, k, rows, fold)
-    t = jnp.transpose(t, (0, 1, 3, 4, 5, 2)).reshape(n_col, c_lo * k * rows, lanes)
+    t = output_map.reshape(n_col, c_lo, rows, fold, k, tile_rows)
+    t = jnp.transpose(t, (0, 1, 4, 2, 3, 5)).reshape(n_col, c_lo * k * rows, lanes)
     t = lax.all_to_all(t, "col", 0, 0, tiled=True)
     t = t.reshape(n_col, c_lo, k, rows, lanes)
     t = jnp.transpose(t, (0, 2, 1, 3, 4)).reshape(n_col * k, c_lo * rows, lanes)
     t = lax.all_to_all(t, "row", 0, 0, tiled=True)
-    t = t.reshape(n_col, k * c_lo * rows, lanes)
-    t = lax.all_to_all(t, "col", 0, 0, tiled=True)
-    t = t.reshape(n_col, k, c_lo, rows, fold, tile_rows)
-    return [t[:, s].reshape(channel_count, tile_rows, tile_rows) for s in range(k)]
+    n_row = n_col * k
+    t = t.reshape(n_row, c_lo, rows, lanes)
+    t = jnp.transpose(t, (1, 0, 2, 3)).reshape(c_lo, n_row * rows, lanes)
+    edge = reach // fold
+    step = tile_cols // fold
+    span = step + 2 * edge
+    t = jnp.pad(t, ((0, 0), (edge, edge), (0, 0)))
+    t = jnp.stack([t[:, z * step:z * step + span] for z in range(n_col)])
+    t = lax.all_to_all(t.reshape(n_col, c_lo * span, lanes), "col", 0, 0, tiled=True)
+    t = t.reshape(channel_count, span, fold, tile_rows)
+    return jnp.transpose(t, (0, 3, 1, 2)).reshape(channel_count, tile_rows, span * fold)
 
 
 def mean_of(a, b):
     return ((a.astype(jnp.float32) + b.astype(jnp.float32)) * 0.5).astype(jnp.bfloat16)
 
 
-def symmetrized(output_map):
-    tile_rows = output_map.shape[1]
-    halves = [
-        mean_of(output_map[:, :, s * tile_rows:(s + 1) * tile_rows], piece)
-        for s, piece in enumerate(mirror_pieces(output_map))
-    ]
-    return jnp.concatenate(halves, axis=2)
-
-
 def body(features, w_dilated, w_pointwise, norm_gain, norm_bias):
     count, tile_rows, tile_cols = features.shape
+    reach = SECOND_DILATION
+
     kernel = w_dilated[0].reshape(9, count, count)
-    extended = padded(features, (("row", 1), ("col", 2)), FIRST_DILATION)
+    extended = padded(features, (("row", 1, FIRST_DILATION), ("col", 2, FIRST_DILATION + reach)))
+    wide = tile_cols + 2 * reach
     hidden = hidden_of(
-        extended, kernel, norm_gain[0, 0], norm_bias[0, 0], FIRST_DILATION, tile_rows, tile_cols
+        extended, kernel, norm_gain[0, 0], norm_bias[0, 0], FIRST_DILATION, tile_rows, wide
     )
-    output_map = block_output(features, hidden, norm_gain[0], norm_bias[0], w_pointwise[0])
-    state = symmetrized(output_map)
+    own = extended[:, FIRST_DILATION:FIRST_DILATION + tile_rows, FIRST_DILATION:FIRST_DILATION + wide]
+    output_map = block_output(own, hidden, norm_gain[0], norm_bias[0], w_pointwise[0])
+    mirrored = mirror_extended(output_map[:, :, reach:reach + tile_cols], reach)
+    first = lax.axis_index("col") * tile_cols - reach
+    columns = first + lax.broadcasted_iota(jnp.int32, (1, 1, wide), 2)
+    inside = (columns >= 0) & (columns < lax.axis_size("col") * tile_cols)
+    state = jnp.where(inside, mean_of(output_map, mirrored), jnp.zeros((), jnp.bfloat16))
 
     kernel = w_dilated[1]
     both = jnp.concatenate([kernel, jnp.swapaxes(kernel, 0, 1)], axis=2).reshape(9, 2 * count, count)
-    extended = padded(state, (("row", 1), ("col", 2)), SECOND_DILATION)
+    extended = padded(state, (("row", 1, SECOND_DILATION),))
     gain = jnp.concatenate([norm_gain[1, 0], norm_gain[1, 0]])
     bias = jnp.concatenate([norm_bias[1, 0], norm_bias[1, 0]])
     hidden = hidden_of(extended, both, gain, bias, SECOND_DILATION, tile_rows, tile_cols)
-    direct = block_output(state, hidden[:count], norm_gain[1], norm_bias[1], w_pointwise[1])
-    mirrored = block_output(state, hidden[count:], norm_gain[1], norm_bias[1], w_pointwise[1])
+    own = state[:, :, reach:reach + tile_cols]
+    direct = block_output(own, hidden[:count], norm_gain[1], norm_bias[1], w_pointwise[1])
+    mirrored = block_output(own, hidden[count:], norm_gain[1], norm_bias[1], w_pointwise[1])
     return mean_of(direct, mirrored)
 
 

time: 188 us -> 216 us (1.15)
  waiting for transfers between devices: 12.5 us -> 36.6 us
  local copies, waits for them, and re-layouts: 31.4 us -> 55.1 us
  blocking collectives: 97.4 us -> 78.2 us
  matrix products: 8.24 us -> 11.2 us
    all_to_all x3 -> x2, blocking collectives: 97.4 us -> 78.2 us  [the longest x1 60.5 us: mirror_extended(): t = lax.all_to_all(t, 'row', 0, 0, tiled=True)]
    all_to_all x0 -> x1, waiting for transfers between devices: none -> 14.6 us  [mirror_extended(): lax.all_to_all(t.reshape(n_col, c_lo * span, lanes), 'col', 0, 0, tiled=T...]
    unnamed x30 -> x63, local copies, waits for them, and re-layouts: 9.64 us -> 23.6 us
    convert_element_type x1 -> x4, local copies, waits for them, and re-layouts: 0.91 us -> 14.3 us  [mean_of(): b.astype(jnp.float32)]
    ppermute x4 -> x3, waiting for transfers between devices: 6.53 us -> 14.7 us  [padded(): before = lax.ppermute(last, axis, up)]
    all_to_all x0 -> x1, starting transfers between devices: none -> 5.61 us  [mirror_extended(): lax.all_to_all(t.reshape(n_col, c_lo * span, lanes), 'col', 0, 0, tiled=T...]
    ppermute x4 -> x3, starting transfers between devices: 14.6 us -> 8.97 us  [padded(): after = lax.ppermute(initial, axis, down)]
    reshape x3 -> x5, local copies, waits for them, and re-layouts: 1.56 us -> 5.87 us  [the longest x2 5.02 us: mirror_extended(): t = output_map.reshape(n_col, c_lo, rows, fold, k, tile_rows)]
  transfers between devices with their start and end apart: 8 -> 7, of which waited for: 5 -> 5; matrix products, arithmetic and copies ran while one was open for 3% -> 3% of each run, Pallas kernels for 0% -> 0%
where the time goes in v7:
time: 216 us; the launch traced here: 214 us
  blocking collectives  78.2 us (36%)
  local copies, waits for them, and re-layouts  55.1 us (26%)
  waiting for transfers between devices  36.6 us (17%)
  starting transfers between devices  26.1 us (12%)
  matrix products  11.2 us (5%)
  other arithmetic  6.64 us (3%)
    all_to_all x1, blocking collectives, mirror_extended(): t = lax.all_to_all(t, 'row', 0, 0, tiled=True)  60.5 us
    unnamed x63, local copies, waits for them, and re-layouts  23.6 us
    all_to_all x1, blocking collectives, mirror_extended(): t = lax.all_to_all(t, 'col', 0, 0, tiled=True)  17.7 us
    ppermute x3, waiting for transfers between devices, padded(): before = lax.ppermute(last, axis, up)  14.7 us
    all_to_all x1, waiting for transfers between devices, mirror_extended(): lax.all_to_all(t.reshape(n_col, c_lo * span, lanes), 'col', 0, 0, tiled=T...  14.6 us
    convert_element_type x4, local copies, waits for them, and re-layouts, mean_of(): b.astype(jnp.float32)  14.3 us
    ppermute x3, starting transfers between devices, padded(): before = lax.ppermute(last, axis, up)  11.5 us
    dot_general x3, matrix products, block_output(): jnp.einsum('oc,chw->ohw', pointwise, hidden, preferred_element_type=jnp.f...  9.81 us
  transfers between devices with their start and end apart: 7, of which 5 were waited for; matrix products, arithmetic and copies ran while one was open for 3% of the time, Pallas kernels for 0%

profile of v7, /device:TPU:7, one launch (start us, length us, event | category | flops | bytes accessed | tf_op | source)
XLA Modules:
  0.0 214.4 jit_solution(17879036479985330146)
XLA Ops:
  0.0 1.0 fusion.54
  1.0 4.4 %collective-permute-start = (bf16[48,8,128]{2,0,1:T(8,128)(2,1)S(1)}, bf16[48,8,128]{2,0,1:T(8,128)(2,1)S(1)}, u32[]{:S(2)}, u32[]{:S(2)}) collective-permute-start(bf16[48,8,128]{2,0,1:T(8,128)(2,1)S(1)} %copy.62), channel_id=1, source_target_pairs={{0,16},{16,32},{32,48},{48,64},{64,80},{80,96},{96,112},{112,128},... | collective-permute-start | bytes 294920 | tf_op jit(solution)/shard_map/ppermute | solution.py:17
  5.4 2.4 %collective-permute-start.1 = (bf16[48,8,128]{2,0,1:T(8,128)(2,1)S(1)}, bf16[48,8,128]{2,0,1:T(8,128)(2,1)S(1)}, u32[]{:S(2)}, u32[]{:S(2)}) collective-permute-start(bf16[48,8,128]{2,0,1:T(8,128)(2,1)S(1)} %copy.63), channel_id=1, source_target_pairs={{16,0},{32,16},{48,32},{64,48},{80,64},{96,80},{112,96},{128,112},... | collective-permute-start | bytes 294920 | tf_op jit(solution)/shard_map/ppermute | solution.py:18
  7.8 1.7 fusion.55
  9.5 1.7 constant_dynamic-update-slice_fusion.1
  11.2 1.9 collective-permute-done.1
  13.6 0.8 copy.44
  14.4 4.6 %collective-permute-start.2 = (bf16[48,80,24]{1,2,0:T(8,128)(2,1)S(1)}, bf16[48,80,24]{1,2,0:T(8,128)(2,1)S(1)}, u32[]{:S(2)}, u32[]{:S(2)}) collective-permute-start(bf16[48,80,24]{1,2,0:T(8,128)(2,1)S(1)} %copy.44), channel_id=1, source_target_pairs={{0,1},{1,2},{2,3},{3,4},{4,5},{5,6},{6,7},{7,8},{8,9},{9,10},{10,1... | collective-permute-start | bytes 552968 | tf_op jit(solution)/shard_map/ppermute | solution.py:17
  19.7 2.1 collective-permute-start.3
  23.3 5.3 %collective-permute-done.3 = bf16[48,80,24]{1,2,0:T(8,128)(2,1)S(1)} collective-permute-done((bf16[48,80,24]{1,2,0:T(8,128)(2,1)S(1)}, bf16[48,80,24]{1,2,0:T(8,128)(2,1)S(1)}, u32[]{:S(2)}, u32[]{:S(2)}) %collective-permute-start.3) | collective-permute-done | bytes 184352 | tf_op jit(solution)/shard_map/ppermute | solution.py:18
  29.4 2.5 %broadcast_maximum_fusion = (bf16[48,80,176]{2,0,1:T(8,128)(2,1)S(1)}, bf16[48,80,176]{2,0,1:T(8,128)(2,1)}) fusion(bf16[48,80,24]{2,0,1:T(8,128)(2,1)S(1)} %copy.47, bf16[48,80,128]{2,0,1:T(8,128)(2,1)S(1)} %constant_dynamic-update-slice_fusion, bf16[48,80,24]{2,0,1:T(8,128)(2,1)S(1)} %copy.46), kind=kLoop, calls=%fused_computation.46 | loop fusion | flops 6082560 | bytes 4055040 | tf_op jit(solution)/shard_map/max | solution.py:24
  36.5 5.0 %copy-done.6 = bf16[9,48,64,160]{3,1,2,0:T(8,128)(2,1)} copy-done((bf16[9,48,64,160]{3,1,2,0:T(8,128)(2,1)}, bf16[9,48,64,160]{3,1,2,0:T(8,128)(2,1)S(1)}, u32[]{:S(2)}) %copy-start.6) | copy-done | bytes 8847384
  41.5 8.6 %fusion.5 = bf16[48,64,160]{2,0,1:T(8,128)(2,1)S(1)} fusion(bf16[48,80,176]{2,0,1:T(8,128)(2,1)S(1)} %copy-done.3, f32[48]{0:T(128)S(1)} %copy-done.11, f32[48]{0:T(128)} %get-tuple-element.42, bf16[9,48,48,1]{2,1,3,0:T(8,128)(2,1)} %bitcast.249, bf16[9,48,64,160]{3,1,2,0:T(8,128)(2,1)} %copy-done.6, f32[48]{0:T(128)S(1)} %copy-done.12, ...), kind=kOutput, calls=%fused_computation.7 | convolution fusion | flops 476774400 | bytes 16246144 | tf_op jit(solution)/shard_map/oc,chw->ohw/dot_general | solution.py:41
  50.1 1.4 slice.275
  51.5 3.2 %reshape.88 = bf16[16,3,32,2,2,64]{5,4,1,0,3,2:T(2,128)(2,1)S(1)} reshape(bf16[48,64,128]{2,0,1:T(8,128)(2,1)} %slice.275) | data formatting | bytes 1572864 | tf_op jit(solution)/shard_map/reshape | solution.py:58
  54.8 1.8 copy.64
  57.3 17.7 %all_to_all.15 = bf16[16,192,128]{2,1,0:T(8,128)(2,1)S(1)} all-to-all(bf16[16,192,128]{2,1,0:T(8,128)(2,1)S(1)} %reshape.89), channel_id=1, replica_groups=mesh['row'=32,'col'=16] {'col'}, dimensions={0} | all-to-all | bytes 1572864 | tf_op jit(solution)/shard_map/all_to_all | solution.py:60
  75.1 60.5 %all_to_all.16 = bf16[32,96,128]{2,1,0:T(8,128)(2,1)S(1)} all-to-all(bf16[32,96,128]{2,1,0:T(8,128)(2,1)S(1)} %bitcast.229), channel_id=1, replica_groups=mesh['row'=32,'col'=16] {'row'}, dimensions={0} | all-to-all | bytes 1572864 | tf_op jit(solution)/shard_map/all_to_all | solution.py:63
  145.7 5.6 %all-to-all-start.2 = ((bf16[16,240,128]{2,1,0:T(8,128)(2,1)}), bf16[16,240,128]{2,1,0:T(8,128)(2,1)S(1)}, u32[]{:S(2)}, u32[]{:S(2)}) async-start(bf16[16,240,128]{2,1,0:T(8,128)(2,1)} %constant_dynamic-update-slice_fusion.3), calls=%async_computation.2 | async-start | bytes 1966080 | tf_op jit(solution)/shard_map/all_to_all | solution.py:72
  151.4 14.6 %all-to-all-done.2 = bf16[16,240,128]{2,1,0:T(8,128)(2,1)S(1)} async-done(((bf16[16,240,128]{2,1,0:T(8,128)(2,1)}), bf16[16,240,128]{2,1,0:T(8,128)(2,1)S(1)}, u32[]{:S(2)}, u32[]{:S(2)}) %all-to-all-start.2) | async-done | bytes 983072 | tf_op jit(solution)/shard_map/all_to_all | solution.py:72
  166.0 1.9 copy.51
  167.9 3.1 %reshape.95 = f32[48,80,2,64]{1,0,3,2:T(8,128)S(1)} reshape(f32[16,240,128]{1,0,2:T(8,128)} %copy.51) | data formatting | bytes 3932160 | tf_op jit(solution)/shard_map/convert_element_type | solution.py:78
  171.0 4.4 %copy.52 = f32[48,64,80,2]{1,0,3,2:T(8,128)} copy(f32[48,64,80,2]{2,0,1,3:T(8,128)S(1)} %bitcast.225) | data formatting | bytes 3932160 | tf_op jit(solution)/shard_map/convert_element_type | solution.py:78
  175.5 4.9 %copy.53 = f32[48,64,160]{2,0,1:T(8,128)S(1)} copy(f32[48,64,160]{1,0,2:T(8,128)} %bitcast.224) | data formatting | bytes 3932160 | tf_op jit(solution)/shard_map/convert_element_type | solution.py:78
  180.4 2.0 fusion.15
  182.4 1.2 copy-done
  183.6 2.6 %collective-permute-start.4 = (bf16[48,16,160]{2,0,1:T(8,128)(2,1)S(1)}, bf16[48,16,160]{2,0,1:T(8,128)(2,1)S(1)}, u32[]{:S(2)}, u32[]{:S(2)}) collective-permute-start(bf16[48,16,160]{2,0,1:T(8,128)(2,1)S(1)} %get-tuple-element.7), channel_id=1, source_target_pairs={{0,16},{16,32},{32,48},{48,64},{64,80},{80,96},{96,112},{112,128},... | collective-permute-start | bytes 737288 | tf_op jit(solution)/shard_map/ppermute | solution.py:17
  186.2 4.5 %collective-permute-start.5 = (bf16[48,16,160]{2,0,1:T(8,128)(2,1)S(1)}, bf16[48,16,160]{2,0,1:T(8,128)(2,1)S(1)}, u32[]{:S(2)}, u32[]{:S(2)}) collective-permute-start(bf16[48,16,160]{2,0,1:T(8,128)(2,1)S(1)} %get-tuple-element.8), channel_id=1, source_target_pairs={{16,0},{32,16},{48,32},{64,48},{80,64},{96,80},{112,96},{128,112},... | collective-permute-start | bytes 737288 | tf_op jit(solution)/shard_map/ppermute | solution.py:18
  191.1 14.6 %collective-permute-done.4 = bf16[48,16,160]{2,0,1:T(8,128)(2,1)S(1)} collective-permute-done((bf16[48,16,160]{2,0,1:T(8,128)(2,1)S(1)}, bf16[48,16,160]{2,0,1:T(8,128)(2,1)S(1)}, u32[]{:S(2)}, u32[]{:S(2)}) %collective-permute-start.4) | collective-permute-done | bytes 245792 | tf_op jit(solution)/shard_map/ppermute | solution.py:17
  205.7 1.9 maximum_maximum_fusion
  210.7 1.4 fusion.2
  213.3 1.1 copy.57
  (84 shorter events, 23.4 us)
Async XLA Ops:
  1.0 8.5 %collective-permute-start = (bf16[48,8,128]{2,0,1:T(8,128)(2,1)S(1)}, bf16[48,8,128]{2,0,1:T(8,128)(2,1)S(1)}, u32[]{:S(2)}, u32[]{:S(2)}) collective-permute-start(bf16[48,8,128]{2,0,1:T(8,128)(2,1)S(1)} %copy.62), channel_id=1, source_target_pairs={{0,16},{16,32},{32,48},{48,64},{64,80},{80,96},{96,112},{112,128},... | collective-permute-start | bytes 294920 | tf_op jit(solution)/shard_map/ppermute | solution.py:17
  5.4 7.8 %collective-permute-start.1 = (bf16[48,8,128]{2,0,1:T(8,128)(2,1)S(1)}, bf16[48,8,128]{2,0,1:T(8,128)(2,1)S(1)}, u32[]{:S(2)}, u32[]{:S(2)}) collective-permute-start(bf16[48,8,128]{2,0,1:T(8,128)(2,1)S(1)} %copy.63), channel_id=1, source_target_pairs={{16,0},{32,16},{48,32},{64,48},{80,64},{96,80},{112,96},{128,112},... | collective-permute-start | bytes 294920 | tf_op jit(solution)/shard_map/ppermute | solution.py:18
  13.2 8.6 %copy-start.7 = (f32[2,2,48]{2,1,0:T(2,128)S(1)}, f32[2,2,48]{2,1,0:T(2,128)}, u32[]{:S(2)}) copy-start(f32[2,2,48]{2,1,0:T(2,128)} %param.9) | copy-start | bytes 2308
  13.2 8.6 %copy-start.8 = (f32[2,2,48]{2,1,0:T(2,128)S(1)}, f32[2,2,48]{2,1,0:T(2,128)}, u32[]{:S(2)}) copy-start(f32[2,2,48]{2,1,0:T(2,128)} %param.8) | copy-start | bytes 2308
  14.4 8.2 %collective-permute-start.2 = (bf16[48,80,24]{1,2,0:T(8,128)(2,1)S(1)}, bf16[48,80,24]{1,2,0:T(8,128)(2,1)S(1)}, u32[]{:S(2)}, u32[]{:S(2)}) collective-permute-start(bf16[48,80,24]{1,2,0:T(8,128)(2,1)S(1)} %copy.44), channel_id=1, source_target_pairs={{0,1},{1,2},{2,3},{3,4},{4,5},{5,6},{6,7},{7,8},{8,9},{9,10},{10,1... | collective-permute-start | bytes 552968 | tf_op jit(solution)/shard_map/ppermute | solution.py:17
  19.7 8.9 %collective-permute-start.3 = (bf16[48,80,24]{1,2,0:T(8,128)(2,1)S(1)}, bf16[48,80,24]{1,2,0:T(8,128)(2,1)S(1)}, u32[]{:S(2)}, u32[]{:S(2)}) collective-permute-start(bf16[48,80,24]{1,2,0:T(8,128)(2,1)S(1)} %copy.45), channel_id=1, source_target_pairs={{1,0},{2,1},{3,2},{4,3},{5,4},{6,5},{7,6},{8,7},{9,8},{10,9},{11,1... | collective-permute-start | bytes 552968 | tf_op jit(solution)/shard_map/ppermute | solution.py:18
  35.0 6.4 %copy-start.3 = (bf16[48,80,176]{2,0,1:T(8,128)(2,1)S(1)}, bf16[48,80,176]{2,0,1:T(8,128)(2,1)}, u32[]{:S(2)}) copy-start(bf16[48,80,176]{2,0,1:T(8,128)(2,1)} %get-tuple-element.6) | copy-start | bytes 4055044
  35.1 6.4 %copy-start.11 = (f32[48]{0:T(128)S(1)}, f32[48]{0:T(128)}, u32[]{:S(2)}) copy-start(f32[48]{0:T(128)} %get-tuple-element.37) | copy-start | bytes 580
  35.1 6.4 %copy-start.12 = (f32[48]{0:T(128)S(1)}, f32[48]{0:T(128)}, u32[]{:S(2)}) copy-start(f32[48]{0:T(128)} %get-tuple-element.38) | copy-start | bytes 580
  36.5 5.0 %copy-start.6 = (bf16[9,48,64,160]{3,1,2,0:T(8,128)(2,1)}, bf16[9,48,64,160]{3,1,2,0:T(8,128)(2,1)S(1)}, u32[]{:S(2)}) copy-start(bf16[9,48,64,160]{3,1,2,0:T(8,128)(2,1)S(1)} %fusion.16) | copy-start | bytes 26542084
  50.1 1.4 copy-start.2
  145.7 20.3 %all-to-all-start.2 = ((bf16[16,240,128]{2,1,0:T(8,128)(2,1)}), bf16[16,240,128]{2,1,0:T(8,128)(2,1)S(1)}, u32[]{:S(2)}, u32[]{:S(2)}) async-start(bf16[16,240,128]{2,1,0:T(8,128)(2,1)} %constant_dynamic-update-slice_fusion.3), calls=%async_computation.2 | async-start | bytes 1966080 | tf_op jit(solution)/shard_map/all_to_all | solution.py:72
  180.3 10.4 %copy-start.5 = (bf16[1,3,3,48,48]{4,3,2,1,0:T(8,128)(2,1)S(1)}, bf16[1,3,3,48,48]{4,3,2,1,0:T(8,128)(2,1)}, u32[]{:S(2)}) copy-start(bf16[1,3,3,48,48]{4,3,2,1,0:T(8,128)(2,1)} %get-tuple-element.29) | copy-start | bytes 124420
  180.3 10.5 %copy-start.4 = (bf16[3,3,48,48]{3,2,0,1:T(8,128)(2,1)S(1)}, bf16[3,3,48,48]{3,2,0,1:T(8,128)(2,1)}, u32[]{:S(2)}) copy-start(bf16[3,3,48,48]{3,2,0,1:T(8,128)(2,1)} %get-tuple-element.30) | copy-start | bytes 124420
  180.3 10.6 %copy-start.10 = (f32[48]{0:T(128)S(1)}, f32[48]{0:T(128)}, u32[]{:S(2)}) copy-start(f32[48]{0:T(128)} %get-tuple-element.40) | copy-start | bytes 580
  180.3 10.7 %copy-start.9 = (f32[48]{0:T(128)S(1)}, f32[48]{0:T(128)}, u32[]{:S(2)}) copy-start(f32[48]{0:T(128)} %get-tuple-element.39) | copy-start | bytes 580
  182.4 1.2 copy-start
  183.6 22.1 %collective-permute-start.4 = (bf16[48,16,160]{2,0,1:T(8,128)(2,1)S(1)}, bf16[48,16,160]{2,0,1:T(8,128)(2,1)S(1)}, u32[]{:S(2)}, u32[]{:S(2)}) collective-permute-start(bf16[48,16,160]{2,0,1:T(8,128)(2,1)S(1)} %get-tuple-element.7), channel_id=1, source_target_pairs={{0,16},{16,32},{32,48},{48,64},{64,80},{80,96},{96,112},{112,128},... | collective-permute-start | bytes 737288 | tf_op jit(solution)/shard_map/ppermute | solution.py:17
  186.2 19.5 %collective-permute-start.5 = (bf16[48,16,160]{2,0,1:T(8,128)(2,1)S(1)}, bf16[48,16,160]{2,0,1:T(8,128)(2,1)S(1)}, u32[]{:S(2)}, u32[]{:S(2)}) collective-permute-start(bf16[48,16,160]{2,0,1:T(8,128)(2,1)S(1)} %get-tuple-element.8), channel_id=1, source_target_pairs={{16,0},{32,16},{48,32},{64,48},{80,64},{96,80},{112,96},{128,112},... | collective-permute-start | bytes 737288 | tf_op jit(solution)/shard_map/ppermute | solution.py:18
  210.6 1.5 copy-start.1
  210.7 1.5 copy-start.13

commit v8 on v6

--- a/solution.py
+++ b/solution.py
@@ -83,7 +83,7 @@
 def body(features, w_dilated, w_pointwise, norm_gain, norm_bias):
     count, tile_rows, tile_cols = features.shape
     kernel = w_dilated[0].reshape(9, count, count)
-    extended = padded(features, (("row", 1), ("col", 2)), FIRST_DILATION)
+    extended = padded(features, (("col", 2), ("row", 1)), FIRST_DILATION)
     hidden = hidden_of(
         extended, kernel, norm_gain[0, 0], norm_bias[0, 0], FIRST_DILATION, tile_rows, tile_cols
     )
@@ -92,7 +92,7 @@
 
     kernel = w_dilated[1]
     both = jnp.concatenate([kernel, jnp.swapaxes(kernel, 0, 1)], axis=2).reshape(9, 2 * count, count)
-    extended = padded(state, (("row", 1), ("col", 2)), SECOND_DILATION)
+    extended = padded(state, (("col", 2), ("row", 1)), SECOND_DILATION)
     gain = jnp.concatenate([norm_gain[1, 0], norm_gain[1, 0]])
     bias = jnp.concatenate([norm_bias[1, 0], norm_bias[1, 0]])
     hidden = hidden_of(extended, both, gain, bias, SECOND_DILATION, tile_rows, tile_cols)

time: 188 us -> 195 us (1.037)
  waiting for transfers between devices: 12.5 us -> 24.5 us
  local copies, waits for them, and re-layouts: 31.4 us -> 27.4 us
    ppermute x4, waiting for transfers between devices: 6.53 us -> 17.8 us  [padded(): before = lax.ppermute(last, axis, up)]
    unnamed x30 -> x29, local copies, waits for them, and re-layouts: 9.64 us -> 12.9 us
    ppermute x4, starting transfers between devices: 12.2 us -> 15.1 us  [padded(): before = lax.ppermute(last, axis, up)]
    slice x3 -> x1, local copies, waits for them, and re-layouts: 3.34 us -> 0.64 us  [padded(): initial = lax.slice_in_dim(value, 0, width, axis=dim)]
    slice x4 -> x3, local copies, waits for them, and re-layouts: 5.39 us -> 2.76 us  [padded(): last = lax.slice_in_dim(value, length - width, length, axis=dim)]
    ppermute x4, starting transfers between devices: 14.6 us -> 12.4 us  [padded(): after = lax.ppermute(initial, axis, down)]
  transfers between devices with their start and end apart: 8 -> 8, of which waited for: 5 -> 6; matrix products, arithmetic and copies ran while one was open for 3% -> 2% of each run, Pallas kernels for 0% -> 0%
where the time goes in v8:
time: 195 us; the launch traced here: 194 us
  blocking collectives  97.1 us (50%)
  local copies, waits for them, and re-layouts  27.4 us (14%)
  starting transfers between devices  27.4 us (14%)
  waiting for transfers between devices  24.5 us (13%)
  other arithmetic  8.69 us (4%)
  matrix products  8.24 us (4%)
    all_to_all x1, blocking collectives, mirror_pieces(): t = lax.all_to_all(t, 'row', 0, 0, tiled=True)  60.5 us
    all_to_all x2, blocking collectives, mirror_pieces(): t = lax.all_to_all(t, 'col', 0, 0, tiled=True)  36.6 us
    ppermute x4, waiting for transfers between devices, padded(): before = lax.ppermute(last, axis, up)  17.8 us
    ppermute x4, starting transfers between devices, padded(): before = lax.ppermute(last, axis, up)  15.1 us
    unnamed x29, local copies, waits for them, and re-layouts  12.9 us
    ppermute x4, starting transfers between devices, padded(): after = lax.ppermute(initial, axis, down)  12.4 us
    dot_general x3, matrix products, block_output(): jnp.einsum('oc,chw->ohw', pointwise, hidden, preferred_element_type=jnp.f...  6.81 us
    ppermute x4, waiting for transfers between devices, padded(): after = lax.ppermute(initial, axis, down)  6.7 us
  transfers between devices with their start and end apart: 8, of which 6 were waited for; matrix products, arithmetic and copies ran while one was open for 2% of the time, Pallas kernels for 0%

profile of v8, /device:TPU:7, one launch (start us, length us, event | category | flops | bytes accessed | tf_op | source)
XLA Modules:
  0.0 193.7 jit_solution(7875081538392009700)
XLA Ops:
  0.0 1.8 fusion.56
  2.1 2.6 %collective-permute-start.1 = (bf16[48,64,8]{1,2,0:T(8,128)(2,1)S(1)}, bf16[48,64,8]{1,2,0:T(8,128)(2,1)}, u32[]{:S(2)}, u32[]{:S(2)}) collective-permute-start(bf16[48,64,8]{1,2,0:T(8,128)(2,1)S(1)} %copy.49), channel_id=1, source_target_pairs={{1,0},{2,1},{3,2},{4,3},{5,4},{6,5},{7,6},{8,7},{9,8},{10,9},{11,1... | collective-permute-start | bytes 147464 | tf_op jit(solution)/shard_map/ppermute | solution.py:18
  5.0 3.9 %collective-permute-start = (bf16[48,64,8]{1,2,0:T(8,128)(2,1)S(1)}, bf16[48,64,8]{1,2,0:T(8,128)(2,1)S(1)}, u32[]{:S(2)}, u32[]{:S(2)}) collective-permute-start(bf16[48,64,8]{1,2,0:T(8,128)(2,1)S(1)} %copy.48), channel_id=1, source_target_pairs={{0,1},{1,2},{2,3},{3,4},{4,5},{5,6},{6,7},{7,8},{8,9},{9,10},{10,1... | collective-permute-start | bytes 147464 | tf_op jit(solution)/shard_map/ppermute | solution.py:17
  11.1 1.5 copy.25
  12.9 4.4 %collective-permute-start.2 = (bf16[48,8,144]{2,0,1:T(8,128)(2,1)S(1)}, bf16[48,8,144]{2,0,1:T(8,128)(2,1)S(1)}, u32[]{:S(2)}, u32[]{:S(2)}) collective-permute-start(bf16[48,8,144]{2,0,1:T(8,128)(2,1)S(1)} %get-tuple-element.7), channel_id=1, source_target_pairs={{0,16},{16,32},{32,48},{48,64},{64,80},{80,96},{96,112},{112,128},... | collective-permute-start | bytes 331784 | tf_op jit(solution)/shard_map/ppermute | solution.py:17
  17.3 2.4 %collective-permute-start.3 = (bf16[48,8,144]{2,0,1:T(8,128)(2,1)S(1)}, bf16[48,8,144]{2,0,1:T(8,128)(2,1)S(1)}, u32[]{:S(2)}, u32[]{:S(2)}) collective-permute-start(bf16[48,8,144]{2,0,1:T(8,128)(2,1)S(1)} %get-tuple-element.8), channel_id=1, source_target_pairs={{16,0},{32,16},{48,32},{64,48},{80,64},{96,80},{112,96},{128,112},... | collective-permute-start | bytes 331784 | tf_op jit(solution)/shard_map/ppermute | solution.py:18
  19.7 1.4 collective-permute-done.2
  21.1 6.2 %collective-permute-done.3 = bf16[48,8,144]{2,0,1:T(8,128)(2,1)S(1)} collective-permute-done((bf16[48,8,144]{2,0,1:T(8,128)(2,1)S(1)}, bf16[48,8,144]{2,0,1:T(8,128)(2,1)S(1)}, u32[]{:S(2)}, u32[]{:S(2)}) %collective-permute-start.3) | collective-permute-done | bytes 110624 | tf_op jit(solution)/shard_map/ppermute | solution.py:18
  27.3 1.3 maximum_maximum_fusion.1
  29.7 1.2 fusion.38
  30.9 1.2 fusion.37
  32.1 1.1 fusion.36
  33.2 1.2 fusion.35
  34.4 1.2 fusion.34
  36.7 1.2 fusion.32
  37.9 1.2 fusion.31
  39.2 5.2 %fusion.11 = bf16[48,64,128]{2,0,1:T(8,128)(2,1)S(1)} fusion(bf16[9,48,48,1]{2,1,0,3:T(8,128)(2,1)S(1)} %bitcast.195, bf16[9,48,64,128]{3,1,0,2:T(8,128)(2,1)} %fusion.31, f32[48]{0:T(128)S(1)} %get-tuple-element.23, f32[48]{0:T(128)S(1)} %get-tuple-element.28, f32[48]{0:T(128)S(1)} %get-tuple-element.24, f32[48]{0:T(128)S(1)} %get-tuple-element.27, ...), kind=kOutput, calls=%fused_computation.17 | convolution fusion | flops 381419520 | bytes 8775680 | tf_op jit(solution)/shard_map/oc,chw->ohw/dot_general | solution.py:41
  46.0 19.5 %all_to_all.15 = bf16[16,192,128]{2,1,0:T(8,128)(2,1)S(1)} all-to-all(bf16[16,192,128]{2,1,0:T(8,128)(2,1)S(1)} %reshape.43), channel_id=1, replica_groups=mesh['row'=32,'col'=16] {'col'}, dimensions={0} | all-to-all | bytes 1572864 | tf_op jit(solution)/shard_map/all_to_all | solution.py:60
  65.6 60.5 %all_to_all.16 = bf16[32,96,128]{2,1,0:T(8,128)(2,1)S(1)} all-to-all(bf16[32,96,128]{2,1,0:T(8,128)(2,1)S(1)} %bitcast.189), channel_id=1, replica_groups=mesh['row'=32,'col'=16] {'row'}, dimensions={0} | all-to-all | bytes 1572864 | tf_op jit(solution)/shard_map/all_to_all | solution.py:63
  126.1 17.1 %all_to_all.17 = bf16[16,192,128]{2,1,0:T(8,128)(2,1)S(1)} all-to-all(bf16[16,192,128]{2,1,0:T(8,128)(2,1)S(1)} %bitcast.190), channel_id=1, replica_groups=mesh['row'=32,'col'=16] {'col'}, dimensions={0} | all-to-all | bytes 1572864 | tf_op jit(solution)/shard_map/all_to_all | solution.py:65
  143.9 1.4 fusion.55
  145.7 2.0 %fusion.16 = (bf16[48,64,64]{2,0,1:T(8,128)(2,1)S(1)}, bf16[48,64,64]{2,0,1:T(8,128)(2,1)S(1)}) fusion(f32[48,64,64]{2,1,0:T(8,128)S(1)} %convert.3, bf16[48,64,128]{2,0,1:T(8,128)(2,1)S(1)} %fusion.11, f32[48,64,64]{2,1,0:T(8,128)S(1)} %convert.2), kind=kLoop, calls=%fused_computation.24 | loop fusion | flops 1572864 | bytes 3145728 | tf_op jit(solution)/shard_map/convert_element_type | solution.py:71
  148.4 2.3 %collective-permute-start.5 = (bf16[48,64,16]{1,2,0:T(8,128)(2,1)S(1)}, bf16[48,64,16]{1,2,0:T(8,128)(2,1)S(1)}, u32[]{:S(2)}, u32[]{:S(2)}) collective-permute-start(bf16[48,64,16]{1,2,0:T(8,128)(2,1)S(1)} %copy.41), channel_id=1, source_target_pairs={{1,0},{2,1},{3,2},{4,3},{5,4},{6,5},{7,6},{8,7},{9,8},{10,9},{11,1... | collective-permute-start | bytes 294920 | tf_op jit(solution)/shard_map/ppermute | solution.py:18
  151.6 4.2 %collective-permute-start.4 = (bf16[48,64,16]{1,2,0:T(8,128)(2,1)S(1)}, bf16[48,64,16]{1,2,0:T(8,128)(2,1)}, u32[]{:S(2)}, u32[]{:S(2)}) collective-permute-start(bf16[48,64,16]{1,2,0:T(8,128)(2,1)S(1)} %copy.40), channel_id=1, source_target_pairs={{0,1},{1,2},{2,3},{3,4},{4,5},{5,6},{6,7},{7,8},{8,9},{9,10},{10,1... | collective-permute-start | bytes 294920 | tf_op jit(solution)/shard_map/ppermute | solution.py:17
  156.9 1.5 collective-permute-done.4
  158.4 1.5 copy.42
  159.9 1.6 pad_maximum_fusion.4
  161.5 2.6 %collective-permute-start.6 = (bf16[48,16,160]{2,0,1:T(8,128)(2,1)}, bf16[48,16,160]{2,0,1:T(8,128)(2,1)}, u32[]{:S(2)}, u32[]{:S(2)}) collective-permute-start(bf16[48,16,160]{2,0,1:T(8,128)(2,1)} %get-tuple-element.5), channel_id=1, source_target_pairs={{0,16},{16,32},{32,48},{48,64},{64,80},{80,96},{96,112},{112,128},... | collective-permute-start | bytes 737288 | tf_op jit(solution)/shard_map/ppermute | solution.py:17
  164.1 5.1 %collective-permute-start.7 = (bf16[48,16,160]{2,0,1:T(8,128)(2,1)}, bf16[48,16,160]{2,0,1:T(8,128)(2,1)}, u32[]{:S(2)}, u32[]{:S(2)}) collective-permute-start(bf16[48,16,160]{2,0,1:T(8,128)(2,1)} %get-tuple-element.6), channel_id=1, source_target_pairs={{16,0},{32,16},{48,32},{64,48},{80,64},{96,80},{112,96},{128,112},... | collective-permute-start | bytes 737288 | tf_op jit(solution)/shard_map/ppermute | solution.py:18
  169.7 13.9 %collective-permute-done.6 = bf16[48,16,160]{2,0,1:T(8,128)(2,1)} collective-permute-done((bf16[48,16,160]{2,0,1:T(8,128)(2,1)}, bf16[48,16,160]{2,0,1:T(8,128)(2,1)}, u32[]{:S(2)}, u32[]{:S(2)}) %collective-permute-start.6) | collective-permute-done | bytes 245792 | tf_op jit(solution)/shard_map/ppermute | solution.py:17
  183.6 3.0 %maximum_maximum_fusion = bf16[48,96,160]{2,0,1:T(8,128)(2,1)S(1)} fusion(bf16[48,16,160]{2,0,1:T(8,128)(2,1)} %collective-permute-done.7, bf16[48,64,16]{2,0,1:T(8,128)(2,1)S(1)} %copy.43, bf16[48,64,64]{2,0,1:T(8,128)(2,1)S(1)} %get-tuple-element.11, bf16[48,64,64]{2,0,1:T(8,128)(2,1)S(1)} %get-tuple-element.12, bf16[48,64,16]{2,0,1:T(8,128)(2,1)S(1)} %copy.42, ...), kind=kLoop, calls=%fused_computation.4 | loop fusion | flops 10321920 | bytes 2949120 | tf_op jit(solution)/shard_map/max | solution.py:24
  189.6 1.4 fusion.2
  (49 shorter events, 16.6 us)
Async XLA Ops:
  0.0 8.9 %copy-start = (bf16[48,64,128]{2,1,0:T(8,128)(2,1)S(1)}, bf16[48,64,128]{2,1,0:T(8,128)(2,1)}, u32[]{:S(2)}) copy-start(bf16[48,64,128]{2,1,0:T(8,128)(2,1)} %param.5) | copy-start | bytes 2359300
  0.0 8.9 %copy-start.1 = (bf16[2,3,3,48,48]{4,3,2,1,0:T(8,128)(2,1)S(1)}, bf16[2,3,3,48,48]{4,3,2,1,0:T(8,128)(2,1)}, u32[]{:S(2)}) copy-start(bf16[2,3,3,48,48]{4,3,2,1,0:T(8,128)(2,1)} %param.6) | copy-start | bytes 248836
  2.1 9.0 %collective-permute-start.1 = (bf16[48,64,8]{1,2,0:T(8,128)(2,1)S(1)}, bf16[48,64,8]{1,2,0:T(8,128)(2,1)}, u32[]{:S(2)}, u32[]{:S(2)}) collective-permute-start(bf16[48,64,8]{1,2,0:T(8,128)(2,1)S(1)} %copy.49), channel_id=1, source_target_pairs={{1,0},{2,1},{3,2},{4,3},{5,4},{6,5},{7,6},{8,7},{9,8},{10,9},{11,1... | collective-permute-start | bytes 147464 | tf_op jit(solution)/shard_map/ppermute | solution.py:18
  5.0 5.5 %collective-permute-start = (bf16[48,64,8]{1,2,0:T(8,128)(2,1)S(1)}, bf16[48,64,8]{1,2,0:T(8,128)(2,1)S(1)}, u32[]{:S(2)}, u32[]{:S(2)}) collective-permute-start(bf16[48,64,8]{1,2,0:T(8,128)(2,1)S(1)} %copy.48), channel_id=1, source_target_pairs={{0,1},{1,2},{2,3},{3,4},{4,5},{5,6},{6,7},{7,8},{8,9},{9,10},{10,1... | collective-permute-start | bytes 147464 | tf_op jit(solution)/shard_map/ppermute | solution.py:17
  9.5 10.2 %copy-start.2 = (f32[2,2,48]{2,1,0:T(2,128)S(1)}, f32[2,2,48]{2,1,0:T(2,128)}, u32[]{:S(2)}) copy-start(f32[2,2,48]{2,1,0:T(2,128)} %param.9) | copy-start | bytes 2308
  9.5 10.2 %copy-start.3 = (f32[2,2,48]{2,1,0:T(2,128)S(1)}, f32[2,2,48]{2,1,0:T(2,128)}, u32[]{:S(2)}) copy-start(f32[2,2,48]{2,1,0:T(2,128)} %param.8) | copy-start | bytes 2308
  12.9 8.2 %collective-permute-start.2 = (bf16[48,8,144]{2,0,1:T(8,128)(2,1)S(1)}, bf16[48,8,144]{2,0,1:T(8,128)(2,1)S(1)}, u32[]{:S(2)}, u32[]{:S(2)}) collective-permute-start(bf16[48,8,144]{2,0,1:T(8,128)(2,1)S(1)} %get-tuple-element.7), channel_id=1, source_target_pairs={{0,16},{16,32},{32,48},{48,64},{64,80},{80,96},{96,112},{112,128},... | collective-permute-start | bytes 331784 | tf_op jit(solution)/shard_map/ppermute | solution.py:17
  17.3 10.0 %collective-permute-start.3 = (bf16[48,8,144]{2,0,1:T(8,128)(2,1)S(1)}, bf16[48,8,144]{2,0,1:T(8,128)(2,1)S(1)}, u32[]{:S(2)}, u32[]{:S(2)}) collective-permute-start(bf16[48,8,144]{2,0,1:T(8,128)(2,1)S(1)} %get-tuple-element.8), channel_id=1, source_target_pairs={{16,0},{32,16},{48,32},{64,48},{80,64},{96,80},{112,96},{128,112},... | collective-permute-start | bytes 331784 | tf_op jit(solution)/shard_map/ppermute | solution.py:18
  35.6 3.5 %copy-start.4 = (bf16[2,48,48]{2,1,0:T(8,128)(2,1)S(1)}, bf16[2,48,48]{2,1,0:T(8,128)(2,1)}, u32[]{:S(2)}) copy-start(bf16[2,48,48]{2,1,0:T(8,128)(2,1)} %param.7) | copy-start | bytes 27652
  148.4 7.9 %collective-permute-start.5 = (bf16[48,64,16]{1,2,0:T(8,128)(2,1)S(1)}, bf16[48,64,16]{1,2,0:T(8,128)(2,1)S(1)}, u32[]{:S(2)}, u32[]{:S(2)}) collective-permute-start(bf16[48,64,16]{1,2,0:T(8,128)(2,1)S(1)} %copy.41), channel_id=1, source_target_pairs={{1,0},{2,1},{3,2},{4,3},{5,4},{6,5},{7,6},{8,7},{9,8},{10,9},{11,1... | collective-permute-start | bytes 294920 | tf_op jit(solution)/shard_map/ppermute | solution.py:18
  151.6 6.8 %collective-permute-start.4 = (bf16[48,64,16]{1,2,0:T(8,128)(2,1)S(1)}, bf16[48,64,16]{1,2,0:T(8,128)(2,1)}, u32[]{:S(2)}, u32[]{:S(2)}) collective-permute-start(bf16[48,64,16]{1,2,0:T(8,128)(2,1)S(1)} %copy.40), channel_id=1, source_target_pairs={{0,1},{1,2},{2,3},{3,4},{4,5},{5,6},{6,7},{7,8},{8,9},{9,10},{10,1... | collective-permute-start | bytes 294920 | tf_op jit(solution)/shard_map/ppermute | solution.py:17
  161.5 22.1 %collective-permute-start.6 = (bf16[48,16,160]{2,0,1:T(8,128)(2,1)}, bf16[48,16,160]{2,0,1:T(8,128)(2,1)}, u32[]{:S(2)}, u32[]{:S(2)}) collective-permute-start(bf16[48,16,160]{2,0,1:T(8,128)(2,1)} %get-tuple-element.5), channel_id=1, source_target_pairs={{0,16},{16,32},{32,48},{48,64},{64,80},{80,96},{96,112},{112,128},... | collective-permute-start | bytes 737288 | tf_op jit(solution)/shard_map/ppermute | solution.py:17
  164.1 19.4 %collective-permute-start.7 = (bf16[48,16,160]{2,0,1:T(8,128)(2,1)}, bf16[48,16,160]{2,0,1:T(8,128)(2,1)}, u32[]{:S(2)}, u32[]{:S(2)}) collective-permute-start(bf16[48,16,160]{2,0,1:T(8,128)(2,1)} %get-tuple-element.6), channel_id=1, source_target_pairs={{16,0},{32,16},{48,32},{64,48},{80,64},{96,80},{112,96},{128,112},... | collective-permute-start | bytes 737288 | tf_op jit(solution)/shard_map/ppermute | solution.py:18

commit v9 on v6

--- a/solution.py
+++ b/solution.py
@@ -87,6 +87,7 @@
     hidden = hidden_of(
         extended, kernel, norm_gain[0, 0], norm_bias[0, 0], FIRST_DILATION, tile_rows, tile_cols
     )
+    hidden = lax.optimization_barrier(hidden)
     output_map = block_output(features, hidden, norm_gain[0], norm_bias[0], w_pointwise[0])
     state = symmetrized(output_map)
 

time: 188 us -> 182 us (0.968)
  matrix products: 8.24 us -> 5.35 us
  local copies, waits for them, and re-layouts: 31.4 us -> 28.6 us
    dot_general x3, matrix products: 6.81 us -> 2.29 us  [block_output(): jnp.einsum('oc,chw->ohw', pointwise, hidden, preferred_element_type=jnp.f...]
    unnamed x30 -> x28, local copies, waits for them, and re-layouts: 9.64 us -> 6.78 us
where the time goes in v9:
time: 182 us; the launch traced here: 179 us
  blocking collectives  97.4 us (54%)
  local copies, waits for them, and re-layouts  28.6 us (16%)
  starting transfers between devices  26.7 us (15%)
  waiting for transfers between devices  12.5 us (7%)
  other arithmetic  8.37 us (5%)
  matrix products  5.35 us (3%)
    all_to_all x1, blocking collectives, mirror_pieces(): t = lax.all_to_all(t, 'row', 0, 0, tiled=True)  60.5 us
    all_to_all x2, blocking collectives, mirror_pieces(): t = lax.all_to_all(t, 'col', 0, 0, tiled=True)  36.9 us
    ppermute x4, starting transfers between devices, padded(): after = lax.ppermute(initial, axis, down)  14.6 us
    ppermute x4, starting transfers between devices, padded(): before = lax.ppermute(last, axis, up)  12.2 us
    unnamed x28, local copies, waits for them, and re-layouts  6.78 us
    ppermute x4, waiting for transfers between devices, padded(): before = lax.ppermute(last, axis, up)  6.53 us
    ppermute x4, waiting for transfers between devices, padded(): after = lax.ppermute(initial, axis, down)  5.98 us
    slice x4, local copies, waits for them, and re-layouts, padded(): last = lax.slice_in_dim(value, length - width, length, axis=dim)  5.41 us
  transfers between devices with their start and end apart: 8, of which 5 were waited for; matrix products, arithmetic and copies ran while one was open for 3% of the time, Pallas kernels for 0%

profile of v9, /device:TPU:7, one launch (start us, length us, event | category | flops | bytes accessed | tf_op | source)
XLA Modules:
  0.0 179.4 jit_solution(13246425249737122460)
XLA Ops:
  0.0 1.0 fusion.56
  1.0 4.4 %collective-permute-start = (bf16[48,8,128]{2,0,1:T(8,128)(2,1)S(1)}, bf16[48,8,128]{2,0,1:T(8,128)(2,1)S(1)}, u32[]{:S(2)}, u32[]{:S(2)}) collective-permute-start(bf16[48,8,128]{2,0,1:T(8,128)(2,1)S(1)} %copy.62), channel_id=1, source_target_pairs={{0,16},{16,32},{32,48},{48,64},{64,80},{80,96},{96,112},{112,128},... | collective-permute-start | bytes 294920 | tf_op jit(solution)/shard_map/ppermute | solution.py:17
  5.4 2.4 %collective-permute-start.1 = (bf16[48,8,128]{2,0,1:T(8,128)(2,1)S(1)}, bf16[48,8,128]{2,0,1:T(8,128)(2,1)S(1)}, u32[]{:S(2)}, u32[]{:S(2)}) collective-permute-start(bf16[48,8,128]{2,0,1:T(8,128)(2,1)S(1)} %copy.63), channel_id=1, source_target_pairs={{16,0},{32,16},{48,32},{64,48},{80,64},{96,80},{112,96},{128,112},... | collective-permute-start | bytes 294920 | tf_op jit(solution)/shard_map/ppermute | solution.py:18
  7.8 1.0 fusion.57
  8.8 1.7 constant_dynamic-update-slice_fusion.1
  10.5 2.6 %collective-permute-done.1 = bf16[48,8,128]{2,0,1:T(8,128)(2,1)S(1)} collective-permute-done((bf16[48,8,128]{2,0,1:T(8,128)(2,1)S(1)}, bf16[48,8,128]{2,0,1:T(8,128)(2,1)S(1)}, u32[]{:S(2)}, u32[]{:S(2)}) %collective-permute-start.1) | collective-permute-done | bytes 98336 | tf_op jit(solution)/shard_map/ppermute | solution.py:18
  15.2 4.0 %collective-permute-start.3 = (bf16[48,80,8]{1,2,0:T(8,128)(2,1)S(1)}, bf16[48,80,8]{1,2,0:T(8,128)(2,1)S(1)}, u32[]{:S(2)}, u32[]{:S(2)}) collective-permute-start(bf16[48,80,8]{1,2,0:T(8,128)(2,1)S(1)} %copy.25), channel_id=1, source_target_pairs={{1,0},{2,1},{3,2},{4,3},{5,4},{6,5},{7,6},{8,7},{9,8},{10,9},{11,1... | collective-permute-start | bytes 184328 | tf_op jit(solution)/shard_map/ppermute | solution.py:18
  19.2 2.5 %collective-permute-start.2 = (bf16[48,80,8]{1,2,0:T(8,128)(2,1)S(1)}, bf16[48,80,8]{1,2,0:T(8,128)(2,1)S(1)}, u32[]{:S(2)}, u32[]{:S(2)}) collective-permute-start(bf16[48,80,8]{1,2,0:T(8,128)(2,1)S(1)} %copy.24), channel_id=1, source_target_pairs={{0,1},{1,2},{2,3},{3,4},{4,5},{5,6},{6,7},{7,8},{8,9},{9,10},{10,1... | collective-permute-start | bytes 184328 | tf_op jit(solution)/shard_map/ppermute | solution.py:17
  21.7 1.6 collective-permute-done.2
  24.8 1.4 maximum_maximum_fusion.1
  29.2 1.6 fusion.19
  33.2 19.7 %all_to_all.15 = bf16[16,192,128]{2,1,0:T(8,128)(2,1)S(1)} all-to-all(bf16[16,192,128]{2,1,0:T(8,128)(2,1)S(1)} %reshape.43), channel_id=1, replica_groups=mesh['row'=32,'col'=16] {'col'}, dimensions={0} | all-to-all | bytes 1572864 | tf_op jit(solution)/shard_map/all_to_all | solution.py:60
  53.0 60.5 %all_to_all.16 = bf16[32,96,128]{2,1,0:T(8,128)(2,1)S(1)} all-to-all(bf16[32,96,128]{2,1,0:T(8,128)(2,1)S(1)} %bitcast.184), channel_id=1, replica_groups=mesh['row'=32,'col'=16] {'row'}, dimensions={0} | all-to-all | bytes 1572864 | tf_op jit(solution)/shard_map/all_to_all | solution.py:63
  113.5 17.1 %all_to_all.17 = bf16[16,192,128]{2,1,0:T(8,128)(2,1)S(1)} all-to-all(bf16[16,192,128]{2,1,0:T(8,128)(2,1)S(1)} %bitcast.185), channel_id=1, replica_groups=mesh['row'=32,'col'=16] {'col'}, dimensions={0} | all-to-all | bytes 1572864 | tf_op jit(solution)/shard_map/all_to_all | solution.py:65
  131.4 1.4 fusion.53
  133.2 2.0 %fusion.16 = (bf16[48,64,64]{2,0,1:T(8,128)(2,1)S(1)}, bf16[48,64,64]{2,0,1:T(8,128)(2,1)S(1)}) fusion(f32[48,64,64]{2,1,0:T(8,128)S(1)} %convert.3, bf16[48,64,128]{2,0,1:T(8,128)(2,1)S(1)} %fusion.11, f32[48,64,64]{2,1,0:T(8,128)S(1)} %convert.2), kind=kLoop, calls=%fused_computation.24 | loop fusion | flops 1572864 | bytes 3145728 | tf_op jit(solution)/shard_map/convert_element_type | solution.py:71
  135.4 2.7 %collective-permute-start.4 = (bf16[48,16,128]{2,0,1:T(8,128)(2,1)S(1)}, bf16[48,16,128]{2,0,1:T(8,128)(2,1)S(1)}, u32[]{:S(2)}, u32[]{:S(2)}) collective-permute-start(bf16[48,16,128]{2,0,1:T(8,128)(2,1)S(1)} %get-tuple-element.5), channel_id=1, source_target_pairs={{0,16},{16,32},{32,48},{48,64},{64,80},{80,96},{96,112},{112,128},... | collective-permute-start | bytes 589832 | tf_op jit(solution)/shard_map/ppermute | solution.py:17
  138.1 4.1 %collective-permute-start.5 = (bf16[48,16,128]{2,0,1:T(8,128)(2,1)S(1)}, bf16[48,16,128]{2,0,1:T(8,128)(2,1)S(1)}, u32[]{:S(2)}, u32[]{:S(2)}) collective-permute-start(bf16[48,16,128]{2,0,1:T(8,128)(2,1)S(1)} %get-tuple-element.6), channel_id=1, source_target_pairs={{16,0},{32,16},{48,32},{64,48},{80,64},{96,80},{112,96},{128,112},... | collective-permute-start | bytes 589832 | tf_op jit(solution)/shard_map/ppermute | solution.py:18
  142.3 2.7 %collective-permute-done.4 = bf16[48,16,128]{2,0,1:T(8,128)(2,1)S(1)} collective-permute-done((bf16[48,16,128]{2,0,1:T(8,128)(2,1)S(1)}, bf16[48,16,128]{2,0,1:T(8,128)(2,1)S(1)}, u32[]{:S(2)}, u32[]{:S(2)}) %collective-permute-start.4) | collective-permute-done | bytes 196640 | tf_op jit(solution)/shard_map/ppermute | solution.py:17
  144.9 3.3 %collective-permute-done.5 = bf16[48,16,128]{2,0,1:T(8,128)(2,1)S(1)} collective-permute-done((bf16[48,16,128]{2,0,1:T(8,128)(2,1)S(1)}, bf16[48,16,128]{2,0,1:T(8,128)(2,1)S(1)}, u32[]{:S(2)}, u32[]{:S(2)}) %collective-permute-start.5) | collective-permute-done | bytes 196640 | tf_op jit(solution)/shard_map/ppermute | solution.py:18
  148.7 1.5 fusion.54
  150.2 2.8 %copy.42 = bf16[48,96,16]{1,2,0:T(8,128)(2,1)} copy(bf16[48,96,16]{2,0,1:T(8,128)(2,1)} %get-tuple-element.9) | data formatting | bytes 294912 | tf_op jit(solution)/shard_map/slice | solution.py:15
  153.0 1.6 copy.43
  154.6 4.0 %collective-permute-start.7 = (bf16[48,96,16]{1,2,0:T(8,128)(2,1)}, bf16[48,96,16]{1,2,0:T(8,128)(2,1)}, u32[]{:S(2)}, u32[]{:S(2)}) collective-permute-start(bf16[48,96,16]{1,2,0:T(8,128)(2,1)} %copy.43), channel_id=1, source_target_pairs={{1,0},{2,1},{3,2},{4,3},{5,4},{6,5},{7,6},{8,7},{9,8},{10,9},{11,1... | collective-permute-start | bytes 442376 | tf_op jit(solution)/shard_map/ppermute | solution.py:18
  158.6 2.7 %collective-permute-start.6 = (bf16[48,96,16]{1,2,0:T(8,128)(2,1)}, bf16[48,96,16]{1,2,0:T(8,128)(2,1)}, u32[]{:S(2)}, u32[]{:S(2)}) collective-permute-start(bf16[48,96,16]{1,2,0:T(8,128)(2,1)} %copy.42), channel_id=1, source_target_pairs={{0,1},{1,2},{2,3},{3,4},{4,5},{5,6},{6,7},{7,8},{8,9},{9,10},{10,1... | collective-permute-start | bytes 442376 | tf_op jit(solution)/shard_map/ppermute | solution.py:17
  161.7 2.3 %collective-permute-done.6 = bf16[48,96,16]{1,2,0:T(8,128)(2,1)} collective-permute-done((bf16[48,96,16]{1,2,0:T(8,128)(2,1)}, bf16[48,96,16]{1,2,0:T(8,128)(2,1)}, u32[]{:S(2)}, u32[]{:S(2)}) %collective-permute-start.6) | collective-permute-done | bytes 147488 | tf_op jit(solution)/shard_map/ppermute | solution.py:17
  163.9 1.8 copy.44
  165.7 2.8 %copy.45 = bf16[48,96,16]{2,0,1:T(8,128)(2,1)} copy(bf16[48,96,16]{1,2,0:T(8,128)(2,1)} %collective-permute-done.7) | data formatting | bytes 294912 | tf_op jit(solution)/shard_map/ppermute | solution.py:18
  168.5 3.8 %maximum_maximum_fusion = bf16[48,96,160]{2,0,1:T(8,128)(2,1)S(1)} fusion(bf16[48,96,16]{2,0,1:T(8,128)(2,1)} %copy.45, bf16[48,16,128]{2,0,1:T(8,128)(2,1)S(1)} %collective-permute-done.5, bf16[48,64,64]{2,0,1:T(8,128)(2,1)S(1)} %get-tuple-element.13, bf16[48,64,64]{2,0,1:T(8,128)(2,1)S(1)} %get-tuple-element.14, ...), kind=kLoop, calls=%fused_computation.4 | loop fusion | flops 10321920 | bytes 2949120 | tf_op jit(solution)/shard_map/max | solution.py:24
  175.3 1.4 fusion.2
  177.4 0.9 multiply_convert_fusion
  178.3 1.1 copy.47
  (53 shorter events, 14.6 us)
Async XLA Ops:
  1.0 7.8 %collective-permute-start = (bf16[48,8,128]{2,0,1:T(8,128)(2,1)S(1)}, bf16[48,8,128]{2,0,1:T(8,128)(2,1)S(1)}, u32[]{:S(2)}, u32[]{:S(2)}) collective-permute-start(bf16[48,8,128]{2,0,1:T(8,128)(2,1)S(1)} %copy.62), channel_id=1, source_target_pairs={{0,16},{16,32},{32,48},{48,64},{64,80},{80,96},{96,112},{112,128},... | collective-permute-start | bytes 294920 | tf_op jit(solution)/shard_map/ppermute | solution.py:17
  5.4 7.8 %collective-permute-start.1 = (bf16[48,8,128]{2,0,1:T(8,128)(2,1)S(1)}, bf16[48,8,128]{2,0,1:T(8,128)(2,1)S(1)}, u32[]{:S(2)}, u32[]{:S(2)}) collective-permute-start(bf16[48,8,128]{2,0,1:T(8,128)(2,1)S(1)} %copy.63), channel_id=1, source_target_pairs={{16,0},{32,16},{48,32},{64,48},{80,64},{96,80},{112,96},{128,112},... | collective-permute-start | bytes 294920 | tf_op jit(solution)/shard_map/ppermute | solution.py:18
  13.2 8.5 %copy-start.1 = (f32[2,2,48]{2,1,0:T(2,128)S(1)}, f32[2,2,48]{2,1,0:T(2,128)}, u32[]{:S(2)}) copy-start(f32[2,2,48]{2,1,0:T(2,128)} %param.9) | copy-start | bytes 2308
  13.2 8.5 %copy-start.2 = (f32[2,2,48]{2,1,0:T(2,128)S(1)}, f32[2,2,48]{2,1,0:T(2,128)}, u32[]{:S(2)}) copy-start(f32[2,2,48]{2,1,0:T(2,128)} %param.8) | copy-start | bytes 2308
  15.2 8.8 %collective-permute-start.3 = (bf16[48,80,8]{1,2,0:T(8,128)(2,1)S(1)}, bf16[48,80,8]{1,2,0:T(8,128)(2,1)S(1)}, u32[]{:S(2)}, u32[]{:S(2)}) collective-permute-start(bf16[48,80,8]{1,2,0:T(8,128)(2,1)S(1)} %copy.25), channel_id=1, source_target_pairs={{1,0},{2,1},{3,2},{4,3},{5,4},{6,5},{7,6},{8,7},{9,8},{10,9},{11,1... | collective-permute-start | bytes 184328 | tf_op jit(solution)/shard_map/ppermute | solution.py:18
  19.2 4.1 %collective-permute-start.2 = (bf16[48,80,8]{1,2,0:T(8,128)(2,1)S(1)}, bf16[48,80,8]{1,2,0:T(8,128)(2,1)S(1)}, u32[]{:S(2)}, u32[]{:S(2)}) collective-permute-start(bf16[48,80,8]{1,2,0:T(8,128)(2,1)S(1)} %copy.24), channel_id=1, source_target_pairs={{0,1},{1,2},{2,3},{3,4},{4,5},{5,6},{6,7},{7,8},{8,9},{9,10},{10,1... | collective-permute-start | bytes 184328 | tf_op jit(solution)/shard_map/ppermute | solution.py:17
  29.1 1.7 copy-start
  29.1 1.7 copy-start.3
  135.4 9.5 %collective-permute-start.4 = (bf16[48,16,128]{2,0,1:T(8,128)(2,1)S(1)}, bf16[48,16,128]{2,0,1:T(8,128)(2,1)S(1)}, u32[]{:S(2)}, u32[]{:S(2)}) collective-permute-start(bf16[48,16,128]{2,0,1:T(8,128)(2,1)S(1)} %get-tuple-element.5), channel_id=1, source_target_pairs={{0,16},{16,32},{32,48},{48,64},{64,80},{80,96},{96,112},{112,128},... | collective-permute-start | bytes 589832 | tf_op jit(solution)/shard_map/ppermute | solution.py:17
  138.1 10.2 %collective-permute-start.5 = (bf16[48,16,128]{2,0,1:T(8,128)(2,1)S(1)}, bf16[48,16,128]{2,0,1:T(8,128)(2,1)S(1)}, u32[]{:S(2)}, u32[]{:S(2)}) collective-permute-start(bf16[48,16,128]{2,0,1:T(8,128)(2,1)S(1)} %get-tuple-element.6), channel_id=1, source_target_pairs={{16,0},{32,16},{48,32},{64,48},{80,64},{96,80},{112,96},{128,112},... | collective-permute-start | bytes 589832 | tf_op jit(solution)/shard_map/ppermute | solution.py:18
  154.6 11.2 %collective-permute-start.7 = (bf16[48,96,16]{1,2,0:T(8,128)(2,1)}, bf16[48,96,16]{1,2,0:T(8,128)(2,1)}, u32[]{:S(2)}, u32[]{:S(2)}) collective-permute-start(bf16[48,96,16]{1,2,0:T(8,128)(2,1)} %copy.43), channel_id=1, source_target_pairs={{1,0},{2,1},{3,2},{4,3},{5,4},{6,5},{7,6},{8,7},{9,8},{10,9},{11,1... | collective-permute-start | bytes 442376 | tf_op jit(solution)/shard_map/ppermute | solution.py:18
  158.6 5.4 %collective-permute-start.6 = (bf16[48,96,16]{1,2,0:T(8,128)(2,1)}, bf16[48,96,16]{1,2,0:T(8,128)(2,1)}, u32[]{:S(2)}, u32[]{:S(2)}) collective-permute-start(bf16[48,96,16]{1,2,0:T(8,128)(2,1)} %copy.42), channel_id=1, source_target_pairs={{0,1},{1,2},{2,3},{3,4},{4,5},{5,6},{6,7},{7,8},{8,9},{9,10},{10,1... | collective-permute-start | bytes 442376 | tf_op jit(solution)/shard_map/ppermute | solution.py:17

commit v10 on v9

--- a/solution.py
+++ b/solution.py
@@ -64,7 +64,8 @@
     t = t.reshape(n_col, k * c_lo * rows, lanes)
     t = lax.all_to_all(t, "col", 0, 0, tiled=True)
     t = t.reshape(n_col, k, c_lo, rows, fold, tile_rows)
-    return [t[:, s].reshape(channel_count, tile_rows, tile_rows) for s in range(k)]
+    t = jnp.transpose(t, (0, 2, 3, 4, 1, 5))
+    return t.reshape(channel_count, tile_rows, tile_cols)
 
 
 def mean_of(a, b):
@@ -72,12 +73,7 @@
 
 
 def symmetrized(output_map):
-    tile_rows = output_map.shape[1]
-    halves = [
-        mean_of(output_map[:, :, s * tile_rows:(s + 1) * tile_rows], piece)
-        for s, piece in enumerate(mirror_pieces(output_map))
-    ]
-    return jnp.concatenate(halves, axis=2)
+    return mean_of(output_map, lax.optimization_barrier(mirror_pieces(output_map)))
 
 
 def body(features, w_dilated, w_pointwise, norm_gain, norm_bias):

time: 182 us -> 176 us (0.967)
  waiting for transfers between devices: 12.5 us -> 9.01 us
  other arithmetic: 8.37 us -> 6.06 us
    ppermute x4, waiting for transfers between devices: 6.53 us -> 3.7 us  [padded(): before = lax.ppermute(last, axis, up)]
    slice x4 -> x5, local copies, waits for them, and re-layouts: 5.41 us -> 3.21 us  [padded(): last = lax.slice_in_dim(value, length - width, length, axis=dim)]
    slice x2, local copies, waits for them, and re-layouts: 1.12 us -> 3.32 us  [body(): kernel = w_dilated[1]]
    unnamed x28 -> x38, local copies, waits for them, and re-layouts: 6.78 us -> 6.84 us
  transfers between devices with their start and end apart: 8 -> 8, of which waited for: 5 -> 4; matrix products, arithmetic and copies ran while one was open for 3% -> 6% of each run, Pallas kernels for 0% -> 0%
where the time goes in v10:
time: 176 us; the launch traced here: 174 us
  blocking collectives  97.4 us (55%)
  local copies, waits for them, and re-layouts  29.8 us (17%)
  starting transfers between devices  26.5 us (15%)
  waiting for transfers between devices  9.01 us (5%)
  other arithmetic  6.06 us (3%)
  matrix products  4.82 us (3%)
    all_to_all x1, blocking collectives, mirror_pieces(): t = lax.all_to_all(t, 'row', 0, 0, tiled=True)  60.5 us
    all_to_all x2, blocking collectives, mirror_pieces(): t = lax.all_to_all(t, 'col', 0, 0, tiled=True)  36.9 us
    ppermute x4, starting transfers between devices, padded(): after = lax.ppermute(initial, axis, down)  14.6 us
    ppermute x4, starting transfers between devices, padded(): before = lax.ppermute(last, axis, up)  12 us
    unnamed x38, local copies, waits for them, and re-layouts  6.84 us
    ppermute x4, waiting for transfers between devices, padded(): after = lax.ppermute(initial, axis, down)  5.32 us
    ppermute x4, waiting for transfers between devices, padded(): before = lax.ppermute(last, axis, up)  3.7 us
    max x2, other arithmetic, hidden_of(): active = jnp.maximum(extended_input, jnp.zeros((), extended_input.dtype))  3.64 us
  transfers between devices with their start and end apart: 8, of which 4 were waited for; matrix products, arithmetic and copies ran while one was open for 6% of the time, Pallas kernels for 0%

profile of v10, /device:TPU:7, one launch (start us, length us, event | category | flops | bytes accessed | tf_op | source)
XLA Modules:
  0.0 174.1 jit_solution(12214516164183255237)
XLA Ops:
  0.0 1.0 fusion.50
  1.0 4.4 %collective-permute-start = (bf16[48,8,128]{2,0,1:T(8,128)(2,1)S(1)}, bf16[48,8,128]{2,0,1:T(8,128)(2,1)S(1)}, u32[]{:S(2)}, u32[]{:S(2)}) collective-permute-start(bf16[48,8,128]{2,0,1:T(8,128)(2,1)S(1)} %copy.50), channel_id=1, source_target_pairs={{0,16},{16,32},{32,48},{48,64},{64,80},{80,96},{96,112},{112,128},... | collective-permute-start | bytes 294920 | tf_op jit(solution)/shard_map/ppermute | solution.py:17
  5.4 2.4 %collective-permute-start.1 = (bf16[48,8,128]{2,0,1:T(8,128)(2,1)S(1)}, bf16[48,8,128]{2,0,1:T(8,128)(2,1)S(1)}, u32[]{:S(2)}, u32[]{:S(2)}) collective-permute-start(bf16[48,8,128]{2,0,1:T(8,128)(2,1)S(1)} %copy.51), channel_id=1, source_target_pairs={{16,0},{32,16},{48,32},{64,48},{80,64},{96,80},{112,96},{128,112},... | collective-permute-start | bytes 294920 | tf_op jit(solution)/shard_map/ppermute | solution.py:18
  7.8 1.7 fusion.51
  9.5 1.7 constant_dynamic-update-slice_fusion.1
  11.2 2.0 %collective-permute-done.1 = bf16[48,8,128]{2,0,1:T(8,128)(2,1)S(1)} collective-permute-done((bf16[48,8,128]{2,0,1:T(8,128)(2,1)S(1)}, bf16[48,8,128]{2,0,1:T(8,128)(2,1)S(1)}, u32[]{:S(2)}, u32[]{:S(2)}) %collective-permute-start.1) | collective-permute-done | bytes 98336 | tf_op jit(solution)/shard_map/ppermute | solution.py:18
  15.2 4.0 %collective-permute-start.3 = (bf16[48,80,8]{1,2,0:T(8,128)(2,1)S(1)}, bf16[48,80,8]{1,2,0:T(8,128)(2,1)S(1)}, u32[]{:S(2)}, u32[]{:S(2)}) collective-permute-start(bf16[48,80,8]{1,2,0:T(8,128)(2,1)S(1)} %copy.24), channel_id=1, source_target_pairs={{1,0},{2,1},{3,2},{4,3},{5,4},{6,5},{7,6},{8,7},{9,8},{10,9},{11,1... | collective-permute-start | bytes 184328 | tf_op jit(solution)/shard_map/ppermute | solution.py:18
  19.2 2.5 %collective-permute-start.2 = (bf16[48,80,8]{1,2,0:T(8,128)(2,1)S(1)}, bf16[48,80,8]{1,2,0:T(8,128)(2,1)S(1)}, u32[]{:S(2)}, u32[]{:S(2)}) collective-permute-start(bf16[48,80,8]{1,2,0:T(8,128)(2,1)S(1)} %copy.23), channel_id=1, source_target_pairs={{0,1},{1,2},{2,3},{3,4},{4,5},{5,6},{6,7},{7,8},{8,9},{9,10},{10,1... | collective-permute-start | bytes 184328 | tf_op jit(solution)/shard_map/ppermute | solution.py:17
  22.3 1.0 collective-permute-done.2
  24.8 1.4 maximum_maximum_fusion.1
  29.2 1.7 fusion.15
  31.6 0.9 copy.35
  33.2 19.7 %all_to_all.15 = bf16[16,192,128]{2,1,0:T(8,128)(2,1)S(1)} all-to-all(bf16[16,192,128]{2,1,0:T(8,128)(2,1)S(1)} %reshape.42), channel_id=1, replica_groups=mesh['row'=32,'col'=16] {'col'}, dimensions={0} | all-to-all | bytes 1572864 | tf_op jit(solution)/shard_map/all_to_all | solution.py:60
  53.0 60.5 %all_to_all.16 = bf16[32,96,128]{2,1,0:T(8,128)(2,1)S(1)} all-to-all(bf16[32,96,128]{2,1,0:T(8,128)(2,1)S(1)} %bitcast.184), channel_id=1, replica_groups=mesh['row'=32,'col'=16] {'row'}, dimensions={0} | all-to-all | bytes 1572864 | tf_op jit(solution)/shard_map/all_to_all | solution.py:63
  113.5 17.1 %all_to_all.17 = bf16[16,192,128]{2,1,0:T(8,128)(2,1)S(1)} all-to-all(bf16[16,192,128]{2,1,0:T(8,128)(2,1)S(1)} %bitcast.185), channel_id=1, replica_groups=mesh['row'=32,'col'=16] {'col'}, dimensions={0} | all-to-all | bytes 1572864 | tf_op jit(solution)/shard_map/all_to_all | solution.py:65
  131.4 1.6 copy.37
  133.0 1.5 reshape.47
  134.5 1.4 multiply_convert_fusion.1
  135.9 2.7 %collective-permute-start.4 = (bf16[48,16,128]{2,0,1:T(8,128)(2,1)S(1)}, bf16[48,16,128]{2,0,1:T(8,128)(2,1)S(1)}, u32[]{:S(2)}, u32[]{:S(2)}) collective-permute-start(bf16[48,16,128]{2,0,1:T(8,128)(2,1)S(1)} %get-tuple-element.9), channel_id=1, source_target_pairs={{0,16},{16,32},{32,48},{48,64},{64,80},{80,96},{96,112},{112,128},... | collective-permute-start | bytes 589832 | tf_op jit(solution)/shard_map/ppermute | solution.py:17
  138.6 4.1 %collective-permute-start.5 = (bf16[48,16,128]{2,0,1:T(8,128)(2,1)S(1)}, bf16[48,16,128]{2,0,1:T(8,128)(2,1)S(1)}, u32[]{:S(2)}, u32[]{:S(2)}) collective-permute-start(bf16[48,16,128]{2,0,1:T(8,128)(2,1)S(1)} %get-tuple-element.10), channel_id=1, source_target_pairs={{16,0},{32,16},{48,32},{64,48},{80,64},{96,80},{112,96},{128,112},... | collective-permute-start | bytes 589832 | tf_op jit(solution)/shard_map/ppermute | solution.py:18
  142.7 2.7 %collective-permute-done.4 = bf16[48,16,128]{2,0,1:T(8,128)(2,1)S(1)} collective-permute-done((bf16[48,16,128]{2,0,1:T(8,128)(2,1)S(1)}, bf16[48,16,128]{2,0,1:T(8,128)(2,1)S(1)}, u32[]{:S(2)}, u32[]{:S(2)}) %collective-permute-start.4) | collective-permute-done | bytes 196640 | tf_op jit(solution)/shard_map/ppermute | solution.py:17
  145.4 3.3 %collective-permute-done.5 = bf16[48,16,128]{2,0,1:T(8,128)(2,1)S(1)} collective-permute-done((bf16[48,16,128]{2,0,1:T(8,128)(2,1)S(1)}, bf16[48,16,128]{2,0,1:T(8,128)(2,1)S(1)}, u32[]{:S(2)}, u32[]{:S(2)}) %collective-permute-start.5) | collective-permute-done | bytes 196640 | tf_op jit(solution)/shard_map/ppermute | solution.py:18
  149.3 1.6 copy.40
  150.9 0.9 copy.41
  151.8 4.0 %collective-permute-start.7 = (bf16[48,96,16]{1,2,0:T(8,128)(2,1)S(1)}, bf16[48,96,16]{1,2,0:T(8,128)(2,1)}, u32[]{:S(2)}, u32[]{:S(2)}) collective-permute-start(bf16[48,96,16]{1,2,0:T(8,128)(2,1)S(1)} %copy.41), channel_id=1, source_target_pairs={{1,0},{2,1},{3,2},{4,3},{5,4},{6,5},{7,6},{8,7},{9,8},{10,9},{11,1... | collective-permute-start | bytes 442376 | tf_op jit(solution)/shard_map/ppermute | solution.py:18
  155.8 2.4 %collective-permute-start.6 = (bf16[48,96,16]{1,2,0:T(8,128)(2,1)}, bf16[48,96,16]{1,2,0:T(8,128)(2,1)S(1)}, u32[]{:S(2)}, u32[]{:S(2)}) collective-permute-start(bf16[48,96,16]{1,2,0:T(8,128)(2,1)} %copy.40), channel_id=1, source_target_pairs={{0,1},{1,2},{2,3},{3,4},{4,5},{5,6},{6,7},{7,8},{8,9},{9,10},{10,1... | collective-permute-start | bytes 442376 | tf_op jit(solution)/shard_map/ppermute | solution.py:17
  158.4 1.6 copy.38
  160.0 1.6 copy.39
  163.4 1.8 %copy.43 = bf16[48,96,16]{2,0,1:T(8,128)(2,1)S(1)} copy(bf16[48,96,16]{1,2,0:T(8,128)(2,1)} %collective-permute-done.7) | data formatting | bytes 294912 | tf_op jit(solution)/shard_map/ppermute | solution.py:18
  165.2 2.3 %maximum_maximum_fusion = bf16[48,96,160]{2,0,1:T(8,128)(2,1)S(1)} fusion(bf16[48,96,16]{2,0,1:T(8,128)(2,1)S(1)} %copy.43, bf16[48,16,128]{2,0,1:T(8,128)(2,1)S(1)} %collective-permute-done.5, bf16[48,64,128]{2,0,1:T(8,128)(2,1)S(1)} %multiply_convert_fusion.1, bf16[48,16,128]{2,0,1:T(8,128)(2,1)S(1)} %collective-permute-done.4, bf16[48,96,16]{2,0,1:T(8,128)(2,1)S(1)} %copy.42), kind=kLoop, calls=%fused_computation.4 | loop fusion | flops 8847360 | bytes 2949120 | tf_op jit(solution)/shard_map/max | solution.py:24
  170.5 1.4 fusion.2
  173.0 1.1 copy.45
  (62 shorter events, 15.5 us)
Async XLA Ops:
  1.0 8.5 %collective-permute-start = (bf16[48,8,128]{2,0,1:T(8,128)(2,1)S(1)}, bf16[48,8,128]{2,0,1:T(8,128)(2,1)S(1)}, u32[]{:S(2)}, u32[]{:S(2)}) collective-permute-start(bf16[48,8,128]{2,0,1:T(8,128)(2,1)S(1)} %copy.50), channel_id=1, source_target_pairs={{0,16},{16,32},{32,48},{48,64},{64,80},{80,96},{96,112},{112,128},... | collective-permute-start | bytes 294920 | tf_op jit(solution)/shard_map/ppermute | solution.py:17
  5.4 7.8 %collective-permute-start.1 = (bf16[48,8,128]{2,0,1:T(8,128)(2,1)S(1)}, bf16[48,8,128]{2,0,1:T(8,128)(2,1)S(1)}, u32[]{:S(2)}, u32[]{:S(2)}) collective-permute-start(bf16[48,8,128]{2,0,1:T(8,128)(2,1)S(1)} %copy.51), channel_id=1, source_target_pairs={{16,0},{32,16},{48,32},{64,48},{80,64},{96,80},{112,96},{128,112},... | collective-permute-start | bytes 294920 | tf_op jit(solution)/shard_map/ppermute | solution.py:18
  13.2 8.5 %copy-start.5 = (f32[2,2,48]{2,1,0:T(2,128)S(1)}, f32[2,2,48]{2,1,0:T(2,128)}, u32[]{:S(2)}) copy-start(f32[2,2,48]{2,1,0:T(2,128)} %param.9) | copy-start | bytes 2308
  13.2 8.5 %copy-start.6 = (f32[2,2,48]{2,1,0:T(2,128)S(1)}, f32[2,2,48]{2,1,0:T(2,128)}, u32[]{:S(2)}) copy-start(f32[2,2,48]{2,1,0:T(2,128)} %param.8) | copy-start | bytes 2308
  15.2 8.8 %collective-permute-start.3 = (bf16[48,80,8]{1,2,0:T(8,128)(2,1)S(1)}, bf16[48,80,8]{1,2,0:T(8,128)(2,1)S(1)}, u32[]{:S(2)}, u32[]{:S(2)}) collective-permute-start(bf16[48,80,8]{1,2,0:T(8,128)(2,1)S(1)} %copy.24), channel_id=1, source_target_pairs={{1,0},{2,1},{3,2},{4,3},{5,4},{6,5},{7,6},{8,7},{9,8},{10,9},{11,1... | collective-permute-start | bytes 184328 | tf_op jit(solution)/shard_map/ppermute | solution.py:18
  19.2 4.1 %collective-permute-start.2 = (bf16[48,80,8]{1,2,0:T(8,128)(2,1)S(1)}, bf16[48,80,8]{1,2,0:T(8,128)(2,1)S(1)}, u32[]{:S(2)}, u32[]{:S(2)}) collective-permute-start(bf16[48,80,8]{1,2,0:T(8,128)(2,1)S(1)} %copy.23), channel_id=1, source_target_pairs={{0,1},{1,2},{2,3},{3,4},{4,5},{5,6},{6,7},{7,8},{8,9},{9,10},{10,1... | collective-permute-start | bytes 184328 | tf_op jit(solution)/shard_map/ppermute | solution.py:17
  29.1 1.7 copy-start.2
  29.1 1.7 copy-start.7
  31.6 0.9 copy-start
  133.0 1.5 copy-start.1
  135.9 9.5 %collective-permute-start.4 = (bf16[48,16,128]{2,0,1:T(8,128)(2,1)S(1)}, bf16[48,16,128]{2,0,1:T(8,128)(2,1)S(1)}, u32[]{:S(2)}, u32[]{:S(2)}) collective-permute-start(bf16[48,16,128]{2,0,1:T(8,128)(2,1)S(1)} %get-tuple-element.9), channel_id=1, source_target_pairs={{0,16},{16,32},{32,48},{48,64},{64,80},{80,96},{96,112},{112,128},... | collective-permute-start | bytes 589832 | tf_op jit(solution)/shard_map/ppermute | solution.py:17
  138.6 10.2 %collective-permute-start.5 = (bf16[48,16,128]{2,0,1:T(8,128)(2,1)S(1)}, bf16[48,16,128]{2,0,1:T(8,128)(2,1)S(1)}, u32[]{:S(2)}, u32[]{:S(2)}) collective-permute-start(bf16[48,16,128]{2,0,1:T(8,128)(2,1)S(1)} %get-tuple-element.10), channel_id=1, source_target_pairs={{16,0},{32,16},{48,32},{64,48},{80,64},{96,80},{112,96},{128,112},... | collective-permute-start | bytes 589832 | tf_op jit(solution)/shard_map/ppermute | solution.py:18
  151.8 11.5 %collective-permute-start.7 = (bf16[48,96,16]{1,2,0:T(8,128)(2,1)S(1)}, bf16[48,96,16]{1,2,0:T(8,128)(2,1)}, u32[]{:S(2)}, u32[]{:S(2)}) collective-permute-start(bf16[48,96,16]{1,2,0:T(8,128)(2,1)S(1)} %copy.41), channel_id=1, source_target_pairs={{1,0},{2,1},{3,2},{4,3},{5,4},{6,5},{7,6},{8,7},{9,8},{10,9},{11,1... | collective-permute-start | bytes 442376 | tf_op jit(solution)/shard_map/ppermute | solution.py:18
  155.8 6.6 %collective-permute-start.6 = (bf16[48,96,16]{1,2,0:T(8,128)(2,1)}, bf16[48,96,16]{1,2,0:T(8,128)(2,1)S(1)}, u32[]{:S(2)}, u32[]{:S(2)}) collective-permute-start(bf16[48,96,16]{1,2,0:T(8,128)(2,1)} %copy.40), channel_id=1, source_target_pairs={{0,1},{1,2},{2,3},{3,4},{4,5},{5,6},{6,7},{7,8},{8,9},{9,10},{10,1... | collective-permute-start | bytes 442376 | tf_op jit(solution)/shard_map/ppermute | solution.py:17
  169.4 1.0 copy-start.3
  169.4 1.0 copy-start.4
  170.5 1.4 copy-start.8

commit v11 on v10

--- a/solution.py
+++ b/solution.py
@@ -83,15 +83,15 @@
     hidden = hidden_of(
         extended, kernel, norm_gain[0, 0], norm_bias[0, 0], FIRST_DILATION, tile_rows, tile_cols
     )
-    hidden = lax.optimization_barrier(hidden)
+    kernel = w_dilated[1]
+    both = jnp.concatenate([kernel, jnp.swapaxes(kernel, 0, 1)], axis=2).reshape(9, 2 * count, count)
+    gain = jnp.concatenate([norm_gain[1, 0], norm_gain[1, 0]])
+    bias = jnp.concatenate([norm_bias[1, 0], norm_bias[1, 0]])
+    hidden, both, gain, bias = lax.optimization_barrier((hidden, both, gain, bias))
     output_map = block_output(features, hidden, norm_gain[0], norm_bias[0], w_pointwise[0])
     state = symmetrized(output_map)
 
-    kernel = w_dilated[1]
-    both = jnp.concatenate([kernel, jnp.swapaxes(kernel, 0, 1)], axis=2).reshape(9, 2 * count, count)
     extended = padded(state, (("row", 1), ("col", 2)), SECOND_DILATION)
-    gain = jnp.concatenate([norm_gain[1, 0], norm_gain[1, 0]])
-    bias = jnp.concatenate([norm_bias[1, 0], norm_bias[1, 0]])
     hidden = hidden_of(extended, both, gain, bias, SECOND_DILATION, tile_rows, tile_cols)
     direct = block_output(state, hidden[:count], norm_gain[1], norm_bias[1], w_pointwise[1])
     mirrored = block_output(state, hidden[count:], norm_gain[1], norm_bias[1], w_pointwise[1])

time: 176 us -> 176 us (level)
  waiting for transfers between devices: 9.01 us -> 14.9 us
  local copies, waits for them, and re-layouts: 29.8 us -> 24.9 us
    ppermute x4, waiting for transfers between devices: 5.32 us -> 10.6 us  [padded(): after = lax.ppermute(initial, axis, down)]
    slice x2 -> x1, local copies, waits for them, and re-layouts: 3.32 us -> 0.97 us  [body(): kernel = w_dilated[1]]
    ppermute x4, starting transfers between devices: 14.6 us -> 12.5 us  [padded(): after = lax.ppermute(initial, axis, down)]
    ppermute x4, starting transfers between devices: 12 us -> 13.8 us  [padded(): before = lax.ppermute(last, axis, up)]
    unnamed x38 -> x35, local copies, waits for them, and re-layouts: 6.84 us -> 5.69 us
  transfers between devices with their start and end apart: 8 -> 8, of which waited for: 4 -> 6; matrix products, arithmetic and copies ran while one was open for 6% -> 3% of each run, Pallas kernels for 0% -> 0%
where the time goes in v11:
time: 176 us; the launch traced here: 175 us
  blocking collectives  97.4 us (55%)
  starting transfers between devices  26.3 us (15%)
  local copies, waits for them, and re-layouts  24.9 us (14%)
  waiting for transfers between devices  14.9 us (8%)
  other arithmetic  6.05 us (3%)
  matrix products  4.81 us (3%)
    all_to_all x1, blocking collectives, mirror_pieces(): t = lax.all_to_all(t, 'row', 0, 0, tiled=True)  60.5 us
    all_to_all x2, blocking collectives, mirror_pieces(): t = lax.all_to_all(t, 'col', 0, 0, tiled=True)  36.9 us
    ppermute x4, starting transfers between devices, padded(): before = lax.ppermute(last, axis, up)  13.8 us
    ppermute x4, starting transfers between devices, padded(): after = lax.ppermute(initial, axis, down)  12.5 us
    ppermute x4, waiting for transfers between devices, padded(): after = lax.ppermute(initial, axis, down)  10.6 us
    unnamed x35, local copies, waits for them, and re-layouts  5.69 us
    ppermute x4, waiting for transfers between devices, padded(): before = lax.ppermute(last, axis, up)  4.28 us
    max x2, other arithmetic, hidden_of(): active = jnp.maximum(extended_input, jnp.zeros((), extended_input.dtype))  3.64 us
  transfers between devices with their start and end apart: 8, of which 6 were waited for; matrix products, arithmetic and copies ran while one was open for 3% of the time, Pallas kernels for 0%

profile of v11, /device:TPU:7, one launch (start us, length us, event | category | flops | bytes accessed | tf_op | source)
XLA Modules:
  0.0 174.8 jit_solution(13505142285663358353)
XLA Ops:
  0.0 1.0 fusion.46
  1.1 4.4 %collective-permute-start = (bf16[48,8,128]{2,0,1:T(8,128)(2,1)S(1)}, bf16[48,8,128]{2,0,1:T(8,128)(2,1)S(1)}, u32[]{:S(2)}, u32[]{:S(2)}) collective-permute-start(bf16[48,8,128]{2,0,1:T(8,128)(2,1)S(1)} %copy.76), channel_id=1, source_target_pairs={{0,16},{16,32},{32,48},{48,64},{64,80},{80,96},{96,112},{112,128},... | collective-permute-start | bytes 294920 | tf_op jit(solution)/shard_map/ppermute | solution.py:17
  5.5 2.4 %collective-permute-start.1 = (bf16[48,8,128]{2,0,1:T(8,128)(2,1)S(1)}, bf16[48,8,128]{2,0,1:T(8,128)(2,1)S(1)}, u32[]{:S(2)}, u32[]{:S(2)}) collective-permute-start(bf16[48,8,128]{2,0,1:T(8,128)(2,1)S(1)} %copy.77), channel_id=1, source_target_pairs={{16,0},{32,16},{48,32},{64,48},{80,64},{96,80},{112,96},{128,112},... | collective-permute-start | bytes 294920 | tf_op jit(solution)/shard_map/ppermute | solution.py:18
  7.9 1.0 fusion.47
  8.9 0.8 slice_bitcast_fusion.18
  11.1 2.2 %collective-permute-done.1 = bf16[48,8,128]{2,0,1:T(8,128)(2,1)S(1)} collective-permute-done((bf16[48,8,128]{2,0,1:T(8,128)(2,1)S(1)}, bf16[48,8,128]{2,0,1:T(8,128)(2,1)S(1)}, u32[]{:S(2)}, u32[]{:S(2)}) %collective-permute-start.1) | collective-permute-done | bytes 98336 | tf_op jit(solution)/shard_map/ppermute | solution.py:18
  15.2 4.0 %collective-permute-start.3 = (bf16[48,80,8]{1,2,0:T(8,128)(2,1)S(1)}, bf16[48,80,8]{1,2,0:T(8,128)(2,1)S(1)}, u32[]{:S(2)}, u32[]{:S(2)}) collective-permute-start(bf16[48,80,8]{1,2,0:T(8,128)(2,1)S(1)} %copy.46), channel_id=1, source_target_pairs={{1,0},{2,1},{3,2},{4,3},{5,4},{6,5},{7,6},{8,7},{9,8},{10,9},{11,1... | collective-permute-start | bytes 184328 | tf_op jit(solution)/shard_map/ppermute | solution.py:18
  19.2 2.5 %collective-permute-start.2 = (bf16[48,80,8]{1,2,0:T(8,128)(2,1)S(1)}, bf16[48,80,8]{1,2,0:T(8,128)(2,1)S(1)}, u32[]{:S(2)}, u32[]{:S(2)}) collective-permute-start(bf16[48,80,8]{1,2,0:T(8,128)(2,1)S(1)} %copy.45), channel_id=1, source_target_pairs={{0,1},{1,2},{2,3},{3,4},{4,5},{5,6},{6,7},{7,8},{8,9},{9,10},{10,1... | collective-permute-start | bytes 184328 | tf_op jit(solution)/shard_map/ppermute | solution.py:17
  21.8 1.5 collective-permute-done.2
  24.8 1.4 maximum_maximum_fusion.1
  29.2 1.7 fusion.15
  31.6 0.9 copy.59
  33.3 19.7 %all_to_all.15 = bf16[16,192,128]{2,1,0:T(8,128)(2,1)S(1)} all-to-all(bf16[16,192,128]{2,1,0:T(8,128)(2,1)S(1)} %reshape.42), channel_id=1, replica_groups=mesh['row'=32,'col'=16] {'col'}, dimensions={0} | all-to-all | bytes 1572864 | tf_op jit(solution)/shard_map/all_to_all | solution.py:60
  53.1 60.5 %all_to_all.16 = bf16[32,96,128]{2,1,0:T(8,128)(2,1)S(1)} all-to-all(bf16[32,96,128]{2,1,0:T(8,128)(2,1)S(1)} %bitcast.184), channel_id=1, replica_groups=mesh['row'=32,'col'=16] {'row'}, dimensions={0} | all-to-all | bytes 1572864 | tf_op jit(solution)/shard_map/all_to_all | solution.py:63
  113.6 17.1 %all_to_all.17 = bf16[16,192,128]{2,1,0:T(8,128)(2,1)S(1)} all-to-all(bf16[16,192,128]{2,1,0:T(8,128)(2,1)S(1)} %bitcast.185), channel_id=1, replica_groups=mesh['row'=32,'col'=16] {'col'}, dimensions={0} | all-to-all | bytes 1572864 | tf_op jit(solution)/shard_map/all_to_all | solution.py:65
  131.4 1.6 copy.61
  133.0 1.5 reshape.47
  134.5 1.4 multiply_convert_fusion.1
  136.0 2.7 %collective-permute-start.4 = (bf16[48,16,128]{2,0,1:T(8,128)(2,1)S(1)}, bf16[48,16,128]{2,0,1:T(8,128)(2,1)S(1)}, u32[]{:S(2)}, u32[]{:S(2)}) collective-permute-start(bf16[48,16,128]{2,0,1:T(8,128)(2,1)S(1)} %get-tuple-element.17), channel_id=1, source_target_pairs={{0,16},{16,32},{32,48},{48,64},{64,80},{80,96},{96,112},{112,128},... | collective-permute-start | bytes 589832 | tf_op jit(solution)/shard_map/ppermute | solution.py:17
  138.6 4.1 %collective-permute-start.5 = (bf16[48,16,128]{2,0,1:T(8,128)(2,1)S(1)}, bf16[48,16,128]{2,0,1:T(8,128)(2,1)S(1)}, u32[]{:S(2)}, u32[]{:S(2)}) collective-permute-start(bf16[48,16,128]{2,0,1:T(8,128)(2,1)S(1)} %get-tuple-element.18), channel_id=1, source_target_pairs={{16,0},{32,16},{48,32},{64,48},{80,64},{96,80},{112,96},{128,112},... | collective-permute-start | bytes 589832 | tf_op jit(solution)/shard_map/ppermute | solution.py:18
  142.8 2.7 %collective-permute-done.4 = bf16[48,16,128]{2,0,1:T(8,128)(2,1)S(1)} collective-permute-done((bf16[48,16,128]{2,0,1:T(8,128)(2,1)S(1)}, bf16[48,16,128]{2,0,1:T(8,128)(2,1)S(1)}, u32[]{:S(2)}, u32[]{:S(2)}) %collective-permute-start.4) | collective-permute-done | bytes 196640 | tf_op jit(solution)/shard_map/ppermute | solution.py:17
  145.4 3.3 %collective-permute-done.5 = bf16[48,16,128]{2,0,1:T(8,128)(2,1)S(1)} collective-permute-done((bf16[48,16,128]{2,0,1:T(8,128)(2,1)S(1)}, bf16[48,16,128]{2,0,1:T(8,128)(2,1)S(1)}, u32[]{:S(2)}, u32[]{:S(2)}) %collective-permute-start.5) | collective-permute-done | bytes 196640 | tf_op jit(solution)/shard_map/ppermute | solution.py:18
  149.4 1.6 copy.62
  151.0 4.3 %collective-permute-start.6 = (bf16[48,96,16]{1,2,0:T(8,128)(2,1)}, bf16[48,96,16]{1,2,0:T(8,128)(2,1)S(1)}, u32[]{:S(2)}, u32[]{:S(2)}) collective-permute-start(bf16[48,96,16]{1,2,0:T(8,128)(2,1)} %copy.62), channel_id=1, source_target_pairs={{0,1},{1,2},{2,3},{3,4},{4,5},{5,6},{6,7},{7,8},{8,9},{9,10},{10,1... | collective-permute-start | bytes 442376 | tf_op jit(solution)/shard_map/ppermute | solution.py:17
  155.3 0.9 copy.63
  156.2 1.9 %collective-permute-start.7 = (bf16[48,96,16]{1,2,0:T(8,128)(2,1)S(1)}, bf16[48,96,16]{1,2,0:T(8,128)(2,1)}, u32[]{:S(2)}, u32[]{:S(2)}) collective-permute-start(bf16[48,96,16]{1,2,0:T(8,128)(2,1)S(1)} %copy.63), channel_id=1, source_target_pairs={{1,0},{2,1},{3,2},{4,3},{5,4},{6,5},{7,6},{8,7},{9,8},{10,9},{11,1... | collective-permute-start | bytes 442376 | tf_op jit(solution)/shard_map/ppermute | solution.py:18
  158.2 0.9 copy.64
  159.0 5.1 %collective-permute-done.7 = bf16[48,96,16]{1,2,0:T(8,128)(2,1)} collective-permute-done((bf16[48,96,16]{1,2,0:T(8,128)(2,1)S(1)}, bf16[48,96,16]{1,2,0:T(8,128)(2,1)}, u32[]{:S(2)}, u32[]{:S(2)}) %collective-permute-start.7) | collective-permute-done | bytes 147488 | tf_op jit(solution)/shard_map/ppermute | solution.py:18
  164.2 1.8 %copy.65 = bf16[48,96,16]{2,0,1:T(8,128)(2,1)S(1)} copy(bf16[48,96,16]{1,2,0:T(8,128)(2,1)} %collective-permute-done.7) | data formatting | bytes 294912 | tf_op jit(solution)/shard_map/ppermute | solution.py:18
  166.0 2.3 %maximum_maximum_fusion = bf16[48,96,160]{2,0,1:T(8,128)(2,1)S(1)} fusion(bf16[48,96,16]{2,0,1:T(8,128)(2,1)S(1)} %copy.65, bf16[48,16,128]{2,0,1:T(8,128)(2,1)S(1)} %collective-permute-done.5, bf16[48,64,128]{2,0,1:T(8,128)(2,1)S(1)} %multiply_convert_fusion.1, bf16[48,16,128]{2,0,1:T(8,128)(2,1)S(1)} %collective-permute-done.4, bf16[48,96,16]{2,0,1:T(8,128)(2,1)S(1)} %copy.64), kind=kLoop, calls=%fused_computation.4 | loop fusion | flops 8847360 | bytes 2949120 | tf_op jit(solution)/shard_map/max | solution.py:24
  171.2 1.4 fusion.2
  173.7 1.1 copy.68
  (58 shorter events, 14.6 us)
Async XLA Ops:
  0.0 10.5 %copy-start.2 = (bf16[48,64,128]{2,1,0:T(8,128)(2,1)S(1)}, bf16[48,64,128]{2,1,0:T(8,128)(2,1)}, u32[]{:S(2)}) copy-start(bf16[48,64,128]{2,1,0:T(8,128)(2,1)} %param.5) | copy-start | bytes 2359300
  1.1 9.4 %collective-permute-start = (bf16[48,8,128]{2,0,1:T(8,128)(2,1)S(1)}, bf16[48,8,128]{2,0,1:T(8,128)(2,1)S(1)}, u32[]{:S(2)}, u32[]{:S(2)}) collective-permute-start(bf16[48,8,128]{2,0,1:T(8,128)(2,1)S(1)} %copy.76), channel_id=1, source_target_pairs={{0,16},{16,32},{32,48},{48,64},{64,80},{80,96},{96,112},{112,128},... | collective-permute-start | bytes 294920 | tf_op jit(solution)/shard_map/ppermute | solution.py:17
  5.5 7.8 %collective-permute-start.1 = (bf16[48,8,128]{2,0,1:T(8,128)(2,1)S(1)}, bf16[48,8,128]{2,0,1:T(8,128)(2,1)S(1)}, u32[]{:S(2)}, u32[]{:S(2)}) collective-permute-start(bf16[48,8,128]{2,0,1:T(8,128)(2,1)S(1)} %copy.77), channel_id=1, source_target_pairs={{16,0},{32,16},{48,32},{64,48},{80,64},{96,80},{112,96},{128,112},... | collective-permute-start | bytes 294920 | tf_op jit(solution)/shard_map/ppermute | solution.py:18
  15.2 8.8 %collective-permute-start.3 = (bf16[48,80,8]{1,2,0:T(8,128)(2,1)S(1)}, bf16[48,80,8]{1,2,0:T(8,128)(2,1)S(1)}, u32[]{:S(2)}, u32[]{:S(2)}) collective-permute-start(bf16[48,80,8]{1,2,0:T(8,128)(2,1)S(1)} %copy.46), channel_id=1, source_target_pairs={{1,0},{2,1},{3,2},{4,3},{5,4},{6,5},{7,6},{8,7},{9,8},{10,9},{11,1... | collective-permute-start | bytes 184328 | tf_op jit(solution)/shard_map/ppermute | solution.py:18
  19.2 4.1 %collective-permute-start.2 = (bf16[48,80,8]{1,2,0:T(8,128)(2,1)S(1)}, bf16[48,80,8]{1,2,0:T(8,128)(2,1)S(1)}, u32[]{:S(2)}, u32[]{:S(2)}) collective-permute-start(bf16[48,80,8]{1,2,0:T(8,128)(2,1)S(1)} %copy.45), channel_id=1, source_target_pairs={{0,1},{1,2},{2,3},{3,4},{4,5},{5,6},{6,7},{7,8},{8,9},{9,10},{10,1... | collective-permute-start | bytes 184328 | tf_op jit(solution)/shard_map/ppermute | solution.py:17
  29.2 1.7 copy-start.3
  29.2 1.7 copy-start.5
  31.6 0.9 copy-start
  133.0 1.5 copy-start.1
  136.0 9.5 %collective-permute-start.4 = (bf16[48,16,128]{2,0,1:T(8,128)(2,1)S(1)}, bf16[48,16,128]{2,0,1:T(8,128)(2,1)S(1)}, u32[]{:S(2)}, u32[]{:S(2)}) collective-permute-start(bf16[48,16,128]{2,0,1:T(8,128)(2,1)S(1)} %get-tuple-element.17), channel_id=1, source_target_pairs={{0,16},{16,32},{32,48},{48,64},{64,80},{80,96},{96,112},{112,128},... | collective-permute-start | bytes 589832 | tf_op jit(solution)/shard_map/ppermute | solution.py:17
  138.6 10.2 %collective-permute-start.5 = (bf16[48,16,128]{2,0,1:T(8,128)(2,1)S(1)}, bf16[48,16,128]{2,0,1:T(8,128)(2,1)S(1)}, u32[]{:S(2)}, u32[]{:S(2)}) collective-permute-start(bf16[48,16,128]{2,0,1:T(8,128)(2,1)S(1)} %get-tuple-element.18), channel_id=1, source_target_pairs={{16,0},{32,16},{48,32},{64,48},{80,64},{96,80},{112,96},{128,112},... | collective-permute-start | bytes 589832 | tf_op jit(solution)/shard_map/ppermute | solution.py:18
  151.0 7.2 %collective-permute-start.6 = (bf16[48,96,16]{1,2,0:T(8,128)(2,1)}, bf16[48,96,16]{1,2,0:T(8,128)(2,1)S(1)}, u32[]{:S(2)}, u32[]{:S(2)}) collective-permute-start(bf16[48,96,16]{1,2,0:T(8,128)(2,1)} %copy.62), channel_id=1, source_target_pairs={{0,1},{1,2},{2,3},{3,4},{4,5},{5,6},{6,7},{7,8},{8,9},{9,10},{10,1... | collective-permute-start | bytes 442376 | tf_op jit(solution)/shard_map/ppermute | solution.py:17
  156.2 8.0 %collective-permute-start.7 = (bf16[48,96,16]{1,2,0:T(8,128)(2,1)S(1)}, bf16[48,96,16]{1,2,0:T(8,128)(2,1)}, u32[]{:S(2)}, u32[]{:S(2)}) collective-permute-start(bf16[48,96,16]{1,2,0:T(8,128)(2,1)S(1)} %copy.63), channel_id=1, source_target_pairs={{1,0},{2,1},{3,2},{4,3},{5,4},{6,5},{7,6},{8,7},{9,8},{10,9},{11,1... | collective-permute-start | bytes 442376 | tf_op jit(solution)/shard_map/ppermute | solution.py:18
  170.2 1.0 copy-start.4
  171.2 1.4 copy-start.6

commit v12 on v10

--- a/solution.py
+++ b/solution.py
@@ -1,6 +1,7 @@
 import jax
 import jax.numpy as jnp
 from jax import lax
+from jax.experimental.layout import Layout, with_layout_constraint
 from jax.sharding import PartitionSpec as P
 
 FIRST_DILATION = 8
@@ -95,7 +96,7 @@
     hidden = hidden_of(extended, both, gain, bias, SECOND_DILATION, tile_rows, tile_cols)
     direct = block_output(state, hidden[:count], norm_gain[1], norm_bias[1], w_pointwise[1])
     mirrored = block_output(state, hidden[count:], norm_gain[1], norm_bias[1], w_pointwise[1])
-    return mean_of(direct, mirrored)
+    return with_layout_constraint(mean_of(direct, mirrored), Layout(major_to_minor=(0, 1, 2)))
 
 
 def solution(mesh):

time: 176 us -> 182 us (1.034)
  matrix products: 4.82 us -> 7.3 us
  other arithmetic: 6.06 us -> 7.99 us
    dot_general x2, matrix products: 3.12 us -> 6.28 us  [hidden_of(): jnp.einsum('toc,tchw->ohw', kernel, stacked, preferred_element_type=jnp.f...]
    transpose x1, local copies, waits for them, and re-layouts: 1.62 us -> 3.96 us  [mirror_pieces(): t = jnp.transpose(t, (0, 2, 3, 4, 1, 5))]
    unnamed x38 -> x36, local copies, waits for them, and re-layouts: 6.84 us -> 7.71 us
  transfers between devices with their start and end apart: 8 -> 8, of which waited for: 4 -> 4; matrix products, arithmetic and copies ran while one was open for 6% -> 5% of each run, Pallas kernels for 0% -> 0%
where the time goes in v12:
time: 182 us; the launch traced here: 180 us
  blocking collectives  97.6 us (54%)
  local copies, waits for them, and re-layouts  31.1 us (17%)
  starting transfers between devices  26.5 us (15%)
  waiting for transfers between devices  9.51 us (5%)
  other arithmetic  7.99 us (4%)
  matrix products  7.3 us (4%)
    all_to_all x1, blocking collectives, mirror_pieces(): t = lax.all_to_all(t, 'row', 0, 0, tiled=True)  60.5 us
    all_to_all x2, blocking collectives, mirror_pieces(): t = lax.all_to_all(t, 'col', 0, 0, tiled=True)  37.1 us
    ppermute x4, starting transfers between devices, padded(): after = lax.ppermute(initial, axis, down)  14.7 us
    ppermute x4, starting transfers between devices, padded(): before = lax.ppermute(last, axis, up)  11.8 us
    unnamed x36, local copies, waits for them, and re-layouts  7.71 us
    dot_general x2, matrix products, hidden_of(): jnp.einsum('toc,tchw->ohw', kernel, stacked, preferred_element_type=jnp.f...  6.28 us
    ppermute x4, waiting for transfers between devices, padded(): after = lax.ppermute(initial, axis, down)  5.24 us
    ppermute x4, waiting for transfers between devices, padded(): before = lax.ppermute(last, axis, up)  4.26 us
  transfers between devices with their start and end apart: 8, of which 4 were waited for; matrix products, arithmetic and copies ran while one was open for 5% of the time, Pallas kernels for 0%

profile of v12, /device:TPU:7, one launch (start us, length us, event | category | flops | bytes accessed | tf_op | source)
XLA Modules:
  0.0 180.5 jit_solution(6198726237676057122)
XLA Ops:
  0.0 1.0 fusion.55
  1.0 4.4 %collective-permute-start = (bf16[48,8,128]{2,0,1:T(8,128)(2,1)S(1)}, bf16[48,8,128]{2,0,1:T(8,128)(2,1)S(1)}, u32[]{:S(2)}, u32[]{:S(2)}) collective-permute-start(bf16[48,8,128]{2,0,1:T(8,128)(2,1)S(1)} %copy.69), channel_id=1, source_target_pairs={{0,16},{16,32},{32,48},{48,64},{64,80},{80,96},{96,112},{112,128},... | collective-permute-start | bytes 294920 | tf_op jit(solution)/shard_map/ppermute | solution.py:18
  5.4 2.4 %collective-permute-start.1 = (bf16[48,8,128]{2,0,1:T(8,128)(2,1)S(1)}, bf16[48,8,128]{2,0,1:T(8,128)(2,1)S(1)}, u32[]{:S(2)}, u32[]{:S(2)}) collective-permute-start(bf16[48,8,128]{2,0,1:T(8,128)(2,1)S(1)} %copy.70), channel_id=1, source_target_pairs={{16,0},{32,16},{48,32},{64,48},{80,64},{96,80},{112,96},{128,112},... | collective-permute-start | bytes 294920 | tf_op jit(solution)/shard_map/ppermute | solution.py:19
  7.8 1.7 fusion.56
  9.5 1.7 constant_dynamic-update-slice_fusion.1
  11.2 2.0 %collective-permute-done.1 = bf16[48,8,128]{2,0,1:T(8,128)(2,1)S(1)} collective-permute-done((bf16[48,8,128]{2,0,1:T(8,128)(2,1)S(1)}, bf16[48,8,128]{2,0,1:T(8,128)(2,1)S(1)}, u32[]{:S(2)}, u32[]{:S(2)}) %collective-permute-start.1) | collective-permute-done | bytes 98336 | tf_op jit(solution)/shard_map/ppermute | solution.py:19
  13.6 0.8 copy.24
  14.4 0.8 copy.25
  15.2 4.0 %collective-permute-start.3 = (bf16[48,80,8]{1,2,0:T(8,128)(2,1)S(1)}, bf16[48,80,8]{1,2,0:T(8,128)(2,1)S(1)}, u32[]{:S(2)}, u32[]{:S(2)}) collective-permute-start(bf16[48,80,8]{1,2,0:T(8,128)(2,1)S(1)} %copy.25), channel_id=1, source_target_pairs={{1,0},{2,1},{3,2},{4,3},{5,4},{6,5},{7,6},{8,7},{9,8},{10,9},{11,1... | collective-permute-start | bytes 184328 | tf_op jit(solution)/shard_map/ppermute | solution.py:19
  19.2 2.5 %collective-permute-start.2 = (bf16[48,80,8]{1,2,0:T(8,128)(2,1)S(1)}, bf16[48,80,8]{1,2,0:T(8,128)(2,1)S(1)}, u32[]{:S(2)}, u32[]{:S(2)}) collective-permute-start(bf16[48,80,8]{1,2,0:T(8,128)(2,1)S(1)} %copy.24), channel_id=1, source_target_pairs={{0,1},{1,2},{2,3},{3,4},{4,5},{5,6},{6,7},{7,8},{8,9},{9,10},{10,1... | collective-permute-start | bytes 184328 | tf_op jit(solution)/shard_map/ppermute | solution.py:18
  21.7 1.6 collective-permute-done.2
  24.8 1.4 maximum_maximum_fusion.1
  29.1 1.7 fusion.19
  32.7 0.9 copy.37
  34.3 19.7 %all_to_all.15 = bf16[16,192,128]{2,1,0:T(8,128)(2,1)S(1)} all-to-all(bf16[16,192,128]{2,1,0:T(8,128)(2,1)S(1)} %reshape.42), channel_id=1, replica_groups=mesh['row'=32,'col'=16] {'col'}, dimensions={0} | all-to-all | bytes 1572864 | tf_op jit(solution)/shard_map/all_to_all | solution.py:61
  54.1 60.5 %all_to_all.16 = bf16[32,96,128]{2,1,0:T(8,128)(2,1)S(1)} all-to-all(bf16[32,96,128]{2,1,0:T(8,128)(2,1)S(1)} %bitcast.179), channel_id=1, replica_groups=mesh['row'=32,'col'=16] {'row'}, dimensions={0} | all-to-all | bytes 1572864 | tf_op jit(solution)/shard_map/all_to_all | solution.py:64
  114.6 17.3 %all_to_all.17 = bf16[16,192,128]{2,1,0:T(8,128)(2,1)S(1)} all-to-all(bf16[16,192,128]{2,1,0:T(8,128)(2,1)S(1)} %bitcast.180), channel_id=1, replica_groups=mesh['row'=32,'col'=16] {'col'}, dimensions={0} | all-to-all | bytes 1572864 | tf_op jit(solution)/shard_map/all_to_all | solution.py:66
  132.6 4.0 %copy.39 = bf16[16,3,32,2,2,64]{5,4,3,2,1,0:T(2,128)(2,1)} copy(bf16[16,3,32,2,2,64]{5,3,2,1,4,0:T(2,128)(2,1)S(1)} %bitcast.176) | data formatting | bytes 1572864 | tf_op jit(solution)/shard_map/transpose | solution.py:68
  136.6 3.1 %reshape.47 = bf16[48,64,128]{2,1,0:T(8,128)(2,1)S(1)} reshape(bf16[16,3,32,2,2,64]{5,4,3,2,1,0:T(2,128)(2,1)} %copy.39) | data formatting | bytes 1572864 | tf_op jit(solution)/shard_map/reshape | solution.py:69
  140.0 2.6 %collective-permute-start.4 = (bf16[48,16,128]{2,1,0:T(8,128)(2,1)S(1)}, bf16[48,16,128]{2,1,0:T(8,128)(2,1)S(1)}, u32[]{:S(2)}, u32[]{:S(2)}) collective-permute-start(bf16[48,16,128]{2,1,0:T(8,128)(2,1)S(1)} %get-tuple-element.9), channel_id=1, source_target_pairs={{0,16},{16,32},{32,48},{48,64},{64,80},{80,96},{96,112},{112,128},... | collective-permute-start | bytes 589832 | tf_op jit(solution)/shard_map/ppermute | solution.py:18
  142.6 4.2 %collective-permute-start.5 = (bf16[48,16,128]{2,1,0:T(8,128)(2,1)S(1)}, bf16[48,16,128]{2,1,0:T(8,128)(2,1)S(1)}, u32[]{:S(2)}, u32[]{:S(2)}) collective-permute-start(bf16[48,16,128]{2,1,0:T(8,128)(2,1)S(1)} %get-tuple-element.10), channel_id=1, source_target_pairs={{16,0},{32,16},{48,32},{64,48},{80,64},{96,80},{112,96},{128,112},... | collective-permute-start | bytes 589832 | tf_op jit(solution)/shard_map/ppermute | solution.py:19
  146.9 2.7 %collective-permute-done.4 = bf16[48,16,128]{2,1,0:T(8,128)(2,1)S(1)} collective-permute-done((bf16[48,16,128]{2,1,0:T(8,128)(2,1)S(1)}, bf16[48,16,128]{2,1,0:T(8,128)(2,1)S(1)}, u32[]{:S(2)}, u32[]{:S(2)}) %collective-permute-start.4) | collective-permute-done | bytes 196640 | tf_op jit(solution)/shard_map/ppermute | solution.py:18
  149.5 3.3 %collective-permute-done.5 = bf16[48,16,128]{2,1,0:T(8,128)(2,1)S(1)} collective-permute-done((bf16[48,16,128]{2,1,0:T(8,128)(2,1)S(1)}, bf16[48,16,128]{2,1,0:T(8,128)(2,1)S(1)}, u32[]{:S(2)}, u32[]{:S(2)}) %collective-permute-start.5) | collective-permute-done | bytes 196640 | tf_op jit(solution)/shard_map/ppermute | solution.py:19
  153.3 1.0 copy.42
  154.7 4.1 %collective-permute-start.7 = (bf16[48,96,16]{1,2,0:T(8,128)(2,1)S(1)}, bf16[48,96,16]{1,2,0:T(8,128)(2,1)}, u32[]{:S(2)}, u32[]{:S(2)}) collective-permute-start(bf16[48,96,16]{1,2,0:T(8,128)(2,1)S(1)} %copy.43), channel_id=1, source_target_pairs={{1,0},{2,1},{3,2},{4,3},{5,4},{6,5},{7,6},{8,7},{9,8},{10,9},{11,1... | collective-permute-start | bytes 442376 | tf_op jit(solution)/shard_map/ppermute | solution.py:19
  158.8 2.4 %collective-permute-start.6 = (bf16[48,96,16]{1,2,0:T(8,128)(2,1)}, bf16[48,96,16]{1,2,0:T(8,128)(2,1)S(1)}, u32[]{:S(2)}, u32[]{:S(2)}) collective-permute-start(bf16[48,96,16]{1,2,0:T(8,128)(2,1)} %copy.42), channel_id=1, source_target_pairs={{0,1},{1,2},{2,3},{3,4},{4,5},{5,6},{6,7},{7,8},{8,9},{9,10},{10,1... | collective-permute-start | bytes 442376 | tf_op jit(solution)/shard_map/ppermute | solution.py:18
  161.9 1.6 copy.40
  163.5 1.6 copy.41
  165.7 1.4 copy.45
  167.2 2.2 %maximum_maximum_fusion = bf16[48,96,160]{2,1,0:T(8,128)(2,1)S(1)} fusion(bf16[48,96,16]{2,1,0:T(8,128)(2,1)S(1)} %copy.45, bf16[48,16,128]{2,1,0:T(8,128)(2,1)S(1)} %collective-permute-done.5, bf16[48,64,128]{2,1,0:T(8,128)(2,1)S(1)} %multiply_convert_fusion.1, bf16[48,16,128]{2,1,0:T(8,128)(2,1)S(1)} %collective-permute-done.4, bf16[48,96,16]{2,1,0:T(8,128)(2,1)S(1)} %copy.44), kind=kLoop, calls=%fused_computation.6 | loop fusion | flops 8847360 | bytes 2949120 | tf_op jit(solution)/shard_map/max | solution.py:25
  172.6 4.6 %fusion.4 = bf16[96,64,128]{2,0,1:T(8,128)(2,1)S(1)} fusion(bf16[9,48,64,128]{3,2,1,0:T(8,128)(2,1)S(1)} %fusion.24, f32[96]{0:T(128)S(1)} %copy-done.7, f32[96]{0:T(128)S(1)} %pad_maximum_fusion.1, bf16[9,48,48]{1,2,0:T(8,128)(2,1)S(1)} %bitcast.183, bf16[9,48,48]{1,2,0:T(8,128)(2,1)S(1)} %bitcast.182), kind=kOutput, calls=%fused_computation.5 | convolution fusion | flops 682788864 | bytes 8734464 | tf_op jit(solution)/shard_map/toc,tchw->ohw/dot_general | solution.py:36
  177.9 2.6 %multiply_convert_fusion = bf16[48,64,128]{2,1,0:T(8,128)(2,1)} fusion(f32[64,128,48]{1,2,0:T(8,128)S(1)} %fusion.20, bf16[48,64,128]{2,1,0:T(8,128)(2,1)S(1)} %multiply_convert_fusion.1, f32[64,128,48]{1,2,0:T(8,128)S(1)} %fusion.22, f32[48]{0:T(128)S(1)} %get-tuple-element.20, f32[48]{0:T(128)S(1)} %get-tuple-element.27), kind=kLoop, calls=%fused_computation.27 | loop fusion | flops 6291456 | bytes 4718976 | tf_op jit(solution)/shard_map/convert_element_type | solution.py:73
  (61 shorter events, 14.3 us)
Async XLA Ops:
  1.0 8.5 %collective-permute-start = (bf16[48,8,128]{2,0,1:T(8,128)(2,1)S(1)}, bf16[48,8,128]{2,0,1:T(8,128)(2,1)S(1)}, u32[]{:S(2)}, u32[]{:S(2)}) collective-permute-start(bf16[48,8,128]{2,0,1:T(8,128)(2,1)S(1)} %copy.69), channel_id=1, source_target_pairs={{0,16},{16,32},{32,48},{48,64},{64,80},{80,96},{96,112},{112,128},... | collective-permute-start | bytes 294920 | tf_op jit(solution)/shard_map/ppermute | solution.py:18
  5.4 7.8 %collective-permute-start.1 = (bf16[48,8,128]{2,0,1:T(8,128)(2,1)S(1)}, bf16[48,8,128]{2,0,1:T(8,128)(2,1)S(1)}, u32[]{:S(2)}, u32[]{:S(2)}) collective-permute-start(bf16[48,8,128]{2,0,1:T(8,128)(2,1)S(1)} %copy.70), channel_id=1, source_target_pairs={{16,0},{32,16},{48,32},{64,48},{80,64},{96,80},{112,96},{128,112},... | collective-permute-start | bytes 294920 | tf_op jit(solution)/shard_map/ppermute | solution.py:19
  13.2 8.5 %copy-start.5 = (f32[2,2,48]{2,1,0:T(2,128)S(1)}, f32[2,2,48]{2,1,0:T(2,128)}, u32[]{:S(2)}) copy-start(f32[2,2,48]{2,1,0:T(2,128)} %param.9) | copy-start | bytes 2308
  13.2 8.5 %copy-start.6 = (f32[2,2,48]{2,1,0:T(2,128)S(1)}, f32[2,2,48]{2,1,0:T(2,128)}, u32[]{:S(2)}) copy-start(f32[2,2,48]{2,1,0:T(2,128)} %param.8) | copy-start | bytes 2308
  15.2 8.8 %collective-permute-start.3 = (bf16[48,80,8]{1,2,0:T(8,128)(2,1)S(1)}, bf16[48,80,8]{1,2,0:T(8,128)(2,1)S(1)}, u32[]{:S(2)}, u32[]{:S(2)}) collective-permute-start(bf16[48,80,8]{1,2,0:T(8,128)(2,1)S(1)} %copy.25), channel_id=1, source_target_pairs={{1,0},{2,1},{3,2},{4,3},{5,4},{6,5},{7,6},{8,7},{9,8},{10,9},{11,1... | collective-permute-start | bytes 184328 | tf_op jit(solution)/shard_map/ppermute | solution.py:19
  19.2 4.1 %collective-permute-start.2 = (bf16[48,80,8]{1,2,0:T(8,128)(2,1)S(1)}, bf16[48,80,8]{1,2,0:T(8,128)(2,1)S(1)}, u32[]{:S(2)}, u32[]{:S(2)}) collective-permute-start(bf16[48,80,8]{1,2,0:T(8,128)(2,1)S(1)} %copy.24), channel_id=1, source_target_pairs={{0,1},{1,2},{2,3},{3,4},{4,5},{5,6},{6,7},{7,8},{8,9},{9,10},{10,1... | collective-permute-start | bytes 184328 | tf_op jit(solution)/shard_map/ppermute | solution.py:18
  29.1 1.7 copy-start.3
  30.9 1.1 copy-start
  140.0 9.5 %collective-permute-start.4 = (bf16[48,16,128]{2,1,0:T(8,128)(2,1)S(1)}, bf16[48,16,128]{2,1,0:T(8,128)(2,1)S(1)}, u32[]{:S(2)}, u32[]{:S(2)}) collective-permute-start(bf16[48,16,128]{2,1,0:T(8,128)(2,1)S(1)} %get-tuple-element.9), channel_id=1, source_target_pairs={{0,16},{16,32},{32,48},{48,64},{64,80},{80,96},{96,112},{112,128},... | collective-permute-start | bytes 589832 | tf_op jit(solution)/shard_map/ppermute | solution.py:18
  142.6 10.2 %collective-permute-start.5 = (bf16[48,16,128]{2,1,0:T(8,128)(2,1)S(1)}, bf16[48,16,128]{2,1,0:T(8,128)(2,1)S(1)}, u32[]{:S(2)}, u32[]{:S(2)}) collective-permute-start(bf16[48,16,128]{2,1,0:T(8,128)(2,1)S(1)} %get-tuple-element.10), channel_id=1, source_target_pairs={{16,0},{32,16},{48,32},{64,48},{80,64},{96,80},{112,96},{128,112},... | collective-permute-start | bytes 589832 | tf_op jit(solution)/shard_map/ppermute | solution.py:19
  154.7 11.0 %collective-permute-start.7 = (bf16[48,96,16]{1,2,0:T(8,128)(2,1)S(1)}, bf16[48,96,16]{1,2,0:T(8,128)(2,1)}, u32[]{:S(2)}, u32[]{:S(2)}) collective-permute-start(bf16[48,96,16]{1,2,0:T(8,128)(2,1)S(1)} %copy.43), channel_id=1, source_target_pairs={{1,0},{2,1},{3,2},{4,3},{5,4},{6,5},{7,6},{8,7},{9,8},{10,9},{11,1... | collective-permute-start | bytes 442376 | tf_op jit(solution)/shard_map/ppermute | solution.py:19
  158.8 6.4 %collective-permute-start.6 = (bf16[48,96,16]{1,2,0:T(8,128)(2,1)}, bf16[48,96,16]{1,2,0:T(8,128)(2,1)S(1)}, u32[]{:S(2)}, u32[]{:S(2)}) collective-permute-start(bf16[48,96,16]{1,2,0:T(8,128)(2,1)} %copy.42), channel_id=1, source_target_pairs={{0,1},{1,2},{2,3},{3,4},{4,5},{5,6},{6,7},{7,8},{8,9},{9,10},{10,1... | collective-permute-start | bytes 442376 | tf_op jit(solution)/shard_map/ppermute | solution.py:18
  171.4 1.1 copy-start.1
  171.5 1.1 copy-start.2
  171.5 1.1 copy-start.7
  172.6 4.6 %copy-start.4 = (bf16[2,48,48]{2,1,0:T(8,128)(2,1)S(1)}, bf16[2,48,48]{2,1,0:T(8,128)(2,1)}, u32[]{:S(2)}) copy-start(bf16[2,48,48]{2,1,0:T(8,128)(2,1)} %param.7) | copy-start | bytes 27652

commit v13 on v10

--- a/solution.py
+++ b/solution.py
@@ -89,7 +89,7 @@
 
     kernel = w_dilated[1]
     both = jnp.concatenate([kernel, jnp.swapaxes(kernel, 0, 1)], axis=2).reshape(9, 2 * count, count)
-    extended = padded(state, (("row", 1), ("col", 2)), SECOND_DILATION)
+    extended = padded(state, (("col", 2), ("row", 1)), SECOND_DILATION)
     gain = jnp.concatenate([norm_gain[1, 0], norm_gain[1, 0]])
     bias = jnp.concatenate([norm_bias[1, 0], norm_bias[1, 0]])
     hidden = hidden_of(extended, both, gain, bias, SECOND_DILATION, tile_rows, tile_cols)

time: 176 us -> 181 us (1.028)
  waiting for transfers between devices: 9.01 us -> 23.9 us
  local copies, waits for them, and re-layouts: 29.8 us -> 22 us
    ppermute x4, waiting for transfers between devices: 3.7 us -> 16.3 us  [padded(): before = lax.ppermute(last, axis, up)]
    ppermute x4, waiting for transfers between devices: 5.32 us -> 7.54 us  [padded(): after = lax.ppermute(initial, axis, down)]
    slice x2, local copies, waits for them, and re-layouts: 3.32 us -> 1.12 us  [body(): kernel = w_dilated[1]]
    unnamed x38 -> x30, local copies, waits for them, and re-layouts: 6.84 us -> 6.78 us
  transfers between devices with their start and end apart: 8 -> 8, of which waited for: 4 -> 4; matrix products, arithmetic and copies ran while one was open for 6% -> 3% of each run, Pallas kernels for 0% -> 0%
where the time goes in v13:
time: 181 us; the launch traced here: 180 us
  blocking collectives  97.4 us (54%)
  starting transfers between devices  25.1 us (14%)
  waiting for transfers between devices  23.9 us (13%)
  local copies, waits for them, and re-layouts  22 us (12%)
  other arithmetic  6.73 us (4%)
  matrix products  4.75 us (3%)
    all_to_all x1, blocking collectives, mirror_pieces(): t = lax.all_to_all(t, 'row', 0, 0, tiled=True)  60.5 us
    all_to_all x2, blocking collectives, mirror_pieces(): t = lax.all_to_all(t, 'col', 0, 0, tiled=True)  36.9 us
    ppermute x4, waiting for transfers between devices, padded(): before = lax.ppermute(last, axis, up)  16.3 us
    ppermute x4, starting transfers between devices, padded(): after = lax.ppermute(initial, axis, down)  13.6 us
    ppermute x4, starting transfers between devices, padded(): before = lax.ppermute(last, axis, up)  11.4 us
    ppermute x4, waiting for transfers between devices, padded(): after = lax.ppermute(initial, axis, down)  7.54 us
    unnamed x30, local copies, waits for them, and re-layouts  6.78 us
    max x2, other arithmetic, hidden_of(): active = jnp.maximum(extended_input, jnp.zeros((), extended_input.dtype))  3.96 us
  transfers between devices with their start and end apart: 8, of which 4 were waited for; matrix products, arithmetic and copies ran while one was open for 3% of the time, Pallas kernels for 0%

profile of v13, /device:TPU:7, one launch (start us, length us, event | category | flops | bytes accessed | tf_op | source)
XLA Modules:
  0.0 180.3 jit_solution(5355316490560582971)
XLA Ops:
  0.0 1.0 fusion.49
  1.0 4.4 %collective-permute-start = (bf16[48,8,128]{2,0,1:T(8,128)(2,1)S(1)}, bf16[48,8,128]{2,0,1:T(8,128)(2,1)S(1)}, u32[]{:S(2)}, u32[]{:S(2)}) collective-permute-start(bf16[48,8,128]{2,0,1:T(8,128)(2,1)S(1)} %copy.50), channel_id=1, source_target_pairs={{0,16},{16,32},{32,48},{48,64},{64,80},{80,96},{96,112},{112,128},... | collective-permute-start | bytes 294920 | tf_op jit(solution)/shard_map/ppermute | solution.py:17
  5.4 2.4 %collective-permute-start.1 = (bf16[48,8,128]{2,0,1:T(8,128)(2,1)S(1)}, bf16[48,8,128]{2,0,1:T(8,128)(2,1)S(1)}, u32[]{:S(2)}, u32[]{:S(2)}) collective-permute-start(bf16[48,8,128]{2,0,1:T(8,128)(2,1)S(1)} %copy.51), channel_id=1, source_target_pairs={{16,0},{32,16},{48,32},{64,48},{80,64},{96,80},{112,96},{128,112},... | collective-permute-start | bytes 294920 | tf_op jit(solution)/shard_map/ppermute | solution.py:18
  7.8 1.0 fusion.50
  8.8 1.7 constant_dynamic-update-slice_fusion.1
  10.6 2.6 %collective-permute-done.1 = bf16[48,8,128]{2,0,1:T(8,128)(2,1)S(1)} collective-permute-done((bf16[48,8,128]{2,0,1:T(8,128)(2,1)S(1)}, bf16[48,8,128]{2,0,1:T(8,128)(2,1)S(1)}, u32[]{:S(2)}, u32[]{:S(2)}) %collective-permute-start.1) | collective-permute-done | bytes 98336 | tf_op jit(solution)/shard_map/ppermute | solution.py:18
  13.6 0.8 copy.23
  14.4 0.8 copy.24
  15.2 4.0 %collective-permute-start.3 = (bf16[48,80,8]{1,2,0:T(8,128)(2,1)S(1)}, bf16[48,80,8]{1,2,0:T(8,128)(2,1)S(1)}, u32[]{:S(2)}, u32[]{:S(2)}) collective-permute-start(bf16[48,80,8]{1,2,0:T(8,128)(2,1)S(1)} %copy.24), channel_id=1, source_target_pairs={{1,0},{2,1},{3,2},{4,3},{5,4},{6,5},{7,6},{8,7},{9,8},{10,9},{11,1... | collective-permute-start | bytes 184328 | tf_op jit(solution)/shard_map/ppermute | solution.py:18
  19.2 2.5 %collective-permute-start.2 = (bf16[48,80,8]{1,2,0:T(8,128)(2,1)S(1)}, bf16[48,80,8]{1,2,0:T(8,128)(2,1)S(1)}, u32[]{:S(2)}, u32[]{:S(2)}) collective-permute-start(bf16[48,80,8]{1,2,0:T(8,128)(2,1)S(1)} %copy.23), channel_id=1, source_target_pairs={{0,1},{1,2},{2,3},{3,4},{4,5},{5,6},{6,7},{7,8},{8,9},{9,10},{10,1... | collective-permute-start | bytes 184328 | tf_op jit(solution)/shard_map/ppermute | solution.py:17
  21.7 1.6 collective-permute-done.2
  24.0 0.7 copy.26
  24.8 1.4 maximum_maximum_fusion.1
  29.1 1.6 fusion.15
  31.5 0.9 copy.35
  32.4 0.8 reshape.42
  33.2 19.7 %all_to_all.15 = bf16[16,192,128]{2,1,0:T(8,128)(2,1)S(1)} all-to-all(bf16[16,192,128]{2,1,0:T(8,128)(2,1)S(1)} %reshape.42), channel_id=1, replica_groups=mesh['row'=32,'col'=16] {'col'}, dimensions={0} | all-to-all | bytes 1572864 | tf_op jit(solution)/shard_map/all_to_all | solution.py:60
  53.0 60.5 %all_to_all.16 = bf16[32,96,128]{2,1,0:T(8,128)(2,1)S(1)} all-to-all(bf16[32,96,128]{2,1,0:T(8,128)(2,1)S(1)} %bitcast.184), channel_id=1, replica_groups=mesh['row'=32,'col'=16] {'row'}, dimensions={0} | all-to-all | bytes 1572864 | tf_op jit(solution)/shard_map/all_to_all | solution.py:63
  113.5 17.1 %all_to_all.17 = bf16[16,192,128]{2,1,0:T(8,128)(2,1)S(1)} all-to-all(bf16[16,192,128]{2,1,0:T(8,128)(2,1)S(1)} %bitcast.185), channel_id=1, replica_groups=mesh['row'=32,'col'=16] {'col'}, dimensions={0} | all-to-all | bytes 1572864 | tf_op jit(solution)/shard_map/all_to_all | solution.py:65
  131.4 1.6 copy.37
  133.0 0.8 reshape.47
  133.8 1.4 multiply_convert_fusion.1
  136.2 2.0 %collective-permute-start.4 = (bf16[48,64,16]{1,2,0:T(8,128)(2,1)S(1)}, bf16[48,64,16]{1,2,0:T(8,128)(2,1)S(1)}, u32[]{:S(2)}, u32[]{:S(2)}) collective-permute-start(bf16[48,64,16]{1,2,0:T(8,128)(2,1)S(1)} %copy.40), channel_id=1, source_target_pairs={{0,1},{1,2},{2,3},{3,4},{4,5},{5,6},{6,7},{7,8},{8,9},{9,10},{10,1... | collective-permute-start | bytes 294920 | tf_op jit(solution)/shard_map/ppermute | solution.py:17
  138.8 2.3 %collective-permute-start.5 = (bf16[48,64,16]{1,2,0:T(8,128)(2,1)S(1)}, bf16[48,64,16]{1,2,0:T(8,128)(2,1)S(1)}, u32[]{:S(2)}, u32[]{:S(2)}) collective-permute-start(bf16[48,64,16]{1,2,0:T(8,128)(2,1)S(1)} %copy.41), channel_id=1, source_target_pairs={{1,0},{2,1},{3,2},{4,3},{5,4},{6,5},{7,6},{8,7},{9,8},{10,9},{11,1... | collective-permute-start | bytes 294920 | tf_op jit(solution)/shard_map/ppermute | solution.py:18
  141.8 4.9 %collective-permute-done.5 = bf16[48,64,16]{1,2,0:T(8,128)(2,1)S(1)} collective-permute-done((bf16[48,64,16]{1,2,0:T(8,128)(2,1)S(1)}, bf16[48,64,16]{1,2,0:T(8,128)(2,1)S(1)}, u32[]{:S(2)}, u32[]{:S(2)}) %collective-permute-start.5) | collective-permute-done | bytes 98336 | tf_op jit(solution)/shard_map/ppermute | solution.py:18
  147.3 1.2 pad_maximum_fusion.2
  148.5 2.6 %collective-permute-start.6 = (bf16[48,16,160]{2,0,1:T(8,128)(2,1)}, bf16[48,16,160]{2,0,1:T(8,128)(2,1)}, u32[]{:S(2)}, u32[]{:S(2)}) collective-permute-start(bf16[48,16,160]{2,0,1:T(8,128)(2,1)} %get-tuple-element.5), channel_id=1, source_target_pairs={{0,16},{16,32},{32,48},{48,64},{64,80},{80,96},{96,112},{112,128},... | collective-permute-start | bytes 737288 | tf_op jit(solution)/shard_map/ppermute | solution.py:17
  151.1 4.9 %collective-permute-start.7 = (bf16[48,16,160]{2,0,1:T(8,128)(2,1)S(1)}, bf16[48,16,160]{2,0,1:T(8,128)(2,1)}, u32[]{:S(2)}, u32[]{:S(2)}) collective-permute-start(bf16[48,16,160]{2,0,1:T(8,128)(2,1)S(1)} %get-tuple-element.6), channel_id=1, source_target_pairs={{16,0},{32,16},{48,32},{64,48},{80,64},{96,80},{112,96},{128,112},... | collective-permute-start | bytes 737288 | tf_op jit(solution)/shard_map/ppermute | solution.py:18
  156.4 14.7 %collective-permute-done.6 = bf16[48,16,160]{2,0,1:T(8,128)(2,1)} collective-permute-done((bf16[48,16,160]{2,0,1:T(8,128)(2,1)}, bf16[48,16,160]{2,0,1:T(8,128)(2,1)}, u32[]{:S(2)}, u32[]{:S(2)}) %collective-permute-start.6) | collective-permute-done | bytes 245792 | tf_op jit(solution)/shard_map/ppermute | solution.py:17
  171.2 2.6 %maximum_maximum_fusion = bf16[48,96,160]{2,0,1:T(8,128)(2,1)S(1)} fusion(bf16[48,16,160]{2,0,1:T(8,128)(2,1)} %collective-permute-done.7, bf16[48,64,16]{2,0,1:T(8,128)(2,1)S(1)} %copy.43, bf16[48,64,128]{2,0,1:T(8,128)(2,1)S(1)} %multiply_convert_fusion.1, bf16[48,64,16]{2,0,1:T(8,128)(2,1)S(1)} %copy.42, bf16[48,16,160]{2,0,1:T(8,128)(2,1)} %collective-permute-done.6), kind=kLoop, calls=%fused_computation.4 | loop fusion | flops 8847360 | bytes 2949120 | tf_op jit(solution)/shard_map/max | solution.py:24
  176.7 1.4 fusion.2
  179.2 1.1 copy.45
  (53 shorter events, 12.7 us)
Async XLA Ops:
  1.0 7.8 %collective-permute-start = (bf16[48,8,128]{2,0,1:T(8,128)(2,1)S(1)}, bf16[48,8,128]{2,0,1:T(8,128)(2,1)S(1)}, u32[]{:S(2)}, u32[]{:S(2)}) collective-permute-start(bf16[48,8,128]{2,0,1:T(8,128)(2,1)S(1)} %copy.50), channel_id=1, source_target_pairs={{0,16},{16,32},{32,48},{48,64},{64,80},{80,96},{96,112},{112,128},... | collective-permute-start | bytes 294920 | tf_op jit(solution)/shard_map/ppermute | solution.py:17
  5.4 7.8 %collective-permute-start.1 = (bf16[48,8,128]{2,0,1:T(8,128)(2,1)S(1)}, bf16[48,8,128]{2,0,1:T(8,128)(2,1)S(1)}, u32[]{:S(2)}, u32[]{:S(2)}) collective-permute-start(bf16[48,8,128]{2,0,1:T(8,128)(2,1)S(1)} %copy.51), channel_id=1, source_target_pairs={{16,0},{32,16},{48,32},{64,48},{80,64},{96,80},{112,96},{128,112},... | collective-permute-start | bytes 294920 | tf_op jit(solution)/shard_map/ppermute | solution.py:18
  10.5 11.1 %copy-start.2 = (f32[2,2,48]{2,1,0:T(2,128)S(1)}, f32[2,2,48]{2,1,0:T(2,128)}, u32[]{:S(2)}) copy-start(f32[2,2,48]{2,1,0:T(2,128)} %param.9) | copy-start | bytes 2308
  10.5 11.1 %copy-start.3 = (f32[2,2,48]{2,1,0:T(2,128)S(1)}, f32[2,2,48]{2,1,0:T(2,128)}, u32[]{:S(2)}) copy-start(f32[2,2,48]{2,1,0:T(2,128)} %param.8) | copy-start | bytes 2308
  15.2 8.8 %collective-permute-start.3 = (bf16[48,80,8]{1,2,0:T(8,128)(2,1)S(1)}, bf16[48,80,8]{1,2,0:T(8,128)(2,1)S(1)}, u32[]{:S(2)}, u32[]{:S(2)}) collective-permute-start(bf16[48,80,8]{1,2,0:T(8,128)(2,1)S(1)} %copy.24), channel_id=1, source_target_pairs={{1,0},{2,1},{3,2},{4,3},{5,4},{6,5},{7,6},{8,7},{9,8},{10,9},{11,1... | collective-permute-start | bytes 184328 | tf_op jit(solution)/shard_map/ppermute | solution.py:18
  19.2 4.1 %collective-permute-start.2 = (bf16[48,80,8]{1,2,0:T(8,128)(2,1)S(1)}, bf16[48,80,8]{1,2,0:T(8,128)(2,1)S(1)}, u32[]{:S(2)}, u32[]{:S(2)}) collective-permute-start(bf16[48,80,8]{1,2,0:T(8,128)(2,1)S(1)} %copy.23), channel_id=1, source_target_pairs={{0,1},{1,2},{2,3},{3,4},{4,5},{5,6},{6,7},{7,8},{8,9},{9,10},{10,1... | collective-permute-start | bytes 184328 | tf_op jit(solution)/shard_map/ppermute | solution.py:17
  29.1 1.7 copy-start.1
  29.1 1.7 copy-start.4
  31.5 0.9 copy-start
  136.2 5.0 %collective-permute-start.4 = (bf16[48,64,16]{1,2,0:T(8,128)(2,1)S(1)}, bf16[48,64,16]{1,2,0:T(8,128)(2,1)S(1)}, u32[]{:S(2)}, u32[]{:S(2)}) collective-permute-start(bf16[48,64,16]{1,2,0:T(8,128)(2,1)S(1)} %copy.40), channel_id=1, source_target_pairs={{0,1},{1,2},{2,3},{3,4},{4,5},{5,6},{6,7},{7,8},{8,9},{9,10},{10,1... | collective-permute-start | bytes 294920 | tf_op jit(solution)/shard_map/ppermute | solution.py:17
  138.8 7.9 %collective-permute-start.5 = (bf16[48,64,16]{1,2,0:T(8,128)(2,1)S(1)}, bf16[48,64,16]{1,2,0:T(8,128)(2,1)S(1)}, u32[]{:S(2)}, u32[]{:S(2)}) collective-permute-start(bf16[48,64,16]{1,2,0:T(8,128)(2,1)S(1)} %copy.41), channel_id=1, source_target_pairs={{1,0},{2,1},{3,2},{4,3},{5,4},{6,5},{7,6},{8,7},{9,8},{10,9},{11,1... | collective-permute-start | bytes 294920 | tf_op jit(solution)/shard_map/ppermute | solution.py:18
  148.5 22.7 %collective-permute-start.6 = (bf16[48,16,160]{2,0,1:T(8,128)(2,1)}, bf16[48,16,160]{2,0,1:T(8,128)(2,1)}, u32[]{:S(2)}, u32[]{:S(2)}) collective-permute-start(bf16[48,16,160]{2,0,1:T(8,128)(2,1)} %get-tuple-element.5), channel_id=1, source_target_pairs={{0,16},{16,32},{32,48},{48,64},{64,80},{80,96},{96,112},{112,128},... | collective-permute-start | bytes 737288 | tf_op jit(solution)/shard_map/ppermute | solution.py:17
  151.1 20.1 %collective-permute-start.7 = (bf16[48,16,160]{2,0,1:T(8,128)(2,1)S(1)}, bf16[48,16,160]{2,0,1:T(8,128)(2,1)}, u32[]{:S(2)}, u32[]{:S(2)}) collective-permute-start(bf16[48,16,160]{2,0,1:T(8,128)(2,1)S(1)} %get-tuple-element.6), channel_id=1, source_target_pairs={{16,0},{32,16},{48,32},{64,48},{80,64},{96,80},{112,96},{128,112},... | collective-permute-start | bytes 737288 | tf_op jit(solution)/shard_map/ppermute | solution.py:18

commit v14 on v13

--- a/solution.py
+++ b/solution.py
@@ -72,8 +72,12 @@
     return ((a.astype(jnp.float32) + b.astype(jnp.float32)) * 0.5).astype(jnp.bfloat16)
 
 
-def symmetrized(output_map):
-    return mean_of(output_map, lax.optimization_barrier(mirror_pieces(output_map)))
+def symmetrized(output_map, width):
+    mirrored = lax.optimization_barrier(mirror_pieces(output_map))
+    rows = output_map.shape[1]
+    head = mean_of(output_map[:, :width], mirrored[:, :width])
+    tail = mean_of(output_map[:, rows - width:], mirrored[:, rows - width:])
+    return mean_of(output_map, mirrored), head, tail
 
 
 def body(features, w_dilated, w_pointwise, norm_gain, norm_bias):
@@ -85,11 +89,15 @@
     )
     hidden = lax.optimization_barrier(hidden)
     output_map = block_output(features, hidden, norm_gain[0], norm_bias[0], w_pointwise[0])
-    state = symmetrized(output_map)
+    state, head, tail = symmetrized(output_map, SECOND_DILATION)
 
     kernel = w_dilated[1]
     both = jnp.concatenate([kernel, jnp.swapaxes(kernel, 0, 1)], axis=2).reshape(9, 2 * count, count)
-    extended = padded(state, (("col", 2), ("row", 1)), SECOND_DILATION)
+    n_row = lax.axis_size("row")
+    up = [(i, i + 1) for i in range(n_row - 1)]
+    down = [(j, i) for i, j in up]
+    rows = jnp.concatenate([lax.ppermute(tail, "row", up), state, lax.ppermute(head, "row", down)], axis=1)
+    extended = padded(rows, (("col", 2),), SECOND_DILATION)
     gain = jnp.concatenate([norm_gain[1, 0], norm_gain[1, 0]])
     bias = jnp.concatenate([norm_bias[1, 0], norm_bias[1, 0]])
     hidden = hidden_of(extended, both, gain, bias, SECOND_DILATION, tile_rows, tile_cols)

time: 181 us -> 174 us (0.961)
  waiting for transfers between devices: 23.9 us -> 7.61 us
  local copies, waits for them, and re-layouts: 22 us -> 29.4 us
    ppermute x4 -> x3, waiting for transfers between devices: 16.3 us -> 1.02 us  [padded(): before = lax.ppermute(last, axis, up)]
    ppermute x0 -> x2, starting transfers between devices: none -> 6.79 us  [the longest x1 4.14 us: body(): lax.ppermute(head, 'row', down)]
    ppermute x4 -> x3, waiting for transfers between devices: 7.54 us -> 1.97 us  [padded(): after = lax.ppermute(initial, axis, down)]
    ppermute x0 -> x2, waiting for transfers between devices: none -> 4.62 us  [the longest x1 3.35 us: body(): lax.ppermute(head, 'row', down)]
    ppermute x4 -> x3, starting transfers between devices: 13.6 us -> 10.4 us  [padded(): after = lax.ppermute(initial, axis, down)]
    slice x2, local copies, waits for them, and re-layouts: 1.12 us -> 3.32 us  [body(): kernel = w_dilated[1]]
    ppermute x4 -> x3, starting transfers between devices: 11.4 us -> 9.31 us  [padded(): before = lax.ppermute(last, axis, up)]
    unnamed x30 -> x40, local copies, waits for them, and re-layouts: 6.78 us -> 7.23 us
  transfers between devices with their start and end apart: 8 -> 8, of which waited for: 4 -> 4; matrix products, arithmetic and copies ran while one was open for 3% -> 6% of each run, Pallas kernels for 0% -> 0%
where the time goes in v14:
time: 174 us; the launch traced here: 172 us
  blocking collectives  97.4 us (56%)
  local copies, waits for them, and re-layouts  29.4 us (17%)
  starting transfers between devices  26.5 us (15%)
  waiting for transfers between devices  7.61 us (4%)
  other arithmetic  6.19 us (4%)
  matrix products  4.82 us (3%)
    all_to_all x1, blocking collectives, mirror_pieces(): t = lax.all_to_all(t, 'row', 0, 0, tiled=True)  60.5 us
    all_to_all x2, blocking collectives, mirror_pieces(): t = lax.all_to_all(t, 'col', 0, 0, tiled=True)  36.9 us
    ppermute x3, starting transfers between devices, padded(): after = lax.ppermute(initial, axis, down)  10.4 us
    ppermute x3, starting transfers between devices, padded(): before = lax.ppermute(last, axis, up)  9.31 us
    unnamed x40, local copies, waits for them, and re-layouts  7.23 us
    ppermute x1, starting transfers between devices, body(): lax.ppermute(head, 'row', down)  4.14 us
    max x2, other arithmetic, hidden_of(): active = jnp.maximum(extended_input, jnp.zeros((), extended_input.dtype))  3.64 us
  transfers between devices with their start and end apart: 8, of which 4 were waited for; matrix products, arithmetic and copies ran while one was open for 6% of the time, Pallas kernels for 0%

profile of v14, /device:TPU:7, one launch (start us, length us, event | category | flops | bytes accessed | tf_op | source)
XLA Modules:
  0.0 172.4 jit_solution(1069747140960928465)
XLA Ops:
  0.0 1.0 fusion.49
  1.0 4.4 %collective-permute-start = (bf16[48,8,128]{2,0,1:T(8,128)(2,1)S(1)}, bf16[48,8,128]{2,0,1:T(8,128)(2,1)S(1)}, u32[]{:S(2)}, u32[]{:S(2)}) collective-permute-start(bf16[48,8,128]{2,0,1:T(8,128)(2,1)S(1)} %copy.50), channel_id=1, source_target_pairs={{0,16},{16,32},{32,48},{48,64},{64,80},{80,96},{96,112},{112,128},... | collective-permute-start | bytes 294920 | tf_op jit(solution)/shard_map/ppermute | solution.py:17
  5.4 2.4 %collective-permute-start.1 = (bf16[48,8,128]{2,0,1:T(8,128)(2,1)S(1)}, bf16[48,8,128]{2,0,1:T(8,128)(2,1)S(1)}, u32[]{:S(2)}, u32[]{:S(2)}) collective-permute-start(bf16[48,8,128]{2,0,1:T(8,128)(2,1)S(1)} %copy.51), channel_id=1, source_target_pairs={{16,0},{32,16},{48,32},{64,48},{80,64},{96,80},{112,96},{128,112},... | collective-permute-start | bytes 294920 | tf_op jit(solution)/shard_map/ppermute | solution.py:18
  7.8 1.7 fusion.50
  9.5 1.7 constant_dynamic-update-slice_fusion.1
  11.2 2.0 %collective-permute-done.1 = bf16[48,8,128]{2,0,1:T(8,128)(2,1)S(1)} collective-permute-done((bf16[48,8,128]{2,0,1:T(8,128)(2,1)S(1)}, bf16[48,8,128]{2,0,1:T(8,128)(2,1)S(1)}, u32[]{:S(2)}, u32[]{:S(2)}) %collective-permute-start.1) | collective-permute-done | bytes 98336 | tf_op jit(solution)/shard_map/ppermute | solution.py:18
  15.2 4.0 %collective-permute-start.3 = (bf16[48,80,8]{1,2,0:T(8,128)(2,1)S(1)}, bf16[48,80,8]{1,2,0:T(8,128)(2,1)S(1)}, u32[]{:S(2)}, u32[]{:S(2)}) collective-permute-start(bf16[48,80,8]{1,2,0:T(8,128)(2,1)S(1)} %copy.24), channel_id=1, source_target_pairs={{1,0},{2,1},{3,2},{4,3},{5,4},{6,5},{7,6},{8,7},{9,8},{10,9},{11,1... | collective-permute-start | bytes 184328 | tf_op jit(solution)/shard_map/ppermute | solution.py:18
  19.2 2.5 %collective-permute-start.2 = (bf16[48,80,8]{1,2,0:T(8,128)(2,1)S(1)}, bf16[48,80,8]{1,2,0:T(8,128)(2,1)S(1)}, u32[]{:S(2)}, u32[]{:S(2)}) collective-permute-start(bf16[48,80,8]{1,2,0:T(8,128)(2,1)S(1)} %copy.23), channel_id=1, source_target_pairs={{0,1},{1,2},{2,3},{3,4},{4,5},{5,6},{6,7},{7,8},{8,9},{9,10},{10,1... | collective-permute-start | bytes 184328 | tf_op jit(solution)/shard_map/ppermute | solution.py:17
  22.3 1.0 collective-permute-done.2
  24.8 1.4 maximum_maximum_fusion.1
  29.2 1.7 fusion.15
  31.6 0.9 copy.35
  33.2 19.7 %all_to_all.15 = bf16[16,192,128]{2,1,0:T(8,128)(2,1)S(1)} all-to-all(bf16[16,192,128]{2,1,0:T(8,128)(2,1)S(1)} %reshape.42), channel_id=1, replica_groups=mesh['row'=32,'col'=16] {'col'}, dimensions={0} | all-to-all | bytes 1572864 | tf_op jit(solution)/shard_map/all_to_all | solution.py:60
  53.0 60.5 %all_to_all.16 = bf16[32,96,128]{2,1,0:T(8,128)(2,1)S(1)} all-to-all(bf16[32,96,128]{2,1,0:T(8,128)(2,1)S(1)} %bitcast.184), channel_id=1, replica_groups=mesh['row'=32,'col'=16] {'row'}, dimensions={0} | all-to-all | bytes 1572864 | tf_op jit(solution)/shard_map/all_to_all | solution.py:63
  113.5 17.1 %all_to_all.17 = bf16[16,192,128]{2,1,0:T(8,128)(2,1)S(1)} all-to-all(bf16[16,192,128]{2,1,0:T(8,128)(2,1)S(1)} %bitcast.185), channel_id=1, replica_groups=mesh['row'=32,'col'=16] {'col'}, dimensions={0} | all-to-all | bytes 1572864 | tf_op jit(solution)/shard_map/all_to_all | solution.py:65
  131.4 1.6 copy.37
  134.3 2.7 %collective-permute-start.4 = (bf16[48,16,128]{2,0,1:T(8,128)(2,1)S(1)}, bf16[48,16,128]{2,0,1:T(8,128)(2,1)S(1)}, u32[]{:S(2)}, u32[]{:S(2)}) collective-permute-start(bf16[48,16,128]{2,0,1:T(8,128)(2,1)S(1)} %get-tuple-element.5), channel_id=1, source_target_pairs={{0,16},{16,32},{32,48},{48,64},{64,80},{80,96},{96,112},{112,128},... | collective-permute-start | bytes 589832 | tf_op jit(solution)/shard_map/ppermute | solution.py:99
  136.9 4.1 %collective-permute-start.5 = (bf16[48,16,128]{2,0,1:T(8,128)(2,1)S(1)}, bf16[48,16,128]{2,0,1:T(8,128)(2,1)S(1)}, u32[]{:S(2)}, u32[]{:S(2)}) collective-permute-start(bf16[48,16,128]{2,0,1:T(8,128)(2,1)S(1)} %get-tuple-element.6), channel_id=1, source_target_pairs={{16,0},{32,16},{48,32},{64,48},{80,64},{96,80},{112,96},{128,112},... | collective-permute-start | bytes 589832 | tf_op jit(solution)/shard_map/ppermute | solution.py:99
  141.1 1.4 multiply_convert_fusion.1
  142.5 1.3 collective-permute-done.4
  143.7 3.3 %collective-permute-done.5 = bf16[48,16,128]{2,0,1:T(8,128)(2,1)S(1)} collective-permute-done((bf16[48,16,128]{2,0,1:T(8,128)(2,1)S(1)}, bf16[48,16,128]{2,0,1:T(8,128)(2,1)S(1)}, u32[]{:S(2)}, u32[]{:S(2)}) %collective-permute-start.5) | collective-permute-done | bytes 196640 | tf_op jit(solution)/shard_map/ppermute | solution.py:99
  147.7 1.6 copy.40
  149.3 0.9 copy.41
  150.2 4.0 %collective-permute-start.7 = (bf16[48,96,16]{1,2,0:T(8,128)(2,1)S(1)}, bf16[48,96,16]{1,2,0:T(8,128)(2,1)}, u32[]{:S(2)}, u32[]{:S(2)}) collective-permute-start(bf16[48,96,16]{1,2,0:T(8,128)(2,1)S(1)} %copy.41), channel_id=1, source_target_pairs={{1,0},{2,1},{3,2},{4,3},{5,4},{6,5},{7,6},{8,7},{9,8},{10,9},{11,1... | collective-permute-start | bytes 442376 | tf_op jit(solution)/shard_map/ppermute | solution.py:18
  154.2 2.5 %collective-permute-start.6 = (bf16[48,96,16]{1,2,0:T(8,128)(2,1)}, bf16[48,96,16]{1,2,0:T(8,128)(2,1)S(1)}, u32[]{:S(2)}, u32[]{:S(2)}) collective-permute-start(bf16[48,96,16]{1,2,0:T(8,128)(2,1)} %copy.40), channel_id=1, source_target_pairs={{0,1},{1,2},{2,3},{3,4},{4,5},{5,6},{6,7},{7,8},{8,9},{9,10},{10,1... | collective-permute-start | bytes 442376 | tf_op jit(solution)/shard_map/ppermute | solution.py:17
  156.7 1.6 copy.38
  158.4 1.6 copy.39
  160.8 0.9 copy.42
  161.7 1.8 %copy.43 = bf16[48,96,16]{2,0,1:T(8,128)(2,1)S(1)} copy(bf16[48,96,16]{1,2,0:T(8,128)(2,1)} %collective-permute-done.7) | data formatting | bytes 294912 | tf_op jit(solution)/shard_map/ppermute | solution.py:18
  163.5 2.3 %maximum_maximum_fusion = bf16[48,96,160]{2,0,1:T(8,128)(2,1)S(1)} fusion(bf16[48,96,16]{2,0,1:T(8,128)(2,1)S(1)} %copy.43, bf16[48,16,128]{2,0,1:T(8,128)(2,1)S(1)} %collective-permute-done.5, bf16[48,64,128]{2,0,1:T(8,128)(2,1)S(1)} %multiply_convert_fusion.1, bf16[48,16,128]{2,0,1:T(8,128)(2,1)S(1)} %collective-permute-done.4, bf16[48,96,16]{2,0,1:T(8,128)(2,1)S(1)} %copy.42), kind=kLoop, calls=%fused_computation.4 | loop fusion | flops 8847360 | bytes 2949120 | tf_op jit(solution)/shard_map/max | solution.py:24
  168.8 1.4 fusion.2
  171.3 1.1 copy.45
  (64 shorter events, 15.9 us)
Async XLA Ops:
  1.0 8.5 %collective-permute-start = (bf16[48,8,128]{2,0,1:T(8,128)(2,1)S(1)}, bf16[48,8,128]{2,0,1:T(8,128)(2,1)S(1)}, u32[]{:S(2)}, u32[]{:S(2)}) collective-permute-start(bf16[48,8,128]{2,0,1:T(8,128)(2,1)S(1)} %copy.50), channel_id=1, source_target_pairs={{0,16},{16,32},{32,48},{48,64},{64,80},{80,96},{96,112},{112,128},... | collective-permute-start | bytes 294920 | tf_op jit(solution)/shard_map/ppermute | solution.py:17
  5.4 7.8 %collective-permute-start.1 = (bf16[48,8,128]{2,0,1:T(8,128)(2,1)S(1)}, bf16[48,8,128]{2,0,1:T(8,128)(2,1)S(1)}, u32[]{:S(2)}, u32[]{:S(2)}) collective-permute-start(bf16[48,8,128]{2,0,1:T(8,128)(2,1)S(1)} %copy.51), channel_id=1, source_target_pairs={{16,0},{32,16},{48,32},{64,48},{80,64},{96,80},{112,96},{128,112},... | collective-permute-start | bytes 294920 | tf_op jit(solution)/shard_map/ppermute | solution.py:18
  13.2 8.5 %copy-start.6 = (f32[2,2,48]{2,1,0:T(2,128)S(1)}, f32[2,2,48]{2,1,0:T(2,128)}, u32[]{:S(2)}) copy-start(f32[2,2,48]{2,1,0:T(2,128)} %param.9) | copy-start | bytes 2308
  13.2 8.5 %copy-start.7 = (f32[2,2,48]{2,1,0:T(2,128)S(1)}, f32[2,2,48]{2,1,0:T(2,128)}, u32[]{:S(2)}) copy-start(f32[2,2,48]{2,1,0:T(2,128)} %param.8) | copy-start | bytes 2308
  15.2 8.8 %collective-permute-start.3 = (bf16[48,80,8]{1,2,0:T(8,128)(2,1)S(1)}, bf16[48,80,8]{1,2,0:T(8,128)(2,1)S(1)}, u32[]{:S(2)}, u32[]{:S(2)}) collective-permute-start(bf16[48,80,8]{1,2,0:T(8,128)(2,1)S(1)} %copy.24), channel_id=1, source_target_pairs={{1,0},{2,1},{3,2},{4,3},{5,4},{6,5},{7,6},{8,7},{9,8},{10,9},{11,1... | collective-permute-start | bytes 184328 | tf_op jit(solution)/shard_map/ppermute | solution.py:18
  19.2 4.1 %collective-permute-start.2 = (bf16[48,80,8]{1,2,0:T(8,128)(2,1)S(1)}, bf16[48,80,8]{1,2,0:T(8,128)(2,1)S(1)}, u32[]{:S(2)}, u32[]{:S(2)}) collective-permute-start(bf16[48,80,8]{1,2,0:T(8,128)(2,1)S(1)} %copy.23), channel_id=1, source_target_pairs={{0,1},{1,2},{2,3},{3,4},{4,5},{5,6},{6,7},{7,8},{8,9},{9,10},{10,1... | collective-permute-start | bytes 184328 | tf_op jit(solution)/shard_map/ppermute | solution.py:17
  29.1 1.7 %copy-start.3 = (bf16[48,64,128]{2,1,0:T(8,128)(2,1)S(1)}, bf16[48,64,128]{2,1,0:T(8,128)(2,1)}, u32[]{:S(2)}) copy-start(bf16[48,64,128]{2,1,0:T(8,128)(2,1)} %param.5) | copy-start | bytes 2359300
  29.1 1.7 %copy-start.8 = (bf16[2,48,48]{2,1,0:T(8,128)(2,1)S(1)}, bf16[2,48,48]{2,1,0:T(8,128)(2,1)}, u32[]{:S(2)}) copy-start(bf16[2,48,48]{2,1,0:T(8,128)(2,1)} %param.7) | copy-start | bytes 27652
  31.6 1.7 copy-start
  133.0 1.1 copy-start.1
  134.1 2.8 %copy-start.2 = (bf16[48,64,128]{2,0,1:T(8,128)(2,1)}, bf16[48,64,128]{2,0,1:T(8,128)(2,1)S(1)}, u32[]{:S(2)}) copy-start(bf16[48,64,128]{2,0,1:T(8,128)(2,1)S(1)} %reshape.47) | copy-start | bytes 2359300
  134.3 9.5 %collective-permute-start.4 = (bf16[48,16,128]{2,0,1:T(8,128)(2,1)S(1)}, bf16[48,16,128]{2,0,1:T(8,128)(2,1)S(1)}, u32[]{:S(2)}, u32[]{:S(2)}) collective-permute-start(bf16[48,16,128]{2,0,1:T(8,128)(2,1)S(1)} %get-tuple-element.5), channel_id=1, source_target_pairs={{0,16},{16,32},{32,48},{48,64},{64,80},{80,96},{96,112},{112,128},... | collective-permute-start | bytes 589832 | tf_op jit(solution)/shard_map/ppermute | solution.py:99
  136.9 10.2 %collective-permute-start.5 = (bf16[48,16,128]{2,0,1:T(8,128)(2,1)S(1)}, bf16[48,16,128]{2,0,1:T(8,128)(2,1)S(1)}, u32[]{:S(2)}, u32[]{:S(2)}) collective-permute-start(bf16[48,16,128]{2,0,1:T(8,128)(2,1)S(1)} %get-tuple-element.6), channel_id=1, source_target_pairs={{16,0},{32,16},{48,32},{64,48},{80,64},{96,80},{112,96},{128,112},... | collective-permute-start | bytes 589832 | tf_op jit(solution)/shard_map/ppermute | solution.py:99
  150.2 11.5 %collective-permute-start.7 = (bf16[48,96,16]{1,2,0:T(8,128)(2,1)S(1)}, bf16[48,96,16]{1,2,0:T(8,128)(2,1)}, u32[]{:S(2)}, u32[]{:S(2)}) collective-permute-start(bf16[48,96,16]{1,2,0:T(8,128)(2,1)S(1)} %copy.41), channel_id=1, source_target_pairs={{1,0},{2,1},{3,2},{4,3},{5,4},{6,5},{7,6},{8,7},{9,8},{10,9},{11,1... | collective-permute-start | bytes 442376 | tf_op jit(solution)/shard_map/ppermute | solution.py:18
  154.2 6.6 %collective-permute-start.6 = (bf16[48,96,16]{1,2,0:T(8,128)(2,1)}, bf16[48,96,16]{1,2,0:T(8,128)(2,1)S(1)}, u32[]{:S(2)}, u32[]{:S(2)}) collective-permute-start(bf16[48,96,16]{1,2,0:T(8,128)(2,1)} %copy.40), channel_id=1, source_target_pairs={{0,1},{1,2},{2,3},{3,4},{4,5},{5,6},{6,7},{7,8},{8,9},{9,10},{10,1... | collective-permute-start | bytes 442376 | tf_op jit(solution)/shard_map/ppermute | solution.py:17
  167.8 1.0 copy-start.4
  167.8 1.0 copy-start.5
  168.8 1.4 copy-start.9

commit v15 on v14

--- a/solution.py
+++ b/solution.py
@@ -96,8 +96,21 @@
     n_row = lax.axis_size("row")
     up = [(i, i + 1) for i in range(n_row - 1)]
     down = [(j, i) for i, j in up]
-    rows = jnp.concatenate([lax.ppermute(tail, "row", up), state, lax.ppermute(head, "row", down)], axis=1)
-    extended = padded(rows, (("col", 2),), SECOND_DILATION)
+    above, below = lax.ppermute(tail, "row", up), lax.ppermute(head, "row", down)
+    width = SECOND_DILATION
+    n_col = lax.axis_size("col")
+    right_of = [(i, i + 1) for i in range(n_col - 1)]
+    left_of = [(j, i) for i, j in right_of]
+
+    def columns(part):
+        return jnp.concatenate([part(above), part(state), part(below)], axis=1)
+
+    last = columns(lambda v: v[:, :, tile_cols - width:])
+    initial = columns(lambda v: v[:, :, :width])
+    before = lax.ppermute(last, "col", right_of)
+    after = lax.ppermute(initial, "col", left_of)
+    rows = jnp.concatenate([above, state, below], axis=1)
+    extended = jnp.concatenate([before, rows, after], axis=2)
     gain = jnp.concatenate([norm_gain[1, 0], norm_gain[1, 0]])
     bias = jnp.concatenate([norm_bias[1, 0], norm_bias[1, 0]])
     hidden = hidden_of(extended, both, gain, bias, SECOND_DILATION, tile_rows, tile_cols)

time: 174 us -> 174 us (level)
    ppermute x0 -> x2, starting transfers between devices: none -> 6.46 us  [the longest x1 3.47 us: body(): after = lax.ppermute(initial, 'col', left_of)]
    ppermute x3 -> x2, starting transfers between devices: 10.4 us -> 6.41 us  [padded(): after = lax.ppermute(initial, axis, down)]
    slice x0 -> x9, local copies, waits for them, and re-layouts: none -> 2.76 us  [the longest x6 1.65 us: body(): last = columns(lambda v: v[:, :, tile_cols - width:])]
    ppermute x0 -> x2, local copies, waits for them, and re-layouts: none -> 2.66 us  [the longest x1 1.79 us: body(): after = lax.ppermute(initial, 'col', left_of)]
    ppermute x3 -> x2, starting transfers between devices: 9.31 us -> 6.86 us  [padded(): before = lax.ppermute(last, axis, up)]
    slice x4 -> x2, local copies, waits for them, and re-layouts: 3.18 us -> 1.14 us  [padded(): last = lax.slice_in_dim(value, length - width, length, axis=dim)]
    ppermute x2 -> x1, local copies, waits for them, and re-layouts: 2.52 us -> 0.73 us  [padded(): after = lax.ppermute(initial, axis, down)]
    unnamed x40 -> x46, local copies, waits for them, and re-layouts: 7.23 us -> 7.73 us
where the time goes in v15:
time: 174 us; the launch traced here: 171 us
  blocking collectives  97.4 us (56%)
  local copies, waits for them, and re-layouts  27.9 us (16%)
  starting transfers between devices  26.5 us (15%)
  waiting for transfers between devices  8.34 us (5%)
  other arithmetic  5.69 us (3%)
  matrix products  4.82 us (3%)
    all_to_all x1, blocking collectives, mirror_pieces(): t = lax.all_to_all(t, 'row', 0, 0, tiled=True)  60.5 us
    all_to_all x2, blocking collectives, mirror_pieces(): t = lax.all_to_all(t, 'col', 0, 0, tiled=True)  36.9 us
    unnamed x46, local copies, waits for them, and re-layouts  7.73 us
    ppermute x2, starting transfers between devices, padded(): before = lax.ppermute(last, axis, up)  6.86 us
    ppermute x2, starting transfers between devices, padded(): after = lax.ppermute(initial, axis, down)  6.41 us
    ppermute x1, waiting for transfers between devices, body(): lax.ppermute(head, 'row', down)  4.42 us
    ppermute x1, starting transfers between devices, body(): lax.ppermute(head, 'row', down)  4.14 us
    max x2, other arithmetic, hidden_of(): active = jnp.maximum(extended_input, jnp.zeros((), extended_input.dtype))  3.63 us
  transfers between devices with their start and end apart: 8, of which 4 were waited for; matrix products, arithmetic and copies ran while one was open for 6% of the time, Pallas kernels for 0%

profile of v15, /device:TPU:7, one launch (start us, length us, event | category | flops | bytes accessed | tf_op | source)
XLA Modules:
  0.0 171.2 jit_solution(8221024753205898536)
XLA Ops:
  0.0 1.0 fusion.49
  1.0 4.4 %collective-permute-start = (bf16[48,8,128]{2,0,1:T(8,128)(2,1)S(1)}, bf16[48,8,128]{2,0,1:T(8,128)(2,1)S(1)}, u32[]{:S(2)}, u32[]{:S(2)}) collective-permute-start(bf16[48,8,128]{2,0,1:T(8,128)(2,1)S(1)} %copy.54), channel_id=1, source_target_pairs={{0,16},{16,32},{32,48},{48,64},{64,80},{80,96},{96,112},{112,128},... | collective-permute-start | bytes 294920 | tf_op jit(solution)/shard_map/ppermute | solution.py:17
  5.4 2.4 %collective-permute-start.1 = (bf16[48,8,128]{2,0,1:T(8,128)(2,1)S(1)}, bf16[48,8,128]{2,0,1:T(8,128)(2,1)S(1)}, u32[]{:S(2)}, u32[]{:S(2)}) collective-permute-start(bf16[48,8,128]{2,0,1:T(8,128)(2,1)S(1)} %copy.55), channel_id=1, source_target_pairs={{16,0},{32,16},{48,32},{64,48},{80,64},{96,80},{112,96},{128,112},... | collective-permute-start | bytes 294920 | tf_op jit(solution)/shard_map/ppermute | solution.py:18
  7.8 1.7 fusion.50
  9.5 1.7 constant_dynamic-update-slice_fusion.1
  11.2 2.0 %collective-permute-done.1 = bf16[48,8,128]{2,0,1:T(8,128)(2,1)S(1)} collective-permute-done((bf16[48,8,128]{2,0,1:T(8,128)(2,1)S(1)}, bf16[48,8,128]{2,0,1:T(8,128)(2,1)S(1)}, u32[]{:S(2)}, u32[]{:S(2)}) %collective-permute-start.1) | collective-permute-done | bytes 98336 | tf_op jit(solution)/shard_map/ppermute | solution.py:18
  13.6 0.8 copy.23
  14.4 0.8 copy.24
  15.1 4.0 %collective-permute-start.3 = (bf16[48,80,8]{1,2,0:T(8,128)(2,1)S(1)}, bf16[48,80,8]{1,2,0:T(8,128)(2,1)S(1)}, u32[]{:S(2)}, u32[]{:S(2)}) collective-permute-start(bf16[48,80,8]{1,2,0:T(8,128)(2,1)S(1)} %copy.24), channel_id=1, source_target_pairs={{1,0},{2,1},{3,2},{4,3},{5,4},{6,5},{7,6},{8,7},{9,8},{10,9},{11,1... | collective-permute-start | bytes 184328 | tf_op jit(solution)/shard_map/ppermute | solution.py:18
  19.1 2.5 %collective-permute-start.2 = (bf16[48,80,8]{1,2,0:T(8,128)(2,1)S(1)}, bf16[48,80,8]{1,2,0:T(8,128)(2,1)S(1)}, u32[]{:S(2)}, u32[]{:S(2)}) collective-permute-start(bf16[48,80,8]{1,2,0:T(8,128)(2,1)S(1)} %copy.23), channel_id=1, source_target_pairs={{0,1},{1,2},{2,3},{3,4},{4,5},{5,6},{6,7},{7,8},{8,9},{9,10},{10,1... | collective-permute-start | bytes 184328 | tf_op jit(solution)/shard_map/ppermute | solution.py:17
  22.2 1.0 collective-permute-done.2
  24.7 1.4 maximum_maximum_fusion.1
  29.1 1.7 fusion.15
  31.5 0.9 copy.35
  33.2 19.7 %all_to_all.15 = bf16[16,192,128]{2,1,0:T(8,128)(2,1)S(1)} all-to-all(bf16[16,192,128]{2,1,0:T(8,128)(2,1)S(1)} %reshape.42), channel_id=1, replica_groups=mesh['row'=32,'col'=16] {'col'}, dimensions={0} | all-to-all | bytes 1572864 | tf_op jit(solution)/shard_map/all_to_all | solution.py:60
  53.0 60.5 %all_to_all.16 = bf16[32,96,128]{2,1,0:T(8,128)(2,1)S(1)} all-to-all(bf16[32,96,128]{2,1,0:T(8,128)(2,1)S(1)} %bitcast.184), channel_id=1, replica_groups=mesh['row'=32,'col'=16] {'row'}, dimensions={0} | all-to-all | bytes 1572864 | tf_op jit(solution)/shard_map/all_to_all | solution.py:63
  113.5 17.1 %all_to_all.17 = bf16[16,192,128]{2,1,0:T(8,128)(2,1)S(1)} all-to-all(bf16[16,192,128]{2,1,0:T(8,128)(2,1)S(1)} %bitcast.185), channel_id=1, replica_groups=mesh['row'=32,'col'=16] {'col'}, dimensions={0} | all-to-all | bytes 1572864 | tf_op jit(solution)/shard_map/all_to_all | solution.py:65
  131.3 1.6 copy.37
  133.7 0.9 copy-done.2
  134.7 1.4 multiply_convert_fusion.1
  136.1 2.7 %collective-permute-start.4 = (bf16[48,16,128]{2,0,1:T(8,128)(2,1)S(1)}, bf16[48,16,128]{2,0,1:T(8,128)(2,1)S(1)}, u32[]{:S(2)}, u32[]{:S(2)}) collective-permute-start(bf16[48,16,128]{2,0,1:T(8,128)(2,1)S(1)} %get-tuple-element.5), channel_id=1, source_target_pairs={{0,16},{16,32},{32,48},{48,64},{64,80},{80,96},{96,112},{112,128},... | collective-permute-start | bytes 589832 | tf_op jit(solution)/shard_map/ppermute | solution.py:99
  138.8 4.1 %collective-permute-start.5 = (bf16[48,16,128]{2,0,1:T(8,128)(2,1)S(1)}, bf16[48,16,128]{2,0,1:T(8,128)(2,1)S(1)}, u32[]{:S(2)}, u32[]{:S(2)}) collective-permute-start(bf16[48,16,128]{2,0,1:T(8,128)(2,1)S(1)} %get-tuple-element.6), channel_id=1, source_target_pairs={{16,0},{32,16},{48,32},{64,48},{80,64},{96,80},{112,96},{128,112},... | collective-permute-start | bytes 589832 | tf_op jit(solution)/shard_map/ppermute | solution.py:99
  144.5 4.4 %collective-permute-done.5 = bf16[48,16,128]{2,0,1:T(8,128)(2,1)S(1)} collective-permute-done((bf16[48,16,128]{2,0,1:T(8,128)(2,1)S(1)}, bf16[48,16,128]{2,0,1:T(8,128)(2,1)S(1)}, u32[]{:S(2)}, u32[]{:S(2)}) %collective-permute-start.5) | collective-permute-done | bytes 196640 | tf_op jit(solution)/shard_map/ppermute | solution.py:99
  150.3 3.5 %collective-permute-start.7 = (bf16[48,96,16]{1,2,0:T(8,128)(2,1)S(1)}, bf16[48,96,16]{1,2,0:T(8,128)(2,1)}, u32[]{:S(2)}, u32[]{:S(2)}) collective-permute-start(bf16[48,96,16]{1,2,0:T(8,128)(2,1)S(1)} %pad_maximum_fusion.1), channel_id=1, source_target_pairs={{1,0},{2,1},{3,2},{4,3},{5,4},{6,5},{7,6},{8,7},{9,8},{10,9},{11,1... | collective-permute-start | bytes 442376 | tf_op jit(solution)/shard_map/ppermute | solution.py:111
  154.0 3.0 %collective-permute-start.6 = (bf16[48,96,16]{1,2,0:T(8,128)(2,1)S(1)}, bf16[48,96,16]{1,2,0:T(8,128)(2,1)S(1)}, u32[]{:S(2)}, u32[]{:S(2)}) collective-permute-start(bf16[48,96,16]{1,2,0:T(8,128)(2,1)S(1)} %pad_maximum_fusion), channel_id=1, source_target_pairs={{0,1},{1,2},{2,3},{3,4},{4,5},{5,6},{6,7},{7,8},{8,9},{9,10},{10,1... | collective-permute-start | bytes 442376 | tf_op jit(solution)/shard_map/ppermute | solution.py:110
  157.9 0.8 copy.39
  158.7 0.9 collective-permute-done.6
  159.6 0.9 copy.46
  160.5 1.8 %copy.47 = bf16[48,96,16]{2,0,1:T(8,128)(2,1)S(1)} copy(bf16[48,96,16]{1,2,0:T(8,128)(2,1)} %collective-permute-done.7) | data formatting | bytes 294912 | tf_op jit(solution)/shard_map/ppermute | solution.py:111
  162.3 2.3 %maximum_maximum_fusion = bf16[48,96,160]{2,0,1:T(8,128)(2,1)S(1)} fusion(bf16[48,96,16]{2,0,1:T(8,128)(2,1)S(1)} %copy.47, bf16[48,16,128]{2,0,1:T(8,128)(2,1)S(1)} %collective-permute-done.5, bf16[48,64,128]{2,0,1:T(8,128)(2,1)S(1)} %multiply_convert_fusion.1, bf16[48,16,128]{2,0,1:T(8,128)(2,1)S(1)} %collective-permute-done.4, bf16[48,96,16]{2,0,1:T(8,128)(2,1)S(1)} %copy.46), kind=kLoop, calls=%fused_computation.4 | loop fusion | flops 8847360 | bytes 2949120 | tf_op jit(solution)/shard_map/max | solution.py:24
  167.6 1.4 fusion.2
  170.1 1.1 copy.49
  (77 shorter events, 16.5 us)
Async XLA Ops:
  1.0 8.5 %collective-permute-start = (bf16[48,8,128]{2,0,1:T(8,128)(2,1)S(1)}, bf16[48,8,128]{2,0,1:T(8,128)(2,1)S(1)}, u32[]{:S(2)}, u32[]{:S(2)}) collective-permute-start(bf16[48,8,128]{2,0,1:T(8,128)(2,1)S(1)} %copy.54), channel_id=1, source_target_pairs={{0,16},{16,32},{32,48},{48,64},{64,80},{80,96},{96,112},{112,128},... | collective-permute-start | bytes 294920 | tf_op jit(solution)/shard_map/ppermute | solution.py:17
  5.4 7.8 %collective-permute-start.1 = (bf16[48,8,128]{2,0,1:T(8,128)(2,1)S(1)}, bf16[48,8,128]{2,0,1:T(8,128)(2,1)S(1)}, u32[]{:S(2)}, u32[]{:S(2)}) collective-permute-start(bf16[48,8,128]{2,0,1:T(8,128)(2,1)S(1)} %copy.55), channel_id=1, source_target_pairs={{16,0},{32,16},{48,32},{64,48},{80,64},{96,80},{112,96},{128,112},... | collective-permute-start | bytes 294920 | tf_op jit(solution)/shard_map/ppermute | solution.py:18
  13.2 8.4 %copy-start.8 = (f32[2,2,48]{2,1,0:T(2,128)S(1)}, f32[2,2,48]{2,1,0:T(2,128)}, u32[]{:S(2)}) copy-start(f32[2,2,48]{2,1,0:T(2,128)} %param.9) | copy-start | bytes 2308
  13.2 8.4 %copy-start.9 = (f32[2,2,48]{2,1,0:T(2,128)S(1)}, f32[2,2,48]{2,1,0:T(2,128)}, u32[]{:S(2)}) copy-start(f32[2,2,48]{2,1,0:T(2,128)} %param.8) | copy-start | bytes 2308
  15.1 8.8 %collective-permute-start.3 = (bf16[48,80,8]{1,2,0:T(8,128)(2,1)S(1)}, bf16[48,80,8]{1,2,0:T(8,128)(2,1)S(1)}, u32[]{:S(2)}, u32[]{:S(2)}) collective-permute-start(bf16[48,80,8]{1,2,0:T(8,128)(2,1)S(1)} %copy.24), channel_id=1, source_target_pairs={{1,0},{2,1},{3,2},{4,3},{5,4},{6,5},{7,6},{8,7},{9,8},{10,9},{11,1... | collective-permute-start | bytes 184328 | tf_op jit(solution)/shard_map/ppermute | solution.py:18
  19.1 4.1 %collective-permute-start.2 = (bf16[48,80,8]{1,2,0:T(8,128)(2,1)S(1)}, bf16[48,80,8]{1,2,0:T(8,128)(2,1)S(1)}, u32[]{:S(2)}, u32[]{:S(2)}) collective-permute-start(bf16[48,80,8]{1,2,0:T(8,128)(2,1)S(1)} %copy.23), channel_id=1, source_target_pairs={{0,1},{1,2},{2,3},{3,4},{4,5},{5,6},{6,7},{7,8},{8,9},{9,10},{10,1... | collective-permute-start | bytes 184328 | tf_op jit(solution)/shard_map/ppermute | solution.py:17
  29.1 1.7 %copy-start.3 = (bf16[48,64,128]{2,1,0:T(8,128)(2,1)S(1)}, bf16[48,64,128]{2,1,0:T(8,128)(2,1)}, u32[]{:S(2)}) copy-start(bf16[48,64,128]{2,1,0:T(8,128)(2,1)} %param.5) | copy-start | bytes 2359300
  29.1 1.7 %copy-start.11 = (bf16[2,48,48]{2,1,0:T(8,128)(2,1)S(1)}, bf16[2,48,48]{2,1,0:T(8,128)(2,1)}, u32[]{:S(2)}) copy-start(bf16[2,48,48]{2,1,0:T(8,128)(2,1)} %param.7) | copy-start | bytes 27652
  31.5 1.7 copy-start
  132.9 1.6 copy-start.1
  133.7 0.9 copy-start.2
  136.1 13.4 %collective-permute-start.4 = (bf16[48,16,128]{2,0,1:T(8,128)(2,1)S(1)}, bf16[48,16,128]{2,0,1:T(8,128)(2,1)S(1)}, u32[]{:S(2)}, u32[]{:S(2)}) collective-permute-start(bf16[48,16,128]{2,0,1:T(8,128)(2,1)S(1)} %get-tuple-element.5), channel_id=1, source_target_pairs={{0,16},{16,32},{32,48},{48,64},{64,80},{80,96},{96,112},{112,128},... | collective-permute-start | bytes 589832 | tf_op jit(solution)/shard_map/ppermute | solution.py:99
  138.8 10.2 %collective-permute-start.5 = (bf16[48,16,128]{2,0,1:T(8,128)(2,1)S(1)}, bf16[48,16,128]{2,0,1:T(8,128)(2,1)S(1)}, u32[]{:S(2)}, u32[]{:S(2)}) collective-permute-start(bf16[48,16,128]{2,0,1:T(8,128)(2,1)S(1)} %get-tuple-element.6), channel_id=1, source_target_pairs={{16,0},{32,16},{48,32},{64,48},{80,64},{96,80},{112,96},{128,112},... | collective-permute-start | bytes 589832 | tf_op jit(solution)/shard_map/ppermute | solution.py:99
  144.5 12.6 %copy-start.5 = (bf16[1,3,3,48,48]{4,3,2,1,0:T(8,128)(2,1)S(1)}, bf16[1,3,3,48,48]{4,3,2,1,0:T(8,128)(2,1)}, u32[]{:S(2)}) copy-start(bf16[1,3,3,48,48]{4,3,2,1,0:T(8,128)(2,1)} %get-tuple-element.13) | copy-start | bytes 124420
  144.5 13.4 %copy-start.4 = (bf16[3,3,48,48]{3,2,0,1:T(8,128)(2,1)S(1)}, bf16[3,3,48,48]{3,2,0,1:T(8,128)(2,1)}, u32[]{:S(2)}) copy-start(bf16[3,3,48,48]{3,2,0,1:T(8,128)(2,1)} %get-tuple-element.14) | copy-start | bytes 124420
  149.1 9.6 %copy-start.10 = (f32[48]{0:T(128)S(1)}, f32[48]{0:T(128)}, u32[]{:S(2)}) copy-start(f32[48]{0:T(128)} %get-tuple-element.28) | copy-start | bytes 580
  150.3 10.2 %collective-permute-start.7 = (bf16[48,96,16]{1,2,0:T(8,128)(2,1)S(1)}, bf16[48,96,16]{1,2,0:T(8,128)(2,1)}, u32[]{:S(2)}, u32[]{:S(2)}) collective-permute-start(bf16[48,96,16]{1,2,0:T(8,128)(2,1)S(1)} %pad_maximum_fusion.1), channel_id=1, source_target_pairs={{1,0},{2,1},{3,2},{4,3},{5,4},{6,5},{7,6},{8,7},{9,8},{10,9},{11,1... | collective-permute-start | bytes 442376 | tf_op jit(solution)/shard_map/ppermute | solution.py:111
  154.0 5.6 %collective-permute-start.6 = (bf16[48,96,16]{1,2,0:T(8,128)(2,1)S(1)}, bf16[48,96,16]{1,2,0:T(8,128)(2,1)S(1)}, u32[]{:S(2)}, u32[]{:S(2)}) collective-permute-start(bf16[48,96,16]{1,2,0:T(8,128)(2,1)S(1)} %pad_maximum_fusion), channel_id=1, source_target_pairs={{0,1},{1,2},{2,3},{3,4},{4,5},{5,6},{6,7},{7,8},{8,9},{9,10},{10,1... | collective-permute-start | bytes 442376 | tf_op jit(solution)/shard_map/ppermute | solution.py:110
  166.5 1.0 copy-start.6
  166.5 1.0 copy-start.7
  167.6 1.5 copy-start.12

commit v16 on v15

--- a/solution.py
+++ b/solution.py
@@ -83,7 +83,24 @@
 def body(features, w_dilated, w_pointwise, norm_gain, norm_bias):
     count, tile_rows, tile_cols = features.shape
     kernel = w_dilated[0].reshape(9, count, count)
-    extended = padded(features, (("row", 1), ("col", 2)), FIRST_DILATION)
+    n_row = lax.axis_size("row")
+    n_col = lax.axis_size("col")
+    down_rows = [(i, i + 1) for i in range(n_row - 1)]
+    up_rows = [(j, i) for i, j in down_rows]
+    width = FIRST_DILATION
+    above = lax.ppermute(features[:, tile_rows - width:], "row", down_rows)
+    below = lax.ppermute(features[:, :width], "row", up_rows)
+
+    def columns(part):
+        return jnp.concatenate([part(above), part(features), part(below)], axis=1)
+
+    right_of = [(i, i + 1) for i in range(n_col - 1)]
+    left_of = [(j, i) for i, j in right_of]
+    before = lax.ppermute(columns(lambda v: v[:, :, tile_cols - width:]), "col", right_of)
+    after = lax.ppermute(columns(lambda v: v[:, :, :width]), "col", left_of)
+    extended = jnp.concatenate(
+        [before, jnp.concatenate([above, features, below], axis=1), after], axis=2
+    )
     hidden = hidden_of(
         extended, kernel, norm_gain[0, 0], norm_bias[0, 0], FIRST_DILATION, tile_rows, tile_cols
     )

time: 174 us -> 175 us (level)
    unnamed x46 -> x47, local copies, waits for them, and re-layouts: 7.73 us -> 8.25 us
where the time goes in v16:
time: 175 us; the launch traced here: 172 us
  blocking collectives  97.4 us (56%)
  local copies, waits for them, and re-layouts  27.1 us (15%)
  starting transfers between devices  26.7 us (15%)
  waiting for transfers between devices  8.53 us (5%)
  other arithmetic  6.96 us (4%)
  matrix products  4.82 us (3%)
    all_to_all x1, blocking collectives, mirror_pieces(): t = lax.all_to_all(t, 'row', 0, 0, tiled=True)  60.5 us
    all_to_all x2, blocking collectives, mirror_pieces(): t = lax.all_to_all(t, 'col', 0, 0, tiled=True)  36.9 us
    unnamed x47, local copies, waits for them, and re-layouts  8.25 us
    ppermute x1, waiting for transfers between devices, body(): lax.ppermute(head, 'row', down)  4.42 us
    ppermute x1, starting transfers between devices, body(): above = lax.ppermute(features[:, tile_rows - width:], 'row', down_rows)  4.39 us
    ppermute x1, starting transfers between devices, body(): lax.ppermute(head, 'row', down)  4.14 us
    ppermute x1, starting transfers between devices, body(): after = lax.ppermute(columns(lambda v: v[:, :, :width]), 'col', left_of)  4.01 us
    max x2, other arithmetic, hidden_of(): active = jnp.maximum(extended_input, jnp.zeros((), extended_input.dtype))  3.63 us
  transfers between devices with their start and end apart: 8, of which 4 were waited for; matrix products, arithmetic and copies ran while one was open for 6% of the time, Pallas kernels for 0%

profile of v16, /device:TPU:7, one launch (start us, length us, event | category | flops | bytes accessed | tf_op | source)
XLA Modules:
  0.0 172.1 jit_solution(16576472568387368056)
XLA Ops:
  0.0 1.7 copy.19
  1.7 4.4 %collective-permute-start = (bf16[48,8,128]{2,0,1:T(8,128)(2,1)S(1)}, bf16[48,8,128]{2,0,1:T(8,128)(2,1)S(1)}, u32[]{:S(2)}, u32[]{:S(2)}) collective-permute-start(bf16[48,8,128]{2,0,1:T(8,128)(2,1)S(1)} %get-tuple-element.11), channel_id=1, source_target_pairs={{0,16},{16,32},{32,48},{48,64},{64,80},{80,96},{96,112},{112,128},... | collective-permute-start | bytes 294920 | tf_op jit(solution)/shard_map/ppermute | solution.py:91
  6.1 2.4 %collective-permute-start.1 = (bf16[48,8,128]{2,0,1:T(8,128)(2,1)S(1)}, bf16[48,8,128]{2,0,1:T(8,128)(2,1)S(1)}, u32[]{:S(2)}, u32[]{:S(2)}) collective-permute-start(bf16[48,8,128]{2,0,1:T(8,128)(2,1)S(1)} %get-tuple-element.12), channel_id=1, source_target_pairs={{16,0},{32,16},{48,32},{64,48},{80,64},{96,80},{112,96},{128,112},... | collective-permute-start | bytes 294920 | tf_op jit(solution)/shard_map/ppermute | solution.py:92
  8.5 1.7 %fusion.48 = (bf16[48,64,8]{2,1,0:T(8,128)(2,1)S(1)}, bf16[48,64,8]{2,1,0:T(8,128)(2,1)S(1)}) fusion(bf16[48,64,128]{2,1,0:T(8,128)(2,1)} %param.5), kind=kLoop, calls=%fused_computation.92 | loop fusion | bytes 196608 | tf_op jit(solution)/shard_map/slice | solution.py:99
  11.6 2.3 %collective-permute-done.1 = bf16[48,8,128]{2,0,1:T(8,128)(2,1)S(1)} collective-permute-done((bf16[48,8,128]{2,0,1:T(8,128)(2,1)S(1)}, bf16[48,8,128]{2,0,1:T(8,128)(2,1)S(1)}, u32[]{:S(2)}, u32[]{:S(2)}) %collective-permute-start.1) | collective-permute-done | bytes 98336 | tf_op jit(solution)/shard_map/ppermute | solution.py:92
  14.9 4.0 %collective-permute-start.3 = (bf16[48,80,8]{1,2,0:T(8,128)(2,1)S(1)}, bf16[48,80,8]{1,2,0:T(8,128)(2,1)S(1)}, u32[]{:S(2)}, u32[]{:S(2)}) collective-permute-start(bf16[48,80,8]{1,2,0:T(8,128)(2,1)S(1)} %pad_maximum_fusion.3), channel_id=1, source_target_pairs={{1,0},{2,1},{3,2},{4,3},{5,4},{6,5},{7,6},{8,7},{9,8},{10,9},{11,1... | collective-permute-start | bytes 184328 | tf_op jit(solution)/shard_map/ppermute | solution.py:100
  19.1 2.5 %collective-permute-start.2 = (bf16[48,80,8]{1,2,0:T(8,128)(2,1)S(1)}, bf16[48,80,8]{1,2,0:T(8,128)(2,1)S(1)}, u32[]{:S(2)}, u32[]{:S(2)}) collective-permute-start(bf16[48,80,8]{1,2,0:T(8,128)(2,1)S(1)} %pad_maximum_fusion.2), channel_id=1, source_target_pairs={{0,1},{1,2},{2,3},{3,4},{4,5},{5,6},{6,7},{7,8},{8,9},{9,10},{10,1... | collective-permute-start | bytes 184328 | tf_op jit(solution)/shard_map/ppermute | solution.py:99
  22.1 1.1 collective-permute-done.2
  24.6 1.4 maximum_maximum_fusion.1
  29.0 1.7 fusion.15
  31.4 0.9 copy.39
  32.3 0.7 reshape.42
  33.1 19.7 %all_to_all.15 = bf16[16,192,128]{2,1,0:T(8,128)(2,1)S(1)} all-to-all(bf16[16,192,128]{2,1,0:T(8,128)(2,1)S(1)} %reshape.42), channel_id=1, replica_groups=mesh['row'=32,'col'=16] {'col'}, dimensions={0} | all-to-all | bytes 1572864 | tf_op jit(solution)/shard_map/all_to_all | solution.py:60
  52.9 60.5 %all_to_all.16 = bf16[32,96,128]{2,1,0:T(8,128)(2,1)S(1)} all-to-all(bf16[32,96,128]{2,1,0:T(8,128)(2,1)S(1)} %bitcast.184), channel_id=1, replica_groups=mesh['row'=32,'col'=16] {'row'}, dimensions={0} | all-to-all | bytes 1572864 | tf_op jit(solution)/shard_map/all_to_all | solution.py:63
  113.4 17.1 %all_to_all.17 = bf16[16,192,128]{2,1,0:T(8,128)(2,1)S(1)} all-to-all(bf16[16,192,128]{2,1,0:T(8,128)(2,1)S(1)} %bitcast.185), channel_id=1, replica_groups=mesh['row'=32,'col'=16] {'col'}, dimensions={0} | all-to-all | bytes 1572864 | tf_op jit(solution)/shard_map/all_to_all | solution.py:65
  131.2 1.6 copy.41
  132.9 0.7 reshape.47
  133.6 0.9 copy-done.3
  134.5 1.2 multiply_convert_fusion.3
  135.6 1.4 multiply_convert_fusion.1
  137.0 2.7 %collective-permute-start.4 = (bf16[48,16,128]{2,0,1:T(8,128)(2,1)S(1)}, bf16[48,16,128]{2,0,1:T(8,128)(2,1)S(1)}, u32[]{:S(2)}, u32[]{:S(2)}) collective-permute-start(bf16[48,16,128]{2,0,1:T(8,128)(2,1)S(1)} %get-tuple-element.5), channel_id=1, source_target_pairs={{0,16},{16,32},{32,48},{48,64},{64,80},{80,96},{96,112},{112,128},... | collective-permute-start | bytes 589832 | tf_op jit(solution)/shard_map/ppermute | solution.py:116
  139.7 4.1 %collective-permute-start.5 = (bf16[48,16,128]{2,0,1:T(8,128)(2,1)S(1)}, bf16[48,16,128]{2,0,1:T(8,128)(2,1)S(1)}, u32[]{:S(2)}, u32[]{:S(2)}) collective-permute-start(bf16[48,16,128]{2,0,1:T(8,128)(2,1)S(1)} %get-tuple-element.6), channel_id=1, source_target_pairs={{16,0},{32,16},{48,32},{64,48},{80,64},{96,80},{112,96},{128,112},... | collective-permute-start | bytes 589832 | tf_op jit(solution)/shard_map/ppermute | solution.py:116
  145.4 4.4 %collective-permute-done.5 = bf16[48,16,128]{2,0,1:T(8,128)(2,1)S(1)} collective-permute-done((bf16[48,16,128]{2,0,1:T(8,128)(2,1)S(1)}, bf16[48,16,128]{2,0,1:T(8,128)(2,1)S(1)}, u32[]{:S(2)}, u32[]{:S(2)}) %collective-permute-start.5) | collective-permute-done | bytes 196640 | tf_op jit(solution)/shard_map/ppermute | solution.py:116
  151.3 3.5 %collective-permute-start.7 = (bf16[48,96,16]{1,2,0:T(8,128)(2,1)S(1)}, bf16[48,96,16]{1,2,0:T(8,128)(2,1)}, u32[]{:S(2)}, u32[]{:S(2)}) collective-permute-start(bf16[48,96,16]{1,2,0:T(8,128)(2,1)S(1)} %pad_maximum_fusion.1), channel_id=1, source_target_pairs={{1,0},{2,1},{3,2},{4,3},{5,4},{6,5},{7,6},{8,7},{9,8},{10,9},{11,1... | collective-permute-start | bytes 442376 | tf_op jit(solution)/shard_map/ppermute | solution.py:128
  154.9 3.2 %collective-permute-start.6 = (bf16[48,96,16]{1,2,0:T(8,128)(2,1)S(1)}, bf16[48,96,16]{1,2,0:T(8,128)(2,1)S(1)}, u32[]{:S(2)}, u32[]{:S(2)}) collective-permute-start(bf16[48,96,16]{1,2,0:T(8,128)(2,1)S(1)} %pad_maximum_fusion), channel_id=1, source_target_pairs={{0,1},{1,2},{2,3},{3,4},{4,5},{5,6},{6,7},{7,8},{8,9},{9,10},{10,1... | collective-permute-start | bytes 442376 | tf_op jit(solution)/shard_map/ppermute | solution.py:127
  158.2 0.7 copy.42
  159.0 0.8 copy.43
  160.5 0.9 copy.50
  161.4 1.8 %copy.51 = bf16[48,96,16]{2,0,1:T(8,128)(2,1)S(1)} copy(bf16[48,96,16]{1,2,0:T(8,128)(2,1)} %collective-permute-done.7) | data formatting | bytes 294912 | tf_op jit(solution)/shard_map/ppermute | solution.py:128
  163.2 2.3 %maximum_maximum_fusion = bf16[48,96,160]{2,0,1:T(8,128)(2,1)S(1)} fusion(bf16[48,96,16]{2,0,1:T(8,128)(2,1)S(1)} %copy.51, bf16[48,16,128]{2,0,1:T(8,128)(2,1)S(1)} %collective-permute-done.5, bf16[48,64,128]{2,0,1:T(8,128)(2,1)S(1)} %multiply_convert_fusion.1, bf16[48,16,128]{2,0,1:T(8,128)(2,1)S(1)} %collective-permute-done.4, bf16[48,96,16]{2,0,1:T(8,128)(2,1)S(1)} %copy.50), kind=kLoop, calls=%fused_computation.4 | loop fusion | flops 8847360 | bytes 2949120 | tf_op jit(solution)/shard_map/max | solution.py:24
  168.5 1.4 fusion.2
  171.0 1.1 copy.53
  (83 shorter events, 16.8 us)
Async XLA Ops:
  0.0 10.3 %copy-start.8 = (bf16[2,3,3,48,48]{4,3,2,1,0:T(8,128)(2,1)S(1)}, bf16[2,3,3,48,48]{4,3,2,1,0:T(8,128)(2,1)}, u32[]{:S(2)}) copy-start(bf16[2,3,3,48,48]{4,3,2,1,0:T(8,128)(2,1)} %param.6) | copy-start | bytes 248836
  1.7 12.6 %collective-permute-start = (bf16[48,8,128]{2,0,1:T(8,128)(2,1)S(1)}, bf16[48,8,128]{2,0,1:T(8,128)(2,1)S(1)}, u32[]{:S(2)}, u32[]{:S(2)}) collective-permute-start(bf16[48,8,128]{2,0,1:T(8,128)(2,1)S(1)} %get-tuple-element.11), channel_id=1, source_target_pairs={{0,16},{16,32},{32,48},{48,64},{64,80},{80,96},{96,112},{112,128},... | collective-permute-start | bytes 294920 | tf_op jit(solution)/shard_map/ppermute | solution.py:91
  6.1 15.4 %copy-start.9 = (f32[2,2,48]{2,1,0:T(2,128)S(1)}, f32[2,2,48]{2,1,0:T(2,128)}, u32[]{:S(2)}) copy-start(f32[2,2,48]{2,1,0:T(2,128)} %param.9) | copy-start | bytes 2308
  6.1 15.4 %copy-start.10 = (f32[2,2,48]{2,1,0:T(2,128)S(1)}, f32[2,2,48]{2,1,0:T(2,128)}, u32[]{:S(2)}) copy-start(f32[2,2,48]{2,1,0:T(2,128)} %param.8) | copy-start | bytes 2308
  6.1 7.8 %collective-permute-start.1 = (bf16[48,8,128]{2,0,1:T(8,128)(2,1)S(1)}, bf16[48,8,128]{2,0,1:T(8,128)(2,1)S(1)}, u32[]{:S(2)}, u32[]{:S(2)}) collective-permute-start(bf16[48,8,128]{2,0,1:T(8,128)(2,1)S(1)} %get-tuple-element.12), channel_id=1, source_target_pairs={{16,0},{32,16},{48,32},{64,48},{80,64},{96,80},{112,96},{128,112},... | collective-permute-start | bytes 294920 | tf_op jit(solution)/shard_map/ppermute | solution.py:92
  14.9 9.0 %collective-permute-start.3 = (bf16[48,80,8]{1,2,0:T(8,128)(2,1)S(1)}, bf16[48,80,8]{1,2,0:T(8,128)(2,1)S(1)}, u32[]{:S(2)}, u32[]{:S(2)}) collective-permute-start(bf16[48,80,8]{1,2,0:T(8,128)(2,1)S(1)} %pad_maximum_fusion.3), channel_id=1, source_target_pairs={{1,0},{2,1},{3,2},{4,3},{5,4},{6,5},{7,6},{8,7},{9,8},{10,9},{11,1... | collective-permute-start | bytes 184328 | tf_op jit(solution)/shard_map/ppermute | solution.py:100
  19.1 4.1 %collective-permute-start.2 = (bf16[48,80,8]{1,2,0:T(8,128)(2,1)S(1)}, bf16[48,80,8]{1,2,0:T(8,128)(2,1)S(1)}, u32[]{:S(2)}, u32[]{:S(2)}) collective-permute-start(bf16[48,80,8]{1,2,0:T(8,128)(2,1)S(1)} %pad_maximum_fusion.2), channel_id=1, source_target_pairs={{0,1},{1,2},{2,3},{3,4},{4,5},{5,6},{6,7},{7,8},{8,9},{9,10},{10,1... | collective-permute-start | bytes 184328 | tf_op jit(solution)/shard_map/ppermute | solution.py:99
  29.0 1.7 %copy-start = (bf16[48,64,128]{2,1,0:T(8,128)(2,1)S(1)}, bf16[48,64,128]{2,1,0:T(8,128)(2,1)}, u32[]{:S(2)}) copy-start(bf16[48,64,128]{2,1,0:T(8,128)(2,1)} %param.5) | copy-start | bytes 2359300
  29.0 1.7 %copy-start.12 = (bf16[2,48,48]{2,1,0:T(8,128)(2,1)S(1)}, bf16[2,48,48]{2,1,0:T(8,128)(2,1)}, u32[]{:S(2)}) copy-start(bf16[2,48,48]{2,1,0:T(8,128)(2,1)} %param.7) | copy-start | bytes 27652
  31.4 21.4 %copy-start.1 = (bf16[48,64,128]{2,0,1:T(8,128)(2,1)}, bf16[48,64,128]{2,0,1:T(8,128)(2,1)S(1)}, u32[]{:S(2)}) copy-start(bf16[48,64,128]{2,0,1:T(8,128)(2,1)S(1)} %fusion.11) | copy-start | bytes 2359300
  132.8 2.8 %copy-start.2 = (bf16[48,64,128]{2,0,1:T(8,128)(2,1)S(1)}, bf16[48,64,128]{2,0,1:T(8,128)(2,1)}, u32[]{:S(2)}) copy-start(bf16[48,64,128]{2,0,1:T(8,128)(2,1)} %copy-done.1) | copy-start | bytes 2359300
  133.6 0.9 copy-start.3
  137.0 13.4 %collective-permute-start.4 = (bf16[48,16,128]{2,0,1:T(8,128)(2,1)S(1)}, bf16[48,16,128]{2,0,1:T(8,128)(2,1)S(1)}, u32[]{:S(2)}, u32[]{:S(2)}) collective-permute-start(bf16[48,16,128]{2,0,1:T(8,128)(2,1)S(1)} %get-tuple-element.5), channel_id=1, source_target_pairs={{0,16},{16,32},{32,48},{48,64},{64,80},{80,96},{96,112},{112,128},... | collective-permute-start | bytes 589832 | tf_op jit(solution)/shard_map/ppermute | solution.py:116
  139.7 10.2 %collective-permute-start.5 = (bf16[48,16,128]{2,0,1:T(8,128)(2,1)S(1)}, bf16[48,16,128]{2,0,1:T(8,128)(2,1)S(1)}, u32[]{:S(2)}, u32[]{:S(2)}) collective-permute-start(bf16[48,16,128]{2,0,1:T(8,128)(2,1)S(1)} %get-tuple-element.6), channel_id=1, source_target_pairs={{16,0},{32,16},{48,32},{64,48},{80,64},{96,80},{112,96},{128,112},... | collective-permute-start | bytes 589832 | tf_op jit(solution)/shard_map/ppermute | solution.py:116
  144.1 14.1 %copy-start.5 = (bf16[1,3,3,48,48]{4,3,2,1,0:T(8,128)(2,1)S(1)}, bf16[1,3,3,48,48]{4,3,2,1,0:T(8,128)(2,1)}, u32[]{:S(2)}) copy-start(bf16[1,3,3,48,48]{4,3,2,1,0:T(8,128)(2,1)} %get-tuple-element.13) | copy-start | bytes 124420
  144.8 14.2 %copy-start.4 = (bf16[3,3,48,48]{3,2,0,1:T(8,128)(2,1)S(1)}, bf16[3,3,48,48]{3,2,0,1:T(8,128)(2,1)}, u32[]{:S(2)}) copy-start(bf16[3,3,48,48]{3,2,0,1:T(8,128)(2,1)} %get-tuple-element.14) | copy-start | bytes 124420
  144.8 15.0 %copy-start.11 = (f32[48]{0:T(128)S(1)}, f32[48]{0:T(128)}, u32[]{:S(2)}) copy-start(f32[48]{0:T(128)} %get-tuple-element.32) | copy-start | bytes 580
  151.3 10.2 %collective-permute-start.7 = (bf16[48,96,16]{1,2,0:T(8,128)(2,1)S(1)}, bf16[48,96,16]{1,2,0:T(8,128)(2,1)}, u32[]{:S(2)}, u32[]{:S(2)}) collective-permute-start(bf16[48,96,16]{1,2,0:T(8,128)(2,1)S(1)} %pad_maximum_fusion.1), channel_id=1, source_target_pairs={{1,0},{2,1},{3,2},{4,3},{5,4},{6,5},{7,6},{8,7},{9,8},{10,9},{11,1... | collective-permute-start | bytes 442376 | tf_op jit(solution)/shard_map/ppermute | solution.py:128
  154.9 5.6 %collective-permute-start.6 = (bf16[48,96,16]{1,2,0:T(8,128)(2,1)S(1)}, bf16[48,96,16]{1,2,0:T(8,128)(2,1)S(1)}, u32[]{:S(2)}, u32[]{:S(2)}) collective-permute-start(bf16[48,96,16]{1,2,0:T(8,128)(2,1)S(1)} %pad_maximum_fusion), channel_id=1, source_target_pairs={{0,1},{1,2},{2,3},{3,4},{4,5},{5,6},{6,7},{7,8},{8,9},{9,10},{10,1... | collective-permute-start | bytes 442376 | tf_op jit(solution)/shard_map/ppermute | solution.py:127
  167.1 1.4 copy-start.6
  167.1 1.4 copy-start.7
  168.5 1.5 copy-start.13

commit v17 on v15

--- a/solution.py
+++ b/solution.py
@@ -87,12 +87,14 @@
     hidden = hidden_of(
         extended, kernel, norm_gain[0, 0], norm_bias[0, 0], FIRST_DILATION, tile_rows, tile_cols
     )
-    hidden = lax.optimization_barrier(hidden)
+    kernel = w_dilated[1]
+    both = jnp.concatenate([kernel, jnp.swapaxes(kernel, 0, 1)], axis=2).reshape(9, 2 * count, count)
+    gain = jnp.concatenate([norm_gain[1, 0], norm_gain[1, 0]])
+    bias = jnp.concatenate([norm_bias[1, 0], norm_bias[1, 0]])
+    hidden, both, gain, bias = lax.optimization_barrier((hidden, both, gain, bias))
     output_map = block_output(features, hidden, norm_gain[0], norm_bias[0], w_pointwise[0])
     state, head, tail = symmetrized(output_map, SECOND_DILATION)
 
-    kernel = w_dilated[1]
-    both = jnp.concatenate([kernel, jnp.swapaxes(kernel, 0, 1)], axis=2).reshape(9, 2 * count, count)
     n_row = lax.axis_size("row")
     up = [(i, i + 1) for i in range(n_row - 1)]
     down = [(j, i) for i, j in up]
@@ -111,8 +113,6 @@
     after = lax.ppermute(initial, "col", left_of)
     rows = jnp.concatenate([above, state, below], axis=1)
     extended = jnp.concatenate([before, rows, after], axis=2)
-    gain = jnp.concatenate([norm_gain[1, 0], norm_gain[1, 0]])
-    bias = jnp.concatenate([norm_bias[1, 0], norm_bias[1, 0]])
     hidden = hidden_of(extended, both, gain, bias, SECOND_DILATION, tile_rows, tile_cols)
     direct = block_output(state, hidden[:count], norm_gain[1], norm_bias[1], w_pointwise[1])
     mirrored = block_output(state, hidden[count:], norm_gain[1], norm_bias[1], w_pointwise[1])

time: 174 us -> 174 us (level)
  waiting for transfers between devices: 8.34 us -> 13.3 us
  local copies, waits for them, and re-layouts: 27.9 us -> 24.8 us
    ppermute x1, waiting for transfers between devices: 0.01 us -> 4.73 us  [body(): after = lax.ppermute(initial, 'col', left_of)]
    unnamed x46 -> x37, local copies, waits for them, and re-layouts: 7.73 us -> 6.56 us
  transfers between devices with their start and end apart: 8 -> 8, of which waited for: 4 -> 5; matrix products, arithmetic and copies ran while one was open for 6% -> 4% of each run, Pallas kernels for 0% -> 0%
where the time goes in v17:
time: 174 us; the launch traced here: 173 us
  blocking collectives  97.4 us (56%)
  starting transfers between devices  25.7 us (15%)
  local copies, waits for them, and re-layouts  24.8 us (14%)
  waiting for transfers between devices  13.3 us (8%)
  other arithmetic  6.41 us (4%)
  matrix products  4.81 us (3%)
    all_to_all x1, blocking collectives, mirror_pieces(): t = lax.all_to_all(t, 'row', 0, 0, tiled=True)  60.5 us
    all_to_all x2, blocking collectives, mirror_pieces(): t = lax.all_to_all(t, 'col', 0, 0, tiled=True)  36.9 us
    ppermute x2, starting transfers between devices, padded(): before = lax.ppermute(last, axis, up)  6.86 us
    unnamed x37, local copies, waits for them, and re-layouts  6.56 us
    ppermute x2, starting transfers between devices, padded(): after = lax.ppermute(initial, axis, down)  6.41 us
    ppermute x1, waiting for transfers between devices, body(): after = lax.ppermute(initial, 'col', left_of)  4.73 us
    ppermute x1, waiting for transfers between devices, body(): lax.ppermute(head, 'row', down)  4.43 us
    ppermute x1, starting transfers between devices, body(): lax.ppermute(head, 'row', down)  4.14 us
  transfers between devices with their start and end apart: 8, of which 5 were waited for; matrix products, arithmetic and copies ran while one was open for 4% of the time, Pallas kernels for 0%

profile of v17, /device:TPU:7, one launch (start us, length us, event | category | flops | bytes accessed | tf_op | source)
XLA Modules:
  0.0 172.9 jit_solution(14228519110664046293)
XLA Ops:
  0.0 1.0 fusion.45
  1.1 4.4 %collective-permute-start = (bf16[48,8,128]{2,0,1:T(8,128)(2,1)S(1)}, bf16[48,8,128]{2,0,1:T(8,128)(2,1)S(1)}, u32[]{:S(2)}, u32[]{:S(2)}) collective-permute-start(bf16[48,8,128]{2,0,1:T(8,128)(2,1)S(1)} %copy.80), channel_id=1, source_target_pairs={{0,16},{16,32},{32,48},{48,64},{64,80},{80,96},{96,112},{112,128},... | collective-permute-start | bytes 294920 | tf_op jit(solution)/shard_map/ppermute | solution.py:17
  5.5 2.4 %collective-permute-start.1 = (bf16[48,8,128]{2,0,1:T(8,128)(2,1)S(1)}, bf16[48,8,128]{2,0,1:T(8,128)(2,1)S(1)}, u32[]{:S(2)}, u32[]{:S(2)}) collective-permute-start(bf16[48,8,128]{2,0,1:T(8,128)(2,1)S(1)} %copy.81), channel_id=1, source_target_pairs={{16,0},{32,16},{48,32},{64,48},{80,64},{96,80},{112,96},{128,112},... | collective-permute-start | bytes 294920 | tf_op jit(solution)/shard_map/ppermute | solution.py:18
  7.9 1.0 fusion.46
  8.9 0.8 slice_bitcast_fusion.18
  11.1 2.2 %collective-permute-done.1 = bf16[48,8,128]{2,0,1:T(8,128)(2,1)S(1)} collective-permute-done((bf16[48,8,128]{2,0,1:T(8,128)(2,1)S(1)}, bf16[48,8,128]{2,0,1:T(8,128)(2,1)S(1)}, u32[]{:S(2)}, u32[]{:S(2)}) %collective-permute-start.1) | collective-permute-done | bytes 98336 | tf_op jit(solution)/shard_map/ppermute | solution.py:18
  13.6 0.8 copy.45
  14.4 0.8 copy.46
  15.2 4.0 %collective-permute-start.3 = (bf16[48,80,8]{1,2,0:T(8,128)(2,1)S(1)}, bf16[48,80,8]{1,2,0:T(8,128)(2,1)S(1)}, u32[]{:S(2)}, u32[]{:S(2)}) collective-permute-start(bf16[48,80,8]{1,2,0:T(8,128)(2,1)S(1)} %copy.46), channel_id=1, source_target_pairs={{1,0},{2,1},{3,2},{4,3},{5,4},{6,5},{7,6},{8,7},{9,8},{10,9},{11,1... | collective-permute-start | bytes 184328 | tf_op jit(solution)/shard_map/ppermute | solution.py:18
  19.2 2.5 %collective-permute-start.2 = (bf16[48,80,8]{1,2,0:T(8,128)(2,1)S(1)}, bf16[48,80,8]{1,2,0:T(8,128)(2,1)S(1)}, u32[]{:S(2)}, u32[]{:S(2)}) collective-permute-start(bf16[48,80,8]{1,2,0:T(8,128)(2,1)S(1)} %copy.45), channel_id=1, source_target_pairs={{0,1},{1,2},{2,3},{3,4},{4,5},{5,6},{6,7},{7,8},{8,9},{9,10},{10,1... | collective-permute-start | bytes 184328 | tf_op jit(solution)/shard_map/ppermute | solution.py:17
  21.8 1.5 collective-permute-done.2
  24.8 1.4 maximum_maximum_fusion.1
  29.2 1.7 fusion.15
  31.6 0.9 copy.59
  33.2 19.7 %all_to_all.15 = bf16[16,192,128]{2,1,0:T(8,128)(2,1)S(1)} all-to-all(bf16[16,192,128]{2,1,0:T(8,128)(2,1)S(1)} %reshape.42), channel_id=1, replica_groups=mesh['row'=32,'col'=16] {'col'}, dimensions={0} | all-to-all | bytes 1572864 | tf_op jit(solution)/shard_map/all_to_all | solution.py:60
  53.0 60.5 %all_to_all.16 = bf16[32,96,128]{2,1,0:T(8,128)(2,1)S(1)} all-to-all(bf16[32,96,128]{2,1,0:T(8,128)(2,1)S(1)} %bitcast.184), channel_id=1, replica_groups=mesh['row'=32,'col'=16] {'row'}, dimensions={0} | all-to-all | bytes 1572864 | tf_op jit(solution)/shard_map/all_to_all | solution.py:63
  113.5 17.1 %all_to_all.17 = bf16[16,192,128]{2,1,0:T(8,128)(2,1)S(1)} all-to-all(bf16[16,192,128]{2,1,0:T(8,128)(2,1)S(1)} %bitcast.185), channel_id=1, replica_groups=mesh['row'=32,'col'=16] {'col'}, dimensions={0} | all-to-all | bytes 1572864 | tf_op jit(solution)/shard_map/all_to_all | solution.py:65
  131.4 1.6 copy.61
  133.0 0.7 reshape.47
  133.8 0.9 copy-done.2
  134.8 1.4 multiply_convert_fusion.1
  136.2 2.7 %collective-permute-start.4 = (bf16[48,16,128]{2,0,1:T(8,128)(2,1)S(1)}, bf16[48,16,128]{2,0,1:T(8,128)(2,1)S(1)}, u32[]{:S(2)}, u32[]{:S(2)}) collective-permute-start(bf16[48,16,128]{2,0,1:T(8,128)(2,1)S(1)} %get-tuple-element.13), channel_id=1, source_target_pairs={{0,16},{16,32},{32,48},{48,64},{64,80},{80,96},{96,112},{112,128},... | collective-permute-start | bytes 589832 | tf_op jit(solution)/shard_map/ppermute | solution.py:101
  138.8 4.1 %collective-permute-start.5 = (bf16[48,16,128]{2,0,1:T(8,128)(2,1)S(1)}, bf16[48,16,128]{2,0,1:T(8,128)(2,1)S(1)}, u32[]{:S(2)}, u32[]{:S(2)}) collective-permute-start(bf16[48,16,128]{2,0,1:T(8,128)(2,1)S(1)} %get-tuple-element.14), channel_id=1, source_target_pairs={{16,0},{32,16},{48,32},{64,48},{80,64},{96,80},{112,96},{128,112},... | collective-permute-start | bytes 589832 | tf_op jit(solution)/shard_map/ppermute | solution.py:101
  144.5 4.4 %collective-permute-done.5 = bf16[48,16,128]{2,0,1:T(8,128)(2,1)S(1)} collective-permute-done((bf16[48,16,128]{2,0,1:T(8,128)(2,1)S(1)}, bf16[48,16,128]{2,0,1:T(8,128)(2,1)S(1)}, u32[]{:S(2)}, u32[]{:S(2)}) %collective-permute-start.5) | collective-permute-done | bytes 196640 | tf_op jit(solution)/shard_map/ppermute | solution.py:101
  150.4 3.7 %collective-permute-start.6 = (bf16[48,96,16]{1,2,0:T(8,128)(2,1)S(1)}, bf16[48,96,16]{1,2,0:T(8,128)(2,1)S(1)}, u32[]{:S(2)}, u32[]{:S(2)}) collective-permute-start(bf16[48,96,16]{1,2,0:T(8,128)(2,1)S(1)} %pad_maximum_fusion.1), channel_id=1, source_target_pairs={{0,1},{1,2},{2,3},{3,4},{4,5},{5,6},{6,7},{7,8},{8,9},{9,10},{10,1... | collective-permute-start | bytes 442376 | tf_op jit(solution)/shard_map/ppermute | solution.py:112
  154.3 1.9 %collective-permute-start.7 = (bf16[48,96,16]{1,2,0:T(8,128)(2,1)S(1)}, bf16[48,96,16]{1,2,0:T(8,128)(2,1)}, u32[]{:S(2)}, u32[]{:S(2)}) collective-permute-start(bf16[48,96,16]{1,2,0:T(8,128)(2,1)S(1)} %pad_maximum_fusion.2), channel_id=1, source_target_pairs={{1,0},{2,1},{3,2},{4,3},{5,4},{6,5},{7,6},{8,7},{9,8},{10,9},{11,1... | collective-permute-start | bytes 442376 | tf_op jit(solution)/shard_map/ppermute | solution.py:113
  156.7 0.9 copy.68
  157.6 4.7 %collective-permute-done.7 = bf16[48,96,16]{1,2,0:T(8,128)(2,1)} collective-permute-done((bf16[48,96,16]{1,2,0:T(8,128)(2,1)S(1)}, bf16[48,96,16]{1,2,0:T(8,128)(2,1)}, u32[]{:S(2)}, u32[]{:S(2)}) %collective-permute-start.7) | collective-permute-done | bytes 147488 | tf_op jit(solution)/shard_map/ppermute | solution.py:113
  162.3 1.8 %copy.69 = bf16[48,96,16]{2,0,1:T(8,128)(2,1)S(1)} copy(bf16[48,96,16]{1,2,0:T(8,128)(2,1)} %collective-permute-done.7) | data formatting | bytes 294912 | tf_op jit(solution)/shard_map/ppermute | solution.py:113
  164.1 2.3 %maximum_maximum_fusion = bf16[48,96,160]{2,0,1:T(8,128)(2,1)S(1)} fusion(bf16[48,96,16]{2,0,1:T(8,128)(2,1)S(1)} %copy.69, bf16[48,16,128]{2,0,1:T(8,128)(2,1)S(1)} %collective-permute-done.5, bf16[48,64,128]{2,0,1:T(8,128)(2,1)S(1)} %multiply_convert_fusion.1, bf16[48,16,128]{2,0,1:T(8,128)(2,1)S(1)} %collective-permute-done.4, bf16[48,96,16]{2,0,1:T(8,128)(2,1)S(1)} %copy.68), kind=kLoop, calls=%fused_computation.4 | loop fusion | flops 8847360 | bytes 2949120 | tf_op jit(solution)/shard_map/max | solution.py:24
  169.3 1.4 fusion.2
  171.8 1.1 copy.72
  (67 shorter events, 16.1 us)
Async XLA Ops:
  0.0 10.5 %copy-start.3 = (bf16[48,64,128]{2,1,0:T(8,128)(2,1)S(1)}, bf16[48,64,128]{2,1,0:T(8,128)(2,1)}, u32[]{:S(2)}) copy-start(bf16[48,64,128]{2,1,0:T(8,128)(2,1)} %param.5) | copy-start | bytes 2359300
  1.1 9.4 %collective-permute-start = (bf16[48,8,128]{2,0,1:T(8,128)(2,1)S(1)}, bf16[48,8,128]{2,0,1:T(8,128)(2,1)S(1)}, u32[]{:S(2)}, u32[]{:S(2)}) collective-permute-start(bf16[48,8,128]{2,0,1:T(8,128)(2,1)S(1)} %copy.80), channel_id=1, source_target_pairs={{0,16},{16,32},{32,48},{48,64},{64,80},{80,96},{96,112},{112,128},... | collective-permute-start | bytes 294920 | tf_op jit(solution)/shard_map/ppermute | solution.py:17
  5.5 7.8 %collective-permute-start.1 = (bf16[48,8,128]{2,0,1:T(8,128)(2,1)S(1)}, bf16[48,8,128]{2,0,1:T(8,128)(2,1)S(1)}, u32[]{:S(2)}, u32[]{:S(2)}) collective-permute-start(bf16[48,8,128]{2,0,1:T(8,128)(2,1)S(1)} %copy.81), channel_id=1, source_target_pairs={{16,0},{32,16},{48,32},{64,48},{80,64},{96,80},{112,96},{128,112},... | collective-permute-start | bytes 294920 | tf_op jit(solution)/shard_map/ppermute | solution.py:18
  15.2 8.8 %collective-permute-start.3 = (bf16[48,80,8]{1,2,0:T(8,128)(2,1)S(1)}, bf16[48,80,8]{1,2,0:T(8,128)(2,1)S(1)}, u32[]{:S(2)}, u32[]{:S(2)}) collective-permute-start(bf16[48,80,8]{1,2,0:T(8,128)(2,1)S(1)} %copy.46), channel_id=1, source_target_pairs={{1,0},{2,1},{3,2},{4,3},{5,4},{6,5},{7,6},{8,7},{9,8},{10,9},{11,1... | collective-permute-start | bytes 184328 | tf_op jit(solution)/shard_map/ppermute | solution.py:18
  19.2 4.1 %collective-permute-start.2 = (bf16[48,80,8]{1,2,0:T(8,128)(2,1)S(1)}, bf16[48,80,8]{1,2,0:T(8,128)(2,1)S(1)}, u32[]{:S(2)}, u32[]{:S(2)}) collective-permute-start(bf16[48,80,8]{1,2,0:T(8,128)(2,1)S(1)} %copy.45), channel_id=1, source_target_pairs={{0,1},{1,2},{2,3},{3,4},{4,5},{5,6},{6,7},{7,8},{8,9},{9,10},{10,1... | collective-permute-start | bytes 184328 | tf_op jit(solution)/shard_map/ppermute | solution.py:17
  29.1 1.7 %copy-start.4 = (bf16[48,64,128]{2,1,0:T(8,128)(2,1)S(1)}, bf16[48,64,128]{2,1,0:T(8,128)(2,1)}, u32[]{:S(2)}) copy-start(bf16[48,64,128]{2,1,0:T(8,128)(2,1)} %param.5) | copy-start | bytes 2359300
  29.1 1.7 copy-start.6
  31.5 1.7 copy-start
  133.0 1.6 copy-start.1
  133.7 0.9 copy-start.2
  136.2 13.4 %collective-permute-start.4 = (bf16[48,16,128]{2,0,1:T(8,128)(2,1)S(1)}, bf16[48,16,128]{2,0,1:T(8,128)(2,1)S(1)}, u32[]{:S(2)}, u32[]{:S(2)}) collective-permute-start(bf16[48,16,128]{2,0,1:T(8,128)(2,1)S(1)} %get-tuple-element.13), channel_id=1, source_target_pairs={{0,16},{16,32},{32,48},{48,64},{64,80},{80,96},{96,112},{112,128},... | collective-permute-start | bytes 589832 | tf_op jit(solution)/shard_map/ppermute | solution.py:101
  138.8 10.2 %collective-permute-start.5 = (bf16[48,16,128]{2,0,1:T(8,128)(2,1)S(1)}, bf16[48,16,128]{2,0,1:T(8,128)(2,1)S(1)}, u32[]{:S(2)}, u32[]{:S(2)}) collective-permute-start(bf16[48,16,128]{2,0,1:T(8,128)(2,1)S(1)} %get-tuple-element.14), channel_id=1, source_target_pairs={{16,0},{32,16},{48,32},{64,48},{80,64},{96,80},{112,96},{128,112},... | collective-permute-start | bytes 589832 | tf_op jit(solution)/shard_map/ppermute | solution.py:101
  150.4 6.3 %collective-permute-start.6 = (bf16[48,96,16]{1,2,0:T(8,128)(2,1)S(1)}, bf16[48,96,16]{1,2,0:T(8,128)(2,1)S(1)}, u32[]{:S(2)}, u32[]{:S(2)}) collective-permute-start(bf16[48,96,16]{1,2,0:T(8,128)(2,1)S(1)} %pad_maximum_fusion.1), channel_id=1, source_target_pairs={{0,1},{1,2},{2,3},{3,4},{4,5},{5,6},{6,7},{7,8},{8,9},{9,10},{10,1... | collective-permute-start | bytes 442376 | tf_op jit(solution)/shard_map/ppermute | solution.py:112
  154.3 8.0 %collective-permute-start.7 = (bf16[48,96,16]{1,2,0:T(8,128)(2,1)S(1)}, bf16[48,96,16]{1,2,0:T(8,128)(2,1)}, u32[]{:S(2)}, u32[]{:S(2)}) collective-permute-start(bf16[48,96,16]{1,2,0:T(8,128)(2,1)S(1)} %pad_maximum_fusion.2), channel_id=1, source_target_pairs={{1,0},{2,1},{3,2},{4,3},{5,4},{6,5},{7,6},{8,7},{9,8},{10,9},{11,1... | collective-permute-start | bytes 442376 | tf_op jit(solution)/shard_map/ppermute | solution.py:113
  168.3 1.0 copy-start.5
  169.3 1.4 copy-start.7
